TPU v7x, 512 devices: a whole 4x8x8 slice. The times are simulated.
512 devices in a mesh: dp: 32 (over z, y_lo, core), feat: 16 (over y_hi, x).
Axes of the slice: x: 4, y: 8 (y_hi: 4, y_lo: 2; y = y_hi * 2 + y_lo), z: 8, core: 2. Of those that a mesh axis runs over, the one named last changes fastest.
Arguments:
- tokens: bfloat16 [8192, 8192], P('dp', 'feat'), may hold values from -6 to 6
- up_left: bfloat16 [16, 512, 2048], P('feat', 'dp'), may hold values from -0.25 to 0.25
- up_right: bfloat16 [2048, 16, 16], P('feat'), may hold values from -1.5 to 1.5
- down_left: bfloat16 [16, 2048, 512], P('feat', 'dp'), may hold values from -0.125 to 0.125
- down_right: bfloat16 [512, 16, 16], P('feat'), may hold values from -1.5 to 1.5
- layer_grad: bfloat16 [8192, 8192], P('dp', 'feat'), may hold values from -6 to 6
Outputs:
- layer_out: bfloat16 [8192, 8192], P('dp', 'feat')
- grad_tokens: bfloat16 [8192, 8192], P('dp', 'feat')
- grad_up_left: float32 [16, 512, 2048], P('feat', 'dp')
- grad_up_right: float32 [2048, 16, 16], P('feat')
- grad_down_left: float32 [16, 2048, 512], P('feat', 'dp')
- grad_down_right: float32 [512, 16, 16], P('feat')
All inputs are finite; a program needn't handle non-finite values.
Results may differ from a plain program's by a relative error of at most 0.0067.
Values may be sent and summed in bfloat16 or wider, within the bound.
No kernel may reach another device: no remote copies, remote signals or barrier semaphores. Data moves between devices by JAX's collectives and lax.ppermute only.
A program may use at most 128 MiB of HBM per device.

v0:
```python
import jax
import jax.numpy as jnp
from jax import lax
from jax.sharding import PartitionSpec as P

TILE_UP = 128
TILE_DOWN = 32


def partner(value, axis, stride):
    mask = 2**stride
    pairs = [(source, source ^ mask) for source in range(lax.axis_size(axis))]
    return lax.ppermute(value, axis, pairs)


def permute_blocks(block_set):
    tok_rows, feat_count, line_len = block_set.shape
    my_index = lax.axis_index("feat")
    buffer = block_set
    for section in range(feat_count.bit_length() - 1):
        half_span = 1 << section
        keep_lower = my_index // half_span % 2 == 0
        shaped = buffer.reshape(tok_rows, feat_count // (2 * half_span), 2, half_span, line_len)
        low_half = shaped[:, :, 0]
        high_half = shaped[:, :, 1]
        outgoing = jnp.where(keep_lower, high_half, low_half)
        incoming = partner(outgoing, "feat", section)
        low_half = jnp.where(keep_lower, low_half, incoming)
        high_half = jnp.where(keep_lower, incoming, high_half)
        buffer = jnp.stack([low_half, high_half], axis=2).reshape(tok_rows, feat_count, line_len)
    return buffer


def to_wire(blocks, feat_count):
    tok_rows, local_blocks, full_width = blocks.shape
    piece = full_width // feat_count
    shaped = blocks.reshape(tok_rows, local_blocks, feat_count, piece).transpose(0, 2, 1, 3)
    return shaped.reshape(tok_rows, feat_count, local_blocks * piece)


def from_wire(wired, local_blocks):
    tok_rows, feat_count, line_len = wired.shape
    piece = line_len // local_blocks
    shaped = wired.reshape(tok_rows, feat_count, local_blocks, piece).transpose(0, 2, 1, 3)
    return shaped.reshape(tok_rows, local_blocks, feat_count * piece)


def on_device(tokens, up_left, up_right, down_left, down_right, layer_grad):
    tok_rows = tokens.shape[0]
    local_blocks = up_left.shape[0]
    hidden_width = up_left.shape[2]
    block_width = down_left.shape[2]
    blocks_all = up_right.shape[1]
    group_up = up_right.shape[0]
    group_down = down_right.shape[0]
    feat_count = lax.axis_size("feat")
    grad_scale = float(tok_rows * lax.axis_size("dp")) ** (-0.5)
    tiles_up = group_up // TILE_UP
    tiles_down = group_down // TILE_DOWN
    up_full = lax.all_gather(up_left, "dp", axis=1, tiled=True)
    token_blocks = tokens.reshape(tok_rows, local_blocks, block_width)
    up_inner = jnp.einsum(
        "tbi,big->tbg", token_blocks, up_full, preferred_element_type=jnp.float32
    ).astype(jnp.bfloat16)
    up_mixed = permute_blocks(to_wire(up_inner, feat_count))
    preact = jnp.einsum("tjg,gjk->tkg", up_mixed, up_right, preferred_element_type=jnp.float32)
    sigmoid_val = jax.nn.sigmoid(preact)
    activated = (
        (preact * sigmoid_val)
        .reshape(tok_rows, blocks_all, tiles_up, TILE_UP)
        .transpose(0, 2, 1, 3)
    )
    hidden = activated.reshape(tok_rows, local_blocks, hidden_width).astype(jnp.bfloat16)
    down_full = lax.all_gather(down_left, "dp", axis=1, tiled=True)
    down_inner = jnp.einsum(
        "tbh,bhc->tbc", hidden, down_full, preferred_element_type=jnp.float32
    ).astype(jnp.bfloat16)
    down_mixed = permute_blocks(to_wire(down_inner, feat_count)).reshape(
        tok_rows, blocks_all * group_down
    )
    identity = jnp.eye(group_down, dtype=jnp.bfloat16).reshape(group_down, tiles_down, TILE_DOWN)
    mix_matrix = jnp.einsum(
        "cjk,cal->jcakl", down_right, identity, preferred_element_type=jnp.float32
    )
    mix_matrix = mix_matrix.astype(jnp.bfloat16).reshape(
        blocks_all * group_down, blocks_all * group_down
    )
    layer_out = jnp.dot(down_mixed, mix_matrix, preferred_element_type=jnp.float32).astype(
        jnp.bfloat16
    )
    grad_down_mixed = lax.dot_general(
        layer_grad, mix_matrix, (((1,), (1,)), ((), ())), preferred_element_type=jnp.float32
    ).astype(jnp.bfloat16)
    grad_by_group = layer_grad.reshape(tok_rows, tiles_down, blocks_all, TILE_DOWN).transpose(
        0, 2, 1, 3
    )
    grad_by_group = grad_by_group.reshape(tok_rows, blocks_all, group_down)
    right_down_term = (
        jnp.einsum(
            "tjc,tkc->cjk",
            down_mixed.reshape(tok_rows, blocks_all, group_down),
            grad_by_group,
            preferred_element_type=jnp.float32,
        )
        * grad_scale
    )
    grad_down_inner = from_wire(
        permute_blocks(grad_down_mixed.reshape(tok_rows, feat_count, local_blocks * group_down)),
        local_blocks,
    )
    part = hidden
    grad_down_left = lax.psum_scatter(
        jnp.einsum("tbh,tbc->hbc", part, grad_down_inner, preferred_element_type=jnp.float32)
        * grad_scale,
        "dp",
        scatter_dimension=0,
        tiled=True,
    ).transpose(1, 0, 2)
    grad_hidden = jnp.einsum(
        "tbc,bhc->tbh", grad_down_inner, down_full, preferred_element_type=jnp.float32
    )
    grad_hidden = grad_hidden.reshape(tok_rows, tiles_up, blocks_all, TILE_UP).transpose(0, 2, 1, 3)
    grad_hidden = grad_hidden.reshape(tok_rows, blocks_all, group_up)
    grad_preact = (grad_hidden * sigmoid_val * (1.0 + preact * (1.0 - sigmoid_val))).astype(
        jnp.bfloat16
    )
    grad_up_mixed = jnp.einsum(
        "tkg,gjk->tjg", grad_preact, up_right, preferred_element_type=jnp.float32
    ).astype(jnp.bfloat16)
    right_up_term = (
        jnp.einsum("tjg,tkg->gjk", up_mixed, grad_preact, preferred_element_type=jnp.float32)
        * grad_scale
    )
    grad_up_inner = from_wire(permute_blocks(grad_up_mixed), local_blocks)
    grad_tokens = jnp.einsum(
        "tbg,big->tbi", grad_up_inner, up_full, preferred_element_type=jnp.float32
    ).astype(jnp.bfloat16)
    grad_tokens = grad_tokens.reshape(tok_rows, local_blocks * block_width)
    part = token_blocks
    grad_up_left = lax.psum_scatter(
        jnp.einsum("tbi,tbg->ibg", part, grad_up_inner, preferred_element_type=jnp.float32)
        * grad_scale,
        "dp",
        scatter_dimension=0,
        tiled=True,
    ).transpose(1, 0, 2)
    grad_up_right, grad_down_right = lax.psum((right_up_term, right_down_term), "dp")
    return (layer_out, grad_tokens, grad_up_left, grad_up_right, grad_down_left, grad_down_right)


def solution(mesh):
    return jax.shard_map(
        on_device,
        mesh=mesh,
        in_specs=(
            P("dp", "feat"),
            P("feat", "dp", None),
            P("feat", None, None),
            P("feat", "dp", None),
            P("feat", None, None),
            P("dp", "feat"),
        ),
        out_specs=(
            P("dp", "feat"),
            P("dp", "feat"),
            P("feat", "dp", None),
            P("feat", None, None),
            P("feat", "dp", None),
            P("feat", None, None),
        ),
        check_vma=False,
    )
```

profile of v0, /device:TPU:1, one launch (start us, length us, event | category | flops | bytes accessed | tf_op | source)
XLA Modules:
  0.0 585.8 jit_solution(3633134355691331185)
XLA Ops:
  8.9 1.4 fusion
  10.4 2.1 reshape.254
  12.8 4.0 collective-permute-start.8
  18.1 65.8 %all-gather.3.cloned.1.call-done = bf16[1,512,2048]{2,1,0:T(8,128)(2,1)} async-done(((bf16[1,16,2048]{2,1,0:T(8,128)(2,1)}), bf16[1,512,2048]{2,1,0:T(8,128)(2,1)}) %all-gather.3.cloned.1.call-update) | async-done | bytes 2097168 | tf_op jit(solution)/shard_map/all_gather | solution.py:60
  83.9 2.3 convolution_convert_fusion
  87.0 3.1 collective-permute-start
  90.2 4.3 collective-permute-start.9
  94.5 7.6 %collective-permute-done = bf16[256,8,1,128]{3,0,1,2:T(8,128)(2,1)S(1)} collective-permute-done((bf16[256,8,1,128]{3,0,1,2:T(8,128)(2,1)S(1)}, bf16[256,8,1,128]{3,0,1,2:T(8,128)(2,1)S(1)}, u32[]{:S(2)}, u32[]{:S(2)}) %collective-permute-start) | collective-permute-done | bytes 524320 | tf_op jit(solution)/shard_map/ppermute | solution.py:13
  102.3 4.6 collective-permute-start.1
  107.2 4.0 collective-permute-start.10
  111.2 6.1 %collective-permute-done.1 = bf16[256,4,2,128]{3,0,1,2:T(8,128)(2,1)S(1)} collective-permute-done((bf16[256,4,2,128]{3,0,1,2:T(8,128)(2,1)S(1)}, bf16[256,4,2,128]{3,0,1,2:T(8,128)(2,1)S(1)}, u32[]{:S(2)}, u32[]{:S(2)}) %collective-permute-start.1) | collective-permute-done | bytes 524320 | tf_op jit(solution)/shard_map/ppermute | solution.py:13
  117.8 4.1 collective-permute-start.2
  122.0 5.2 collective-permute-start.11
  127.2 23.3 %collective-permute-done.2 = bf16[256,2,4,128]{3,0,2,1:T(8,128)(2,1)S(1)} collective-permute-done((bf16[256,2,4,128]{3,0,2,1:T(8,128)(2,1)S(1)}, bf16[256,2,4,128]{3,0,2,1:T(8,128)(2,1)S(1)}, u32[]{:S(2)}, u32[]{:S(2)}) %collective-permute-start.2) | collective-permute-done | bytes 524320 | tf_op jit(solution)/shard_map/ppermute | solution.py:13
  151.8 7.1 %collective-permute-start.3 = (bf16[256,1,8,128]{3,0,2,1:T(8,128)(2,1)}, bf16[256,1,8,128]{3,0,2,1:T(8,128)(2,1)}, u32[]{:S(2)}, u32[]{:S(2)}) collective-permute-start(bf16[256,1,8,128]{3,0,2,1:T(8,128)(2,1)} %broadcast_select_fusion.5), channel_id=1, source_target_pairs={{0,8},{1,9},{2,10},{3,11},{4,12},{5,13},{6,14},{7,15},{8,0},{9,1},... | collective-permute-start | bytes 1572872 | tf_op jit(solution)/shard_map/ppermute | solution.py:13
  159.7 2.3 fusion.1
  162.0 19.3 %collective-permute-done.3 = bf16[256,1,8,128]{3,0,2,1:T(8,128)(2,1)} collective-permute-done((bf16[256,1,8,128]{3,0,2,1:T(8,128)(2,1)}, bf16[256,1,8,128]{3,0,2,1:T(8,128)(2,1)}, u32[]{:S(2)}, u32[]{:S(2)}) %collective-permute-start.3) | collective-permute-done | bytes 524320 | tf_op jit(solution)/shard_map/ppermute | solution.py:13
  183.5 1.9 copy.166
  185.4 4.1 fusion.11
  191.4 1.5 fusion.41
  194.7 3.1 collective-permute-start.12
  197.8 9.9 %collective-permute-done.12 = bf16[256,8,1,128]{3,0,1,2:T(8,128)(2,1)S(1)} collective-permute-done((bf16[256,8,1,128]{3,0,1,2:T(8,128)(2,1)S(1)}, bf16[256,8,1,128]{3,0,1,2:T(8,128)(2,1)S(1)}, u32[]{:S(2)}, u32[]{:S(2)}) %collective-permute-start.12) | collective-permute-done | bytes 524320 | tf_op jit(solution)/shard_map/ppermute | solution.py:13
  207.8 4.5 collective-permute-start.13
  212.3 9.0 %collective-permute-done.13 = bf16[256,4,2,128]{3,0,1,2:T(8,128)(2,1)S(1)} collective-permute-done((bf16[256,4,2,128]{3,0,1,2:T(8,128)(2,1)S(1)}, bf16[256,4,2,128]{3,0,1,2:T(8,128)(2,1)S(1)}, u32[]{:S(2)}, u32[]{:S(2)}) %collective-permute-start.13) | collective-permute-done | bytes 524320 | tf_op jit(solution)/shard_map/ppermute | solution.py:13
  221.7 2.1 collective-permute-start.14
  223.8 21.1 %collective-permute-done.14 = bf16[256,2,4,128]{3,0,2,1:T(8,128)(2,1)S(1)} collective-permute-done((bf16[256,2,4,128]{3,0,2,1:T(8,128)(2,1)S(1)}, bf16[256,2,4,128]{3,0,2,1:T(8,128)(2,1)S(1)}, u32[]{:S(2)}, u32[]{:S(2)}) %collective-permute-start.14) | collective-permute-done | bytes 524320 | tf_op jit(solution)/shard_map/ppermute | solution.py:13
  246.1 4.6 collective-permute-start.15
  252.1 2.7 multiply_bitcast_fusion
  254.8 11.0 %copy.199 = f32[2048,1,512]{2,1,0:T(1,128)} copy(f32[2048,1,512]{0,2,1:T(8,128)} %multiply_bitcast_fusion) | data formatting | bytes 8388608 | tf_op jit(solution)/shard_map/mul | solution.py:113
  265.9 1.4 convolution_multiply_fusion
  267.3 9.6 %collective-permute-done.15 = bf16[256,1,8,128]{3,0,2,1:T(8,128)(2,1)} collective-permute-done((bf16[256,1,8,128]{3,0,2,1:T(8,128)(2,1)}, bf16[256,1,8,128]{3,0,2,1:T(8,128)(2,1)}, u32[]{:S(2)}, u32[]{:S(2)}) %collective-permute-start.15) | collective-permute-done | bytes 524320 | tf_op jit(solution)/shard_map/ppermute | solution.py:13
  278.7 2.8 multiply_bitcast_fusion.1
  281.5 11.0 %copy.198 = f32[512,1,2048]{2,1,0:T(1,128)} copy(f32[512,1,2048]{0,2,1:T(8,128)} %multiply_bitcast_fusion.1) | data formatting | bytes 8388608 | tf_op jit(solution)/shard_map/mul | solution.py:141
  292.5 1.6 copy-done.1
  294.0 2.7 fusion.22
  297.8 3.0 collective-permute-start.4
  300.8 3.4 collective-permute-done.4
  304.3 4.7 collective-permute-start.5
  309.0 2.7 collective-permute-done.5
  311.8 1.9 collective-permute-start.6
  313.7 5.1 collective-permute-done.6
  319.0 4.7 collective-permute-start.7
  323.9 1.3 dynamic-slice
  326.4 4.6 collective-permute-done.7
  331.5 113.7 %psum.15 = f32[32,16,16]{2,1,0:T(8,128)S(1)} all-reduce(f32[32,16,16]{2,1,0:T(8,128)S(1)} %convolution_multiply_fusion.1), channel_id=1, replica_groups=mesh['dp'=32,'feat'=16] {'dp'}, use_global_device_ids=true, to_apply=%region_3.4 | all-reduce | flops 8192 | bytes 65536 | tf_op jit(solution)/shard_map/psum | solution.py:147
  447.0 3.0 fusion.16
  450.1 123.8 %all-reduce.5.cloned.1.call-done = (f32[512,1,2048]{2,1,0:T(1,128)}, f32[128,16,16]{2,1,0:T(8,128)}, f32[2048,1,512]{2,1,0:T(1,128)}) async-done(((f32[512,1,2048]{2,1,0:T(1,128)}, f32[128,16,16]{2,1,0:T(8,128)}, f32[2048,1,512]{2,1,0:T(1,128)}), (f32[512,1,2048]{2,1,0:T(1,128)}, f32[128,16,16]{2,1,0:T(8,128)}, f32[2048,1,512]{2,1,0:T(1,128)})) %all-reduce.5.cloned.1.call-update) | async-done | bytes 8519696
  577.0 2.3 copy.204
  (116 shorter events, 24.7 us)
Async XLA Ops:
  7.2 76.8 %copy-start = (bf16[256,512]{1,0:T(8,128)(2,1)S(1)}, bf16[256,512]{1,0:T(8,128)(2,1)}, u32[]{:S(2)}) copy-start(bf16[256,512]{1,0:T(8,128)(2,1)} %param.6) | copy-start | bytes 786436
  7.2 76.7 %all-gather.3.cloned.1.call-start = ((), (), s32[]{:S(2)}) async-start(), calls=%async_computation | async-start | bytes 2162688 | tf_op jit(solution)/shard_map/all_gather | solution.py:60
  7.9 151.8 %all-gather.5.cloned.1.call-start = ((), (), s32[]{:S(2)}) async-start(), calls=%async_computation.1 | async-start | bytes 2162688 | tf_op jit(solution)/shard_map/all_gather | solution.py:74
  8.9 3.5 copy-start.12
  10.3 6.6 %copy-start.14 = (bf16[128,16,16]{0,2,1:T(8,128)(2,1)S(1)}, bf16[128,16,16]{0,2,1:T(8,128)(2,1)}, u32[]{:S(2)}) copy-start(bf16[128,16,16]{0,2,1:T(8,128)(2,1)} %param.8) | copy-start | bytes 196612
  12.4 73.8 %copy-start.2 = (bf16[512,512]{1,0:T(8,128)(2,1)}, bf16[512,512]{1,0:T(8,128)(2,1)S(1)}, u32[]{:S(2)}) copy-start(bf16[512,512]{1,0:T(8,128)(2,1)S(1)} %reshape.254) | copy-start | bytes 1572868
  12.8 77.3 %collective-permute-start.8 = (bf16[256,8,1,32]{0,3,1,2:T(8,128)(2,1)S(1)}, bf16[256,8,1,32]{0,3,1,2:T(8,128)(2,1)S(1)}, u32[]{:S(2)}, u32[]{:S(2)}) collective-permute-start(bf16[256,8,1,32]{0,3,1,2:T(8,128)(2,1)S(1)} %broadcast_select_fusion.8), channel_id=1, source_target_pairs={{0,1},{1,0},{2,3},{3,2},{4,5},{5,4},{6,7},{7,6},{8,9},{9,8},{10,11... | collective-permute-start | bytes 393224 | tf_op jit(solution)/shard_map/ppermute | solution.py:13
  16.8 557.0 %all-reduce.5.cloned.1.call-start = ((), (), s32[]{:S(2)}) async-start(), calls=%async_computation.2 | async-start | bytes 18874368
  87.0 15.1 %collective-permute-start = (bf16[256,8,1,128]{3,0,1,2:T(8,128)(2,1)S(1)}, bf16[256,8,1,128]{3,0,1,2:T(8,128)(2,1)S(1)}, u32[]{:S(2)}, u32[]{:S(2)}) collective-permute-start(bf16[256,8,1,128]{3,0,1,2:T(8,128)(2,1)S(1)} %bitcast_select_fusion.4), channel_id=1, source_target_pairs={{0,1},{1,0},{2,3},{3,2},{4,5},{5,4},{6,7},{7,6},{8,9},{9,8},{10,11... | collective-permute-start | bytes 1572872 | tf_op jit(solution)/shard_map/ppermute | solution.py:13
  90.2 16.9 %collective-permute-start.9 = (bf16[256,4,2,32]{0,3,2,1:T(8,128)(2,1)S(1)}, bf16[256,4,2,32]{0,3,2,1:T(8,128)(2,1)S(1)}, u32[]{:S(2)}, u32[]{:S(2)}) collective-permute-start(bf16[256,4,2,32]{0,3,2,1:T(8,128)(2,1)S(1)} %broadcast_select_fusion.12), channel_id=1, source_target_pairs={{0,2},{1,3},{2,0},{3,1},{4,6},{5,7},{6,4},{7,5},{8,10},{9,11},{10,... | collective-permute-start | bytes 393224 | tf_op jit(solution)/shard_map/ppermute | solution.py:13
  102.3 15.0 %collective-permute-start.1 = (bf16[256,4,2,128]{3,0,1,2:T(8,128)(2,1)S(1)}, bf16[256,4,2,128]{3,0,1,2:T(8,128)(2,1)S(1)}, u32[]{:S(2)}, u32[]{:S(2)}) collective-permute-start(bf16[256,4,2,128]{3,0,1,2:T(8,128)(2,1)S(1)} %broadcast_select_fusion.1), channel_id=1, source_target_pairs={{0,2},{1,3},{2,0},{3,1},{4,6},{5,7},{6,4},{7,5},{8,10},{9,11},{10,... | collective-permute-start | bytes 1572872 | tf_op jit(solution)/shard_map/ppermute | solution.py:13
  107.2 14.7 %collective-permute-start.10 = (bf16[256,2,4,32]{0,3,2,1:T(8,128)(2,1)S(1)}, bf16[256,2,4,32]{0,3,2,1:T(8,128)(2,1)S(1)}, u32[]{:S(2)}, u32[]{:S(2)}) collective-permute-start(bf16[256,2,4,32]{0,3,2,1:T(8,128)(2,1)S(1)} %broadcast_select_fusion.14), channel_id=1, source_target_pairs={{0,4},{1,5},{2,6},{3,7},{4,0},{5,1},{6,2},{7,3},{8,12},{9,13},{10,... | collective-permute-start | bytes 393224 | tf_op jit(solution)/shard_map/ppermute | solution.py:13
  117.8 32.7 %collective-permute-start.2 = (bf16[256,2,4,128]{3,0,2,1:T(8,128)(2,1)S(1)}, bf16[256,2,4,128]{3,0,2,1:T(8,128)(2,1)S(1)}, u32[]{:S(2)}, u32[]{:S(2)}) collective-permute-start(bf16[256,2,4,128]{3,0,2,1:T(8,128)(2,1)S(1)} %broadcast_select_fusion.3), channel_id=1, source_target_pairs={{0,4},{1,5},{2,6},{3,7},{4,0},{5,1},{6,2},{7,3},{8,12},{9,13},{10,... | collective-permute-start | bytes 1572872 | tf_op jit(solution)/shard_map/ppermute | solution.py:13
  122.0 36.9 %collective-permute-start.11 = (bf16[256,1,8,32]{0,3,2,1:T(8,128)(2,1)S(1)}, bf16[256,1,8,32]{0,3,2,1:T(8,128)(2,1)S(1)}, u32[]{:S(2)}, u32[]{:S(2)}) collective-permute-start(bf16[256,1,8,32]{0,3,2,1:T(8,128)(2,1)S(1)} %broadcast_select_fusion.16), channel_id=1, source_target_pairs={{0,8},{1,9},{2,10},{3,11},{4,12},{5,13},{6,14},{7,15},{8,0},{9,1},... | collective-permute-start | bytes 393224 | tf_op jit(solution)/shard_map/ppermute | solution.py:13
  151.8 29.5 %collective-permute-start.3 = (bf16[256,1,8,128]{3,0,2,1:T(8,128)(2,1)}, bf16[256,1,8,128]{3,0,2,1:T(8,128)(2,1)}, u32[]{:S(2)}, u32[]{:S(2)}) collective-permute-start(bf16[256,1,8,128]{3,0,2,1:T(8,128)(2,1)} %broadcast_select_fusion.5), channel_id=1, source_target_pairs={{0,8},{1,9},{2,10},{3,11},{4,12},{5,13},{6,14},{7,15},{8,0},{9,1},... | collective-permute-start | bytes 1572872 | tf_op jit(solution)/shard_map/ppermute | solution.py:13
  185.4 4.1 copy-start.4
  185.4 5.1 copy-start.10
  189.5 1.0 copy-start.6
  194.7 13.0 %collective-permute-start.12 = (bf16[256,8,1,128]{3,0,1,2:T(8,128)(2,1)S(1)}, bf16[256,8,1,128]{3,0,1,2:T(8,128)(2,1)S(1)}, u32[]{:S(2)}, u32[]{:S(2)}) collective-permute-start(bf16[256,8,1,128]{3,0,1,2:T(8,128)(2,1)S(1)} %bitcast_select_fusion.1), channel_id=1, source_target_pairs={{0,1},{1,0},{2,3},{3,2},{4,5},{5,4},{6,7},{7,6},{8,9},{9,8},{10,11... | collective-permute-start | bytes 1572872 | tf_op jit(solution)/shard_map/ppermute | solution.py:13
  207.8 13.5 %collective-permute-start.13 = (bf16[256,4,2,128]{3,0,1,2:T(8,128)(2,1)S(1)}, bf16[256,4,2,128]{3,0,1,2:T(8,128)(2,1)S(1)}, u32[]{:S(2)}, u32[]{:S(2)}) collective-permute-start(bf16[256,4,2,128]{3,0,1,2:T(8,128)(2,1)S(1)} %broadcast_select_fusion), channel_id=1, source_target_pairs={{0,2},{1,3},{2,0},{3,1},{4,6},{5,7},{6,4},{7,5},{8,10},{9,11},{10,... | collective-permute-start | bytes 1572872 | tf_op jit(solution)/shard_map/ppermute | solution.py:13
  221.7 23.2 %collective-permute-start.14 = (bf16[256,2,4,128]{3,0,2,1:T(8,128)(2,1)S(1)}, bf16[256,2,4,128]{3,0,2,1:T(8,128)(2,1)S(1)}, u32[]{:S(2)}, u32[]{:S(2)}) collective-permute-start(bf16[256,2,4,128]{3,0,2,1:T(8,128)(2,1)S(1)} %broadcast_select_fusion.2), channel_id=1, source_target_pairs={{0,4},{1,5},{2,6},{3,7},{4,0},{5,1},{6,2},{7,3},{8,12},{9,13},{10,... | collective-permute-start | bytes 1572872 | tf_op jit(solution)/shard_map/ppermute | solution.py:13
  245.2 5.6 copy-start.11
  245.3 6.8 %copy-start.9 = (bf16[256,1,2,8,32]{0,4,3,2,1:T(8,128)(2,1)S(1)}, bf16[256,1,2,8,32]{0,4,3,2,1:T(8,128)(2,1)}, u32[]{:S(2)}) copy-start(bf16[256,1,2,8,32]{0,4,3,2,1:T(8,128)(2,1)} %pad_maximum_fusion.13) | copy-start | bytes 786436
  246.1 30.8 %collective-permute-start.15 = (bf16[256,1,8,128]{3,0,2,1:T(8,128)(2,1)}, bf16[256,1,8,128]{3,0,2,1:T(8,128)(2,1)}, u32[]{:S(2)}, u32[]{:S(2)}) collective-permute-start(bf16[256,1,8,128]{3,0,2,1:T(8,128)(2,1)} %broadcast_select_fusion.4), channel_id=1, source_target_pairs={{0,8},{1,9},{2,10},{3,11},{4,12},{5,13},{6,14},{7,15},{8,0},{9,1},... | collective-permute-start | bytes 1572872 | tf_op jit(solution)/shard_map/ppermute | solution.py:13
  251.1 1.0 copy-start.8
  254.8 11.0 %copy-start.5 = (bf16[256,1,2,8,128]{0,3,2,4,1:T(8,128)(2,1)S(1)}, bf16[256,1,2,8,128]{0,3,2,4,1:T(8,128)(2,1)}, u32[]{:S(2)}) copy-start(bf16[256,1,2,8,128]{0,3,2,4,1:T(8,128)(2,1)} %copy-done.4) | copy-start | bytes 3145732
  254.8 11.0 %copy-start.7 = (bf16[256,16,128]{0,1,2:T(8,128)(2,1)S(1)}, bf16[256,16,128]{0,1,2:T(8,128)(2,1)}, u32[]{:S(2)}) copy-start(bf16[256,16,128]{0,1,2:T(8,128)(2,1)} %copy-done.6) | copy-start | bytes 3145732
  292.4 1.6 copy-start.1
  297.8 6.5 %collective-permute-start.4 = (bf16[256,8,1,32]{0,3,1,2:T(8,128)(2,1)S(1)}, bf16[256,8,1,32]{0,3,1,2:T(8,128)(2,1)S(1)}, u32[]{:S(2)}, u32[]{:S(2)}) collective-permute-start(bf16[256,8,1,32]{0,3,1,2:T(8,128)(2,1)S(1)} %broadcast_select_fusion.11), channel_id=1, source_target_pairs={{0,1},{1,0},{2,3},{3,2},{4,5},{5,4},{6,7},{7,6},{8,9},{9,8},{10,11... | collective-permute-start | bytes 393224 | tf_op jit(solution)/shard_map/ppermute | solution.py:13
  304.3 19.4 %copy-start.13 = (bf16[256,512]{1,0:T(8,128)(2,1)S(1)}, bf16[256,512]{1,0:T(8,128)(2,1)}, u32[]{:S(2)}) copy-start(bf16[256,512]{1,0:T(8,128)(2,1)} %param.11) | copy-start | bytes 786436
  304.3 7.3 %collective-permute-start.5 = (bf16[256,4,2,32]{0,3,2,1:T(8,128)(2,1)S(1)}, bf16[256,4,2,32]{0,3,2,1:T(8,128)(2,1)S(1)}, u32[]{:S(2)}, u32[]{:S(2)}) collective-permute-start(bf16[256,4,2,32]{0,3,2,1:T(8,128)(2,1)S(1)} %broadcast_select_fusion.13), channel_id=1, source_target_pairs={{0,2},{1,3},{2,0},{3,1},{4,6},{5,7},{6,4},{7,5},{8,10},{9,11},{10,... | collective-permute-start | bytes 393224 | tf_op jit(solution)/shard_map/ppermute | solution.py:13
  311.8 7.1 %collective-permute-start.6 = (bf16[256,2,4,32]{0,3,2,1:T(8,128)(2,1)S(1)}, bf16[256,2,4,32]{0,3,2,1:T(8,128)(2,1)S(1)}, u32[]{:S(2)}, u32[]{:S(2)}) collective-permute-start(bf16[256,2,4,32]{0,3,2,1:T(8,128)(2,1)S(1)} %broadcast_select_fusion.15), channel_id=1, source_target_pairs={{0,4},{1,5},{2,6},{3,7},{4,0},{5,1},{6,2},{7,3},{8,12},{9,13},{10,... | collective-permute-start | bytes 393224 | tf_op jit(solution)/shard_map/ppermute | solution.py:13
  318.9 127.0 %copy-start.3 = (bf16[512,512]{1,0:T(8,128)(2,1)S(1)}, bf16[512,512]{1,0:T(8,128)(2,1)}, u32[]{:S(2)}) copy-start(bf16[512,512]{1,0:T(8,128)(2,1)} %copy-done.2) | copy-start | bytes 1572868
  319.0 12.0 %collective-permute-start.7 = (bf16[256,1,8,32]{0,3,2,1:T(8,128)(2,1)S(1)}, bf16[256,1,8,32]{0,3,2,1:T(8,128)(2,1)S(1)}, u32[]{:S(2)}, u32[]{:S(2)}) collective-permute-start(bf16[256,1,8,32]{0,3,2,1:T(8,128)(2,1)S(1)} %broadcast_select_fusion.17), channel_id=1, source_target_pairs={{0,8},{1,9},{2,10},{3,11},{4,12},{5,13},{6,14},{7,15},{8,0},{9,1},... | collective-permute-start | bytes 393224 | tf_op jit(solution)/shard_map/ppermute | solution.py:13
Sparse Core Ops, SparseCore 0:
  10.2 73.7 all-gather.2
  86.1 68.0 all-gather.4
  292.6 281.1 all-reduce.4
where the time goes:
time: 588 us; the launch traced here: 586 us
  waiting for transfers between devices  312 us (53%)
  blocking collectives  114 us (19%)
  starting transfers between devices  65.1 us (11%)
  local copies, waits for them, and re-layouts  46 us (8%)
  matrix products  23.5 us (4%)
  between operations  15.9 us (3%)
  other arithmetic  9.48 us (2%)
    unnamed x4, waiting for transfers between devices  124 us
    ppermute x16, waiting for transfers between devices, partner(): return lax.ppermute(value, axis, pairs)  122 us
    psum x1, blocking collectives, on_device(): lax.psum((right_up_term, right_down_term), 'dp')  114 us
    all_gather x1, waiting for transfers between devices, on_device(): up_full = lax.all_gather(up_left, 'dp', axis=1, tiled=True)  65.8 us
    ppermute x16, starting transfers between devices, partner(): return lax.ppermute(value, axis, pairs)  65 us
    unnamed x41, local copies, waits for them, and re-layouts  12.9 us
  transfers between devices with their start and end apart: 19, of which 15 were waited for; matrix products, arithmetic and copies ran while one was open for 7% of the time, Pallas kernels for 0%

commit v1 on v0

v1 whole, which is shorter than its diff:
```python
import jax
import jax.numpy as jnp
import numpy as np
from jax import lax
from jax.sharding import Mesh
from jax.sharding import PartitionSpec as P

TILE_UP = 128
TILE_DOWN = 32

DP_AXES = ("z", "ylo", "core")
FEAT_AXES = ("yhi", "x")


def split_mesh(mesh):
    n_dp = mesh.shape["dp"]
    n_feat = mesh.shape["feat"]
    sizes = (n_dp // 4, 2, 2, n_feat // 4, 4)
    devices = np.asarray(mesh.devices).reshape(sizes)
    return Mesh(devices, DP_AXES + FEAT_AXES)


def exchange(wired):
    rows, feat_count, piece = wired.shape
    n_x = lax.axis_size("x")
    n_y = feat_count // n_x
    shaped = wired.reshape(rows, n_y, n_x, piece)
    shaped = lax.all_to_all(shaped, "x", 2, 2, tiled=True)
    shaped = lax.all_to_all(shaped, "yhi", 1, 1, tiled=True)
    return shaped.reshape(rows, feat_count, piece)


def dp_reduce_scatter(part, row_axis):
    shape = part.shape
    rows = shape[row_axis]
    n_z = lax.axis_size("z")
    split = shape[:row_axis] + (n_z, 2, 2, rows // (4 * n_z)) + shape[row_axis + 1 :]
    x = part.reshape(split)
    x = lax.psum_scatter(x, "core", scatter_dimension=row_axis + 2, tiled=True)
    x = lax.psum_scatter(x, "z", scatter_dimension=row_axis, tiled=True)
    x = lax.psum_scatter(x, "ylo", scatter_dimension=row_axis + 1, tiled=True)
    return x.reshape(shape[:row_axis] + (rows // (4 * n_z),) + shape[row_axis + 1 :])


def dp_all_gather(local, row_axis):
    shape = local.shape
    rows = shape[row_axis]
    x = local.reshape(shape[:row_axis] + (1, 1, 1, rows) + shape[row_axis + 1 :])
    x = lax.all_gather(x, "ylo", axis=row_axis + 1, tiled=True)
    x = lax.all_gather(x, "z", axis=row_axis, tiled=True)
    x = lax.all_gather(x, "core", axis=row_axis + 2, tiled=True)
    total = x.shape[row_axis] * x.shape[row_axis + 1] * x.shape[row_axis + 2] * rows
    return x.reshape(shape[:row_axis] + (total,) + shape[row_axis + 1 :])


def to_wire(blocks, feat_count):
    tok_rows, local_blocks, full_width = blocks.shape
    piece = full_width // feat_count
    shaped = blocks.reshape(tok_rows, local_blocks, feat_count, piece).transpose(0, 2, 1, 3)
    return shaped.reshape(tok_rows, feat_count, local_blocks * piece)


def from_wire(wired, local_blocks):
    tok_rows, feat_count, line_len = wired.shape
    piece = line_len // local_blocks
    shaped = wired.reshape(tok_rows, feat_count, local_blocks, piece).transpose(0, 2, 1, 3)
    return shaped.reshape(tok_rows, local_blocks, feat_count * piece)


def on_device(tokens, up_left, up_right, down_left, down_right, layer_grad):
    tok_rows = tokens.shape[0]
    local_blocks = up_left.shape[0]
    hidden_width = up_left.shape[2]
    block_width = down_left.shape[2]
    blocks_all = up_right.shape[1]
    group_up = up_right.shape[0]
    group_down = down_right.shape[0]
    feat_count = lax.axis_size("yhi") * lax.axis_size("x")
    n_dp = lax.axis_size("z") * lax.axis_size("ylo") * lax.axis_size("core")
    grad_scale = float(tok_rows * n_dp) ** (-0.5)
    tiles_up = group_up // TILE_UP
    tiles_down = group_down // TILE_DOWN
    up_full = dp_all_gather(up_left, 1)
    token_blocks = tokens.reshape(tok_rows, local_blocks, block_width)
    up_inner = jnp.einsum(
        "tbi,big->tbg", token_blocks, up_full, preferred_element_type=jnp.float32
    ).astype(jnp.bfloat16)
    up_mixed = exchange(to_wire(up_inner, feat_count))
    preact = jnp.einsum("tjg,gjk->tkg", up_mixed, up_right, preferred_element_type=jnp.float32)
    sigmoid_val = jax.nn.sigmoid(preact)
    activated = (
        (preact * sigmoid_val)
        .reshape(tok_rows, blocks_all, tiles_up, TILE_UP)
        .transpose(0, 2, 1, 3)
    )
    hidden = activated.reshape(tok_rows, local_blocks, hidden_width).astype(jnp.bfloat16)
    down_full = dp_all_gather(down_left, 1)
    down_inner = jnp.einsum(
        "tbh,bhc->tbc", hidden, down_full, preferred_element_type=jnp.float32
    ).astype(jnp.bfloat16)
    down_mixed = exchange(to_wire(down_inner, feat_count)).reshape(
        tok_rows, blocks_all * group_down
    )
    identity = jnp.eye(group_down, dtype=jnp.bfloat16).reshape(group_down, tiles_down, TILE_DOWN)
    mix_matrix = jnp.einsum(
        "cjk,cal->jcakl", down_right, identity, preferred_element_type=jnp.float32
    )
    mix_matrix = mix_matrix.astype(jnp.bfloat16).reshape(
        blocks_all * group_down, blocks_all * group_down
    )
    layer_out = jnp.dot(down_mixed, mix_matrix, preferred_element_type=jnp.float32).astype(
        jnp.bfloat16
    )
    grad_down_mixed = lax.dot_general(
        layer_grad, mix_matrix, (((1,), (1,)), ((), ())), preferred_element_type=jnp.float32
    ).astype(jnp.bfloat16)
    grad_by_group = layer_grad.reshape(tok_rows, tiles_down, blocks_all, TILE_DOWN).transpose(
        0, 2, 1, 3
    )
    grad_by_group = grad_by_group.reshape(tok_rows, blocks_all, group_down)
    right_down_term = (
        jnp.einsum(
            "tjc,tkc->cjk",
            down_mixed.reshape(tok_rows, blocks_all, group_down),
            grad_by_group,
            preferred_element_type=jnp.float32,
        )
        * grad_scale
    )
    grad_down_inner = from_wire(
        exchange(grad_down_mixed.reshape(tok_rows, feat_count, local_blocks * group_down)),
        local_blocks,
    )
    grad_down_left = dp_reduce_scatter(
        jnp.einsum("tbh,tbc->hbc", hidden, grad_down_inner, preferred_element_type=jnp.float32)
        * grad_scale,
        0,
    ).transpose(1, 0, 2)
    grad_hidden = jnp.einsum(
        "tbc,bhc->tbh", grad_down_inner, down_full, preferred_element_type=jnp.float32
    )
    grad_hidden = grad_hidden.reshape(tok_rows, tiles_up, blocks_all, TILE_UP).transpose(0, 2, 1, 3)
    grad_hidden = grad_hidden.reshape(tok_rows, blocks_all, group_up)
    grad_preact = (grad_hidden * sigmoid_val * (1.0 + preact * (1.0 - sigmoid_val))).astype(
        jnp.bfloat16
    )
    grad_up_mixed = jnp.einsum(
        "tkg,gjk->tjg", grad_preact, up_right, preferred_element_type=jnp.float32
    ).astype(jnp.bfloat16)
    right_up_term = (
        jnp.einsum("tjg,tkg->gjk", up_mixed, grad_preact, preferred_element_type=jnp.float32)
        * grad_scale
    )
    grad_up_inner = from_wire(exchange(grad_up_mixed), local_blocks)
    grad_tokens = jnp.einsum(
        "tbg,big->tbi", grad_up_inner, up_full, preferred_element_type=jnp.float32
    ).astype(jnp.bfloat16)
    grad_tokens = grad_tokens.reshape(tok_rows, local_blocks * block_width)
    grad_up_left = dp_reduce_scatter(
        jnp.einsum("tbi,tbg->ibg", token_blocks, grad_up_inner, preferred_element_type=jnp.float32)
        * grad_scale,
        0,
    ).transpose(1, 0, 2)
    rights = jnp.concatenate([right_up_term, right_down_term], axis=0)
    rights = lax.psum(rights, DP_AXES)
    grad_up_right = rights[:group_up]
    grad_down_right = rights[group_up:]
    return (layer_out, grad_tokens, grad_up_left, grad_up_right, grad_down_left, grad_down_right)


def solution(mesh):
    fine = split_mesh(mesh)
    row = P(DP_AXES, FEAT_AXES)
    weight = P(FEAT_AXES, DP_AXES, None)
    mixer = P(FEAT_AXES, None, None)
    return jax.shard_map(
        on_device,
        mesh=fine,
        in_specs=(row, weight, mixer, weight, mixer, row),
        out_specs=(row, row, weight, mixer, weight, mixer),
        check_vma=False,
    )
```

time: 588 us -> 652 us (1.11)
  waiting for transfers between devices: 312 us -> 509 us
  blocking collectives: 114 us -> 35.8 us
  starting transfers between devices: 65.1 us -> 31.5 us
  local copies, waits for them, and re-layouts: 46 us -> 33.3 us
  other arithmetic: 9.48 us -> 2.13 us
    psum x0 -> x1, waiting for transfers between devices: none -> 233 us  [on_device(): rights = lax.psum(rights, DP_AXES)]
    ppermute x16 -> x0, waiting for transfers between devices: 122 us -> none  [partner(): return lax.ppermute(value, axis, pairs)]
    psum x1 -> x0, blocking collectives: 114 us -> none  [on_device(): lax.psum((right_up_term, right_down_term), 'dp')]
    reduce_scatter x0 -> x4, waiting for transfers between devices: none -> 93.7 us  [the longest x2 53.9 us: dp_reduce_scatter(): x = lax.psum_scatter(x, 'z', scatter_dimension=row_axis, tiled=True)]
    unnamed x4 -> x11, waiting for transfers between devices: 124 us -> 53.1 us
    ppermute x16 -> x0, starting transfers between devices: 65 us -> none  [partner(): return lax.ppermute(value, axis, pairs)]
    all_to_all x0 -> x6, waiting for transfers between devices: none -> 40.3 us  [the longest x4 40.3 us: exchange(): shaped = lax.all_to_all(shaped, 'yhi', 1, 1, tiled=True)]
    all_to_all x0 -> x6, starting transfers between devices: none -> 31.2 us  [the longest x4 23.7 us: exchange(): shaped = lax.all_to_all(shaped, 'yhi', 1, 1, tiled=True)]
  transfers between devices with their start and end apart: 19 -> 16, of which waited for: 15 -> 14; matrix products, arithmetic and copies ran while one was open for 7% -> 7% of each run, Pallas kernels for 0% -> 0%
where the time goes in v1:
time: 652 us; the launch traced here: 650 us
  waiting for transfers between devices  509 us (78%)
  blocking collectives  35.8 us (5%)
  local copies, waits for them, and re-layouts  33.3 us (5%)
  starting transfers between devices  31.5 us (5%)
  matrix products  23.7 us (4%)
  between operations  14.3 us (2%)
    psum x1, waiting for transfers between devices, on_device(): rights = lax.psum(rights, DP_AXES)  233 us
    all_gather x2, waiting for transfers between devices, dp_all_gather(): x = lax.all_gather(x, 'z', axis=row_axis, tiled=True)  75 us
    reduce_scatter x2, waiting for transfers between devices, dp_reduce_scatter(): x = lax.psum_scatter(x, 'z', scatter_dimension=row_axis, tiled=True)  53.9 us
    unnamed x11, waiting for transfers between devices  53.1 us
    all_to_all x4, waiting for transfers between devices, exchange(): shaped = lax.all_to_all(shaped, 'yhi', 1, 1, tiled=True)  40.3 us
    reduce_scatter x2, waiting for transfers between devices, dp_reduce_scatter(): x = lax.psum_scatter(x, 'ylo', scatter_dimension=row_axis + 1, tiled=True)  39.8 us
    all_to_all x2, blocking collectives, exchange(): shaped = lax.all_to_all(shaped, 'x', 2, 2, tiled=True)  24.2 us
    all_to_all x4, starting transfers between devices, exchange(): shaped = lax.all_to_all(shaped, 'yhi', 1, 1, tiled=True)  23.7 us
  transfers between devices with their start and end apart: 16, of which 14 were waited for; matrix products, arithmetic and copies ran while one was open for 7% of the time, Pallas kernels for 0%

profile of v1, /device:TPU:1, one launch (start us, length us, event | category | flops | bytes accessed | tf_op | source)
XLA Modules:
  0.0 650.3 jit_solution(2913419054008153790)
XLA Ops:
  7.2 6.3 all-gather
  13.6 42.4 %all-gather.13.cloned.1.call-done = bf16[16,16,2048]{2,1,0:T(8,128)(2,1)} async-done(((bf16[2,16,2048]{2,1,0:T(8,128)(2,1)}), bf16[16,16,2048]{2,1,0:T(8,128)(2,1)}) %all-gather.13.cloned.1.call-update) | async-done | bytes 1048592 | tf_op jit(solution)/shard_map/all_gather | solution.py:50
  56.1 5.3 all-gather.2
  62.4 1.4 fusion
  63.8 2.1 reshape.98
  66.9 4.0 all-to-all-start.4
  70.8 10.1 %all-gather.9.cloned.1.call-done = bf16[1,8,2,2,16,2048]{5,4,3,2,1,0:T(8,128)(2,1)} async-done(((bf16[1,8,2,1,16,2048]{5,4,3,2,1,0:T(8,128)(2,1)}), bf16[1,8,2,2,16,2048]{5,4,3,2,1,0:T(8,128)(2,1)}) %all-gather.9.cloned.1.call-update) | async-done | bytes 2097168 | tf_op jit(solution)/shard_map/all_gather | solution.py:51
  80.9 2.3 convolution_convert_fusion
  83.3 1.1 copy.81
  84.4 3.5 all-to-all-start
  87.9 32.6 %all-gather.15.cloned.1.call-done = bf16[16,64,512]{2,1,0:T(8,128)(2,1)} async-done(((bf16[2,64,512]{2,1,0:T(8,128)(2,1)}), bf16[16,64,512]{2,1,0:T(8,128)(2,1)}) %all-gather.15.cloned.1.call-update) | async-done | bytes 1048592 | tf_op jit(solution)/shard_map/all_gather | solution.py:50
  121.3 6.5 all-to-all-start.5
  127.8 1.0 copy.82
  128.8 6.9 %all-to-all-done.5 = bf16[256,4,4,32]{0,3,2,1:T(8,128)(2,1)S(1)} async-done(((bf16[256,4,4,32]{0,3,2,1:T(8,128)(2,1)}), bf16[256,4,4,32]{0,3,2,1:T(8,128)(2,1)S(1)}, u32[]{:S(2)}, u32[]{:S(2)}) %all-to-all-start.5) | async-done | bytes 262176 | tf_op jit(solution)/shard_map/all_to_all | solution.py:29
  135.7 4.3 all-to-all-start.1
  140.0 1.2 copy.94
  141.2 4.1 all-gather.11.cloned.1.call-done
  145.3 2.3 fusion.16
  147.6 18.1 %all-to-all-done.1 = bf16[256,4,4,128]{0,3,2,1:T(8,128)(2,1)} async-done(((bf16[256,4,4,128]{0,3,2,1:T(8,128)(2,1)}), bf16[256,4,4,128]{0,3,2,1:T(8,128)(2,1)}, u32[]{:S(2)}, u32[]{:S(2)}) %all-to-all-start.1) | async-done | bytes 1048608 | tf_op jit(solution)/shard_map/all_to_all | solution.py:29
  165.8 4.5 fusion.7
  170.2 1.0 copy-done.2
  172.3 15.0 %all_to_all.40 = bf16[256,4,4,128]{0,3,1,2:T(8,128)(2,1)S(1)} all-to-all(bf16[256,4,4,128]{0,3,1,2:T(8,128)(2,1)S(1)} %copy.95), channel_id=1, replica_groups=mesh['z'=8,'ylo'=2,'core'=2,'yhi'=4,'x'=4] {'x'}, dimensions={2} | all-to-all | bytes 2097152 | tf_op jit(solution)/shard_map/all_to_all | solution.py:28
  187.3 1.0 copy.96
  188.4 6.5 %all-to-all-start.7 = ((bf16[256,4,4,128]{0,3,2,1:T(8,128)(2,1)}), bf16[256,4,4,128]{0,3,2,1:T(8,128)(2,1)S(1)}, u32[]{:S(2)}, u32[]{:S(2)}) async-start(bf16[256,4,4,128]{0,3,2,1:T(8,128)(2,1)} %copy.96), calls=%async_computation.7 | async-start | bytes 2097152 | tf_op jit(solution)/shard_map/all_to_all | solution.py:29
  195.2 1.1 copy-done.6
  196.3 2.7 multiply_bitcast_fusion
  199.0 5.4 copy.103
  204.5 10.2 %all-to-all-done.7 = bf16[256,4,4,128]{0,3,2,1:T(8,128)(2,1)S(1)} async-done(((bf16[256,4,4,128]{0,3,2,1:T(8,128)(2,1)}), bf16[256,4,4,128]{0,3,2,1:T(8,128)(2,1)S(1)}, u32[]{:S(2)}, u32[]{:S(2)}) %all-to-all-start.7) | async-done | bytes 1048608 | tf_op jit(solution)/shard_map/all_to_all | solution.py:29
  214.7 2.7 convolution_multiply_fusion
  217.4 1.3 dynamic-slice
  218.7 53.0 %all-reduce.8.cloned.1.call-done = (f32[8,2,2,16,1,2048]{5,3,4,2,1,0:T(8,128)}, f32[8,2,2,64,1,512]{5,3,2,1,0,4:T(8,128)}) async-done(((f32[8,2,2,16,1,2048]{5,3,4,2,1,0:T(8,128)}, f32[8,2,2,64,1,512]{5,3,2,1,0,4:T(8,128)}), (f32[8,2,2,16,1,2048]{5,3,4,2,1,0:T(8,128)}, f32[8,2,2,64,1,512]{5,3,2,1,0,4:T(8,128)})) %all-reduce.8.cloned.1.call-update) | async-done | bytes 8388624
  271.7 3.9 constant_dynamic-slice_fusion
  275.6 3.9 constant_dynamic-slice_fusion.1
  279.5 1.6 copy-done.1
  281.1 1.9 fusion.9
  283.2 9.2 %all_to_all.41 = bf16[256,4,4,32]{0,3,1,2:T(8,128)(2,1)S(1)} all-to-all(bf16[256,4,4,32]{0,3,1,2:T(8,128)(2,1)S(1)} %copy.87), channel_id=1, replica_groups=mesh['z'=8,'ylo'=2,'core'=2,'yhi'=4,'x'=4] {'x'}, dimensions={2} | all-to-all | bytes 524288 | tf_op jit(solution)/shard_map/all_to_all | solution.py:28
  293.1 6.5 all-to-all-start.3
  300.4 2.0 convolution_multiply_fusion.1
  302.9 5.1 all-to-all-done.3
  309.3 7.6 %reduce-scatter.13.cloned.1.call-done = f32[1,2,1,64,1,512]{5,3,2,1,0,4:T(8,128)} async-done(((f32[8,2,1,64,1,512]{5,3,2,1,0,4:T(8,128)}), f32[1,2,1,64,1,512]{5,3,2,1,0,4:T(8,128)}) %reduce-scatter.13.cloned.1.call-update) | async-done | bytes 262160 | tf_op jit(solution)/shard_map/reduce_scatter | solution.py:40
  317.0 46.2 %reduce-scatter.9.cloned.1.call-done = f32[1,2,1,16,1,2048]{5,3,4,2,1,0:T(8,128)} async-done(((f32[8,2,1,16,1,2048]{5,3,4,2,1,0:T(8,128)}), f32[1,2,1,16,1,2048]{5,3,4,2,1,0:T(8,128)}) %reduce-scatter.9.cloned.1.call-update) | async-done | bytes 262160 | tf_op jit(solution)/shard_map/reduce_scatter | solution.py:40
  363.3 1.0 convolution_convert_fusion.4
  364.3 233.1 %all-reduce.6.cloned.1.call-done = f32[160,16,16]{0,2,1:T(8,128)} async-done(((f32[160,16,16]{0,2,1:T(8,128)}), f32[160,16,16]{0,2,1:T(8,128)}) %all-reduce.6.cloned.1.call-update) | async-done | bytes 163856 | tf_op jit(solution)/shard_map/psum | solution.py:165
  597.4 1.6 slice.9
  599.0 1.6 slice.8
  600.6 3.0 convolution_convert_fusion.2
  603.6 16.7 %reduce-scatter.15.cloned.1.call-done = f32[1,1,1,64,1,512]{5,3,2,1,0,4:T(8,128)} async-done(((f32[1,2,1,64,1,512]{5,3,2,1,0,4:T(8,128)}), f32[1,1,1,64,1,512]{5,3,2,1,0,4:T(8,128)}) %reduce-scatter.15.cloned.1.call-update) | async-done | bytes 131088 | tf_op jit(solution)/shard_map/reduce_scatter | solution.py:41
  620.3 23.2 %reduce-scatter.11.cloned.1.call-done = f32[1,1,1,16,1,2048]{5,3,4,2,1,0:T(8,128)} async-done(((f32[1,2,1,16,1,2048]{5,3,4,2,1,0:T(8,128)}), f32[1,1,1,16,1,2048]{5,3,4,2,1,0:T(8,128)}) %reduce-scatter.11.cloned.1.call-update) | async-done | bytes 131088 | tf_op jit(solution)/shard_map/reduce_scatter | solution.py:41
  (60 shorter events, 8.0 us)
Async XLA Ops:
  7.2 73.8 %copy-start = (bf16[256,512]{1,0:T(8,128)(2,1)S(1)}, bf16[256,512]{1,0:T(8,128)(2,1)}, u32[]{:S(2)}) copy-start(bf16[256,512]{1,0:T(8,128)(2,1)} %param.6) | copy-start | bytes 786436
  7.2 48.8 %all-gather.13.cloned.1.call-start = ((), (), s32[]{:S(2)}) async-start(), calls=%async_computation.19 | async-start | bytes 1179648 | tf_op jit(solution)/shard_map/all_gather | solution.py:50
  13.6 67.3 %all-gather.9.cloned.1.call-start = ((), (), s32[]{:S(2)}) async-start(), calls=%async_computation.12 | async-start | bytes 3145728 | tf_op jit(solution)/shard_map/all_gather | solution.py:51
  56.0 64.5 %all-gather.15.cloned.1.call-start = ((), (), s32[]{:S(2)}) async-start(), calls=%async_computation.20 | async-start | bytes 1179648 | tf_op jit(solution)/shard_map/all_gather | solution.py:50
  62.3 3.5 copy-start.9
  66.9 17.5 %all-to-all-start.4 = ((bf16[256,4,4,32]{0,3,1,2:T(8,128)(2,1)}), bf16[256,4,4,32]{0,3,1,2:T(8,128)(2,1)S(1)}, u32[]{:S(2)}, u32[]{:S(2)}) async-start(bf16[256,4,4,32]{0,3,1,2:T(8,128)(2,1)} %copy.90), calls=%async_computation.4 | async-start | bytes 524288 | tf_op jit(solution)/shard_map/all_to_all | solution.py:28
  84.4 37.0 %all-to-all-start = ((bf16[256,4,4,128]{0,3,1,2:T(8,128)(2,1)}), bf16[256,4,4,128]{0,3,1,2:T(8,128)(2,1)S(1)}, u32[]{:S(2)}, u32[]{:S(2)}) async-start(bf16[256,4,4,128]{0,3,1,2:T(8,128)(2,1)} %copy.81), calls=%async_computation | async-start | bytes 2097152 | tf_op jit(solution)/shard_map/all_to_all | solution.py:28
  87.9 57.4 %all-gather.11.cloned.1.call-start = ((), (), s32[]{:S(2)}) async-start(), calls=%async_computation.13 | async-start | bytes 3145728 | tf_op jit(solution)/shard_map/all_gather | solution.py:51
  121.3 14.4 %all-to-all-start.5 = ((bf16[256,4,4,32]{0,3,2,1:T(8,128)(2,1)}), bf16[256,4,4,32]{0,3,2,1:T(8,128)(2,1)S(1)}, u32[]{:S(2)}, u32[]{:S(2)}) async-start(bf16[256,4,4,32]{0,3,2,1:T(8,128)(2,1)} %copy.91), calls=%async_computation.5 | async-start | bytes 524288 | tf_op jit(solution)/shard_map/all_to_all | solution.py:29
  127.8 12.2 %copy-start.11 = (bf16[128,16,16]{0,2,1:T(8,128)(2,1)S(1)}, bf16[128,16,16]{0,2,1:T(8,128)(2,1)}, u32[]{:S(2)}) copy-start(bf16[128,16,16]{0,2,1:T(8,128)(2,1)} %param.8) | copy-start | bytes 196612
  135.7 30.0 %all-to-all-start.1 = ((bf16[256,4,4,128]{0,3,2,1:T(8,128)(2,1)}), bf16[256,4,4,128]{0,3,2,1:T(8,128)(2,1)}, u32[]{:S(2)}, u32[]{:S(2)}) async-start(bf16[256,4,4,128]{0,3,2,1:T(8,128)(2,1)} %copy.82), calls=%async_computation.1 | async-start | bytes 2097152 | tf_op jit(solution)/shard_map/all_to_all | solution.py:29
  165.7 5.5 copy-start.7
  170.2 1.0 copy-start.2
  187.3 7.6 %copy-start.8 = (bf16[256,16,128]{0,1,2:T(8,128)(2,1)S(1)}, bf16[256,16,128]{0,1,2:T(8,128)(2,1)}, u32[]{:S(2)}) copy-start(bf16[256,16,128]{0,1,2:T(8,128)(2,1)} %get-tuple-element.21) | copy-start | bytes 3145732
  188.4 26.3 %all-to-all-start.7 = ((bf16[256,4,4,128]{0,3,2,1:T(8,128)(2,1)}), bf16[256,4,4,128]{0,3,2,1:T(8,128)(2,1)S(1)}, u32[]{:S(2)}, u32[]{:S(2)}) async-start(bf16[256,4,4,128]{0,3,2,1:T(8,128)(2,1)} %copy.96), calls=%async_computation.7 | async-start | bytes 2097152 | tf_op jit(solution)/shard_map/all_to_all | solution.py:29
  194.9 76.8 %all-reduce.8.cloned.1.call-start = ((), (), s32[]{:S(2)}) async-start(), calls=%async_computation.21 | async-start | bytes 16777216
  195.2 1.1 copy-start.6
  214.7 2.7 copy-start.4
  217.4 99.6 %reduce-scatter.13.cloned.1.call-start = ((), (), s32[]{:S(2)}) async-start(), calls=%async_computation.17 | async-start | bytes 2359296 | tf_op jit(solution)/shard_map/reduce_scatter | solution.py:40
  275.6 87.7 %reduce-scatter.9.cloned.1.call-start = ((), (), s32[]{:S(2)}) async-start(), calls=%async_computation.14 | async-start | bytes 2359296 | tf_op jit(solution)/shard_map/reduce_scatter | solution.py:40
  279.5 1.6 copy-start.1
  283.1 17.4 %copy-start.3 = (bf16[256,16,128]{0,1,2:T(8,128)(2,1)S(1)}, bf16[256,16,128]{0,1,2:T(8,128)(2,1)}, u32[]{:S(2)}) copy-start(bf16[256,16,128]{0,1,2:T(8,128)(2,1)} %copy-done.2) | copy-start | bytes 3145732
  293.1 14.8 %all-to-all-start.3 = ((bf16[256,4,4,32]{0,3,2,1:T(8,128)(2,1)}), bf16[256,4,4,32]{0,3,2,1:T(8,128)(2,1)S(1)}, u32[]{:S(2)}, u32[]{:S(2)}) async-start(bf16[256,4,4,32]{0,3,2,1:T(8,128)(2,1)} %copy.88), calls=%async_computation.3 | async-start | bytes 524288 | tf_op jit(solution)/shard_map/all_to_all | solution.py:29
  299.6 297.9 %all-reduce.6.cloned.1.call-start = ((), (), s32[]{:S(2)}) async-start(), calls=%async_computation.16 | async-start | bytes 524288 | tf_op jit(solution)/shard_map/psum | solution.py:165
  300.4 7.5 %copy-start.10 = (bf16[256,512]{0,1:T(8,128)(2,1)S(1)}, bf16[256,512]{0,1:T(8,128)(2,1)}, u32[]{:S(2)}) copy-start(bf16[256,512]{0,1:T(8,128)(2,1)} %copy.99) | copy-start | bytes 786436
  302.9 297.7 %copy-start.5 = (bf16[256,4,4,128]{0,3,2,1:T(8,128)(2,1)S(1)}, bf16[256,4,4,128]{0,3,2,1:T(8,128)(2,1)}, u32[]{:S(2)}) copy-start(bf16[256,4,4,128]{0,3,2,1:T(8,128)(2,1)} %copy-done.4) | copy-start | bytes 3145732
  309.3 311.0 %reduce-scatter.15.cloned.1.call-start = ((), (), s32[]{:S(2)}) async-start(), calls=%async_computation.18 | async-start | bytes 393216 | tf_op jit(solution)/shard_map/reduce_scatter | solution.py:41
  317.0 326.5 %reduce-scatter.11.cloned.1.call-start = ((), (), s32[]{:S(2)}) async-start(), calls=%async_computation.15 | async-start | bytes 393216 | tf_op jit(solution)/shard_map/reduce_scatter | solution.py:41
Sparse Core Ops, SparseCore 0:
  13.7 42.2 all-gather.12
  58.1 22.8 all-gather.8
  83.0 37.5 all-gather.14
  122.5 22.7 all-gather.10
  217.5 54.1 all-reduce.7
  275.7 41.1 reduce-scatter.12
  319.8 43.4 reduce-scatter.8
  366.7 230.6 all-reduce.5
  601.0 19.2 reduce-scatter.14
  623.5 19.9 reduce-scatter.10

commit v2 on v1

--- a/solution.py
+++ b/solution.py
@@ -30,27 +30,87 @@
     return shaped.reshape(rows, feat_count, piece)
 
 
-def dp_reduce_scatter(part, row_axis):
-    shape = part.shape
-    rows = shape[row_axis]
+def shift(value, axis, step):
+    n = lax.axis_size(axis)
+    return lax.ppermute(value, axis, [(i, (i + step) % n) for i in range(n)])
+
+
+def swap(value, axis, mask):
+    n = lax.axis_size(axis)
+    return lax.ppermute(value, axis, [(i, i ^ mask) for i in range(n)])
+
+
+def z_ring_reduce_scatter(x):
+    n = x.shape[0]
+    me = lax.axis_index("z")
+    lo, hi = jnp.split(x, 2, axis=-1)
+    fwd = None
+    bwd = None
+    for step in range(1, n):
+        own_f = lax.dynamic_index_in_dim(lo, (me - step) % n, 0, keepdims=False)
+        own_b = lax.dynamic_index_in_dim(hi, (me + step) % n, 0, keepdims=False)
+        fwd = shift(own_f if fwd is None else fwd + own_f, "z", 1)
+        bwd = shift(own_b if bwd is None else bwd + own_b, "z", -1)
+    fwd = fwd + lax.dynamic_index_in_dim(lo, me, 0, keepdims=False)
+    bwd = bwd + lax.dynamic_index_in_dim(hi, me, 0, keepdims=False)
+    return jnp.concatenate([fwd, bwd], axis=-1)
+
+
+def z_ring_all_gather(chunk):
+    n = lax.axis_size("z")
+    me = lax.axis_index("z")
+    out = jnp.zeros((n,) + chunk.shape, chunk.dtype)
+    out = lax.dynamic_update_index_in_dim(out, chunk, me, 0)
+    fwd = chunk
+    bwd = chunk
+    half = n // 2
+    for step in range(1, half):
+        fwd = shift(fwd, "z", 1)
+        bwd = shift(bwd, "z", -1)
+        out = lax.dynamic_update_index_in_dim(out, fwd, (me - step) % n, 0)
+        out = lax.dynamic_update_index_in_dim(out, bwd, (me + step) % n, 0)
+    lo, _ = jnp.split(fwd, 2, axis=-1)
+    _, hi = jnp.split(bwd, 2, axis=-1)
+    last = jnp.concatenate([shift(lo, "z", 1), shift(hi, "z", -1)], axis=-1)
+    out = lax.dynamic_update_index_in_dim(out, last, (me + half) % n, 0)
+    return out
+
+
+def dp_reduce_scatter(part):
+    rows = part.shape[0]
+    rest = part.shape[1:]
     n_z = lax.axis_size("z")
-    split = shape[:row_axis] + (n_z, 2, 2, rows // (4 * n_z)) + shape[row_axis + 1 :]
-    x = part.reshape(split)
-    x = lax.psum_scatter(x, "core", scatter_dimension=row_axis + 2, tiled=True)
-    x = lax.psum_scatter(x, "z", scatter_dimension=row_axis, tiled=True)
-    x = lax.psum_scatter(x, "ylo", scatter_dimension=row_axis + 1, tiled=True)
-    return x.reshape(shape[:row_axis] + (rows // (4 * n_z),) + shape[row_axis + 1 :])
-
-
-def dp_all_gather(local, row_axis):
-    shape = local.shape
-    rows = shape[row_axis]
-    x = local.reshape(shape[:row_axis] + (1, 1, 1, rows) + shape[row_axis + 1 :])
-    x = lax.all_gather(x, "ylo", axis=row_axis + 1, tiled=True)
-    x = lax.all_gather(x, "z", axis=row_axis, tiled=True)
-    x = lax.all_gather(x, "core", axis=row_axis + 2, tiled=True)
-    total = x.shape[row_axis] * x.shape[row_axis + 1] * x.shape[row_axis + 2] * rows
-    return x.reshape(shape[:row_axis] + (total,) + shape[row_axis + 1 :])
+    x = part.reshape((n_z, 2, 2, rows // (4 * n_z)) + rest)
+    core = lax.axis_index("core")
+    mine = lax.dynamic_index_in_dim(x, core, 2, keepdims=False)
+    other = lax.dynamic_index_in_dim(x, 1 - core, 2, keepdims=False)
+    x = mine + swap(other, "core", 1)
+    x = z_ring_reduce_scatter(x)
+    ylo = lax.axis_index("ylo")
+    mine = lax.dynamic_index_in_dim(x, ylo, 0, keepdims=False)
+    other = lax.dynamic_index_in_dim(x, 1 - ylo, 0, keepdims=False)
+    return mine + swap(other, "ylo", 1)
+
+
+def dp_all_gather(local):
+    ylo = lax.axis_index("ylo")
+    got = swap(local, "ylo", 1)
+    pair = jnp.where(ylo == 0, jnp.stack([local, got]), jnp.stack([got, local]))
+    ring = z_ring_all_gather(pair)
+    core = lax.axis_index("core")
+    other = swap(ring, "core", 1)
+    both = jnp.where(core == 0, jnp.stack([ring, other], 2), jnp.stack([other, ring], 2))
+    return both.reshape((-1,) + local.shape[1:])
+
+
+def dp_all_reduce(x):
+    x = x + swap(x, "core", 1)
+    x = x + swap(x, "ylo", 1)
+    mask = 1
+    while mask < lax.axis_size("z"):
+        x = x + swap(x, "z", mask)
+        mask *= 2
+    return x
 
 
 def to_wire(blocks, feat_count):
@@ -80,7 +140,7 @@
     grad_scale = float(tok_rows * n_dp) ** (-0.5)
     tiles_up = group_up // TILE_UP
     tiles_down = group_down // TILE_DOWN
-    up_full = dp_all_gather(up_left, 1)
+    up_full = dp_all_gather(up_left[0])[None]
     token_blocks = tokens.reshape(tok_rows, local_blocks, block_width)
     up_inner = jnp.einsum(
         "tbi,big->tbg", token_blocks, up_full, preferred_element_type=jnp.float32
@@ -94,7 +154,7 @@
         .transpose(0, 2, 1, 3)
     )
     hidden = activated.reshape(tok_rows, local_blocks, hidden_width).astype(jnp.bfloat16)
-    down_full = dp_all_gather(down_left, 1)
+    down_full = dp_all_gather(down_left[0])[None]
     down_inner = jnp.einsum(
         "tbh,bhc->tbc", hidden, down_full, preferred_element_type=jnp.float32
     ).astype(jnp.bfloat16)
@@ -133,8 +193,7 @@
     )
     grad_down_left = dp_reduce_scatter(
         jnp.einsum("tbh,tbc->hbc", hidden, grad_down_inner, preferred_element_type=jnp.float32)
-        * grad_scale,
-        0,
+        * grad_scale
     ).transpose(1, 0, 2)
     grad_hidden = jnp.einsum(
         "tbc,bhc->tbh", grad_down_inner, down_full, preferred_element_type=jnp.float32
@@ -158,11 +217,10 @@
     grad_tokens = grad_tokens.reshape(tok_rows, local_blocks * block_width)
     grad_up_left = dp_reduce_scatter(
         jnp.einsum("tbi,tbg->ibg", token_blocks, grad_up_inner, preferred_element_type=jnp.float32)
-        * grad_scale,
-        0,
+        * grad_scale
     ).transpose(1, 0, 2)
     rights = jnp.concatenate([right_up_term, right_down_term], axis=0)
-    rights = lax.psum(rights, DP_AXES)
+    rights = dp_all_reduce(rights)
     grad_up_right = rights[:group_up]
     grad_down_right = rights[group_up:]
     return (layer_out, grad_tokens, grad_up_left, grad_up_right, grad_down_left, grad_down_right)

time: 652 us -> 406 us (0.62)
  the two profiles are of different devices: /device:TPU:1 before, /device:TPU:2 now
where the time goes in v2:
time: 406 us; the launch traced here: 403 us
  starting transfers between devices  232 us (57%)
  waiting for transfers between devices  83.6 us (21%)
  local copies, waits for them, and re-layouts  35.4 us (9%)
  matrix products  21.7 us (5%)
  other arithmetic  17.4 us (4%)
  blocking collectives  10.6 us (3%)
    ppermute x44, starting transfers between devices, shift(): return lax.ppermute(value, axis, [(i, (i + step) % n) for i in range(n)])  160 us
    ppermute x13, starting transfers between devices, swap(): return lax.ppermute(value, axis, [(i, i ^ mask) for i in range(n)])  35.8 us
    ppermute x13, waiting for transfers between devices, swap(): return lax.ppermute(value, axis, [(i, i ^ mask) for i in range(n)])  35.6 us
    all_to_all x4, waiting for transfers between devices, exchange(): shaped = lax.all_to_all(shaped, 'yhi', 1, 1, tiled=True)  28.6 us
    all_to_all x4, starting transfers between devices, exchange(): shaped = lax.all_to_all(shaped, 'yhi', 1, 1, tiled=True)  21.9 us
    ppermute x44, waiting for transfers between devices, shift(): return lax.ppermute(value, axis, [(i, (i + step) % n) for i in range(n)])  19.4 us
    all_to_all x3, starting transfers between devices, exchange(): shaped = lax.all_to_all(shaped, 'x', 2, 2, tiled=True)  14.6 us
    all_to_all x1, blocking collectives, exchange(): shaped = lax.all_to_all(shaped, 'x', 2, 2, tiled=True)  10.6 us
  transfers between devices with their start and end apart: 64, of which 24 were waited for; matrix products, arithmetic and copies ran while one was open for 13% of the time, Pallas kernels for 0%

profile of v2, /device:TPU:2, one launch (start us, length us, event | category | flops | bytes accessed | tf_op | source)
XLA Modules:
  0.0 402.8 jit_solution(4166939783515984938)
XLA Ops:
  0.7 3.6 collective-permute-start.10
  8.1 10.9 %collective-permute-start.12 = (bf16[2,16,2048]{2,1,0:T(8,128)(2,1)S(1)}, bf16[2,16,2048]{2,1,0:T(8,128)(2,1)S(1)}, u32[]{:S(2)}, u32[]{:S(2)}) collective-permute-start(bf16[2,16,2048]{2,1,0:T(8,128)(2,1)S(1)} %maximum_select_fusion.5), channel_id=1, source_target_pairs={{0,448},{64,0},{128,64},{192,128},{256,192},{320,256},{384,320},{4... | collective-permute-start | bytes 393224 | tf_op jit(solution)/shard_map/ppermute | solution.py:35
  23.7 5.1 %collective-permute-start.14 = (bf16[2,16,2048]{2,1,0:T(8,128)(2,1)S(1)}, bf16[2,16,2048]{2,1,0:T(8,128)(2,1)S(1)}, u32[]{:S(2)}, u32[]{:S(2)}) collective-permute-start(bf16[2,16,2048]{2,1,0:T(8,128)(2,1)S(1)} %collective-permute-done.12), channel_id=1, source_target_pairs={{0,448},{64,0},{128,64},{192,128},{256,192},{320,256},{384,320},{4... | collective-permute-start | bytes 393224 | tf_op jit(solution)/shard_map/ppermute | solution.py:35
  32.1 5.1 %collective-permute-start.16 = (bf16[2,16,2048]{2,1,0:T(8,128)(2,1)S(1)}, bf16[2,16,2048]{2,1,0:T(8,128)(2,1)S(1)}, u32[]{:S(2)}, u32[]{:S(2)}) collective-permute-start(bf16[2,16,2048]{2,1,0:T(8,128)(2,1)S(1)} %collective-permute-done.14), channel_id=1, source_target_pairs={{0,448},{64,0},{128,64},{192,128},{256,192},{320,256},{384,320},{4... | collective-permute-start | bytes 393224 | tf_op jit(solution)/shard_map/ppermute | solution.py:35
  40.5 5.1 %collective-permute-start.18 = (bf16[2,16,1024]{2,1,0:T(8,128)(2,1)S(1)}, bf16[2,16,1024]{2,1,0:T(8,128)(2,1)S(1)}, u32[]{:S(2)}, u32[]{:S(2)}) collective-permute-start(bf16[2,16,1024]{2,1,0:T(8,128)(2,1)S(1)} %split.35), channel_id=1, source_target_pairs={{0,448},{64,0},{128,64},{192,128},{256,192},{320,256},{384,320},{4... | collective-permute-start | bytes 196616 | tf_op jit(solution)/shard_map/ppermute | solution.py:35
  48.9 4.1 %collective-permute-done.17 = bf16[2,16,1024]{2,1,0:T(8,128)(2,1)S(1)} collective-permute-done((bf16[2,16,1024]{2,1,0:T(8,128)(2,1)S(1)}, bf16[2,16,1024]{2,1,0:T(8,128)(2,1)S(1)}, u32[]{:S(2)}, u32[]{:S(2)}) %collective-permute-start.17) | collective-permute-done | bytes 65568 | tf_op jit(solution)/shard_map/ppermute | solution.py:35
  55.6 3.5 collective-permute-start
  64.7 3.9 collective-permute-start.1
  69.7 4.8 %all-to-all-start.4 = ((bf16[256,4,4,32]{0,3,1,2:T(8,128)(2,1)}), bf16[256,4,4,32]{0,3,1,2:T(8,128)(2,1)S(1)}, u32[]{:S(2)}, u32[]{:S(2)}) async-start(bf16[256,4,4,32]{0,3,1,2:T(8,128)(2,1)} %copy.97), calls=%async_computation.4 | async-start | bytes 524288 | tf_op jit(solution)/shard_map/all_to_all | solution.py:28
  74.7 3.1 collective-permute-start.4
  85.5 4.8 %all-to-all-start = ((bf16[256,4,4,128]{0,3,1,2:T(8,128)(2,1)}), bf16[256,4,4,128]{0,3,1,2:T(8,128)(2,1)S(1)}, u32[]{:S(2)}, u32[]{:S(2)}) async-start(bf16[256,4,4,128]{0,3,1,2:T(8,128)(2,1)} %copy.89), calls=%async_computation | async-start | bytes 2097152 | tf_op jit(solution)/shard_map/all_to_all | solution.py:28
  91.1 4.3 %collective-permute-start.6 = (bf16[2,64,512]{2,1,0:T(8,128)(2,1)}, bf16[2,64,512]{2,1,0:T(8,128)(2,1)S(1)}, u32[]{:S(2)}, u32[]{:S(2)}) collective-permute-start(bf16[2,64,512]{2,1,0:T(8,128)(2,1)} %collective-permute-done.4), channel_id=1, source_target_pairs={{0,448},{64,0},{128,64},{192,128},{256,192},{320,256},{384,320},{4... | collective-permute-start | bytes 393224 | tf_op jit(solution)/shard_map/ppermute | solution.py:35
  98.3 5.4 %collective-permute-start.8 = (bf16[2,64,256]{2,1,0:T(8,128)(2,1)S(1)}, bf16[2,64,256]{2,1,0:T(8,128)(2,1)S(1)}, u32[]{:S(2)}, u32[]{:S(2)}) collective-permute-start(bf16[2,64,256]{2,1,0:T(8,128)(2,1)S(1)} %split.33), channel_id=1, source_target_pairs={{0,448},{64,0},{128,64},{192,128},{256,192},{320,256},{384,320},{4... | collective-permute-start | bytes 196616 | tf_op jit(solution)/shard_map/ppermute | solution.py:35
  105.6 6.4 %all-to-all-start.5 = ((bf16[256,4,4,32]{0,3,2,1:T(8,128)(2,1)}), bf16[256,4,4,32]{0,3,2,1:T(8,128)(2,1)S(1)}, u32[]{:S(2)}, u32[]{:S(2)}) async-start(bf16[256,4,4,32]{0,3,2,1:T(8,128)(2,1)} %copy.98), calls=%async_computation.5 | async-start | bytes 524288 | tf_op jit(solution)/shard_map/all_to_all | solution.py:29
  115.2 6.5 %all-to-all-done.5 = bf16[256,4,4,32]{0,3,2,1:T(8,128)(2,1)S(1)} async-done(((bf16[256,4,4,32]{0,3,2,1:T(8,128)(2,1)}), bf16[256,4,4,32]{0,3,2,1:T(8,128)(2,1)S(1)}, u32[]{:S(2)}, u32[]{:S(2)}) %all-to-all-start.5) | async-done | bytes 262176 | tf_op jit(solution)/shard_map/all_to_all | solution.py:29
  122.4 3.5 all-to-all-start.1
  131.8 14.1 %all-to-all-done.1 = bf16[256,4,4,128]{0,3,2,1:T(8,128)(2,1)S(1)} async-done(((bf16[256,4,4,128]{0,3,2,1:T(8,128)(2,1)}), bf16[256,4,4,128]{0,3,2,1:T(8,128)(2,1)S(1)}, u32[]{:S(2)}, u32[]{:S(2)}) %all-to-all-start.1) | async-done | bytes 1048608 | tf_op jit(solution)/shard_map/all_to_all | solution.py:29
  145.9 5.2 %fusion.7 = (bf16[256,16,128]{0,1,2:T(8,128)(2,1)}, bf16[256,16,128]{0,1,2:T(8,128)(2,1)S(1)}) fusion(f32[256,16,128]{0,2,1:T(8,128)} %bitcast.241, bf16[128,16,16]{2,1,0:T(8,128)(2,1)} %copy.100, bf16[256,16,128]{0,2,1:T(8,128)(2,1)S(1)} %bitcast.242), kind=kOutput, calls=%fused_computation.18 | convolution fusion | flops 22544384 | bytes 5308416 | tf_op jit(solution)/shard_map/tjg,gjk->tkg/dot_general | solution.py:149
  154.8 5.4 %copy.108 = f32[2048,1,512]{2,0,1:T(8,128)} copy(f32[2048,1,512]{0,2,1:T(8,128)} %multiply_bitcast_fusion) | data formatting | bytes 8388608 | tf_op jit(solution)/shard_map/mul | solution.py:195
  160.2 3.2 dynamic-slice_bitcast_fusion
  166.3 10.6 %all_to_all.40 = bf16[256,4,4,32]{0,3,1,2:T(8,128)(2,1)S(1)} all-to-all(bf16[256,4,4,32]{0,3,1,2:T(8,128)(2,1)S(1)} %copy.94), channel_id=1, replica_groups=mesh['z'=8,'ylo'=2,'core'=2,'yhi'=4,'x'=4] {'x'}, dimensions={2} | all-to-all | bytes 524288 | tf_op jit(solution)/shard_map/all_to_all | solution.py:28
  177.7 8.5 %all-to-all-start.3 = ((bf16[256,4,4,32]{0,3,2,1:T(8,128)(2,1)}), bf16[256,4,4,32]{0,3,2,1:T(8,128)(2,1)}, u32[]{:S(2)}, u32[]{:S(2)}) async-start(bf16[256,4,4,32]{0,3,2,1:T(8,128)(2,1)} %copy.95), calls=%async_computation.3 | async-start | bytes 524288 | tf_op jit(solution)/shard_map/all_to_all | solution.py:29
  189.2 8.0 %all-to-all-done.3 = bf16[256,4,4,32]{0,3,2,1:T(8,128)(2,1)} async-done(((bf16[256,4,4,32]{0,3,2,1:T(8,128)(2,1)}), bf16[256,4,4,32]{0,3,2,1:T(8,128)(2,1)}, u32[]{:S(2)}, u32[]{:S(2)}) %all-to-all-start.3) | async-done | bytes 262176 | tf_op jit(solution)/shard_map/all_to_all | solution.py:29
  203.8 4.9 %all-to-all-start.6 = ((bf16[256,4,4,128]{0,3,1,2:T(8,128)(2,1)}), bf16[256,4,4,128]{0,3,1,2:T(8,128)(2,1)S(1)}, u32[]{:S(2)}, u32[]{:S(2)}) async-start(bf16[256,4,4,128]{0,3,1,2:T(8,128)(2,1)} %copy.101), calls=%async_computation.6 | async-start | bytes 2097152 | tf_op jit(solution)/shard_map/all_to_all | solution.py:28
  208.8 4.2 %collective-permute-start.37 = (f32[160,16,16]{0,2,1:T(8,128)S(1)}, f32[160,16,16]{0,2,1:T(8,128)S(1)}, u32[]{:S(2)}, u32[]{:S(2)}) collective-permute-start(f32[160,16,16]{0,2,1:T(8,128)S(1)} %fusion.32), channel_id=1, source_target_pairs={{0,32},{32,0},{1,33},{33,1},{2,34},{34,2},{3,35},{35,3},{4,36},{36... | collective-permute-start | bytes 491528 | tf_op jit(solution)/shard_map/ppermute | solution.py:40
  213.0 6.7 %collective-permute-done.37 = f32[160,16,16]{0,2,1:T(8,128)S(1)} collective-permute-done((f32[160,16,16]{0,2,1:T(8,128)S(1)}, f32[160,16,16]{0,2,1:T(8,128)S(1)}, u32[]{:S(2)}, u32[]{:S(2)}) %collective-permute-start.37) | collective-permute-done | bytes 163872 | tf_op jit(solution)/shard_map/ppermute | solution.py:40
  221.6 7.9 %collective-permute-done.38 = f32[160,16,16]{0,2,1:T(8,128)S(1)} collective-permute-done((f32[160,16,16]{0,2,1:T(8,128)S(1)}, f32[160,16,16]{0,2,1:T(8,128)S(1)}, u32[]{:S(2)}, u32[]{:S(2)}) %collective-permute-start.38) | collective-permute-done | bytes 163872 | tf_op jit(solution)/shard_map/ppermute | solution.py:40
  232.7 3.5 all-to-all-start.7
  236.2 8.8 %collective-permute-done.39 = f32[160,16,16]{0,2,1:T(8,128)S(1)} collective-permute-done((f32[160,16,16]{0,2,1:T(8,128)S(1)}, f32[160,16,16]{0,2,1:T(8,128)S(1)}, u32[]{:S(2)}, u32[]{:S(2)}) %collective-permute-start.39) | collective-permute-done | bytes 163872 | tf_op jit(solution)/shard_map/ppermute | solution.py:40
  245.1 4.9 %collective-permute-start.40 = (f32[160,16,16]{0,2,1:T(8,128)S(1)}, f32[160,16,16]{0,2,1:T(8,128)S(1)}, u32[]{:S(2)}, u32[]{:S(2)}) collective-permute-start(f32[160,16,16]{0,2,1:T(8,128)S(1)} %add.396), channel_id=1, source_target_pairs={{0,256},{64,320},{128,384},{192,448},{256,0},{320,64},{384,128},{4... | collective-permute-start | bytes 491528 | tf_op jit(solution)/shard_map/ppermute | solution.py:40
  257.6 6.1 %collective-permute-done.40 = f32[160,16,16]{0,2,1:T(8,128)S(1)} collective-permute-done((f32[160,16,16]{0,2,1:T(8,128)S(1)}, f32[160,16,16]{0,2,1:T(8,128)S(1)}, u32[]{:S(2)}, u32[]{:S(2)}) %collective-permute-start.40) | collective-permute-done | bytes 163872 | tf_op jit(solution)/shard_map/ppermute | solution.py:40
  265.1 3.4 collective-permute-start.49
  272.9 4.3 %collective-permute-start.50 = (f32[2,64,1,256]{3,1,2,0:T(8,128)}, f32[2,64,1,256]{3,1,2,0:T(8,128)}, u32[]{:S(2)}, u32[]{:S(2)}) collective-permute-start(f32[2,64,1,256]{3,1,2,0:T(8,128)} %bitcast_add_fusion.8), channel_id=1, source_target_pairs={{0,448},{64,0},{128,64},{192,128},{256,192},{320,256},{384,320},{4... | collective-permute-start | bytes 393224 | tf_op jit(solution)/shard_map/ppermute | solution.py:35
  287.0 5.1 %collective-permute-start.51 = (f32[2,64,1,256]{3,1,2,0:T(8,128)S(1)}, f32[2,64,1,256]{3,1,2,0:T(8,128)S(1)}, u32[]{:S(2)}, u32[]{:S(2)}) collective-permute-start(f32[2,64,1,256]{3,1,2,0:T(8,128)S(1)} %bitcast_add_fusion.7), channel_id=1, source_target_pairs={{0,448},{64,0},{128,64},{192,128},{256,192},{320,256},{384,320},{4... | collective-permute-start | bytes 393224 | tf_op jit(solution)/shard_map/ppermute | solution.py:35
  298.0 5.1 %collective-permute-start.52 = (f32[2,64,1,256]{3,1,2,0:T(8,128)S(1)}, f32[2,64,1,256]{3,1,2,0:T(8,128)S(1)}, u32[]{:S(2)}, u32[]{:S(2)}) collective-permute-start(f32[2,64,1,256]{3,1,2,0:T(8,128)S(1)} %bitcast_add_fusion.6), channel_id=1, source_target_pairs={{0,448},{64,0},{128,64},{192,128},{256,192},{320,256},{384,320},{4... | collective-permute-start | bytes 393224 | tf_op jit(solution)/shard_map/ppermute | solution.py:35
  307.1 5.1 %collective-permute-start.53 = (f32[2,64,1,256]{3,1,2,0:T(8,128)S(1)}, f32[2,64,1,256]{3,1,2,0:T(8,128)S(1)}, u32[]{:S(2)}, u32[]{:S(2)}) collective-permute-start(f32[2,64,1,256]{3,1,2,0:T(8,128)S(1)} %bitcast_add_fusion.5), channel_id=1, source_target_pairs={{0,448},{64,0},{128,64},{192,128},{256,192},{320,256},{384,320},{4... | collective-permute-start | bytes 393224 | tf_op jit(solution)/shard_map/ppermute | solution.py:35
  315.3 5.1 %collective-permute-start.54 = (f32[2,64,1,256]{3,1,2,0:T(8,128)S(1)}, f32[2,64,1,256]{3,1,2,0:T(8,128)S(1)}, u32[]{:S(2)}, u32[]{:S(2)}) collective-permute-start(f32[2,64,1,256]{3,1,2,0:T(8,128)S(1)} %bitcast_add_fusion.4), channel_id=1, source_target_pairs={{0,448},{64,0},{128,64},{192,128},{256,192},{320,256},{384,320},{4... | collective-permute-start | bytes 393224 | tf_op jit(solution)/shard_map/ppermute | solution.py:35
  323.4 5.1 %collective-permute-start.55 = (f32[2,64,1,256]{3,1,2,0:T(8,128)S(1)}, f32[2,64,1,256]{3,1,2,0:T(8,128)S(1)}, u32[]{:S(2)}, u32[]{:S(2)}) collective-permute-start(f32[2,64,1,256]{3,1,2,0:T(8,128)S(1)} %bitcast_add_fusion.3), channel_id=1, source_target_pairs={{0,448},{64,0},{128,64},{192,128},{256,192},{320,256},{384,320},{4... | collective-permute-start | bytes 393224 | tf_op jit(solution)/shard_map/ppermute | solution.py:35
  333.7 3.0 collective-permute-start.56
  336.7 5.6 %collective-permute-start.28 = (f32[2,16,1,1024]{3,1,2,0:T(8,128)S(1)}, f32[2,16,1,1024]{3,1,2,0:T(8,128)S(1)}, u32[]{:S(2)}, u32[]{:S(2)}) collective-permute-start(f32[2,16,1,1024]{3,1,2,0:T(8,128)S(1)} %dynamic-slice_bitcast_fusion.4), channel_id=1, source_target_pairs={{0,448},{64,0},{128,64},{192,128},{256,192},{320,256},{384,320},{4... | collective-permute-start | bytes 393224 | tf_op jit(solution)/shard_map/ppermute | solution.py:35
  344.8 5.6 %collective-permute-start.29 = (f32[2,16,1,1024]{3,1,2,0:T(8,128)S(1)}, f32[2,16,1,1024]{3,1,2,0:T(8,128)S(1)}, u32[]{:S(2)}, u32[]{:S(2)}) collective-permute-start(f32[2,16,1,1024]{3,1,2,0:T(8,128)S(1)} %bitcast_add_fusion.22), channel_id=1, source_target_pairs={{0,448},{64,0},{128,64},{192,128},{256,192},{320,256},{384,320},{4... | collective-permute-start | bytes 393224 | tf_op jit(solution)/shard_map/ppermute | solution.py:35
  353.5 5.6 %collective-permute-start.30 = (f32[2,16,1,1024]{3,1,2,0:T(8,128)S(1)}, f32[2,16,1,1024]{3,1,2,0:T(8,128)S(1)}, u32[]{:S(2)}, u32[]{:S(2)}) collective-permute-start(f32[2,16,1,1024]{3,1,2,0:T(8,128)S(1)} %bitcast_add_fusion.21), channel_id=1, source_target_pairs={{0,448},{64,0},{128,64},{192,128},{256,192},{320,256},{384,320},{4... | collective-permute-start | bytes 393224 | tf_op jit(solution)/shard_map/ppermute | solution.py:35
  362.6 5.6 %collective-permute-start.31 = (f32[2,16,1,1024]{3,1,2,0:T(8,128)S(1)}, f32[2,16,1,1024]{3,1,2,0:T(8,128)S(1)}, u32[]{:S(2)}, u32[]{:S(2)}) collective-permute-start(f32[2,16,1,1024]{3,1,2,0:T(8,128)S(1)} %bitcast_add_fusion.20), channel_id=1, source_target_pairs={{0,448},{64,0},{128,64},{192,128},{256,192},{320,256},{384,320},{4... | collective-permute-start | bytes 393224 | tf_op jit(solution)/shard_map/ppermute | solution.py:35
  370.9 5.6 %collective-permute-start.32 = (f32[2,16,1,1024]{3,1,2,0:T(8,128)S(1)}, f32[2,16,1,1024]{3,1,2,0:T(8,128)S(1)}, u32[]{:S(2)}, u32[]{:S(2)}) collective-permute-start(f32[2,16,1,1024]{3,1,2,0:T(8,128)S(1)} %bitcast_add_fusion.19), channel_id=1, source_target_pairs={{0,448},{64,0},{128,64},{192,128},{256,192},{320,256},{384,320},{4... | collective-permute-start | bytes 393224 | tf_op jit(solution)/shard_map/ppermute | solution.py:35
  379.0 5.6 %collective-permute-start.33 = (f32[2,16,1,1024]{3,1,2,0:T(8,128)S(1)}, f32[2,16,1,1024]{3,1,2,0:T(8,128)S(1)}, u32[]{:S(2)}, u32[]{:S(2)}) collective-permute-start(f32[2,16,1,1024]{3,1,2,0:T(8,128)S(1)} %bitcast_add_fusion.18), channel_id=1, source_target_pairs={{0,448},{64,0},{128,64},{192,128},{256,192},{320,256},{384,320},{4... | collective-permute-start | bytes 393224 | tf_op jit(solution)/shard_map/ppermute | solution.py:35
  387.1 5.6 %collective-permute-start.34 = (f32[2,16,1,1024]{3,1,2,0:T(8,128)S(1)}, f32[2,16,1,1024]{3,1,2,0:T(8,128)S(1)}, u32[]{:S(2)}, u32[]{:S(2)}) collective-permute-start(f32[2,16,1,1024]{3,1,2,0:T(8,128)S(1)} %bitcast_add_fusion.17), channel_id=1, source_target_pairs={{0,448},{64,0},{128,64},{192,128},{256,192},{320,256},{384,320},{4... | collective-permute-start | bytes 393224 | tf_op jit(solution)/shard_map/ppermute | solution.py:35
  395.3 2.9 collective-permute-start.35
  398.8 3.3 collective-permute-done.35
  (223 shorter events, 136.7 us)
Async XLA Ops:
  8.1 15.6 %collective-permute-start.12 = (bf16[2,16,2048]{2,1,0:T(8,128)(2,1)S(1)}, bf16[2,16,2048]{2,1,0:T(8,128)(2,1)S(1)}, u32[]{:S(2)}, u32[]{:S(2)}) collective-permute-start(bf16[2,16,2048]{2,1,0:T(8,128)(2,1)S(1)} %maximum_select_fusion.5), channel_id=1, source_target_pairs={{0,448},{64,0},{128,64},{192,128},{256,192},{320,256},{384,320},{4... | collective-permute-start | bytes 393224 | tf_op jit(solution)/shard_map/ppermute | solution.py:35
  19.1 9.8 %collective-permute-start.11 = (bf16[2,16,2048]{2,1,0:T(8,128)(2,1)S(1)}, bf16[2,16,2048]{2,1,0:T(8,128)(2,1)S(1)}, u32[]{:S(2)}, u32[]{:S(2)}) collective-permute-start(bf16[2,16,2048]{2,1,0:T(8,128)(2,1)S(1)} %maximum_select_fusion.5), channel_id=1, source_target_pairs={{0,64},{64,128},{128,192},{192,256},{256,320},{320,384},{384,448},... | collective-permute-start | bytes 393224 | tf_op jit(solution)/shard_map/ppermute | solution.py:35
  23.7 8.4 %collective-permute-start.14 = (bf16[2,16,2048]{2,1,0:T(8,128)(2,1)S(1)}, bf16[2,16,2048]{2,1,0:T(8,128)(2,1)S(1)}, u32[]{:S(2)}, u32[]{:S(2)}) collective-permute-start(bf16[2,16,2048]{2,1,0:T(8,128)(2,1)S(1)} %collective-permute-done.12), channel_id=1, source_target_pairs={{0,448},{64,0},{128,64},{192,128},{256,192},{320,256},{384,320},{4... | collective-permute-start | bytes 393224 | tf_op jit(solution)/shard_map/ppermute | solution.py:35
  28.8 8.4 %collective-permute-start.13 = (bf16[2,16,2048]{2,1,0:T(8,128)(2,1)S(1)}, bf16[2,16,2048]{2,1,0:T(8,128)(2,1)S(1)}, u32[]{:S(2)}, u32[]{:S(2)}) collective-permute-start(bf16[2,16,2048]{2,1,0:T(8,128)(2,1)S(1)} %collective-permute-done.11), channel_id=1, source_target_pairs={{0,64},{64,128},{128,192},{192,256},{256,320},{320,384},{384,448},... | collective-permute-start | bytes 393224 | tf_op jit(solution)/shard_map/ppermute | solution.py:35
  32.1 8.4 %collective-permute-start.16 = (bf16[2,16,2048]{2,1,0:T(8,128)(2,1)S(1)}, bf16[2,16,2048]{2,1,0:T(8,128)(2,1)S(1)}, u32[]{:S(2)}, u32[]{:S(2)}) collective-permute-start(bf16[2,16,2048]{2,1,0:T(8,128)(2,1)S(1)} %collective-permute-done.14), channel_id=1, source_target_pairs={{0,448},{64,0},{128,64},{192,128},{256,192},{320,256},{384,320},{4... | collective-permute-start | bytes 393224 | tf_op jit(solution)/shard_map/ppermute | solution.py:35
  37.2 8.4 %collective-permute-start.15 = (bf16[2,16,2048]{2,1,0:T(8,128)(2,1)S(1)}, bf16[2,16,2048]{2,1,0:T(8,128)(2,1)S(1)}, u32[]{:S(2)}, u32[]{:S(2)}) collective-permute-start(bf16[2,16,2048]{2,1,0:T(8,128)(2,1)S(1)} %collective-permute-done.13), channel_id=1, source_target_pairs={{0,64},{64,128},{128,192},{192,256},{256,320},{320,384},{384,448},... | collective-permute-start | bytes 393224 | tf_op jit(solution)/shard_map/ppermute | solution.py:35
  40.5 8.4 %collective-permute-start.18 = (bf16[2,16,1024]{2,1,0:T(8,128)(2,1)S(1)}, bf16[2,16,1024]{2,1,0:T(8,128)(2,1)S(1)}, u32[]{:S(2)}, u32[]{:S(2)}) collective-permute-start(bf16[2,16,1024]{2,1,0:T(8,128)(2,1)S(1)} %split.35), channel_id=1, source_target_pairs={{0,448},{64,0},{128,64},{192,128},{256,192},{320,256},{384,320},{4... | collective-permute-start | bytes 196616 | tf_op jit(solution)/shard_map/ppermute | solution.py:35
  53.7 26.8 %collective-permute-start.19 = (bf16[8,2,16,2048]{3,2,1,0:T(8,128)(2,1)}, bf16[8,2,16,2048]{3,2,1,0:T(8,128)(2,1)}, u32[]{:S(2)}, u32[]{:S(2)}) collective-permute-start(bf16[8,2,16,2048]{3,2,1,0:T(8,128)(2,1)} %fusion.30), channel_id=1, source_target_pairs={{0,16},{16,0},{1,17},{17,1},{2,18},{18,2},{3,19},{19,3},{4,20},{20... | collective-permute-start | bytes 3145736 | tf_op jit(solution)/shard_map/ppermute | solution.py:40
  62.8 11.9 %collective-permute-start.2 = (bf16[2,64,512]{2,1,0:T(8,128)(2,1)S(1)}, bf16[2,64,512]{2,1,0:T(8,128)(2,1)S(1)}, u32[]{:S(2)}, u32[]{:S(2)}) collective-permute-start(bf16[2,64,512]{2,1,0:T(8,128)(2,1)S(1)} %maximum_select_fusion.3), channel_id=1, source_target_pairs={{0,448},{64,0},{128,64},{192,128},{256,192},{320,256},{384,320},{4... | collective-permute-start | bytes 393224 | tf_op jit(solution)/shard_map/ppermute | solution.py:35
  64.7 13.1 %collective-permute-start.1 = (bf16[2,64,512]{2,1,0:T(8,128)(2,1)S(1)}, bf16[2,64,512]{2,1,0:T(8,128)(2,1)S(1)}, u32[]{:S(2)}, u32[]{:S(2)}) collective-permute-start(bf16[2,64,512]{2,1,0:T(8,128)(2,1)S(1)} %maximum_select_fusion.3), channel_id=1, source_target_pairs={{0,64},{64,128},{128,192},{192,256},{256,320},{320,384},{384,448},... | collective-permute-start | bytes 393224 | tf_op jit(solution)/shard_map/ppermute | solution.py:35
  69.7 15.8 %all-to-all-start.4 = ((bf16[256,4,4,32]{0,3,1,2:T(8,128)(2,1)}), bf16[256,4,4,32]{0,3,1,2:T(8,128)(2,1)S(1)}, u32[]{:S(2)}, u32[]{:S(2)}) async-start(bf16[256,4,4,32]{0,3,1,2:T(8,128)(2,1)} %copy.97), calls=%async_computation.4 | async-start | bytes 524288 | tf_op jit(solution)/shard_map/all_to_all | solution.py:28
  74.7 16.4 %collective-permute-start.4 = (bf16[2,64,512]{2,1,0:T(8,128)(2,1)S(1)}, bf16[2,64,512]{2,1,0:T(8,128)(2,1)}, u32[]{:S(2)}, u32[]{:S(2)}) collective-permute-start(bf16[2,64,512]{2,1,0:T(8,128)(2,1)S(1)} %collective-permute-done.2), channel_id=1, source_target_pairs={{0,448},{64,0},{128,64},{192,128},{256,192},{320,256},{384,320},{4... | collective-permute-start | bytes 393224 | tf_op jit(solution)/shard_map/ppermute | solution.py:35
  77.8 17.6 %collective-permute-start.3 = (bf16[2,64,512]{2,1,0:T(8,128)(2,1)S(1)}, bf16[2,64,512]{2,1,0:T(8,128)(2,1)S(1)}, u32[]{:S(2)}, u32[]{:S(2)}) collective-permute-start(bf16[2,64,512]{2,1,0:T(8,128)(2,1)S(1)} %collective-permute-done.1), channel_id=1, source_target_pairs={{0,64},{64,128},{128,192},{192,256},{256,320},{320,384},{384,448},... | collective-permute-start | bytes 393224 | tf_op jit(solution)/shard_map/ppermute | solution.py:35
  85.5 20.1 %all-to-all-start = ((bf16[256,4,4,128]{0,3,1,2:T(8,128)(2,1)}), bf16[256,4,4,128]{0,3,1,2:T(8,128)(2,1)S(1)}, u32[]{:S(2)}, u32[]{:S(2)}) async-start(bf16[256,4,4,128]{0,3,1,2:T(8,128)(2,1)} %copy.89), calls=%async_computation | async-start | bytes 2097152 | tf_op jit(solution)/shard_map/all_to_all | solution.py:28
  95.4 8.3 %collective-permute-start.5 = (bf16[2,64,512]{2,1,0:T(8,128)(2,1)S(1)}, bf16[2,64,512]{2,1,0:T(8,128)(2,1)S(1)}, u32[]{:S(2)}, u32[]{:S(2)}) collective-permute-start(bf16[2,64,512]{2,1,0:T(8,128)(2,1)S(1)} %collective-permute-done.3), channel_id=1, source_target_pairs={{0,64},{64,128},{128,192},{192,256},{256,320},{320,384},{384,448},... | collective-permute-start | bytes 393224 | tf_op jit(solution)/shard_map/ppermute | solution.py:35
  98.3 13.7 %collective-permute-start.8 = (bf16[2,64,256]{2,1,0:T(8,128)(2,1)S(1)}, bf16[2,64,256]{2,1,0:T(8,128)(2,1)S(1)}, u32[]{:S(2)}, u32[]{:S(2)}) collective-permute-start(bf16[2,64,256]{2,1,0:T(8,128)(2,1)S(1)} %split.33), channel_id=1, source_target_pairs={{0,448},{64,0},{128,64},{192,128},{256,192},{320,256},{384,320},{4... | collective-permute-start | bytes 196616 | tf_op jit(solution)/shard_map/ppermute | solution.py:35
  103.7 8.4 %collective-permute-start.7 = (bf16[2,64,256]{2,1,0:T(8,128)(2,1)S(1)}, bf16[2,64,256]{2,1,0:T(8,128)(2,1)S(1)}, u32[]{:S(2)}, u32[]{:S(2)}) collective-permute-start(bf16[2,64,256]{2,1,0:T(8,128)(2,1)S(1)} %split.32), channel_id=1, source_target_pairs={{0,64},{64,128},{128,192},{192,256},{256,320},{320,384},{384,448},... | collective-permute-start | bytes 196616 | tf_op jit(solution)/shard_map/ppermute | solution.py:35
  105.6 16.1 %all-to-all-start.5 = ((bf16[256,4,4,32]{0,3,2,1:T(8,128)(2,1)}), bf16[256,4,4,32]{0,3,2,1:T(8,128)(2,1)S(1)}, u32[]{:S(2)}, u32[]{:S(2)}) async-start(bf16[256,4,4,32]{0,3,2,1:T(8,128)(2,1)} %copy.98), calls=%async_computation.5 | async-start | bytes 524288 | tf_op jit(solution)/shard_map/all_to_all | solution.py:29
  112.1 15.1 %collective-permute-start.9 = (bf16[8,2,64,512]{3,2,1,0:T(8,128)(2,1)S(1)}, bf16[8,2,64,512]{3,2,1,0:T(8,128)(2,1)}, u32[]{:S(2)}, u32[]{:S(2)}) collective-permute-start(bf16[8,2,64,512]{3,2,1,0:T(8,128)(2,1)S(1)} %fusion.28), channel_id=1, source_target_pairs={{0,16},{16,0},{1,17},{17,1},{2,18},{18,2},{3,19},{19,3},{4,20},{20... | collective-permute-start | bytes 3145736 | tf_op jit(solution)/shard_map/ppermute | solution.py:40
  122.4 23.4 %all-to-all-start.1 = ((bf16[256,4,4,128]{0,3,2,1:T(8,128)(2,1)}), bf16[256,4,4,128]{0,3,2,1:T(8,128)(2,1)S(1)}, u32[]{:S(2)}, u32[]{:S(2)}) async-start(bf16[256,4,4,128]{0,3,2,1:T(8,128)(2,1)} %copy.90), calls=%async_computation.1 | async-start | bytes 2097152 | tf_op jit(solution)/shard_map/all_to_all | solution.py:29
  163.4 86.6 %collective-permute-start.41 = (f32[8,2,64,1,512]{4,2,1,0,3:T(8,128)}, f32[8,2,64,1,512]{4,2,1,0,3:T(8,128)}, u32[]{:S(2)}, u32[]{:S(2)}) collective-permute-start(f32[8,2,64,1,512]{4,2,1,0,3:T(8,128)} %dynamic-slice_bitcast_fusion), channel_id=1, source_target_pairs={{0,16},{16,0},{1,17},{17,1},{2,18},{18,2},{3,19},{19,3},{4,20},{20... | collective-permute-start | bytes 6291464 | tf_op jit(solution)/shard_map/ppermute | solution.py:40
  177.7 19.5 %all-to-all-start.3 = ((bf16[256,4,4,32]{0,3,2,1:T(8,128)(2,1)}), bf16[256,4,4,32]{0,3,2,1:T(8,128)(2,1)}, u32[]{:S(2)}, u32[]{:S(2)}) async-start(bf16[256,4,4,32]{0,3,2,1:T(8,128)(2,1)} %copy.95), calls=%async_computation.3 | async-start | bytes 524288 | tf_op jit(solution)/shard_map/all_to_all | solution.py:29
  198.8 10.0 %collective-permute-start.36 = (f32[160,16,16]{0,2,1:T(8,128)S(1)}, f32[160,16,16]{0,2,1:T(8,128)S(1)}, u32[]{:S(2)}, u32[]{:S(2)}) collective-permute-start(f32[160,16,16]{0,2,1:T(8,128)S(1)} %pad_maximum_fusion), channel_id=1, source_target_pairs={{0,16},{16,0},{1,17},{17,1},{2,18},{18,2},{3,19},{19,3},{4,20},{20... | collective-permute-start | bytes 491528 | tf_op jit(solution)/shard_map/ppermute | solution.py:40
  203.8 27.8 %all-to-all-start.6 = ((bf16[256,4,4,128]{0,3,1,2:T(8,128)(2,1)}), bf16[256,4,4,128]{0,3,1,2:T(8,128)(2,1)S(1)}, u32[]{:S(2)}, u32[]{:S(2)}) async-start(bf16[256,4,4,128]{0,3,1,2:T(8,128)(2,1)} %copy.101), calls=%async_computation.6 | async-start | bytes 2097152 | tf_op jit(solution)/shard_map/all_to_all | solution.py:28
  208.8 10.9 %collective-permute-start.37 = (f32[160,16,16]{0,2,1:T(8,128)S(1)}, f32[160,16,16]{0,2,1:T(8,128)S(1)}, u32[]{:S(2)}, u32[]{:S(2)}) collective-permute-start(f32[160,16,16]{0,2,1:T(8,128)S(1)} %fusion.32), channel_id=1, source_target_pairs={{0,32},{32,0},{1,33},{33,1},{2,34},{34,2},{3,35},{35,3},{4,36},{36... | collective-permute-start | bytes 491528 | tf_op jit(solution)/shard_map/ppermute | solution.py:40
  219.7 9.8 %collective-permute-start.38 = (f32[160,16,16]{0,2,1:T(8,128)S(1)}, f32[160,16,16]{0,2,1:T(8,128)S(1)}, u32[]{:S(2)}, u32[]{:S(2)}) collective-permute-start(f32[160,16,16]{0,2,1:T(8,128)S(1)} %add.394), channel_id=1, source_target_pairs={{0,64},{64,0},{128,192},{192,128},{256,320},{320,256},{384,448},{4... | collective-permute-start | bytes 491528 | tf_op jit(solution)/shard_map/ppermute | solution.py:40
  229.6 15.5 %collective-permute-start.39 = (f32[160,16,16]{0,2,1:T(8,128)S(1)}, f32[160,16,16]{0,2,1:T(8,128)S(1)}, u32[]{:S(2)}, u32[]{:S(2)}) collective-permute-start(f32[160,16,16]{0,2,1:T(8,128)S(1)} %add.395), channel_id=1, source_target_pairs={{0,128},{64,192},{128,0},{192,64},{256,384},{320,448},{384,256},{4... | collective-permute-start | bytes 491528 | tf_op jit(solution)/shard_map/ppermute | solution.py:40
  232.7 44.5 %all-to-all-start.7 = ((bf16[256,4,4,128]{0,3,2,1:T(8,128)(2,1)}), bf16[256,4,4,128]{0,3,2,1:T(8,128)(2,1)S(1)}, u32[]{:S(2)}, u32[]{:S(2)}) async-start(bf16[256,4,4,128]{0,3,2,1:T(8,128)(2,1)} %copy.102), calls=%async_computation.7 | async-start | bytes 2097152 | tf_op jit(solution)/shard_map/all_to_all | solution.py:29
  245.1 18.6 %collective-permute-start.40 = (f32[160,16,16]{0,2,1:T(8,128)S(1)}, f32[160,16,16]{0,2,1:T(8,128)S(1)}, u32[]{:S(2)}, u32[]{:S(2)}) collective-permute-start(f32[160,16,16]{0,2,1:T(8,128)S(1)} %add.396), channel_id=1, source_target_pairs={{0,256},{64,320},{128,384},{192,448},{256,0},{320,64},{384,128},{4... | collective-permute-start | bytes 491528 | tf_op jit(solution)/shard_map/ppermute | solution.py:40
  253.0 15.4 %collective-permute-start.42 = (f32[2,64,1,256]{3,1,2,0:T(8,128)S(1)}, f32[2,64,1,256]{3,1,2,0:T(8,128)S(1)}, u32[]{:S(2)}, u32[]{:S(2)}) collective-permute-start(f32[2,64,1,256]{3,1,2,0:T(8,128)S(1)} %dynamic-slice_bitcast_fusion.3), channel_id=1, source_target_pairs={{0,64},{64,128},{128,192},{192,256},{256,320},{320,384},{384,448},... | collective-permute-start | bytes 393224 | tf_op jit(solution)/shard_map/ppermute | solution.py:35
  268.5 14.7 %collective-permute-start.43 = (f32[2,64,1,256]{3,1,2,0:T(8,128)S(1)}, f32[2,64,1,256]{3,1,2,0:T(8,128)}, u32[]{:S(2)}, u32[]{:S(2)}) collective-permute-start(f32[2,64,1,256]{3,1,2,0:T(8,128)S(1)} %bitcast_add_fusion.15), channel_id=1, source_target_pairs={{0,64},{64,128},{128,192},{192,256},{256,320},{320,384},{384,448},... | collective-permute-start | bytes 393224 | tf_op jit(solution)/shard_map/ppermute | solution.py:35
  272.9 13.2 %collective-permute-start.50 = (f32[2,64,1,256]{3,1,2,0:T(8,128)}, f32[2,64,1,256]{3,1,2,0:T(8,128)}, u32[]{:S(2)}, u32[]{:S(2)}) collective-permute-start(f32[2,64,1,256]{3,1,2,0:T(8,128)} %bitcast_add_fusion.8), channel_id=1, source_target_pairs={{0,448},{64,0},{128,64},{192,128},{256,192},{320,256},{384,320},{4... | collective-permute-start | bytes 393224 | tf_op jit(solution)/shard_map/ppermute | solution.py:35
  284.2 11.9 %collective-permute-start.44 = (f32[2,64,1,256]{3,1,2,0:T(8,128)S(1)}, f32[2,64,1,256]{3,1,2,0:T(8,128)S(1)}, u32[]{:S(2)}, u32[]{:S(2)}) collective-permute-start(f32[2,64,1,256]{3,1,2,0:T(8,128)S(1)} %bitcast_add_fusion.14), channel_id=1, source_target_pairs={{0,64},{64,128},{128,192},{192,256},{256,320},{320,384},{384,448},... | collective-permute-start | bytes 393224 | tf_op jit(solution)/shard_map/ppermute | solution.py:35
  287.0 11.0 %collective-permute-start.51 = (f32[2,64,1,256]{3,1,2,0:T(8,128)S(1)}, f32[2,64,1,256]{3,1,2,0:T(8,128)S(1)}, u32[]{:S(2)}, u32[]{:S(2)}) collective-permute-start(f32[2,64,1,256]{3,1,2,0:T(8,128)S(1)} %bitcast_add_fusion.7), channel_id=1, source_target_pairs={{0,448},{64,0},{128,64},{192,128},{256,192},{320,256},{384,320},{4... | collective-permute-start | bytes 393224 | tf_op jit(solution)/shard_map/ppermute | solution.py:35
  294.1 37.0 %collective-permute-start.20 = (f32[8,2,16,1,2048]{4,2,1,0,3:T(8,128)S(1)}, f32[8,2,16,1,2048]{4,2,1,0,3:T(8,128)S(1)}, u32[]{:S(2)}, u32[]{:S(2)}) collective-permute-start(f32[8,2,16,1,2048]{4,2,1,0,3:T(8,128)S(1)} %dynamic-slice_bitcast_fusion.1), channel_id=1, source_target_pairs={{0,16},{16,0},{1,17},{17,1},{2,18},{18,2},{3,19},{19,3},{4,20},{20... | collective-permute-start | bytes 6291464 | tf_op jit(solution)/shard_map/ppermute | solution.py:40
  296.1 9.0 %collective-permute-start.45 = (f32[2,64,1,256]{3,1,2,0:T(8,128)S(1)}, f32[2,64,1,256]{3,1,2,0:T(8,128)S(1)}, u32[]{:S(2)}, u32[]{:S(2)}) collective-permute-start(f32[2,64,1,256]{3,1,2,0:T(8,128)S(1)} %bitcast_add_fusion.13), channel_id=1, source_target_pairs={{0,64},{64,128},{128,192},{192,256},{256,320},{320,384},{384,448},... | collective-permute-start | bytes 393224 | tf_op jit(solution)/shard_map/ppermute | solution.py:35
  298.0 9.0 %collective-permute-start.52 = (f32[2,64,1,256]{3,1,2,0:T(8,128)S(1)}, f32[2,64,1,256]{3,1,2,0:T(8,128)S(1)}, u32[]{:S(2)}, u32[]{:S(2)}) collective-permute-start(f32[2,64,1,256]{3,1,2,0:T(8,128)S(1)} %bitcast_add_fusion.6), channel_id=1, source_target_pairs={{0,448},{64,0},{128,64},{192,128},{256,192},{320,256},{384,320},{4... | collective-permute-start | bytes 393224 | tf_op jit(solution)/shard_map/ppermute | solution.py:35
  305.1 8.2 %collective-permute-start.46 = (f32[2,64,1,256]{3,1,2,0:T(8,128)S(1)}, f32[2,64,1,256]{3,1,2,0:T(8,128)S(1)}, u32[]{:S(2)}, u32[]{:S(2)}) collective-permute-start(f32[2,64,1,256]{3,1,2,0:T(8,128)S(1)} %bitcast_add_fusion.12), channel_id=1, source_target_pairs={{0,64},{64,128},{128,192},{192,256},{256,320},{320,384},{384,448},... | collective-permute-start | bytes 393224 | tf_op jit(solution)/shard_map/ppermute | solution.py:35
  307.1 8.2 %collective-permute-start.53 = (f32[2,64,1,256]{3,1,2,0:T(8,128)S(1)}, f32[2,64,1,256]{3,1,2,0:T(8,128)S(1)}, u32[]{:S(2)}, u32[]{:S(2)}) collective-permute-start(f32[2,64,1,256]{3,1,2,0:T(8,128)S(1)} %bitcast_add_fusion.5), channel_id=1, source_target_pairs={{0,448},{64,0},{128,64},{192,128},{256,192},{320,256},{384,320},{4... | collective-permute-start | bytes 393224 | tf_op jit(solution)/shard_map/ppermute | solution.py:35
  331.7 10.5 %collective-permute-start.21 = (f32[2,16,1,1024]{3,1,2,0:T(8,128)S(1)}, f32[2,16,1,1024]{3,1,2,0:T(8,128)S(1)}, u32[]{:S(2)}, u32[]{:S(2)}) collective-permute-start(f32[2,16,1,1024]{3,1,2,0:T(8,128)S(1)} %dynamic-slice_bitcast_fusion.5), channel_id=1, source_target_pairs={{0,64},{64,128},{128,192},{192,256},{256,320},{320,384},{384,448},... | collective-permute-start | bytes 393224 | tf_op jit(solution)/shard_map/ppermute | solution.py:35
  333.7 64.5 %collective-permute-start.56 = (f32[64,1,512]{2,0,1:T(8,128)S(1)}, f32[64,1,512]{2,0,1:T(8,128)S(1)}, u32[]{:S(2)}, u32[]{:S(2)}) collective-permute-start(f32[64,1,512]{2,0,1:T(8,128)S(1)} %fusion.16), channel_id=1, source_target_pairs={{0,32},{32,0},{1,33},{33,1},{2,34},{34,2},{3,35},{35,3},{4,36},{36... | collective-permute-start | bytes 393224 | tf_op jit(solution)/shard_map/ppermute | solution.py:40
  344.8 8.7 %collective-permute-start.29 = (f32[2,16,1,1024]{3,1,2,0:T(8,128)S(1)}, f32[2,16,1,1024]{3,1,2,0:T(8,128)S(1)}, u32[]{:S(2)}, u32[]{:S(2)}) collective-permute-start(f32[2,16,1,1024]{3,1,2,0:T(8,128)S(1)} %bitcast_add_fusion.22), channel_id=1, source_target_pairs={{0,448},{64,0},{128,64},{192,128},{256,192},{320,256},{384,320},{4... | collective-permute-start | bytes 393224 | tf_op jit(solution)/shard_map/ppermute | solution.py:35
  350.4 9.0 %collective-permute-start.23 = (f32[2,16,1,1024]{3,1,2,0:T(8,128)S(1)}, f32[2,16,1,1024]{3,1,2,0:T(8,128)S(1)}, u32[]{:S(2)}, u32[]{:S(2)}) collective-permute-start(f32[2,16,1,1024]{3,1,2,0:T(8,128)S(1)} %bitcast_add_fusion.28), channel_id=1, source_target_pairs={{0,64},{64,128},{128,192},{192,256},{256,320},{320,384},{384,448},... | collective-permute-start | bytes 393224 | tf_op jit(solution)/shard_map/ppermute | solution.py:35
  353.5 9.1 %collective-permute-start.30 = (f32[2,16,1,1024]{3,1,2,0:T(8,128)S(1)}, f32[2,16,1,1024]{3,1,2,0:T(8,128)S(1)}, u32[]{:S(2)}, u32[]{:S(2)}) collective-permute-start(f32[2,16,1,1024]{3,1,2,0:T(8,128)S(1)} %bitcast_add_fusion.21), channel_id=1, source_target_pairs={{0,448},{64,0},{128,64},{192,128},{256,192},{320,256},{384,320},{4... | collective-permute-start | bytes 393224 | tf_op jit(solution)/shard_map/ppermute | solution.py:35
  359.4 8.8 %collective-permute-start.24 = (f32[2,16,1,1024]{3,1,2,0:T(8,128)S(1)}, f32[2,16,1,1024]{3,1,2,0:T(8,128)S(1)}, u32[]{:S(2)}, u32[]{:S(2)}) collective-permute-start(f32[2,16,1,1024]{3,1,2,0:T(8,128)S(1)} %bitcast_add_fusion.27), channel_id=1, source_target_pairs={{0,64},{64,128},{128,192},{192,256},{256,320},{320,384},{384,448},... | collective-permute-start | bytes 393224 | tf_op jit(solution)/shard_map/ppermute | solution.py:35
  362.6 8.3 %collective-permute-start.31 = (f32[2,16,1,1024]{3,1,2,0:T(8,128)S(1)}, f32[2,16,1,1024]{3,1,2,0:T(8,128)S(1)}, u32[]{:S(2)}, u32[]{:S(2)}) collective-permute-start(f32[2,16,1,1024]{3,1,2,0:T(8,128)S(1)} %bitcast_add_fusion.20), channel_id=1, source_target_pairs={{0,448},{64,0},{128,64},{192,128},{256,192},{320,256},{384,320},{4... | collective-permute-start | bytes 393224 | tf_op jit(solution)/shard_map/ppermute | solution.py:35
  368.2 8.3 %collective-permute-start.25 = (f32[2,16,1,1024]{3,1,2,0:T(8,128)S(1)}, f32[2,16,1,1024]{3,1,2,0:T(8,128)S(1)}, u32[]{:S(2)}, u32[]{:S(2)}) collective-permute-start(f32[2,16,1,1024]{3,1,2,0:T(8,128)S(1)} %bitcast_add_fusion.26), channel_id=1, source_target_pairs={{0,64},{64,128},{128,192},{192,256},{256,320},{320,384},{384,448},... | collective-permute-start | bytes 393224 | tf_op jit(solution)/shard_map/ppermute | solution.py:35
  370.9 8.1 %collective-permute-start.32 = (f32[2,16,1,1024]{3,1,2,0:T(8,128)S(1)}, f32[2,16,1,1024]{3,1,2,0:T(8,128)S(1)}, u32[]{:S(2)}, u32[]{:S(2)}) collective-permute-start(f32[2,16,1,1024]{3,1,2,0:T(8,128)S(1)} %bitcast_add_fusion.19), channel_id=1, source_target_pairs={{0,448},{64,0},{128,64},{192,128},{256,192},{320,256},{384,320},{4... | collective-permute-start | bytes 393224 | tf_op jit(solution)/shard_map/ppermute | solution.py:35
  (33 other events, 471.1 us)

commit v3 on v2

--- a/solution.py
+++ b/solution.py
@@ -140,12 +140,40 @@
     grad_scale = float(tok_rows * n_dp) ** (-0.5)
     tiles_up = group_up // TILE_UP
     tiles_down = group_down // TILE_DOWN
-    up_full = dp_all_gather(up_left[0])[None]
+    hidden_rows = down_left.shape[1]
+    up_rows = up_left.shape[1]
+    weights = jnp.concatenate(
+        [up_left[0], down_left[0].reshape(up_rows, hidden_rows * block_width // up_rows)], axis=1
+    )
+    weights = dp_all_gather(weights)
+    up_full = weights[:, :hidden_width][None]
+    down_full = weights[:, hidden_width:].reshape(1, -1, block_width)
     token_blocks = tokens.reshape(tok_rows, local_blocks, block_width)
+    identity = jnp.eye(group_down, dtype=jnp.bfloat16).reshape(group_down, tiles_down, TILE_DOWN)
+    mix_matrix = jnp.einsum(
+        "cjk,cal->jcakl", down_right, identity, preferred_element_type=jnp.float32
+    )
+    mix_matrix = mix_matrix.astype(jnp.bfloat16).reshape(
+        blocks_all * group_down, blocks_all * group_down
+    )
+    grad_down_mixed = lax.dot_general(
+        layer_grad, mix_matrix, (((1,), (1,)), ((), ())), preferred_element_type=jnp.float32
+    ).astype(jnp.bfloat16)
     up_inner = jnp.einsum(
         "tbi,big->tbg", token_blocks, up_full, preferred_element_type=jnp.float32
     ).astype(jnp.bfloat16)
-    up_mixed = exchange(to_wire(up_inner, feat_count))
+    up_piece = hidden_width // feat_count
+    first = exchange(
+        jnp.concatenate(
+            [
+                to_wire(up_inner, feat_count),
+                grad_down_mixed.reshape(tok_rows, feat_count, local_blocks * group_down),
+            ],
+            axis=2,
+        )
+    )
+    up_mixed = first[:, :, :up_piece]
+    grad_down_inner = from_wire(first[:, :, up_piece:], local_blocks)
     preact = jnp.einsum("tjg,gjk->tkg", up_mixed, up_right, preferred_element_type=jnp.float32)
     sigmoid_val = jax.nn.sigmoid(preact)
     activated = (
@@ -154,26 +182,36 @@
         .transpose(0, 2, 1, 3)
     )
     hidden = activated.reshape(tok_rows, local_blocks, hidden_width).astype(jnp.bfloat16)
-    down_full = dp_all_gather(down_left[0])[None]
     down_inner = jnp.einsum(
         "tbh,bhc->tbc", hidden, down_full, preferred_element_type=jnp.float32
     ).astype(jnp.bfloat16)
-    down_mixed = exchange(to_wire(down_inner, feat_count)).reshape(
-        tok_rows, blocks_all * group_down
-    )
-    identity = jnp.eye(group_down, dtype=jnp.bfloat16).reshape(group_down, tiles_down, TILE_DOWN)
-    mix_matrix = jnp.einsum(
-        "cjk,cal->jcakl", down_right, identity, preferred_element_type=jnp.float32
-    )
-    mix_matrix = mix_matrix.astype(jnp.bfloat16).reshape(
-        blocks_all * group_down, blocks_all * group_down
-    )
+    grad_hidden = jnp.einsum(
+        "tbc,bhc->tbh", grad_down_inner, down_full, preferred_element_type=jnp.float32
+    )
+    grad_hidden = grad_hidden.reshape(tok_rows, tiles_up, blocks_all, TILE_UP).transpose(0, 2, 1, 3)
+    grad_hidden = grad_hidden.reshape(tok_rows, blocks_all, group_up)
+    grad_preact = (grad_hidden * sigmoid_val * (1.0 + preact * (1.0 - sigmoid_val))).astype(
+        jnp.bfloat16
+    )
+    grad_up_mixed = jnp.einsum(
+        "tkg,gjk->tjg", grad_preact, up_right, preferred_element_type=jnp.float32
+    ).astype(jnp.bfloat16)
+    right_up_term = (
+        jnp.einsum("tjg,tkg->gjk", up_mixed, grad_preact, preferred_element_type=jnp.float32)
+        * grad_scale
+    )
+    down_part = jnp.einsum(
+        "tbh,tbc->hbc", hidden, grad_down_inner, preferred_element_type=jnp.float32
+    )
+    down_piece = block_width // feat_count
+    second = exchange(
+        jnp.concatenate([to_wire(down_inner, feat_count), grad_up_mixed], axis=2)
+    )
+    down_mixed = second[:, :, :down_piece].reshape(tok_rows, blocks_all * group_down)
+    grad_up_inner = from_wire(second[:, :, down_piece:], local_blocks)
     layer_out = jnp.dot(down_mixed, mix_matrix, preferred_element_type=jnp.float32).astype(
         jnp.bfloat16
     )
-    grad_down_mixed = lax.dot_general(
-        layer_grad, mix_matrix, (((1,), (1,)), ((), ())), preferred_element_type=jnp.float32
-    ).astype(jnp.bfloat16)
     grad_by_group = layer_grad.reshape(tok_rows, tiles_down, blocks_all, TILE_DOWN).transpose(
         0, 2, 1, 3
     )
@@ -187,38 +225,24 @@
         )
         * grad_scale
     )
-    grad_down_inner = from_wire(
-        exchange(grad_down_mixed.reshape(tok_rows, feat_count, local_blocks * group_down)),
-        local_blocks,
-    )
-    grad_down_left = dp_reduce_scatter(
-        jnp.einsum("tbh,tbc->hbc", hidden, grad_down_inner, preferred_element_type=jnp.float32)
-        * grad_scale
-    ).transpose(1, 0, 2)
-    grad_hidden = jnp.einsum(
-        "tbc,bhc->tbh", grad_down_inner, down_full, preferred_element_type=jnp.float32
-    )
-    grad_hidden = grad_hidden.reshape(tok_rows, tiles_up, blocks_all, TILE_UP).transpose(0, 2, 1, 3)
-    grad_hidden = grad_hidden.reshape(tok_rows, blocks_all, group_up)
-    grad_preact = (grad_hidden * sigmoid_val * (1.0 + preact * (1.0 - sigmoid_val))).astype(
-        jnp.bfloat16
-    )
-    grad_up_mixed = jnp.einsum(
-        "tkg,gjk->tjg", grad_preact, up_right, preferred_element_type=jnp.float32
-    ).astype(jnp.bfloat16)
-    right_up_term = (
-        jnp.einsum("tjg,tkg->gjk", up_mixed, grad_preact, preferred_element_type=jnp.float32)
-        * grad_scale
-    )
-    grad_up_inner = from_wire(exchange(grad_up_mixed), local_blocks)
     grad_tokens = jnp.einsum(
         "tbg,big->tbi", grad_up_inner, up_full, preferred_element_type=jnp.float32
     ).astype(jnp.bfloat16)
     grad_tokens = grad_tokens.reshape(tok_rows, local_blocks * block_width)
-    grad_up_left = dp_reduce_scatter(
-        jnp.einsum("tbi,tbg->ibg", token_blocks, grad_up_inner, preferred_element_type=jnp.float32)
-        * grad_scale
-    ).transpose(1, 0, 2)
+    up_part = jnp.einsum(
+        "tbi,tbg->ibg", token_blocks, grad_up_inner, preferred_element_type=jnp.float32
+    )
+    n_rows = up_part.shape[0] // up_rows
+    parts = jnp.stack(
+        [
+            up_part.reshape(n_rows, up_rows, hidden_width),
+            down_part.reshape(n_rows, up_rows, hidden_width),
+        ],
+        axis=1,
+    )
+    summed = dp_reduce_scatter(parts * grad_scale)[0]
+    grad_up_left = summed[0][None]
+    grad_down_left = summed[1].reshape(1, hidden_rows, block_width)
     rights = jnp.concatenate([right_up_term, right_down_term], axis=0)
     rights = dp_all_reduce(rights)
     grad_up_right = rights[:group_up]

time: 406 us -> 345 us (0.85)
  the two profiles are of different devices: /device:TPU:2 before, /device:TPU:1 now
where the time goes in v3:
time: 345 us; the launch traced here: 342 us
  starting transfers between devices  124 us (36%)
  waiting for transfers between devices  73.7 us (21%)
  local copies, waits for them, and re-layouts  55.4 us (16%)
  blocking collectives  40.4 us (12%)
  other arithmetic  30.9 us (9%)
  matrix products  16.1 us (5%)
    ppermute x22, starting transfers between devices, shift(): return lax.ppermute(value, axis, [(i, (i + step) % n) for i in range(n)])  79.7 us
    all_to_all x2, blocking collectives, exchange(): shaped = lax.all_to_all(shaped, 'x', 2, 2, tiled=True)  40.4 us
    all_to_all x2, waiting for transfers between devices, exchange(): shaped = lax.all_to_all(shaped, 'yhi', 1, 1, tiled=True)  35.6 us
    ppermute x9, starting transfers between devices, swap(): return lax.ppermute(value, axis, [(i, i ^ mask) for i in range(n)])  33.4 us
    ppermute x9, waiting for transfers between devices, swap(): return lax.ppermute(value, axis, [(i, i ^ mask) for i in range(n)])  28.4 us
    all_to_all x2, starting transfers between devices, exchange(): shaped = lax.all_to_all(shaped, 'yhi', 1, 1, tiled=True)  10.9 us
    ppermute x22, waiting for transfers between devices, shift(): return lax.ppermute(value, axis, [(i, (i + step) % n) for i in range(n)])  9.69 us
    unnamed x57, local copies, waits for them, and re-layouts  8.7 us
  transfers between devices with their start and end apart: 33, of which 11 were waited for; matrix products, arithmetic and copies ran while one was open for 19% of the time, Pallas kernels for 0%

profile of v3, /device:TPU:1, one launch (start us, length us, event | category | flops | bytes accessed | tf_op | source)
XLA Modules:
  0.0 342.4 jit_solution(16554616765255038953)
XLA Ops:
  2.5 4.0 %collective-permute-start = (bf16[16,4096]{1,0:T(8,128)(2,1)S(1)}, bf16[16,4096]{1,0:T(8,128)(2,1)S(1)}, u32[]{:S(2)}, u32[]{:S(2)}) collective-permute-start(bf16[16,4096]{1,0:T(8,128)(2,1)S(1)} %get-tuple-element.52), channel_id=1, source_target_pairs={{0,32},{32,0},{1,33},{33,1},{2,34},{34,2},{3,35},{35,3},{4,36},{36... | collective-permute-start | bytes 393224 | tf_op jit(solution)/shard_map/ppermute | solution.py:40
  6.6 2.2 collective-permute-done
  8.9 11.4 %collective-permute-start.2 = (bf16[2,16,4096]{2,1,0:T(8,128)(2,1)S(1)}, bf16[2,16,4096]{2,1,0:T(8,128)(2,1)S(1)}, u32[]{:S(2)}, u32[]{:S(2)}) collective-permute-start(bf16[2,16,4096]{2,1,0:T(8,128)(2,1)S(1)} %maximum_select_fusion.2), channel_id=1, source_target_pairs={{0,448},{64,0},{128,64},{192,128},{256,192},{320,256},{384,320},{4... | collective-permute-start | bytes 786440 | tf_op jit(solution)/shard_map/ppermute | solution.py:35
  20.2 1.9 collective-permute-start.1
  24.5 5.1 %collective-permute-start.4 = (bf16[2,16,4096]{2,1,0:T(8,128)(2,1)S(1)}, bf16[2,16,4096]{2,1,0:T(8,128)(2,1)S(1)}, u32[]{:S(2)}, u32[]{:S(2)}) collective-permute-start(bf16[2,16,4096]{2,1,0:T(8,128)(2,1)S(1)} %collective-permute-done.2), channel_id=1, source_target_pairs={{0,448},{64,0},{128,64},{192,128},{256,192},{320,256},{384,320},{4... | collective-permute-start | bytes 786440 | tf_op jit(solution)/shard_map/ppermute | solution.py:35
  29.6 1.9 collective-permute-start.3
  33.0 4.9 %collective-permute-start.6 = (bf16[2,16,4096]{2,1,0:T(8,128)(2,1)S(1)}, bf16[2,16,4096]{2,1,0:T(8,128)(2,1)S(1)}, u32[]{:S(2)}, u32[]{:S(2)}) collective-permute-start(bf16[2,16,4096]{2,1,0:T(8,128)(2,1)S(1)} %collective-permute-done.4), channel_id=1, source_target_pairs={{0,448},{64,0},{128,64},{192,128},{256,192},{320,256},{384,320},{4... | collective-permute-start | bytes 786440 | tf_op jit(solution)/shard_map/ppermute | solution.py:35
  41.3 4.9 %collective-permute-start.8 = (bf16[2,16,2048]{2,1,0:T(8,128)(2,1)S(1)}, bf16[2,16,2048]{2,1,0:T(8,128)(2,1)S(1)}, u32[]{:S(2)}, u32[]{:S(2)}) collective-permute-start(bf16[2,16,2048]{2,1,0:T(8,128)(2,1)S(1)} %split.17), channel_id=1, source_target_pairs={{0,448},{64,0},{128,64},{192,128},{256,192},{320,256},{384,320},{4... | collective-permute-start | bytes 393224 | tf_op jit(solution)/shard_map/ppermute | solution.py:35
  46.3 1.9 collective-permute-start.7
  49.7 3.5 %collective-permute-done.7 = bf16[2,16,2048]{2,1,0:T(8,128)(2,1)S(1)} collective-permute-done((bf16[2,16,2048]{2,1,0:T(8,128)(2,1)S(1)}, bf16[2,16,2048]{2,1,0:T(8,128)(2,1)S(1)}, u32[]{:S(2)}, u32[]{:S(2)}) %collective-permute-start.7) | collective-permute-done | bytes 131104 | tf_op jit(solution)/shard_map/ppermute | solution.py:35
  53.9 8.1 %collective-permute-start.9 = (bf16[8,2,16,4096]{3,2,1,0:T(8,128)(2,1)}, bf16[8,2,16,4096]{3,2,1,0:T(8,128)(2,1)}, u32[]{:S(2)}, u32[]{:S(2)}) collective-permute-start(bf16[8,2,16,4096]{3,2,1,0:T(8,128)(2,1)} %fusion.27), channel_id=1, source_target_pairs={{0,16},{16,0},{1,17},{17,1},{2,18},{18,2},{3,19},{19,3},{4,20},{20... | collective-permute-start | bytes 6291464 | tf_op jit(solution)/shard_map/ppermute | solution.py:40
  63.6 2.1 reshape.189
  66.1 4.2 %maximum_select_fusion = bf16[8,2,2,16,4096]{4,3,2,1,0:T(8,128)(2,1)S(1)} fusion(bf16[8,2,1,16,4096]{4,3,2,1,0:T(8,128)(2,1)} %bitcast.13, bf16[8,2,1,16,4096]{4,3,2,1,0:T(8,128)(2,1)} %bitcast.12, pred[]{:T(512)S(6)} %eq.33), kind=kLoop, calls=%fused_computation.1 | loop fusion | flops 6291456 | bytes 8388609 | tf_op jit(solution)/shard_map/jit(_where)/select_n | solution.py:102
  72.6 20.9 %all_to_all.20 = bf16[256,4,4,160]{0,3,1,2:T(8,128)(2,1)S(1)} all-to-all(bf16[256,4,4,160]{0,3,1,2:T(8,128)(2,1)S(1)} %copy.134), channel_id=1, replica_groups=mesh['z'=8,'ylo'=2,'core'=2,'yhi'=4,'x'=4] {'x'}, dimensions={2} | all-to-all | bytes 2621440 | tf_op jit(solution)/shard_map/all_to_all | solution.py:28
  94.6 6.8 %all-to-all-start.1 = ((bf16[256,4,4,160]{0,3,2,1:T(8,128)(2,1)}), bf16[256,4,4,160]{0,3,2,1:T(8,128)(2,1)}, u32[]{:S(2)}, u32[]{:S(2)}) async-start(bf16[256,4,4,160]{0,3,2,1:T(8,128)(2,1)} %copy.113), calls=%async_computation.1 | async-start | bytes 2621440 | tf_op jit(solution)/shard_map/all_to_all | solution.py:29
  101.9 3.4 slice.45
  105.3 3.1 reshape.188
  108.4 24.8 %all-to-all-done.1 = bf16[256,4,4,160]{0,3,2,1:T(8,128)(2,1)} async-done(((bf16[256,4,4,160]{0,3,2,1:T(8,128)(2,1)}), bf16[256,4,4,160]{0,3,2,1:T(8,128)(2,1)}, u32[]{:S(2)}, u32[]{:S(2)}) %all-to-all-start.1) | async-done | bytes 1310752 | tf_op jit(solution)/shard_map/all_to_all | solution.py:29
  136.6 2.1 fusion.4
  143.3 19.5 %all_to_all.21 = bf16[256,4,4,160]{0,1,3,2:T(4,128)(2,1)S(1)} all-to-all(bf16[256,4,4,160]{0,1,3,2:T(4,128)(2,1)S(1)} %pad_maximum_fusion.1), channel_id=1, replica_groups=mesh['z'=8,'ylo'=2,'core'=2,'yhi'=4,'x'=4] {'x'}, dimensions={2} | all-to-all | bytes 2621440 | tf_op jit(solution)/shard_map/all_to_all | solution.py:28
  162.8 2.1 copy.122
  164.9 4.1 %all-to-all-start.3 = ((bf16[256,4,4,160]{0,2,3,1:T(4,128)(2,1)}), bf16[256,4,4,160]{0,2,3,1:T(4,128)(2,1)S(1)}, u32[]{:S(2)}, u32[]{:S(2)}) async-start(bf16[256,4,4,160]{0,2,3,1:T(4,128)(2,1)} %copy.122), calls=%async_computation.3 | async-start | bytes 2621440 | tf_op jit(solution)/shard_map/all_to_all | solution.py:29
  169.0 2.7 convolution_bitcast_fusion
  171.7 5.4 %copy.126 = f32[2048,1,512]{2,0,1:T(8,128)} copy(f32[2048,1,512]{0,2,1:T(8,128)} %convolution_bitcast_fusion) | data formatting | bytes 8388608 | tf_op jit(solution)/shard_map/tbh,tbc->hbc/transpose | solution.py:203
  177.1 5.7 %stack.56 = f32[8,2,2,1,1,16,2048]{6,5,2,1,0,4,3:T(8,128)} reshape(f32[2048,1,512]{2,0,1:T(8,128)} %copy.126) | data formatting | bytes 8388608 | tf_op jit(solution)/shard_map/stack | solution.py:236
  182.8 10.8 %all-to-all-done.3 = bf16[256,4,4,160]{0,2,3,1:T(4,128)(2,1)S(1)} async-done(((bf16[256,4,4,160]{0,2,3,1:T(4,128)(2,1)}), bf16[256,4,4,160]{0,2,3,1:T(4,128)(2,1)S(1)}, u32[]{:S(2)}, u32[]{:S(2)}) %all-to-all-start.3) | async-done | bytes 1310752 | tf_op jit(solution)/shard_map/all_to_all | solution.py:29
  195.1 2.5 reshape.192
  204.7 5.6 %collective-permute-start.10 = (f32[8,2,1,2,16,2048]{5,4,3,1,0,2:T(8,128)S(1)}, f32[8,2,1,2,16,2048]{5,4,3,1,0,2:T(8,128)S(1)}, u32[]{:S(2)}, u32[]{:S(2)}) collective-permute-start(f32[8,2,1,2,16,2048]{5,4,3,1,0,2:T(8,128)S(1)} %bitcast.176), channel_id=1, source_target_pairs={{0,16},{16,0},{1,17},{17,1},{2,18},{18,2},{3,19},{19,3},{4,20},{20... | collective-permute-start | bytes 12582920 | tf_op jit(solution)/shard_map/ppermute | solution.py:40
  210.3 6.8 %collective-permute-done.10 = f32[8,2,1,2,16,2048]{5,4,3,1,0,2:T(8,128)S(1)} collective-permute-done((f32[8,2,1,2,16,2048]{5,4,3,1,0,2:T(8,128)S(1)}, f32[8,2,1,2,16,2048]{5,4,3,1,0,2:T(8,128)S(1)}, u32[]{:S(2)}, u32[]{:S(2)}) %collective-permute-start.10) | collective-permute-done | bytes 4194336 | tf_op jit(solution)/shard_map/ppermute | solution.py:40
  222.9 4.6 %collective-permute-start.18 = (f32[2,1,2,16,1024]{4,3,2,0,1:T(8,128)}, f32[2,1,2,16,1024]{4,3,2,0,1:T(8,128)}, u32[]{:S(2)}, u32[]{:S(2)}) collective-permute-start(f32[2,1,2,16,1024]{4,3,2,0,1:T(8,128)} %dynamic-slice_bitcast_fusion), channel_id=1, source_target_pairs={{0,448},{64,0},{128,64},{192,128},{256,192},{320,256},{384,320},{4... | collective-permute-start | bytes 786440 | tf_op jit(solution)/shard_map/ppermute | solution.py:35
  228.4 2.8 collective-permute-done.11
  236.6 4.6 %collective-permute-start.19 = (f32[2,1,2,16,1024]{4,3,2,0,1:T(8,128)}, f32[2,1,2,16,1024]{4,3,2,0,1:T(8,128)}, u32[]{:S(2)}, u32[]{:S(2)}) collective-permute-start(f32[2,1,2,16,1024]{4,3,2,0,1:T(8,128)} %bitcast_add_fusion.7), channel_id=1, source_target_pairs={{0,448},{64,0},{128,64},{192,128},{256,192},{320,256},{384,320},{4... | collective-permute-start | bytes 786440 | tf_op jit(solution)/shard_map/ppermute | solution.py:35
  241.1 3.0 convolution_multiply_fusion
  250.5 4.6 %collective-permute-start.20 = (f32[2,1,2,16,1024]{4,3,2,0,1:T(8,128)}, f32[2,1,2,16,1024]{4,3,2,0,1:T(8,128)}, u32[]{:S(2)}, u32[]{:S(2)}) collective-permute-start(f32[2,1,2,16,1024]{4,3,2,0,1:T(8,128)} %bitcast_add_fusion.6), channel_id=1, source_target_pairs={{0,448},{64,0},{128,64},{192,128},{256,192},{320,256},{384,320},{4... | collective-permute-start | bytes 786440 | tf_op jit(solution)/shard_map/ppermute | solution.py:35
  257.4 1.9 collective-permute-start.14
  260.3 4.8 %collective-permute-start.21 = (f32[2,1,2,16,1024]{4,3,2,0,1:T(8,128)S(1)}, f32[2,1,2,16,1024]{4,3,2,0,1:T(8,128)S(1)}, u32[]{:S(2)}, u32[]{:S(2)}) collective-permute-start(f32[2,1,2,16,1024]{4,3,2,0,1:T(8,128)S(1)} %bitcast_add_fusion.5), channel_id=1, source_target_pairs={{0,448},{64,0},{128,64},{192,128},{256,192},{320,256},{384,320},{4... | collective-permute-start | bytes 786440 | tf_op jit(solution)/shard_map/ppermute | solution.py:35
  265.2 5.2 %collective-permute-start.26 = (f32[160,16,16]{0,2,1:T(8,128)S(1)}, f32[160,16,16]{0,2,1:T(8,128)S(1)}, u32[]{:S(2)}, u32[]{:S(2)}) collective-permute-start(f32[160,16,16]{0,2,1:T(8,128)S(1)} %pad_maximum_fusion.2), channel_id=1, source_target_pairs={{0,16},{16,0},{1,17},{17,1},{2,18},{18,2},{3,19},{19,3},{4,20},{20... | collective-permute-start | bytes 491528 | tf_op jit(solution)/shard_map/ppermute | solution.py:40
  273.4 4.6 %collective-permute-start.22 = (f32[2,1,2,16,1024]{4,3,2,0,1:T(8,128)S(1)}, f32[2,1,2,16,1024]{4,3,2,0,1:T(8,128)S(1)}, u32[]{:S(2)}, u32[]{:S(2)}) collective-permute-start(f32[2,1,2,16,1024]{4,3,2,0,1:T(8,128)S(1)} %bitcast_add_fusion.4), channel_id=1, source_target_pairs={{0,448},{64,0},{128,64},{192,128},{256,192},{320,256},{384,320},{4... | collective-permute-start | bytes 786440 | tf_op jit(solution)/shard_map/ppermute | solution.py:35
  279.9 2.5 collective-permute-done.15
  286.1 4.6 %collective-permute-start.23 = (f32[2,1,2,16,1024]{4,3,2,0,1:T(8,128)}, f32[2,1,2,16,1024]{4,3,2,0,1:T(8,128)}, u32[]{:S(2)}, u32[]{:S(2)}) collective-permute-start(f32[2,1,2,16,1024]{4,3,2,0,1:T(8,128)} %bitcast_add_fusion.3), channel_id=1, source_target_pairs={{0,448},{64,0},{128,64},{192,128},{256,192},{320,256},{384,320},{4... | collective-permute-start | bytes 786440 | tf_op jit(solution)/shard_map/ppermute | solution.py:35
  290.8 1.9 collective-permute-start.28
  295.2 2.6 collective-permute-start.17
  299.6 4.0 %collective-permute-start.24 = (f32[2,1,2,16,1024]{4,3,2,0,1:T(8,128)}, f32[2,1,2,16,1024]{4,3,2,0,1:T(8,128)}, u32[]{:S(2)}, u32[]{:S(2)}) collective-permute-start(f32[2,1,2,16,1024]{4,3,2,0,1:T(8,128)} %bitcast_add_fusion.2), channel_id=1, source_target_pairs={{0,448},{64,0},{128,64},{192,128},{256,192},{320,256},{384,320},{4... | collective-permute-start | bytes 786440 | tf_op jit(solution)/shard_map/ppermute | solution.py:35
  310.1 2.0 collective-permute-start.25
  312.2 2.3 fusion.15
  315.4 5.9 %collective-permute-done.29 = f32[160,16,16]{0,2,1:T(8,128)} collective-permute-done((f32[160,16,16]{0,2,1:T(8,128)}, f32[160,16,16]{0,2,1:T(8,128)}, u32[]{:S(2)}, u32[]{:S(2)}) %collective-permute-start.29) | collective-permute-done | bytes 163872 | tf_op jit(solution)/shard_map/ppermute | solution.py:40
  322.4 2.8 collective-permute-start.30
  326.2 13.4 %collective-permute-done.30 = f32[160,16,16]{0,2,1:T(8,128)S(1)} collective-permute-done((f32[160,16,16]{0,2,1:T(8,128)S(1)}, f32[160,16,16]{0,2,1:T(8,128)S(1)}, u32[]{:S(2)}, u32[]{:S(2)}) %collective-permute-start.30) | collective-permute-done | bytes 163872 | tf_op jit(solution)/shard_map/ppermute | solution.py:40
  (165 shorter events, 80.3 us)
Async XLA Ops:
  0.6 69.7 %copy-start = (bf16[256,512]{1,0:T(8,128)(2,1)S(1)}, bf16[256,512]{1,0:T(8,128)(2,1)}, u32[]{:S(2)}) copy-start(bf16[256,512]{1,0:T(8,128)(2,1)} %param.6) | copy-start | bytes 786436
  2.5 6.4 %collective-permute-start = (bf16[16,4096]{1,0:T(8,128)(2,1)S(1)}, bf16[16,4096]{1,0:T(8,128)(2,1)S(1)}, u32[]{:S(2)}, u32[]{:S(2)}) collective-permute-start(bf16[16,4096]{1,0:T(8,128)(2,1)S(1)} %get-tuple-element.52), channel_id=1, source_target_pairs={{0,32},{32,0},{1,33},{33,1},{2,34},{34,2},{3,35},{35,3},{4,36},{36... | collective-permute-start | bytes 393224 | tf_op jit(solution)/shard_map/ppermute | solution.py:40
  8.9 15.6 %collective-permute-start.2 = (bf16[2,16,4096]{2,1,0:T(8,128)(2,1)S(1)}, bf16[2,16,4096]{2,1,0:T(8,128)(2,1)S(1)}, u32[]{:S(2)}, u32[]{:S(2)}) collective-permute-start(bf16[2,16,4096]{2,1,0:T(8,128)(2,1)S(1)} %maximum_select_fusion.2), channel_id=1, source_target_pairs={{0,448},{64,0},{128,64},{192,128},{256,192},{320,256},{384,320},{4... | collective-permute-start | bytes 786440 | tf_op jit(solution)/shard_map/ppermute | solution.py:35
  20.2 9.3 %collective-permute-start.1 = (bf16[2,16,4096]{2,1,0:T(8,128)(2,1)S(1)}, bf16[2,16,4096]{2,1,0:T(8,128)(2,1)S(1)}, u32[]{:S(2)}, u32[]{:S(2)}) collective-permute-start(bf16[2,16,4096]{2,1,0:T(8,128)(2,1)S(1)} %maximum_select_fusion.2), channel_id=1, source_target_pairs={{0,64},{64,128},{128,192},{192,256},{256,320},{320,384},{384,448},... | collective-permute-start | bytes 786440 | tf_op jit(solution)/shard_map/ppermute | solution.py:35
  24.5 37.5 %copy-start.25 = (bf16[32,16,16]{0,2,1:T(8,128)(2,1)S(1)}, bf16[32,16,16]{0,2,1:T(8,128)(2,1)}, u32[]{:S(2)}) copy-start(bf16[32,16,16]{0,2,1:T(8,128)(2,1)} %param.10) | copy-start | bytes 49156
  24.5 8.5 %collective-permute-start.4 = (bf16[2,16,4096]{2,1,0:T(8,128)(2,1)S(1)}, bf16[2,16,4096]{2,1,0:T(8,128)(2,1)S(1)}, u32[]{:S(2)}, u32[]{:S(2)}) collective-permute-start(bf16[2,16,4096]{2,1,0:T(8,128)(2,1)S(1)} %collective-permute-done.2), channel_id=1, source_target_pairs={{0,448},{64,0},{128,64},{192,128},{256,192},{320,256},{384,320},{4... | collective-permute-start | bytes 786440 | tf_op jit(solution)/shard_map/ppermute | solution.py:35
  29.6 8.3 %collective-permute-start.3 = (bf16[2,16,4096]{2,1,0:T(8,128)(2,1)S(1)}, bf16[2,16,4096]{2,1,0:T(8,128)(2,1)S(1)}, u32[]{:S(2)}, u32[]{:S(2)}) collective-permute-start(bf16[2,16,4096]{2,1,0:T(8,128)(2,1)S(1)} %collective-permute-done.1), channel_id=1, source_target_pairs={{0,64},{64,128},{128,192},{192,256},{256,320},{320,384},{384,448},... | collective-permute-start | bytes 786440 | tf_op jit(solution)/shard_map/ppermute | solution.py:35
  33.0 8.3 %collective-permute-start.6 = (bf16[2,16,4096]{2,1,0:T(8,128)(2,1)S(1)}, bf16[2,16,4096]{2,1,0:T(8,128)(2,1)S(1)}, u32[]{:S(2)}, u32[]{:S(2)}) collective-permute-start(bf16[2,16,4096]{2,1,0:T(8,128)(2,1)S(1)} %collective-permute-done.4), channel_id=1, source_target_pairs={{0,448},{64,0},{128,64},{192,128},{256,192},{320,256},{384,320},{4... | collective-permute-start | bytes 786440 | tf_op jit(solution)/shard_map/ppermute | solution.py:35
  37.9 8.3 %collective-permute-start.5 = (bf16[2,16,4096]{2,1,0:T(8,128)(2,1)S(1)}, bf16[2,16,4096]{2,1,0:T(8,128)(2,1)S(1)}, u32[]{:S(2)}, u32[]{:S(2)}) collective-permute-start(bf16[2,16,4096]{2,1,0:T(8,128)(2,1)S(1)} %collective-permute-done.3), channel_id=1, source_target_pairs={{0,64},{64,128},{128,192},{192,256},{256,320},{320,384},{384,448},... | collective-permute-start | bytes 786440 | tf_op jit(solution)/shard_map/ppermute | solution.py:35
  41.3 8.4 %collective-permute-start.8 = (bf16[2,16,2048]{2,1,0:T(8,128)(2,1)S(1)}, bf16[2,16,2048]{2,1,0:T(8,128)(2,1)S(1)}, u32[]{:S(2)}, u32[]{:S(2)}) collective-permute-start(bf16[2,16,2048]{2,1,0:T(8,128)(2,1)S(1)} %split.17), channel_id=1, source_target_pairs={{0,448},{64,0},{128,64},{192,128},{256,192},{320,256},{384,320},{4... | collective-permute-start | bytes 393224 | tf_op jit(solution)/shard_map/ppermute | solution.py:35
  46.3 6.9 %collective-permute-start.7 = (bf16[2,16,2048]{2,1,0:T(8,128)(2,1)S(1)}, bf16[2,16,2048]{2,1,0:T(8,128)(2,1)S(1)}, u32[]{:S(2)}, u32[]{:S(2)}) collective-permute-start(bf16[2,16,2048]{2,1,0:T(8,128)(2,1)S(1)} %split.16), channel_id=1, source_target_pairs={{0,64},{64,128},{128,192},{192,256},{256,320},{320,384},{384,448},... | collective-permute-start | bytes 393224 | tf_op jit(solution)/shard_map/ppermute | solution.py:35
  53.9 12.2 %collective-permute-start.9 = (bf16[8,2,16,4096]{3,2,1,0:T(8,128)(2,1)}, bf16[8,2,16,4096]{3,2,1,0:T(8,128)(2,1)}, u32[]{:S(2)}, u32[]{:S(2)}) collective-permute-start(bf16[8,2,16,4096]{3,2,1,0:T(8,128)(2,1)} %fusion.27), channel_id=1, source_target_pairs={{0,16},{16,0},{1,17},{17,1},{2,18},{18,2},{3,19},{19,3},{4,20},{20... | collective-permute-start | bytes 6291464 | tf_op jit(solution)/shard_map/ppermute | solution.py:40
  65.7 4.7 %copy-start.6 = (bf16[512,512]{1,0:T(8,128)(2,1)}, bf16[512,512]{1,0:T(8,128)(2,1)S(1)}, u32[]{:S(2)}) copy-start(bf16[512,512]{1,0:T(8,128)(2,1)S(1)} %reshape.189) | copy-start | bytes 1572868
  93.4 8.1 %copy-start.26 = (bf16[128,16,16]{0,2,1:T(8,128)(2,1)S(1)}, bf16[128,16,16]{0,2,1:T(8,128)(2,1)}, u32[]{:S(2)}) copy-start(bf16[128,16,16]{0,2,1:T(8,128)(2,1)} %param.8) | copy-start | bytes 196612
  94.6 38.6 %all-to-all-start.1 = ((bf16[256,4,4,160]{0,3,2,1:T(8,128)(2,1)}), bf16[256,4,4,160]{0,3,2,1:T(8,128)(2,1)}, u32[]{:S(2)}, u32[]{:S(2)}) async-start(bf16[256,4,4,160]{0,3,2,1:T(8,128)(2,1)} %copy.113), calls=%async_computation.1 | async-start | bytes 2621440 | tf_op jit(solution)/shard_map/all_to_all | solution.py:29
  101.9 34.5 %copy-start.19 = (bf16[128,16,16]{2,1,0:T(8,128)(2,1)}, bf16[128,16,16]{2,1,0:T(8,128)(2,1)S(1)}, u32[]{:S(2)}) copy-start(bf16[128,16,16]{2,1,0:T(8,128)(2,1)S(1)} %copy.119) | copy-start | bytes 196612
  162.8 6.2 %copy-start.18 = (bf16[256,16,32]{0,2,1:T(8,128)(2,1)S(1)}, bf16[256,16,32]{0,2,1:T(8,128)(2,1)}, u32[]{:S(2)}) copy-start(bf16[256,16,32]{0,2,1:T(8,128)(2,1)} %copy-done.17) | copy-start | bytes 786436
  164.9 28.7 %all-to-all-start.3 = ((bf16[256,4,4,160]{0,2,3,1:T(4,128)(2,1)}), bf16[256,4,4,160]{0,2,3,1:T(4,128)(2,1)S(1)}, u32[]{:S(2)}, u32[]{:S(2)}) async-start(bf16[256,4,4,160]{0,2,3,1:T(4,128)(2,1)} %copy.122), calls=%async_computation.3 | async-start | bytes 2621440 | tf_op jit(solution)/shard_map/all_to_all | solution.py:29
  204.7 12.4 %collective-permute-start.10 = (f32[8,2,1,2,16,2048]{5,4,3,1,0,2:T(8,128)S(1)}, f32[8,2,1,2,16,2048]{5,4,3,1,0,2:T(8,128)S(1)}, u32[]{:S(2)}, u32[]{:S(2)}) collective-permute-start(f32[8,2,1,2,16,2048]{5,4,3,1,0,2:T(8,128)S(1)} %bitcast.176), channel_id=1, source_target_pairs={{0,16},{16,0},{1,17},{17,1},{2,18},{18,2},{3,19},{19,3},{4,20},{20... | collective-permute-start | bytes 12582920 | tf_op jit(solution)/shard_map/ppermute | solution.py:40
  217.8 9.7 %copy-start.23 = (bf16[256,512]{1,0:T(8,128)(2,1)S(1)}, bf16[256,512]{1,0:T(8,128)(2,1)}, u32[]{:S(2)}) copy-start(bf16[256,512]{1,0:T(8,128)(2,1)} %param.11) | copy-start | bytes 786436
  218.2 23.0 %copy-start.9 = (bf16[256,16,128]{0,2,1:T(8,128)(2,1)S(1)}, bf16[256,16,128]{0,2,1:T(8,128)(2,1)}, u32[]{:S(2)}) copy-start(bf16[256,16,128]{0,2,1:T(8,128)(2,1)} %copy-done.8) | copy-start | bytes 3145732
  220.2 10.9 %collective-permute-start.11 = (f32[2,1,2,16,1024]{4,3,2,0,1:T(8,128)}, f32[2,1,2,16,1024]{4,3,2,0,1:T(8,128)}, u32[]{:S(2)}, u32[]{:S(2)}) collective-permute-start(f32[2,1,2,16,1024]{4,3,2,0,1:T(8,128)} %dynamic-slice_bitcast_fusion.1), channel_id=1, source_target_pairs={{0,64},{64,128},{128,192},{192,256},{256,320},{320,384},{384,448},... | collective-permute-start | bytes 786440 | tf_op jit(solution)/shard_map/ppermute | solution.py:35
  222.9 12.0 %collective-permute-start.18 = (f32[2,1,2,16,1024]{4,3,2,0,1:T(8,128)}, f32[2,1,2,16,1024]{4,3,2,0,1:T(8,128)}, u32[]{:S(2)}, u32[]{:S(2)}) collective-permute-start(f32[2,1,2,16,1024]{4,3,2,0,1:T(8,128)} %dynamic-slice_bitcast_fusion), channel_id=1, source_target_pairs={{0,448},{64,0},{128,64},{192,128},{256,192},{320,256},{384,320},{4... | collective-permute-start | bytes 786440 | tf_op jit(solution)/shard_map/ppermute | solution.py:35
  232.9 12.8 %collective-permute-start.12 = (f32[2,1,2,16,1024]{4,3,2,0,1:T(8,128)}, f32[2,1,2,16,1024]{4,3,2,0,1:T(8,128)}, u32[]{:S(2)}, u32[]{:S(2)}) collective-permute-start(f32[2,1,2,16,1024]{4,3,2,0,1:T(8,128)} %bitcast_add_fusion.14), channel_id=1, source_target_pairs={{0,64},{64,128},{128,192},{192,256},{256,320},{320,384},{384,448},... | collective-permute-start | bytes 786440 | tf_op jit(solution)/shard_map/ppermute | solution.py:35
  236.6 12.2 %collective-permute-start.19 = (f32[2,1,2,16,1024]{4,3,2,0,1:T(8,128)}, f32[2,1,2,16,1024]{4,3,2,0,1:T(8,128)}, u32[]{:S(2)}, u32[]{:S(2)}) collective-permute-start(f32[2,1,2,16,1024]{4,3,2,0,1:T(8,128)} %bitcast_add_fusion.7), channel_id=1, source_target_pairs={{0,448},{64,0},{128,64},{192,128},{256,192},{320,256},{384,320},{4... | collective-permute-start | bytes 786440 | tf_op jit(solution)/shard_map/ppermute | solution.py:35
  244.1 10.9 %copy-start.24 = (bf16[256,512]{0,1:T(8,128)(2,1)S(1)}, bf16[256,512]{0,1:T(8,128)(2,1)}, u32[]{:S(2)}) copy-start(bf16[256,512]{0,1:T(8,128)(2,1)} %copy.129) | copy-start | bytes 786436
  246.8 9.6 %collective-permute-start.13 = (f32[2,1,2,16,1024]{4,3,2,0,1:T(8,128)S(1)}, f32[2,1,2,16,1024]{4,3,2,0,1:T(8,128)S(1)}, u32[]{:S(2)}, u32[]{:S(2)}) collective-permute-start(f32[2,1,2,16,1024]{4,3,2,0,1:T(8,128)S(1)} %bitcast_add_fusion.13), channel_id=1, source_target_pairs={{0,64},{64,128},{128,192},{192,256},{256,320},{320,384},{384,448},... | collective-permute-start | bytes 786440 | tf_op jit(solution)/shard_map/ppermute | solution.py:35
  250.5 8.9 %collective-permute-start.20 = (f32[2,1,2,16,1024]{4,3,2,0,1:T(8,128)}, f32[2,1,2,16,1024]{4,3,2,0,1:T(8,128)}, u32[]{:S(2)}, u32[]{:S(2)}) collective-permute-start(f32[2,1,2,16,1024]{4,3,2,0,1:T(8,128)} %bitcast_add_fusion.6), channel_id=1, source_target_pairs={{0,448},{64,0},{128,64},{192,128},{256,192},{320,256},{384,320},{4... | collective-permute-start | bytes 786440 | tf_op jit(solution)/shard_map/ppermute | solution.py:35
  257.4 13.0 %collective-permute-start.14 = (f32[2,1,2,16,1024]{4,3,2,0,1:T(8,128)S(1)}, f32[2,1,2,16,1024]{4,3,2,0,1:T(8,128)S(1)}, u32[]{:S(2)}, u32[]{:S(2)}) collective-permute-start(f32[2,1,2,16,1024]{4,3,2,0,1:T(8,128)S(1)} %bitcast_add_fusion.12), channel_id=1, source_target_pairs={{0,64},{64,128},{128,192},{192,256},{256,320},{320,384},{384,448},... | collective-permute-start | bytes 786440 | tf_op jit(solution)/shard_map/ppermute | solution.py:35
  260.3 13.0 %collective-permute-start.21 = (f32[2,1,2,16,1024]{4,3,2,0,1:T(8,128)S(1)}, f32[2,1,2,16,1024]{4,3,2,0,1:T(8,128)S(1)}, u32[]{:S(2)}, u32[]{:S(2)}) collective-permute-start(f32[2,1,2,16,1024]{4,3,2,0,1:T(8,128)S(1)} %bitcast_add_fusion.5), channel_id=1, source_target_pairs={{0,448},{64,0},{128,64},{192,128},{256,192},{320,256},{384,320},{4... | collective-permute-start | bytes 786440 | tf_op jit(solution)/shard_map/ppermute | solution.py:35
  265.2 12.7 %collective-permute-start.26 = (f32[160,16,16]{0,2,1:T(8,128)S(1)}, f32[160,16,16]{0,2,1:T(8,128)S(1)}, u32[]{:S(2)}, u32[]{:S(2)}) collective-permute-start(f32[160,16,16]{0,2,1:T(8,128)S(1)} %pad_maximum_fusion.2), channel_id=1, source_target_pairs={{0,16},{16,0},{1,17},{17,1},{2,18},{18,2},{3,19},{19,3},{4,20},{20... | collective-permute-start | bytes 491528 | tf_op jit(solution)/shard_map/ppermute | solution.py:40
  271.4 11.0 %collective-permute-start.15 = (f32[2,1,2,16,1024]{4,3,2,0,1:T(8,128)S(1)}, f32[2,1,2,16,1024]{4,3,2,0,1:T(8,128)S(1)}, u32[]{:S(2)}, u32[]{:S(2)}) collective-permute-start(f32[2,1,2,16,1024]{4,3,2,0,1:T(8,128)S(1)} %bitcast_add_fusion.11), channel_id=1, source_target_pairs={{0,64},{64,128},{128,192},{192,256},{256,320},{320,384},{384,448},... | collective-permute-start | bytes 786440 | tf_op jit(solution)/shard_map/ppermute | solution.py:35
  273.4 12.0 %collective-permute-start.22 = (f32[2,1,2,16,1024]{4,3,2,0,1:T(8,128)S(1)}, f32[2,1,2,16,1024]{4,3,2,0,1:T(8,128)S(1)}, u32[]{:S(2)}, u32[]{:S(2)}) collective-permute-start(f32[2,1,2,16,1024]{4,3,2,0,1:T(8,128)S(1)} %bitcast_add_fusion.4), channel_id=1, source_target_pairs={{0,448},{64,0},{128,64},{192,128},{256,192},{320,256},{384,320},{4... | collective-permute-start | bytes 786440 | tf_op jit(solution)/shard_map/ppermute | solution.py:35
  278.0 12.7 %collective-permute-start.27 = (f32[160,16,16]{0,2,1:T(8,128)S(1)}, f32[160,16,16]{0,2,1:T(8,128)S(1)}, u32[]{:S(2)}, u32[]{:S(2)}) collective-permute-start(f32[160,16,16]{0,2,1:T(8,128)S(1)} %fusion.30), channel_id=1, source_target_pairs={{0,32},{32,0},{1,33},{33,1},{2,34},{34,2},{3,35},{35,3},{4,36},{36... | collective-permute-start | bytes 491528 | tf_op jit(solution)/shard_map/ppermute | solution.py:40
  283.4 10.1 %collective-permute-start.16 = (f32[2,1,2,16,1024]{4,3,2,0,1:T(8,128)S(1)}, f32[2,1,2,16,1024]{4,3,2,0,1:T(8,128)S(1)}, u32[]{:S(2)}, u32[]{:S(2)}) collective-permute-start(f32[2,1,2,16,1024]{4,3,2,0,1:T(8,128)S(1)} %bitcast_add_fusion.10), channel_id=1, source_target_pairs={{0,64},{64,128},{128,192},{192,256},{256,320},{320,384},{384,448},... | collective-permute-start | bytes 786440 | tf_op jit(solution)/shard_map/ppermute | solution.py:35
  286.1 11.8 %collective-permute-start.23 = (f32[2,1,2,16,1024]{4,3,2,0,1:T(8,128)}, f32[2,1,2,16,1024]{4,3,2,0,1:T(8,128)}, u32[]{:S(2)}, u32[]{:S(2)}) collective-permute-start(f32[2,1,2,16,1024]{4,3,2,0,1:T(8,128)} %bitcast_add_fusion.3), channel_id=1, source_target_pairs={{0,448},{64,0},{128,64},{192,128},{256,192},{320,256},{384,320},{4... | collective-permute-start | bytes 786440 | tf_op jit(solution)/shard_map/ppermute | solution.py:35
  290.8 12.8 %collective-permute-start.28 = (f32[160,16,16]{0,2,1:T(8,128)S(1)}, f32[160,16,16]{0,2,1:T(8,128)}, u32[]{:S(2)}, u32[]{:S(2)}) collective-permute-start(f32[160,16,16]{0,2,1:T(8,128)S(1)} %add.282), channel_id=1, source_target_pairs={{0,64},{64,0},{128,192},{192,128},{256,320},{320,256},{384,448},{4... | collective-permute-start | bytes 491528 | tf_op jit(solution)/shard_map/ppermute | solution.py:40
  295.2 16.9 %copy-start.12 = (bf16[256,16,128]{0,2,1:T(8,128)(2,1)S(1)}, bf16[256,16,128]{0,2,1:T(8,128)(2,1)}, u32[]{:S(2)}) copy-start(bf16[256,16,128]{0,2,1:T(8,128)(2,1)} %copy-done.11) | copy-start | bytes 3145732
  295.2 11.9 %collective-permute-start.17 = (f32[2,1,2,16,1024]{4,3,2,0,1:T(8,128)}, f32[2,1,2,16,1024]{4,3,2,0,1:T(8,128)}, u32[]{:S(2)}, u32[]{:S(2)}) collective-permute-start(f32[2,1,2,16,1024]{4,3,2,0,1:T(8,128)} %bitcast_add_fusion.9), channel_id=1, source_target_pairs={{0,64},{64,128},{128,192},{192,256},{256,320},{320,384},{384,448},... | collective-permute-start | bytes 786440 | tf_op jit(solution)/shard_map/ppermute | solution.py:35
  299.6 8.7 %collective-permute-start.24 = (f32[2,1,2,16,1024]{4,3,2,0,1:T(8,128)}, f32[2,1,2,16,1024]{4,3,2,0,1:T(8,128)}, u32[]{:S(2)}, u32[]{:S(2)}) collective-permute-start(f32[2,1,2,16,1024]{4,3,2,0,1:T(8,128)} %bitcast_add_fusion.2), channel_id=1, source_target_pairs={{0,448},{64,0},{128,64},{192,128},{256,192},{320,256},{384,320},{4... | collective-permute-start | bytes 786440 | tf_op jit(solution)/shard_map/ppermute | solution.py:35
  305.3 16.1 %collective-permute-start.29 = (f32[160,16,16]{0,2,1:T(8,128)}, f32[160,16,16]{0,2,1:T(8,128)}, u32[]{:S(2)}, u32[]{:S(2)}) collective-permute-start(f32[160,16,16]{0,2,1:T(8,128)} %add.283), channel_id=1, source_target_pairs={{0,128},{64,192},{128,0},{192,64},{256,384},{320,448},{384,256},{4... | collective-permute-start | bytes 491528 | tf_op jit(solution)/shard_map/ppermute | solution.py:40
  310.1 5.2 %slice-start = ((bf16[256,16,160]{0,1,2:T(8,128)(2,1)}), bf16[256,16,32]{0,1,2:T(8,128)(2,1)S(1)}, s32[]{:S(2)}) async-start(bf16[256,16,160]{0,1,2:T(8,128)(2,1)} %copy-done.5), calls=%async_computation.4 | async-start | bytes 524288 | tf_op jit(solution)/shard_map/slice | solution.py:210
  310.1 30.9 %collective-permute-start.25 = (f32[1,2,16,2048]{3,2,1,0:T(8,128)S(1)}, f32[1,2,16,2048]{3,2,1,0:T(8,128)S(1)}, u32[]{:S(2)}, u32[]{:S(2)}) collective-permute-start(f32[1,2,16,2048]{3,2,1,0:T(8,128)S(1)} %fusion.22), channel_id=1, source_target_pairs={{0,32},{32,0},{1,33},{33,1},{2,34},{34,2},{3,35},{35,3},{4,36},{36... | collective-permute-start | bytes 786440 | tf_op jit(solution)/shard_map/ppermute | solution.py:40
  314.5 10.7 %copy-start.7 = (bf16[512,512]{1,0:T(8,128)(2,1)S(1)}, bf16[512,512]{1,0:T(8,128)(2,1)}, u32[]{:S(2)}) copy-start(bf16[512,512]{1,0:T(8,128)(2,1)} %copy-done.6) | copy-start | bytes 1572868
  314.5 26.5 %copy-start.14 = (f32[2,1,2,16,1024]{4,3,2,0,1:T(8,128)S(1)}, f32[2,1,2,16,1024]{4,3,2,0,1:T(8,128)}, u32[]{:S(2)}) copy-start(f32[2,1,2,16,1024]{4,3,2,0,1:T(8,128)} %copy-done.13) | copy-start | bytes 786436
  314.5 26.5 %copy-start.16 = (f32[2,1,2,16,1024]{4,3,2,0,1:T(8,128)S(1)}, f32[2,1,2,16,1024]{4,3,2,0,1:T(8,128)}, u32[]{:S(2)}) copy-start(f32[2,1,2,16,1024]{4,3,2,0,1:T(8,128)} %copy-done.15) | copy-start | bytes 786436
  322.4 17.2 %collective-permute-start.30 = (f32[160,16,16]{0,2,1:T(8,128)S(1)}, f32[160,16,16]{0,2,1:T(8,128)S(1)}, u32[]{:S(2)}, u32[]{:S(2)}) collective-permute-start(f32[160,16,16]{0,2,1:T(8,128)S(1)} %add.284), channel_id=1, source_target_pairs={{0,256},{64,320},{128,384},{192,448},{256,0},{320,64},{384,128},{4... | collective-permute-start | bytes 491528 | tf_op jit(solution)/shard_map/ppermute | solution.py:40
  325.1 17.2 %copy-start.1 = (bf16[256,512]{1,0:T(8,128)(2,1)S(1)}, bf16[256,512]{1,0:T(8,128)(2,1)}, u32[]{:S(2)}) copy-start(bf16[256,512]{1,0:T(8,128)(2,1)} %param.6) | copy-start | bytes 786436
  (13 other events, 21.1 us)

commit v4 on v3

--- a/solution.py
+++ b/solution.py
@@ -43,17 +43,17 @@
 def z_ring_reduce_scatter(x):
     n = x.shape[0]
     me = lax.axis_index("z")
-    lo, hi = jnp.split(x, 2, axis=-1)
+    n_fwd = n // 2
+    n_bwd = n - 1 - n_fwd
     fwd = None
     bwd = None
-    for step in range(1, n):
-        own_f = lax.dynamic_index_in_dim(lo, (me - step) % n, 0, keepdims=False)
-        own_b = lax.dynamic_index_in_dim(hi, (me + step) % n, 0, keepdims=False)
-        fwd = shift(own_f if fwd is None else fwd + own_f, "z", 1)
-        bwd = shift(own_b if bwd is None else bwd + own_b, "z", -1)
-    fwd = fwd + lax.dynamic_index_in_dim(lo, me, 0, keepdims=False)
-    bwd = bwd + lax.dynamic_index_in_dim(hi, me, 0, keepdims=False)
-    return jnp.concatenate([fwd, bwd], axis=-1)
+    for step in range(1, n_fwd + 1):
+        own = lax.dynamic_index_in_dim(x, (me + n_fwd + 1 - step) % n, 0, keepdims=False)
+        fwd = shift(own if fwd is None else fwd + own, "z", 1)
+        if step <= n_bwd:
+            own = lax.dynamic_index_in_dim(x, (me - n_bwd - 1 + step) % n, 0, keepdims=False)
+            bwd = shift(own if bwd is None else bwd + own, "z", -1)
+    return fwd + bwd + lax.dynamic_index_in_dim(x, me, 0, keepdims=False)
 
 
 def z_ring_all_gather(chunk):
@@ -63,20 +63,23 @@
     out = lax.dynamic_update_index_in_dim(out, chunk, me, 0)
     fwd = chunk
     bwd = chunk
-    half = n // 2
-    for step in range(1, half):
+    n_fwd = n // 2
+    for step in range(1, n_fwd + 1):
         fwd = shift(fwd, "z", 1)
-        bwd = shift(bwd, "z", -1)
         out = lax.dynamic_update_index_in_dim(out, fwd, (me - step) % n, 0)
-        out = lax.dynamic_update_index_in_dim(out, bwd, (me + step) % n, 0)
-    lo, _ = jnp.split(fwd, 2, axis=-1)
-    _, hi = jnp.split(bwd, 2, axis=-1)
-    last = jnp.concatenate([shift(lo, "z", 1), shift(hi, "z", -1)], axis=-1)
-    out = lax.dynamic_update_index_in_dim(out, last, (me + half) % n, 0)
+        if step < n - n_fwd:
+            bwd = shift(bwd, "z", -1)
+            out = lax.dynamic_update_index_in_dim(out, bwd, (me + step) % n, 0)
     return out
 
 
-def dp_reduce_scatter(part):
+def swap_with(value, extra, axis):
+    flat = jnp.concatenate([value.reshape(-1), extra.reshape(-1)])
+    got = swap(flat, axis, 1)
+    return got[: value.size].reshape(value.shape), got[value.size :].reshape(extra.shape)
+
+
+def dp_reduce_scatter(part, small):
     rows = part.shape[0]
     rest = part.shape[1:]
     n_z = lax.axis_size("z")
@@ -84,12 +87,19 @@
     core = lax.axis_index("core")
     mine = lax.dynamic_index_in_dim(x, core, 2, keepdims=False)
     other = lax.dynamic_index_in_dim(x, 1 - core, 2, keepdims=False)
-    x = mine + swap(other, "core", 1)
+    got, got_small = swap_with(other, small, "core")
+    x = mine + got
+    small = small + got_small
+    mask = 1
+    while mask < n_z:
+        small = small + swap(small, "z", mask)
+        mask *= 2
     x = z_ring_reduce_scatter(x)
     ylo = lax.axis_index("ylo")
     mine = lax.dynamic_index_in_dim(x, ylo, 0, keepdims=False)
     other = lax.dynamic_index_in_dim(x, 1 - ylo, 0, keepdims=False)
-    return mine + swap(other, "ylo", 1)
+    got, got_small = swap_with(other, small, "ylo")
+    return mine + got, small + got_small
 
 
 def dp_all_gather(local):
@@ -101,16 +111,6 @@
     other = swap(ring, "core", 1)
     both = jnp.where(core == 0, jnp.stack([ring, other], 2), jnp.stack([other, ring], 2))
     return both.reshape((-1,) + local.shape[1:])
-
-
-def dp_all_reduce(x):
-    x = x + swap(x, "core", 1)
-    x = x + swap(x, "ylo", 1)
-    mask = 1
-    while mask < lax.axis_size("z"):
-        x = x + swap(x, "z", mask)
-        mask *= 2
-    return x
 
 
 def to_wire(blocks, feat_count):
@@ -240,11 +240,11 @@
         ],
         axis=1,
     )
-    summed = dp_reduce_scatter(parts * grad_scale)[0]
+    rights = jnp.concatenate([right_up_term, right_down_term], axis=0)
+    summed, rights = dp_reduce_scatter(parts * grad_scale, rights)
+    summed = summed[0]
     grad_up_left = summed[0][None]
     grad_down_left = summed[1].reshape(1, hidden_rows, block_width)
-    rights = jnp.concatenate([right_up_term, right_down_term], axis=0)
-    rights = dp_all_reduce(rights)
     grad_up_right = rights[:group_up]
     grad_down_right = rights[group_up:]
     return (layer_out, grad_tokens, grad_up_left, grad_up_right, grad_down_left, grad_down_right)

time: 345 us -> 362 us (1.049)
  waiting for transfers between devices: 73.7 us -> 120 us
  starting transfers between devices: 124 us -> 88.7 us
  local copies, waits for them, and re-layouts: 55.4 us -> 67.8 us
  other arithmetic: 30.9 us -> 22.7 us
    ppermute x22 -> x14, starting transfers between devices: 79.7 us -> 48.6 us  [shift(): return lax.ppermute(value, axis, [(i, (i + step) % n) for i in range(n)])]
    ppermute x22 -> x14, waiting for transfers between devices: 9.69 us -> 39.1 us  [shift(): return lax.ppermute(value, axis, [(i, (i + step) % n) for i in range(n)])]
    ppermute x9 -> x7, waiting for transfers between devices: 28.4 us -> 51.3 us  [swap(): return lax.ppermute(value, axis, [(i, i ^ mask) for i in range(n)])]
    add x21 -> x11, other arithmetic: 20.1 us -> 9.71 us  [the longest x1 4.22 us: dp_reduce_scatter(): x = mine + got]
    reshape x0 -> x8, local copies, waits for them, and re-layouts: none -> 7.66 us  [the longest x2 4.95 us: swap_with(): got[:value.size].reshape(value.shape)]
    all_to_all x2, waiting for transfers between devices: 35.6 us -> 29.8 us  [exchange(): shaped = lax.all_to_all(shaped, 'yhi', 1, 1, tiled=True)]
    slice x0 -> x4, local copies, waits for them, and re-layouts: none -> 5.43 us  [the longest x2 4.49 us: swap_with(): got[:value.size].reshape(value.shape)]
    ppermute x9 -> x7, starting transfers between devices: 33.4 us -> 29.2 us  [swap(): return lax.ppermute(value, axis, [(i, i ^ mask) for i in range(n)])]
  transfers between devices with their start and end apart: 33 -> 23, of which waited for: 11 -> 17; matrix products, arithmetic and copies ran while one was open for 19% -> 12% of each run, Pallas kernels for 0% -> 0%
where the time goes in v4:
time: 362 us; the launch traced here: 361 us
  waiting for transfers between devices  120 us (33%)
  starting transfers between devices  88.7 us (25%)
  local copies, waits for them, and re-layouts  67.8 us (19%)
  blocking collectives  40.4 us (11%)
  other arithmetic  22.7 us (6%)
  matrix products  19 us (5%)
    ppermute x7, waiting for transfers between devices, swap(): return lax.ppermute(value, axis, [(i, i ^ mask) for i in range(n)])  51.3 us
    ppermute x14, starting transfers between devices, shift(): return lax.ppermute(value, axis, [(i, (i + step) % n) for i in range(n)])  48.6 us
    all_to_all x2, blocking collectives, exchange(): shaped = lax.all_to_all(shaped, 'x', 2, 2, tiled=True)  40.4 us
    ppermute x14, waiting for transfers between devices, shift(): return lax.ppermute(value, axis, [(i, (i + step) % n) for i in range(n)])  39.1 us
    all_to_all x2, waiting for transfers between devices, exchange(): shaped = lax.all_to_all(shaped, 'yhi', 1, 1, tiled=True)  29.8 us
    ppermute x7, starting transfers between devices, swap(): return lax.ppermute(value, axis, [(i, i ^ mask) for i in range(n)])  29.2 us
    all_to_all x2, starting transfers between devices, exchange(): shaped = lax.all_to_all(shaped, 'yhi', 1, 1, tiled=True)  10.9 us
  transfers between devices with their start and end apart: 23, of which 17 were waited for; matrix products, arithmetic and copies ran while one was open for 12% of the time, Pallas kernels for 0%

profile of v4, /device:TPU:1, one launch (start us, length us, event | category | flops | bytes accessed | tf_op | source)
XLA Modules:
  0.0 360.5 jit_solution(18334333047314049228)
XLA Ops:
  2.5 4.0 %collective-permute-start = (bf16[16,4096]{1,0:T(8,128)(2,1)S(1)}, bf16[16,4096]{1,0:T(8,128)(2,1)S(1)}, u32[]{:S(2)}, u32[]{:S(2)}) collective-permute-start(bf16[16,4096]{1,0:T(8,128)(2,1)S(1)} %get-tuple-element.62), channel_id=1, source_target_pairs={{0,32},{32,0},{1,33},{33,1},{2,34},{34,2},{3,35},{35,3},{4,36},{36... | collective-permute-start | bytes 393224 | tf_op jit(solution)/shard_map/ppermute | solution.py:40
  6.6 2.2 collective-permute-done
  8.9 4.7 %collective-permute-start.1 = (bf16[2,16,4096]{2,1,0:T(8,128)(2,1)S(1)}, bf16[2,16,4096]{2,1,0:T(8,128)(2,1)S(1)}, u32[]{:S(2)}, u32[]{:S(2)}) collective-permute-start(bf16[2,16,4096]{2,1,0:T(8,128)(2,1)S(1)} %maximum_select_fusion.2), channel_id=1, source_target_pairs={{0,64},{64,128},{128,192},{192,256},{256,320},{320,384},{384,448},... | collective-permute-start | bytes 786440 | tf_op jit(solution)/shard_map/ppermute | solution.py:35
  13.6 8.6 %collective-permute-start.2 = (bf16[2,16,4096]{2,1,0:T(8,128)(2,1)S(1)}, bf16[2,16,4096]{2,1,0:T(8,128)(2,1)S(1)}, u32[]{:S(2)}, u32[]{:S(2)}) collective-permute-start(bf16[2,16,4096]{2,1,0:T(8,128)(2,1)S(1)} %maximum_select_fusion.2), channel_id=1, source_target_pairs={{0,448},{64,0},{128,64},{192,128},{256,192},{320,256},{384,320},{4... | collective-permute-start | bytes 786440 | tf_op jit(solution)/shard_map/ppermute | solution.py:35
  27.2 4.6 %collective-permute-start.4 = (bf16[2,16,4096]{2,1,0:T(8,128)(2,1)S(1)}, bf16[2,16,4096]{2,1,0:T(8,128)(2,1)S(1)}, u32[]{:S(2)}, u32[]{:S(2)}) collective-permute-start(bf16[2,16,4096]{2,1,0:T(8,128)(2,1)S(1)} %collective-permute-done.2), channel_id=1, source_target_pairs={{0,448},{64,0},{128,64},{192,128},{256,192},{320,256},{384,320},{4... | collective-permute-start | bytes 786440 | tf_op jit(solution)/shard_map/ppermute | solution.py:35
  35.9 4.6 %collective-permute-start.6 = (bf16[2,16,4096]{2,1,0:T(8,128)(2,1)S(1)}, bf16[2,16,4096]{2,1,0:T(8,128)(2,1)S(1)}, u32[]{:S(2)}, u32[]{:S(2)}) collective-permute-start(bf16[2,16,4096]{2,1,0:T(8,128)(2,1)S(1)} %collective-permute-done.4), channel_id=1, source_target_pairs={{0,448},{64,0},{128,64},{192,128},{256,192},{320,256},{384,320},{4... | collective-permute-start | bytes 786440 | tf_op jit(solution)/shard_map/ppermute | solution.py:35
  45.7 4.9 %collective-permute-done.7 = bf16[2,16,4096]{2,1,0:T(8,128)(2,1)S(1)} collective-permute-done((bf16[2,16,4096]{2,1,0:T(8,128)(2,1)S(1)}, bf16[2,16,4096]{2,1,0:T(8,128)(2,1)S(1)}, u32[]{:S(2)}, u32[]{:S(2)}) %collective-permute-start.7) | collective-permute-done | bytes 262176 | tf_op jit(solution)/shard_map/ppermute | solution.py:35
  51.4 7.3 %collective-permute-start.8 = (bf16[8,2,16,4096]{3,2,1,0:T(8,128)(2,1)}, bf16[8,2,16,4096]{3,2,1,0:T(8,128)(2,1)}, u32[]{:S(2)}, u32[]{:S(2)}) collective-permute-start(bf16[8,2,16,4096]{3,2,1,0:T(8,128)(2,1)} %bitcast_dynamic-update-slice_fusion), channel_id=1, source_target_pairs={{0,16},{16,0},{1,17},{17,1},{2,18},{18,2},{3,19},{19,3},{4,20},{20... | collective-permute-start | bytes 6291464 | tf_op jit(solution)/shard_map/ppermute | solution.py:40
  60.2 2.1 reshape.271
  62.8 4.2 %maximum_select_fusion = bf16[8,2,2,16,4096]{4,3,2,1,0:T(8,128)(2,1)S(1)} fusion(bf16[8,2,1,16,4096]{4,3,2,1,0:T(8,128)(2,1)} %bitcast.13, bf16[8,2,1,16,4096]{4,3,2,1,0:T(8,128)(2,1)} %bitcast.12, pred[]{:T(512)S(6)} %eq.26), kind=kLoop, calls=%fused_computation.2 | loop fusion | flops 6291456 | bytes 8388609 | tf_op jit(solution)/shard_map/jit(_where)/select_n | solution.py:112
  69.2 20.9 %all_to_all.20 = bf16[256,4,4,160]{0,3,1,2:T(8,128)(2,1)S(1)} all-to-all(bf16[256,4,4,160]{0,3,1,2:T(8,128)(2,1)S(1)} %copy.189), channel_id=1, replica_groups=mesh['z'=8,'ylo'=2,'core'=2,'yhi'=4,'x'=4] {'x'}, dimensions={2} | all-to-all | bytes 2621440 | tf_op jit(solution)/shard_map/all_to_all | solution.py:28
  91.3 6.8 %all-to-all-start.1 = ((bf16[256,4,4,160]{0,3,2,1:T(8,128)(2,1)}), bf16[256,4,4,160]{0,3,2,1:T(8,128)(2,1)}, u32[]{:S(2)}, u32[]{:S(2)}) async-start(bf16[256,4,4,160]{0,3,2,1:T(8,128)(2,1)} %copy.164), calls=%async_computation.1 | async-start | bytes 2621440 | tf_op jit(solution)/shard_map/all_to_all | solution.py:29
  98.5 3.4 slice.77
  101.9 3.1 reshape.270
  105.1 24.8 %all-to-all-done.1 = bf16[256,4,4,160]{0,3,2,1:T(8,128)(2,1)} async-done(((bf16[256,4,4,160]{0,3,2,1:T(8,128)(2,1)}), bf16[256,4,4,160]{0,3,2,1:T(8,128)(2,1)}, u32[]{:S(2)}, u32[]{:S(2)}) %all-to-all-start.1) | async-done | bytes 1310752 | tf_op jit(solution)/shard_map/all_to_all | solution.py:29
  133.2 3.1 fusion.4
  143.9 19.5 %all_to_all.21 = bf16[256,4,4,160]{0,1,3,2:T(4,128)(2,1)S(1)} all-to-all(bf16[256,4,4,160]{0,1,3,2:T(4,128)(2,1)S(1)} %pad_maximum_fusion.2), channel_id=1, replica_groups=mesh['z'=8,'ylo'=2,'core'=2,'yhi'=4,'x'=4] {'x'}, dimensions={2} | all-to-all | bytes 2621440 | tf_op jit(solution)/shard_map/all_to_all | solution.py:28
  163.5 2.1 copy.173
  165.6 4.1 %all-to-all-start.3 = ((bf16[256,4,4,160]{0,2,3,1:T(4,128)(2,1)}), bf16[256,4,4,160]{0,2,3,1:T(4,128)(2,1)S(1)}, u32[]{:S(2)}, u32[]{:S(2)}) async-start(bf16[256,4,4,160]{0,2,3,1:T(4,128)(2,1)} %copy.173), calls=%async_computation.3 | async-start | bytes 2621440 | tf_op jit(solution)/shard_map/all_to_all | solution.py:29
  170.5 3.4 fusion.18
  175.5 2.8 convolution_bitcast_fusion
  178.3 5.3 %copy.177 = f32[2048,1,512]{2,0,1:T(8,128)} copy(f32[2048,1,512]{0,2,1:T(8,128)} %convolution_bitcast_fusion) | data formatting | bytes 8388608 | tf_op jit(solution)/shard_map/tbh,tbc->hbc/transpose | solution.py:203
  183.7 5.6 %stack.56 = f32[8,2,2,1,1,16,2048]{6,5,2,1,0,4,3:T(8,128)} reshape(f32[2048,1,512]{2,0,1:T(8,128)} %copy.177) | data formatting | bytes 8388608 | tf_op jit(solution)/shard_map/stack | solution.py:236
  189.3 5.0 %all-to-all-done.3 = bf16[256,4,4,160]{0,2,3,1:T(4,128)(2,1)S(1)} async-done(((bf16[256,4,4,160]{0,2,3,1:T(4,128)(2,1)}), bf16[256,4,4,160]{0,2,3,1:T(4,128)(2,1)S(1)}, u32[]{:S(2)}, u32[]{:S(2)}) %all-to-all-start.3) | async-done | bytes 1310752 | tf_op jit(solution)/shard_map/all_to_all | solution.py:29
  198.1 2.1 fusion.31
  202.4 2.9 constant_dynamic-slice_fusion.2
  206.7 2.9 pad_maximum_fusion
  209.6 5.5 %collective-permute-start.9 = (f32[1089536]{0:T(1024)}, f32[1089536]{0:T(1024)}, u32[]{:S(2)}, u32[]{:S(2)}) collective-permute-start(f32[1089536]{0:T(1024)} %pad_maximum_fusion), channel_id=1, source_target_pairs={{0,16},{16,0},{1,17},{17,1},{2,18},{18,2},{3,19},{19,3},{4,20},{20... | collective-permute-start | bytes 13074440 | tf_op jit(solution)/shard_map/ppermute | solution.py:40
  215.2 7.3 %collective-permute-done.9 = f32[1089536]{0:T(1024)} collective-permute-done((f32[1089536]{0:T(1024)}, f32[1089536]{0:T(1024)}, u32[]{:S(2)}, u32[]{:S(2)}) %collective-permute-start.9) | collective-permute-done | bytes 4358176 | tf_op jit(solution)/shard_map/ppermute | solution.py:40
  222.5 4.5 %slice.83 = f32[1048576]{0:T(1024)} slice(f32[1089536]{0:T(1024)} %collective-permute-done.9), slice={[0:1048576]} | slice | bytes 8388608 | tf_op jit(solution)/shard_map/slice | solution.py:79
  227.0 4.9 %reshape.280 = f32[8,2,1,2,16,2048]{5,4,3,1,0,2:T(8,128)} reshape(f32[1048576]{0:T(1024)} %slice.83) | data formatting | bytes 8388608 | tf_op jit(solution)/shard_map/reshape | solution.py:79
  231.9 4.2 %bitcast_add_fusion = f32[8,2,1,2,16,2048]{5,4,3,1,0,2:T(8,128)S(1)} fusion(f32[8,2,1,2,16,2048]{5,4,3,1,0,2:T(8,128)} %reshape.280, f32[8,2,1,1,2,16,2048]{6,5,2,1,0,4,3:T(8,128)} %get-tuple-element.48), kind=kLoop, calls=%fused_computation.3 | loop fusion | flops 1048576 | bytes 12582912 | tf_op jit(solution)/shard_map/add | solution.py:91
  238.1 4.6 %collective-permute-start.14 = (f32[2,1,2,16,2048]{4,3,2,0,1:T(8,128)S(1)}, f32[2,1,2,16,2048]{4,3,2,0,1:T(8,128)S(1)}, u32[]{:S(2)}, u32[]{:S(2)}) collective-permute-start(f32[2,1,2,16,2048]{4,3,2,0,1:T(8,128)S(1)} %get-tuple-element.54), channel_id=1, source_target_pairs={{0,448},{64,0},{128,64},{192,128},{256,192},{320,256},{384,320},{4... | collective-permute-start | bytes 1572872 | tf_op jit(solution)/shard_map/ppermute | solution.py:35
  242.7 9.7 %collective-permute-done.10 = f32[2,1,2,16,2048]{4,3,2,0,1:T(8,128)S(1)} collective-permute-done((f32[2,1,2,16,2048]{4,3,2,0,1:T(8,128)S(1)}, f32[2,1,2,16,2048]{4,3,2,0,1:T(8,128)S(1)}, u32[]{:S(2)}, u32[]{:S(2)}) %collective-permute-start.10) | collective-permute-done | bytes 524320 | tf_op jit(solution)/shard_map/ppermute | solution.py:35
  254.5 13.4 %collective-permute-done.11 = f32[2,1,2,16,2048]{4,3,2,0,1:T(8,128)S(1)} collective-permute-done((f32[2,1,2,16,2048]{4,3,2,0,1:T(8,128)S(1)}, f32[2,1,2,16,2048]{4,3,2,0,1:T(8,128)S(1)}, u32[]{:S(2)}, u32[]{:S(2)}) %collective-permute-start.11) | collective-permute-done | bytes 524320 | tf_op jit(solution)/shard_map/ppermute | solution.py:35
  270.9 3.6 %collective-permute-start.12 = (f32[2,1,2,16,2048]{4,3,2,0,1:T(8,128)}, f32[2,1,2,16,2048]{4,3,2,0,1:T(8,128)}, u32[]{:S(2)}, u32[]{:S(2)}) collective-permute-start(f32[2,1,2,16,2048]{4,3,2,0,1:T(8,128)} %get-tuple-element.53), channel_id=1, source_target_pairs={{0,64},{64,128},{128,192},{192,256},{256,320},{320,384},{384,448},... | collective-permute-start | bytes 1572872 | tf_op jit(solution)/shard_map/ppermute | solution.py:35
  276.5 6.0 %collective-permute-done.15 = f32[2,1,2,16,2048]{4,3,2,0,1:T(8,128)} collective-permute-done((f32[2,1,2,16,2048]{4,3,2,0,1:T(8,128)}, f32[2,1,2,16,2048]{4,3,2,0,1:T(8,128)}, u32[]{:S(2)}, u32[]{:S(2)}) %collective-permute-start.15) | collective-permute-done | bytes 524320 | tf_op jit(solution)/shard_map/ppermute | solution.py:35
  282.5 3.1 collective-permute-done.12
  285.6 2.6 bitcast_add_fusion.2
  290.2 4.6 %collective-permute-start.16 = (f32[2,1,2,16,2048]{4,3,2,0,1:T(8,128)}, f32[2,1,2,16,2048]{4,3,2,0,1:T(8,128)}, u32[]{:S(2)}, u32[]{:S(2)}) collective-permute-start(f32[2,1,2,16,2048]{4,3,2,0,1:T(8,128)} %get-tuple-element.50), channel_id=1, source_target_pairs={{0,448},{64,0},{128,64},{192,128},{256,192},{320,256},{384,320},{4... | collective-permute-start | bytes 1572872 | tf_op jit(solution)/shard_map/ppermute | solution.py:35
  296.7 11.1 %collective-permute-done.17 = f32[160,16,16]{0,2,1:T(8,128)S(1)} collective-permute-done((f32[160,16,16]{0,2,1:T(8,128)S(1)}, f32[160,16,16]{0,2,1:T(8,128)S(1)}, u32[]{:S(2)}, u32[]{:S(2)}) %collective-permute-start.17) | collective-permute-done | bytes 163872 | tf_op jit(solution)/shard_map/ppermute | solution.py:40
  307.9 4.0 %collective-permute-start.18 = (f32[160,16,16]{0,2,1:T(8,128)S(1)}, f32[160,16,16]{0,2,1:T(8,128)S(1)}, u32[]{:S(2)}, u32[]{:S(2)}) collective-permute-start(f32[160,16,16]{0,2,1:T(8,128)S(1)} %add.229), channel_id=1, source_target_pairs={{0,128},{64,192},{128,0},{192,64},{256,384},{320,448},{384,256},{4... | collective-permute-start | bytes 491528 | tf_op jit(solution)/shard_map/ppermute | solution.py:40
  311.9 10.5 %collective-permute-done.18 = f32[160,16,16]{0,2,1:T(8,128)S(1)} collective-permute-done((f32[160,16,16]{0,2,1:T(8,128)S(1)}, f32[160,16,16]{0,2,1:T(8,128)S(1)}, u32[]{:S(2)}, u32[]{:S(2)}) %collective-permute-start.18) | collective-permute-done | bytes 163872 | tf_op jit(solution)/shard_map/ppermute | solution.py:40
  322.4 4.3 %collective-permute-start.19 = (f32[160,16,16]{0,2,1:T(8,128)S(1)}, f32[160,16,16]{0,2,1:T(8,128)S(1)}, u32[]{:S(2)}, u32[]{:S(2)}) collective-permute-start(f32[160,16,16]{0,2,1:T(8,128)S(1)} %add.230), channel_id=1, source_target_pairs={{0,256},{64,320},{128,384},{192,448},{256,0},{320,64},{384,128},{4... | collective-permute-start | bytes 491528 | tf_op jit(solution)/shard_map/ppermute | solution.py:40
  326.9 14.0 %collective-permute-done.19 = f32[160,16,16]{0,2,1:T(8,128)S(1)} collective-permute-done((f32[160,16,16]{0,2,1:T(8,128)S(1)}, f32[160,16,16]{0,2,1:T(8,128)S(1)}, u32[]{:S(2)}, u32[]{:S(2)}) %collective-permute-start.19) | collective-permute-done | bytes 163872 | tf_op jit(solution)/shard_map/ppermute | solution.py:40
  344.3 2.1 collective-permute-start.20
  346.4 2.3 fusion.15
  350.5 6.1 %collective-permute-done.20 = f32[106496]{0:T(1024)S(1)} collective-permute-done((f32[106496]{0:T(1024)S(1)}, f32[106496]{0:T(1024)S(1)}, u32[]{:S(2)}, u32[]{:S(2)}) %collective-permute-start.20) | collective-permute-done | bytes 426016 | tf_op jit(solution)/shard_map/ppermute | solution.py:40
  (136 shorter events, 65.3 us)
Async XLA Ops:
  0.6 66.4 %copy-start = (bf16[256,512]{1,0:T(8,128)(2,1)S(1)}, bf16[256,512]{1,0:T(8,128)(2,1)}, u32[]{:S(2)}) copy-start(bf16[256,512]{1,0:T(8,128)(2,1)} %param.6) | copy-start | bytes 786436
  2.5 6.4 %collective-permute-start = (bf16[16,4096]{1,0:T(8,128)(2,1)S(1)}, bf16[16,4096]{1,0:T(8,128)(2,1)S(1)}, u32[]{:S(2)}, u32[]{:S(2)}) collective-permute-start(bf16[16,4096]{1,0:T(8,128)(2,1)S(1)} %get-tuple-element.62), channel_id=1, source_target_pairs={{0,32},{32,0},{1,33},{33,1},{2,34},{34,2},{3,35},{35,3},{4,36},{36... | collective-permute-start | bytes 393224 | tf_op jit(solution)/shard_map/ppermute | solution.py:40
  8.9 16.4 %collective-permute-start.1 = (bf16[2,16,4096]{2,1,0:T(8,128)(2,1)S(1)}, bf16[2,16,4096]{2,1,0:T(8,128)(2,1)S(1)}, u32[]{:S(2)}, u32[]{:S(2)}) collective-permute-start(bf16[2,16,4096]{2,1,0:T(8,128)(2,1)S(1)} %maximum_select_fusion.2), channel_id=1, source_target_pairs={{0,64},{64,128},{128,192},{192,256},{256,320},{320,384},{384,448},... | collective-permute-start | bytes 786440 | tf_op jit(solution)/shard_map/ppermute | solution.py:35
  13.6 13.6 %collective-permute-start.2 = (bf16[2,16,4096]{2,1,0:T(8,128)(2,1)S(1)}, bf16[2,16,4096]{2,1,0:T(8,128)(2,1)S(1)}, u32[]{:S(2)}, u32[]{:S(2)}) collective-permute-start(bf16[2,16,4096]{2,1,0:T(8,128)(2,1)S(1)} %maximum_select_fusion.2), channel_id=1, source_target_pairs={{0,448},{64,0},{128,64},{192,128},{256,192},{320,256},{384,320},{4... | collective-permute-start | bytes 786440 | tf_op jit(solution)/shard_map/ppermute | solution.py:35
  23.7 35.0 %copy-start.18 = (bf16[32,16,16]{0,2,1:T(8,128)(2,1)S(1)}, bf16[32,16,16]{0,2,1:T(8,128)(2,1)}, u32[]{:S(2)}) copy-start(bf16[32,16,16]{0,2,1:T(8,128)(2,1)} %param.10) | copy-start | bytes 49156
  25.3 8.7 %collective-permute-start.3 = (bf16[2,16,4096]{2,1,0:T(8,128)(2,1)S(1)}, bf16[2,16,4096]{2,1,0:T(8,128)(2,1)S(1)}, u32[]{:S(2)}, u32[]{:S(2)}) collective-permute-start(bf16[2,16,4096]{2,1,0:T(8,128)(2,1)S(1)} %collective-permute-done.1), channel_id=1, source_target_pairs={{0,64},{64,128},{128,192},{192,256},{256,320},{320,384},{384,448},... | collective-permute-start | bytes 786440 | tf_op jit(solution)/shard_map/ppermute | solution.py:35
  27.2 8.7 %collective-permute-start.4 = (bf16[2,16,4096]{2,1,0:T(8,128)(2,1)S(1)}, bf16[2,16,4096]{2,1,0:T(8,128)(2,1)S(1)}, u32[]{:S(2)}, u32[]{:S(2)}) collective-permute-start(bf16[2,16,4096]{2,1,0:T(8,128)(2,1)S(1)} %collective-permute-done.2), channel_id=1, source_target_pairs={{0,448},{64,0},{128,64},{192,128},{256,192},{320,256},{384,320},{4... | collective-permute-start | bytes 786440 | tf_op jit(solution)/shard_map/ppermute | solution.py:35
  34.0 8.3 %collective-permute-start.5 = (bf16[2,16,4096]{2,1,0:T(8,128)(2,1)S(1)}, bf16[2,16,4096]{2,1,0:T(8,128)(2,1)S(1)}, u32[]{:S(2)}, u32[]{:S(2)}) collective-permute-start(bf16[2,16,4096]{2,1,0:T(8,128)(2,1)S(1)} %collective-permute-done.3), channel_id=1, source_target_pairs={{0,64},{64,128},{128,192},{192,256},{256,320},{320,384},{384,448},... | collective-permute-start | bytes 786440 | tf_op jit(solution)/shard_map/ppermute | solution.py:35
  35.9 9.0 %collective-permute-start.6 = (bf16[2,16,4096]{2,1,0:T(8,128)(2,1)S(1)}, bf16[2,16,4096]{2,1,0:T(8,128)(2,1)S(1)}, u32[]{:S(2)}, u32[]{:S(2)}) collective-permute-start(bf16[2,16,4096]{2,1,0:T(8,128)(2,1)S(1)} %collective-permute-done.4), channel_id=1, source_target_pairs={{0,448},{64,0},{128,64},{192,128},{256,192},{320,256},{384,320},{4... | collective-permute-start | bytes 786440 | tf_op jit(solution)/shard_map/ppermute | solution.py:35
  42.3 8.3 %collective-permute-start.7 = (bf16[2,16,4096]{2,1,0:T(8,128)(2,1)S(1)}, bf16[2,16,4096]{2,1,0:T(8,128)(2,1)S(1)}, u32[]{:S(2)}, u32[]{:S(2)}) collective-permute-start(bf16[2,16,4096]{2,1,0:T(8,128)(2,1)S(1)} %collective-permute-done.5), channel_id=1, source_target_pairs={{0,64},{64,128},{128,192},{192,256},{256,320},{320,384},{384,448},... | collective-permute-start | bytes 786440 | tf_op jit(solution)/shard_map/ppermute | solution.py:35
  51.4 11.4 %collective-permute-start.8 = (bf16[8,2,16,4096]{3,2,1,0:T(8,128)(2,1)}, bf16[8,2,16,4096]{3,2,1,0:T(8,128)(2,1)}, u32[]{:S(2)}, u32[]{:S(2)}) collective-permute-start(bf16[8,2,16,4096]{3,2,1,0:T(8,128)(2,1)} %bitcast_dynamic-update-slice_fusion), channel_id=1, source_target_pairs={{0,16},{16,0},{1,17},{17,1},{2,18},{18,2},{3,19},{19,3},{4,20},{20... | collective-permute-start | bytes 6291464 | tf_op jit(solution)/shard_map/ppermute | solution.py:40
  58.8 3.5 copy-start.14
  62.3 4.7 %copy-start.5 = (bf16[512,512]{1,0:T(8,128)(2,1)}, bf16[512,512]{1,0:T(8,128)(2,1)S(1)}, u32[]{:S(2)}) copy-start(bf16[512,512]{1,0:T(8,128)(2,1)S(1)} %reshape.271) | copy-start | bytes 1572868
  67.0 2.0 copy-start.4
  90.1 8.0 %copy-start.19 = (bf16[128,16,16]{0,2,1:T(8,128)(2,1)S(1)}, bf16[128,16,16]{0,2,1:T(8,128)(2,1)}, u32[]{:S(2)}) copy-start(bf16[128,16,16]{0,2,1:T(8,128)(2,1)} %param.8) | copy-start | bytes 196612
  91.3 38.6 %all-to-all-start.1 = ((bf16[256,4,4,160]{0,3,2,1:T(8,128)(2,1)}), bf16[256,4,4,160]{0,3,2,1:T(8,128)(2,1)}, u32[]{:S(2)}, u32[]{:S(2)}) async-start(bf16[256,4,4,160]{0,3,2,1:T(8,128)(2,1)} %copy.164), calls=%async_computation.1 | async-start | bytes 2621440 | tf_op jit(solution)/shard_map/all_to_all | solution.py:29
  98.5 34.5 %copy-start.12 = (bf16[128,16,16]{2,1,0:T(8,128)(2,1)}, bf16[128,16,16]{2,1,0:T(8,128)(2,1)S(1)}, u32[]{:S(2)}) copy-start(bf16[128,16,16]{2,1,0:T(8,128)(2,1)S(1)} %copy.170) | copy-start | bytes 196612
  130.9 2.1 copy-start.10
  132.3 1.0 copy-start.7
  136.3 1.1 copy-start.8
  140.0 1.7 copy-start.13
  163.5 6.2 %copy-start.15 = (bf16[256,512]{1,0:T(8,128)(2,1)S(1)}, bf16[256,512]{1,0:T(8,128)(2,1)}, u32[]{:S(2)}) copy-start(bf16[256,512]{1,0:T(8,128)(2,1)} %param.11) | copy-start | bytes 786436
  165.6 28.7 %all-to-all-start.3 = ((bf16[256,4,4,160]{0,2,3,1:T(4,128)(2,1)}), bf16[256,4,4,160]{0,2,3,1:T(4,128)(2,1)S(1)}, u32[]{:S(2)}, u32[]{:S(2)}) async-start(bf16[256,4,4,160]{0,2,3,1:T(4,128)(2,1)} %copy.173), calls=%async_computation.3 | async-start | bytes 2621440 | tf_op jit(solution)/shard_map/all_to_all | solution.py:29
  170.5 5.0 %copy-start.11 = (bf16[256,16,32]{0,2,1:T(8,128)(2,1)S(1)}, bf16[256,16,32]{0,2,1:T(8,128)(2,1)}, u32[]{:S(2)}) copy-start(bf16[256,16,32]{0,2,1:T(8,128)(2,1)} %copy-done.10) | copy-start | bytes 786436
  195.1 1.4 copy-start.17
  198.1 2.5 copy-start.3
  209.6 12.9 %collective-permute-start.9 = (f32[1089536]{0:T(1024)}, f32[1089536]{0:T(1024)}, u32[]{:S(2)}, u32[]{:S(2)}) collective-permute-start(f32[1089536]{0:T(1024)} %pad_maximum_fusion), channel_id=1, source_target_pairs={{0,16},{16,0},{1,17},{17,1},{2,18},{18,2},{3,19},{19,3},{4,20},{20... | collective-permute-start | bytes 13074440 | tf_op jit(solution)/shard_map/ppermute | solution.py:40
  236.1 32.9 %copy-start.2 = (f32[8,2,1,2,16,2048]{5,4,3,1,0,2:T(8,128)}, f32[8,2,1,2,16,2048]{5,4,3,1,0,2:T(8,128)S(1)}, u32[]{:S(2)}) copy-start(f32[8,2,1,2,16,2048]{5,4,3,1,0,2:T(8,128)S(1)} %bitcast_add_fusion) | copy-start | bytes 12582916
  236.2 16.2 %collective-permute-start.10 = (f32[2,1,2,16,2048]{4,3,2,0,1:T(8,128)S(1)}, f32[2,1,2,16,2048]{4,3,2,0,1:T(8,128)S(1)}, u32[]{:S(2)}, u32[]{:S(2)}) collective-permute-start(f32[2,1,2,16,2048]{4,3,2,0,1:T(8,128)S(1)} %get-tuple-element.55), channel_id=1, source_target_pairs={{0,64},{64,128},{128,192},{192,256},{256,320},{320,384},{384,448},... | collective-permute-start | bytes 1572872 | tf_op jit(solution)/shard_map/ppermute | solution.py:35
  238.1 16.3 %collective-permute-start.14 = (f32[2,1,2,16,2048]{4,3,2,0,1:T(8,128)S(1)}, f32[2,1,2,16,2048]{4,3,2,0,1:T(8,128)S(1)}, u32[]{:S(2)}, u32[]{:S(2)}) collective-permute-start(f32[2,1,2,16,2048]{4,3,2,0,1:T(8,128)S(1)} %get-tuple-element.54), channel_id=1, source_target_pairs={{0,448},{64,0},{128,64},{192,128},{256,192},{320,256},{384,320},{4... | collective-permute-start | bytes 1572872 | tf_op jit(solution)/shard_map/ppermute | solution.py:35
  252.5 15.3 %collective-permute-start.11 = (f32[2,1,2,16,2048]{4,3,2,0,1:T(8,128)S(1)}, f32[2,1,2,16,2048]{4,3,2,0,1:T(8,128)S(1)}, u32[]{:S(2)}, u32[]{:S(2)}) collective-permute-start(f32[2,1,2,16,2048]{4,3,2,0,1:T(8,128)S(1)} %bitcast_add_fusion.6), channel_id=1, source_target_pairs={{0,64},{64,128},{128,192},{192,256},{256,320},{320,384},{384,448},... | collective-permute-start | bytes 1572872 | tf_op jit(solution)/shard_map/ppermute | solution.py:35
  269.0 13.5 %collective-permute-start.15 = (f32[2,1,2,16,2048]{4,3,2,0,1:T(8,128)}, f32[2,1,2,16,2048]{4,3,2,0,1:T(8,128)}, u32[]{:S(2)}, u32[]{:S(2)}) collective-permute-start(f32[2,1,2,16,2048]{4,3,2,0,1:T(8,128)} %get-tuple-element.52), channel_id=1, source_target_pairs={{0,448},{64,0},{128,64},{192,128},{256,192},{320,256},{384,320},{4... | collective-permute-start | bytes 1572872 | tf_op jit(solution)/shard_map/ppermute | solution.py:35
  270.9 14.7 %collective-permute-start.12 = (f32[2,1,2,16,2048]{4,3,2,0,1:T(8,128)}, f32[2,1,2,16,2048]{4,3,2,0,1:T(8,128)}, u32[]{:S(2)}, u32[]{:S(2)}) collective-permute-start(f32[2,1,2,16,2048]{4,3,2,0,1:T(8,128)} %get-tuple-element.53), channel_id=1, source_target_pairs={{0,64},{64,128},{128,192},{192,256},{256,320},{320,384},{384,448},... | collective-permute-start | bytes 1572872 | tf_op jit(solution)/shard_map/ppermute | solution.py:35
  288.2 53.7 %collective-permute-start.13 = (f32[2,1,2,16,2048]{4,3,2,0,1:T(8,128)}, f32[2,1,2,16,2048]{4,3,2,0,1:T(8,128)S(1)}, u32[]{:S(2)}, u32[]{:S(2)}) collective-permute-start(f32[2,1,2,16,2048]{4,3,2,0,1:T(8,128)} %get-tuple-element.51), channel_id=1, source_target_pairs={{0,64},{64,128},{128,192},{192,256},{256,320},{320,384},{384,448},... | collective-permute-start | bytes 1572872 | tf_op jit(solution)/shard_map/ppermute | solution.py:35
  290.2 52.6 %collective-permute-start.16 = (f32[2,1,2,16,2048]{4,3,2,0,1:T(8,128)}, f32[2,1,2,16,2048]{4,3,2,0,1:T(8,128)}, u32[]{:S(2)}, u32[]{:S(2)}) collective-permute-start(f32[2,1,2,16,2048]{4,3,2,0,1:T(8,128)} %get-tuple-element.50), channel_id=1, source_target_pairs={{0,448},{64,0},{128,64},{192,128},{256,192},{320,256},{384,320},{4... | collective-permute-start | bytes 1572872 | tf_op jit(solution)/shard_map/ppermute | solution.py:35
  294.8 13.1 %collective-permute-start.17 = (f32[160,16,16]{0,2,1:T(8,128)S(1)}, f32[160,16,16]{0,2,1:T(8,128)S(1)}, u32[]{:S(2)}, u32[]{:S(2)}) collective-permute-start(f32[160,16,16]{0,2,1:T(8,128)S(1)} %fusion.26), channel_id=1, source_target_pairs={{0,64},{64,0},{128,192},{192,128},{256,320},{320,256},{384,448},{4... | collective-permute-start | bytes 491528 | tf_op jit(solution)/shard_map/ppermute | solution.py:40
  307.9 14.5 %collective-permute-start.18 = (f32[160,16,16]{0,2,1:T(8,128)S(1)}, f32[160,16,16]{0,2,1:T(8,128)S(1)}, u32[]{:S(2)}, u32[]{:S(2)}) collective-permute-start(f32[160,16,16]{0,2,1:T(8,128)S(1)} %add.229), channel_id=1, source_target_pairs={{0,128},{64,192},{128,0},{192,64},{256,384},{320,448},{384,256},{4... | collective-permute-start | bytes 491528 | tf_op jit(solution)/shard_map/ppermute | solution.py:40
  322.4 18.4 %collective-permute-start.19 = (f32[160,16,16]{0,2,1:T(8,128)S(1)}, f32[160,16,16]{0,2,1:T(8,128)S(1)}, u32[]{:S(2)}, u32[]{:S(2)}) collective-permute-start(f32[160,16,16]{0,2,1:T(8,128)S(1)} %add.230), channel_id=1, source_target_pairs={{0,256},{64,320},{128,384},{192,448},{256,0},{320,64},{384,128},{4... | collective-permute-start | bytes 491528 | tf_op jit(solution)/shard_map/ppermute | solution.py:40
  341.9 4.4 %copy-start.9 = (bf16[256,16,128]{0,2,1:T(8,128)(2,1)S(1)}, bf16[256,16,128]{0,2,1:T(8,128)(2,1)}, u32[]{:S(2)}) copy-start(bf16[256,16,128]{0,2,1:T(8,128)(2,1)} %copy.176) | copy-start | bytes 3145732
  341.9 0.8 copy-start.16
  344.3 5.2 %copy-start.6 = (bf16[512,512]{1,0:T(8,128)(2,1)S(1)}, bf16[512,512]{1,0:T(8,128)(2,1)}, u32[]{:S(2)}) copy-start(bf16[512,512]{1,0:T(8,128)(2,1)} %copy-done.5) | copy-start | bytes 1572868
  344.3 12.3 %collective-permute-start.20 = (f32[106496]{0:T(1024)S(1)}, f32[106496]{0:T(1024)S(1)}, u32[]{:S(2)}, u32[]{:S(2)}) collective-permute-start(f32[106496]{0:T(1024)S(1)} %pad_maximum_fusion.3), channel_id=1, source_target_pairs={{0,32},{32,0},{1,33},{33,1},{2,34},{34,2},{3,35},{35,3},{4,36},{36... | collective-permute-start | bytes 1277960 | tf_op jit(solution)/shard_map/ppermute | solution.py:40
  357.0 3.5 copy-start.1

commit v5 on v3

--- a/solution.py
+++ b/solution.py
@@ -21,13 +21,7 @@
 
 
 def exchange(wired):
-    rows, feat_count, piece = wired.shape
-    n_x = lax.axis_size("x")
-    n_y = feat_count // n_x
-    shaped = wired.reshape(rows, n_y, n_x, piece)
-    shaped = lax.all_to_all(shaped, "x", 2, 2, tiled=True)
-    shaped = lax.all_to_all(shaped, "yhi", 1, 1, tiled=True)
-    return shaped.reshape(rows, feat_count, piece)
+    return lax.all_to_all(wired, FEAT_AXES, 1, 1, tiled=True)
 
 
 def shift(value, axis, step):

time: 345 us -> 312 us (0.904)
  blocking collectives: 40.4 us -> 0 us
  waiting for transfers between devices: 73.7 us -> 87.9 us
  local copies, waits for them, and re-layouts: 55.4 us -> 47.6 us
    all_to_all x2 -> x0, blocking collectives: 40.4 us -> none  [exchange(): shaped = lax.all_to_all(shaped, 'x', 2, 2, tiled=True)]
    all_to_all x2, waiting for transfers between devices: 35.6 us -> 49.3 us  [exchange(): return lax.all_to_all(wired, FEAT_AXES, 1, 1, tiled=True)]
    all_to_all x3 -> x0, local copies, waits for them, and re-layouts: 4.85 us -> none  [the longest x2 3.32 us: exchange(): shaped = lax.all_to_all(shaped, 'x', 2, 2, tiled=True)]
    all_to_all x2, starting transfers between devices: 10.9 us -> 15.2 us  [exchange(): return lax.all_to_all(wired, FEAT_AXES, 1, 1, tiled=True)]
    unnamed x57 -> x59, local copies, waits for them, and re-layouts: 8.7 us -> 7.82 us
  transfers between devices with their start and end apart: 33 -> 33, of which waited for: 11 -> 12; matrix products, arithmetic and copies ran while one was open for 19% -> 21% of each run, Pallas kernels for 0% -> 0%
where the time goes in v5:
time: 312 us; the launch traced here: 310 us
  starting transfers between devices  126 us (40%)
  waiting for transfers between devices  87.9 us (28%)
  local copies, waits for them, and re-layouts  47.6 us (15%)
  other arithmetic  31.4 us (10%)
  matrix products  15.3 us (5%)
    ppermute x22, starting transfers between devices, shift(): return lax.ppermute(value, axis, [(i, (i + step) % n) for i in range(n)])  80.2 us
    all_to_all x2, waiting for transfers between devices, exchange(): return lax.all_to_all(wired, FEAT_AXES, 1, 1, tiled=True)  49.3 us
    ppermute x9, starting transfers between devices, swap(): return lax.ppermute(value, axis, [(i, i ^ mask) for i in range(n)])  30.8 us
    ppermute x9, waiting for transfers between devices, swap(): return lax.ppermute(value, axis, [(i, i ^ mask) for i in range(n)])  28.6 us
    all_to_all x2, starting transfers between devices, exchange(): return lax.all_to_all(wired, FEAT_AXES, 1, 1, tiled=True)  15.2 us
    ppermute x22, waiting for transfers between devices, shift(): return lax.ppermute(value, axis, [(i, (i + step) % n) for i in range(n)])  10 us
    unnamed x59, local copies, waits for them, and re-layouts  7.82 us
    add x6, other arithmetic, z_ring_reduce_scatter(): fwd = shift(own_f if fwd is None else fwd + own_f, 'z', 1)  7.56 us
  transfers between devices with their start and end apart: 33, of which 12 were waited for; matrix products, arithmetic and copies ran while one was open for 21% of the time, Pallas kernels for 0%

profile of v5, /device:TPU:1, one launch (start us, length us, event | category | flops | bytes accessed | tf_op | source)
XLA Modules:
  0.0 310.2 jit_solution(3027116970484276672)
XLA Ops:
  2.5 4.0 %collective-permute-start = (bf16[16,4096]{1,0:T(8,128)(2,1)S(1)}, bf16[16,4096]{1,0:T(8,128)(2,1)S(1)}, u32[]{:S(2)}, u32[]{:S(2)}) collective-permute-start(bf16[16,4096]{1,0:T(8,128)(2,1)S(1)} %get-tuple-element.46), channel_id=1, source_target_pairs={{0,32},{32,0},{1,33},{33,1},{2,34},{34,2},{3,35},{35,3},{4,36},{36... | collective-permute-start | bytes 393224 | tf_op jit(solution)/shard_map/ppermute | solution.py:34
  6.6 2.2 collective-permute-done
  8.9 11.4 %collective-permute-start.2 = (bf16[2,16,4096]{2,1,0:T(8,128)(2,1)S(1)}, bf16[2,16,4096]{2,1,0:T(8,128)(2,1)S(1)}, u32[]{:S(2)}, u32[]{:S(2)}) collective-permute-start(bf16[2,16,4096]{2,1,0:T(8,128)(2,1)S(1)} %maximum_select_fusion.2), channel_id=1, source_target_pairs={{0,448},{64,0},{128,64},{192,128},{256,192},{320,256},{384,320},{4... | collective-permute-start | bytes 786440 | tf_op jit(solution)/shard_map/ppermute | solution.py:29
  20.2 1.9 collective-permute-start.1
  24.5 5.1 %collective-permute-start.4 = (bf16[2,16,4096]{2,1,0:T(8,128)(2,1)S(1)}, bf16[2,16,4096]{2,1,0:T(8,128)(2,1)S(1)}, u32[]{:S(2)}, u32[]{:S(2)}) collective-permute-start(bf16[2,16,4096]{2,1,0:T(8,128)(2,1)S(1)} %collective-permute-done.2), channel_id=1, source_target_pairs={{0,448},{64,0},{128,64},{192,128},{256,192},{320,256},{384,320},{4... | collective-permute-start | bytes 786440 | tf_op jit(solution)/shard_map/ppermute | solution.py:29
  29.6 1.9 collective-permute-start.3
  33.0 4.9 %collective-permute-start.6 = (bf16[2,16,4096]{2,1,0:T(8,128)(2,1)S(1)}, bf16[2,16,4096]{2,1,0:T(8,128)(2,1)S(1)}, u32[]{:S(2)}, u32[]{:S(2)}) collective-permute-start(bf16[2,16,4096]{2,1,0:T(8,128)(2,1)S(1)} %collective-permute-done.4), channel_id=1, source_target_pairs={{0,448},{64,0},{128,64},{192,128},{256,192},{320,256},{384,320},{4... | collective-permute-start | bytes 786440 | tf_op jit(solution)/shard_map/ppermute | solution.py:29
  41.3 4.9 %collective-permute-start.8 = (bf16[2,16,2048]{2,1,0:T(8,128)(2,1)S(1)}, bf16[2,16,2048]{2,1,0:T(8,128)(2,1)S(1)}, u32[]{:S(2)}, u32[]{:S(2)}) collective-permute-start(bf16[2,16,2048]{2,1,0:T(8,128)(2,1)S(1)} %split.17), channel_id=1, source_target_pairs={{0,448},{64,0},{128,64},{192,128},{256,192},{320,256},{384,320},{4... | collective-permute-start | bytes 393224 | tf_op jit(solution)/shard_map/ppermute | solution.py:29
  46.3 1.9 collective-permute-start.7
  49.7 3.5 %collective-permute-done.7 = bf16[2,16,2048]{2,1,0:T(8,128)(2,1)S(1)} collective-permute-done((bf16[2,16,2048]{2,1,0:T(8,128)(2,1)S(1)}, bf16[2,16,2048]{2,1,0:T(8,128)(2,1)S(1)}, u32[]{:S(2)}, u32[]{:S(2)}) %collective-permute-start.7) | collective-permute-done | bytes 131104 | tf_op jit(solution)/shard_map/ppermute | solution.py:29
  53.9 8.1 %collective-permute-start.9 = (bf16[8,2,16,4096]{3,2,1,0:T(8,128)(2,1)}, bf16[8,2,16,4096]{3,2,1,0:T(8,128)(2,1)}, u32[]{:S(2)}, u32[]{:S(2)}) collective-permute-start(bf16[8,2,16,4096]{3,2,1,0:T(8,128)(2,1)} %fusion.27), channel_id=1, source_target_pairs={{0,16},{16,0},{1,17},{17,1},{2,18},{18,2},{3,19},{19,3},{4,20},{20... | collective-permute-start | bytes 6291464 | tf_op jit(solution)/shard_map/ppermute | solution.py:34
  63.6 2.1 reshape.176
  66.1 4.2 %maximum_select_fusion = bf16[8,2,2,16,4096]{4,3,2,1,0:T(8,128)(2,1)S(1)} fusion(bf16[8,2,1,16,4096]{4,3,2,1,0:T(8,128)(2,1)} %bitcast.13, bf16[8,2,1,16,4096]{4,3,2,1,0:T(8,128)(2,1)} %bitcast.12, pred[]{:T(512)S(6)} %eq.33), kind=kLoop, calls=%fused_computation.1 | loop fusion | flops 6291456 | bytes 8388609 | tf_op jit(solution)/shard_map/jit(_where)/select_n | solution.py:96
  73.5 9.4 %all-to-all-start = ((bf16[256,16,160]{0,2,1:T(8,128)(2,1)}), bf16[256,16,160]{0,2,1:T(8,128)(2,1)}, u32[]{:S(2)}, u32[]{:S(2)}) async-start(bf16[256,16,160]{0,2,1:T(8,128)(2,1)} %pad_maximum_fusion), calls=%async_computation | async-start | bytes 2621440 | tf_op jit(solution)/shard_map/all_to_all | solution.py:24
  83.4 3.4 %slice.45 = bf16[512,2048]{1,0:T(8,128)(2,1)} slice(bf16[512,4096]{1,0:T(8,128)(2,1)} %bitcast.165), slice={[0:512], [2048:4096]} | slice | bytes 4194304 | tf_op jit(solution)/shard_map/slice | solution.py:144
  86.8 3.1 reshape.175
  89.9 27.2 %all-to-all-done = bf16[256,16,160]{0,2,1:T(8,128)(2,1)} async-done(((bf16[256,16,160]{0,2,1:T(8,128)(2,1)}), bf16[256,16,160]{0,2,1:T(8,128)(2,1)}, u32[]{:S(2)}, u32[]{:S(2)}) %all-to-all-start) | async-done | bytes 1310752 | tf_op jit(solution)/shard_map/all_to_all | solution.py:24
  120.2 2.1 fusion.4
  125.8 5.8 %all-to-all-start.1 = ((bf16[256,16,160]{0,2,1:T(8,128)(2,1)}), bf16[256,16,160]{0,2,1:T(8,128)(2,1)S(1)}, u32[]{:S(2)}, u32[]{:S(2)}) async-start(bf16[256,16,160]{0,2,1:T(8,128)(2,1)} %copy.98), calls=%async_computation.1 | async-start | bytes 2621440 | tf_op jit(solution)/shard_map/all_to_all | solution.py:24
  131.5 2.8 convolution_bitcast_fusion
  134.3 5.4 %copy.101 = f32[2048,1,512]{2,0,1:T(8,128)} copy(f32[2048,1,512]{0,2,1:T(8,128)} %convolution_bitcast_fusion) | data formatting | bytes 8388608 | tf_op jit(solution)/shard_map/tbh,tbc->hbc/transpose | solution.py:197
  139.7 5.7 %stack.56 = f32[8,2,2,1,1,16,2048]{6,5,2,1,0,4,3:T(8,128)} reshape(f32[2048,1,512]{2,0,1:T(8,128)} %copy.101) | data formatting | bytes 8388608 | tf_op jit(solution)/shard_map/stack | solution.py:230
  145.4 22.0 %all-to-all-done.1 = bf16[256,16,160]{0,2,1:T(8,128)(2,1)S(1)} async-done(((bf16[256,16,160]{0,2,1:T(8,128)(2,1)}), bf16[256,16,160]{0,2,1:T(8,128)(2,1)S(1)}, u32[]{:S(2)}, u32[]{:S(2)}) %all-to-all-start.1) | async-done | bytes 1310752 | tf_op jit(solution)/shard_map/all_to_all | solution.py:24
  173.9 2.9 collective-permute-start.10
  176.8 6.8 %collective-permute-done.10 = f32[8,2,1,2,16,2048]{5,4,3,1,0,2:T(8,128)S(1)} collective-permute-done((f32[8,2,1,2,16,2048]{5,4,3,1,0,2:T(8,128)S(1)}, f32[8,2,1,2,16,2048]{5,4,3,1,0,2:T(8,128)S(1)}, u32[]{:S(2)}, u32[]{:S(2)}) %collective-permute-start.10) | collective-permute-done | bytes 4194336 | tf_op jit(solution)/shard_map/ppermute | solution.py:34
  189.4 4.6 %collective-permute-start.18 = (f32[2,1,2,16,1024]{4,3,2,0,1:T(8,128)}, f32[2,1,2,16,1024]{4,3,2,0,1:T(8,128)}, u32[]{:S(2)}, u32[]{:S(2)}) collective-permute-start(f32[2,1,2,16,1024]{4,3,2,0,1:T(8,128)} %dynamic-slice_bitcast_fusion), channel_id=1, source_target_pairs={{0,448},{64,0},{128,64},{192,128},{256,192},{320,256},{384,320},{4... | collective-permute-start | bytes 786440 | tf_op jit(solution)/shard_map/ppermute | solution.py:29
  194.9 2.8 collective-permute-done.11
  203.1 4.6 %collective-permute-start.19 = (f32[2,1,2,16,1024]{4,3,2,0,1:T(8,128)}, f32[2,1,2,16,1024]{4,3,2,0,1:T(8,128)}, u32[]{:S(2)}, u32[]{:S(2)}) collective-permute-start(f32[2,1,2,16,1024]{4,3,2,0,1:T(8,128)} %bitcast_add_fusion.7), channel_id=1, source_target_pairs={{0,448},{64,0},{128,64},{192,128},{256,192},{320,256},{384,320},{4... | collective-permute-start | bytes 786440 | tf_op jit(solution)/shard_map/ppermute | solution.py:29
  207.6 3.0 convolution_multiply_fusion
  214.4 1.9 collective-permute-start.13
  218.1 4.6 %collective-permute-start.20 = (f32[2,1,2,16,1024]{4,3,2,0,1:T(8,128)}, f32[2,1,2,16,1024]{4,3,2,0,1:T(8,128)}, u32[]{:S(2)}, u32[]{:S(2)}) collective-permute-start(f32[2,1,2,16,1024]{4,3,2,0,1:T(8,128)} %bitcast_add_fusion.6), channel_id=1, source_target_pairs={{0,448},{64,0},{128,64},{192,128},{256,192},{320,256},{384,320},{4... | collective-permute-start | bytes 786440 | tf_op jit(solution)/shard_map/ppermute | solution.py:29
  224.6 1.9 collective-permute-start.14
  227.5 5.3 %collective-permute-start.21 = (f32[2,1,2,16,1024]{4,3,2,0,1:T(8,128)S(1)}, f32[2,1,2,16,1024]{4,3,2,0,1:T(8,128)S(1)}, u32[]{:S(2)}, u32[]{:S(2)}) collective-permute-start(f32[2,1,2,16,1024]{4,3,2,0,1:T(8,128)S(1)} %bitcast_add_fusion.5), channel_id=1, source_target_pairs={{0,448},{64,0},{128,64},{192,128},{256,192},{320,256},{384,320},{4... | collective-permute-start | bytes 786440 | tf_op jit(solution)/shard_map/ppermute | solution.py:29
  232.8 5.2 %collective-permute-start.26 = (f32[160,16,16]{0,2,1:T(8,128)S(1)}, f32[160,16,16]{0,2,1:T(8,128)S(1)}, u32[]{:S(2)}, u32[]{:S(2)}) collective-permute-start(f32[160,16,16]{0,2,1:T(8,128)S(1)} %pad_maximum_fusion.2), channel_id=1, source_target_pairs={{0,16},{16,0},{1,17},{17,1},{2,18},{18,2},{3,19},{19,3},{4,20},{20... | collective-permute-start | bytes 491528 | tf_op jit(solution)/shard_map/ppermute | solution.py:34
  239.0 1.9 collective-permute-start.15
  241.0 4.6 %collective-permute-start.22 = (f32[2,1,2,16,1024]{4,3,2,0,1:T(8,128)S(1)}, f32[2,1,2,16,1024]{4,3,2,0,1:T(8,128)S(1)}, u32[]{:S(2)}, u32[]{:S(2)}) collective-permute-start(f32[2,1,2,16,1024]{4,3,2,0,1:T(8,128)S(1)} %bitcast_add_fusion.4), channel_id=1, source_target_pairs={{0,448},{64,0},{128,64},{192,128},{256,192},{320,256},{384,320},{4... | collective-permute-start | bytes 786440 | tf_op jit(solution)/shard_map/ppermute | solution.py:29
  245.6 1.9 collective-permute-start.27
  247.5 2.5 collective-permute-done.15
  251.0 1.9 collective-permute-start.16
  253.7 4.6 %collective-permute-start.23 = (f32[2,1,2,16,1024]{4,3,2,0,1:T(8,128)}, f32[2,1,2,16,1024]{4,3,2,0,1:T(8,128)}, u32[]{:S(2)}, u32[]{:S(2)}) collective-permute-start(f32[2,1,2,16,1024]{4,3,2,0,1:T(8,128)} %bitcast_add_fusion.3), channel_id=1, source_target_pairs={{0,448},{64,0},{128,64},{192,128},{256,192},{320,256},{384,320},{4... | collective-permute-start | bytes 786440 | tf_op jit(solution)/shard_map/ppermute | solution.py:29
  258.4 1.9 collective-permute-start.28
  262.8 2.7 collective-permute-start.17
  267.3 3.9 %collective-permute-start.24 = (f32[2,1,2,16,1024]{4,3,2,0,1:T(8,128)}, f32[2,1,2,16,1024]{4,3,2,0,1:T(8,128)}, u32[]{:S(2)}, u32[]{:S(2)}) collective-permute-start(f32[2,1,2,16,1024]{4,3,2,0,1:T(8,128)} %bitcast_add_fusion.2), channel_id=1, source_target_pairs={{0,448},{64,0},{128,64},{192,128},{256,192},{320,256},{384,320},{4... | collective-permute-start | bytes 786440 | tf_op jit(solution)/shard_map/ppermute | solution.py:29
  277.7 2.1 collective-permute-start.25
  279.8 2.3 fusion.15
  283.0 6.0 %collective-permute-done.29 = f32[160,16,16]{0,2,1:T(8,128)} collective-permute-done((f32[160,16,16]{0,2,1:T(8,128)}, f32[160,16,16]{0,2,1:T(8,128)}, u32[]{:S(2)}, u32[]{:S(2)}) %collective-permute-start.29) | collective-permute-done | bytes 163872 | tf_op jit(solution)/shard_map/ppermute | solution.py:34
  290.0 2.8 collective-permute-start.30
  294.0 13.5 %collective-permute-done.30 = f32[160,16,16]{0,2,1:T(8,128)S(1)} collective-permute-done((f32[160,16,16]{0,2,1:T(8,128)S(1)}, f32[160,16,16]{0,2,1:T(8,128)S(1)}, u32[]{:S(2)}, u32[]{:S(2)}) %collective-permute-start.30) | collective-permute-done | bytes 163872 | tf_op jit(solution)/shard_map/ppermute | solution.py:34
  (156 shorter events, 69.4 us)
Async XLA Ops:
  0.6 69.7 %copy-start = (bf16[256,512]{1,0:T(8,128)(2,1)S(1)}, bf16[256,512]{1,0:T(8,128)(2,1)}, u32[]{:S(2)}) copy-start(bf16[256,512]{1,0:T(8,128)(2,1)} %param.6) | copy-start | bytes 786436
  2.5 6.4 %collective-permute-start = (bf16[16,4096]{1,0:T(8,128)(2,1)S(1)}, bf16[16,4096]{1,0:T(8,128)(2,1)S(1)}, u32[]{:S(2)}, u32[]{:S(2)}) collective-permute-start(bf16[16,4096]{1,0:T(8,128)(2,1)S(1)} %get-tuple-element.46), channel_id=1, source_target_pairs={{0,32},{32,0},{1,33},{33,1},{2,34},{34,2},{3,35},{35,3},{4,36},{36... | collective-permute-start | bytes 393224 | tf_op jit(solution)/shard_map/ppermute | solution.py:34
  8.9 15.6 %collective-permute-start.2 = (bf16[2,16,4096]{2,1,0:T(8,128)(2,1)S(1)}, bf16[2,16,4096]{2,1,0:T(8,128)(2,1)S(1)}, u32[]{:S(2)}, u32[]{:S(2)}) collective-permute-start(bf16[2,16,4096]{2,1,0:T(8,128)(2,1)S(1)} %maximum_select_fusion.2), channel_id=1, source_target_pairs={{0,448},{64,0},{128,64},{192,128},{256,192},{320,256},{384,320},{4... | collective-permute-start | bytes 786440 | tf_op jit(solution)/shard_map/ppermute | solution.py:29
  20.2 9.3 %collective-permute-start.1 = (bf16[2,16,4096]{2,1,0:T(8,128)(2,1)S(1)}, bf16[2,16,4096]{2,1,0:T(8,128)(2,1)S(1)}, u32[]{:S(2)}, u32[]{:S(2)}) collective-permute-start(bf16[2,16,4096]{2,1,0:T(8,128)(2,1)S(1)} %maximum_select_fusion.2), channel_id=1, source_target_pairs={{0,64},{64,128},{128,192},{192,256},{256,320},{320,384},{384,448},... | collective-permute-start | bytes 786440 | tf_op jit(solution)/shard_map/ppermute | solution.py:29
  24.5 37.5 %copy-start.26 = (bf16[32,16,16]{0,2,1:T(8,128)(2,1)S(1)}, bf16[32,16,16]{0,2,1:T(8,128)(2,1)}, u32[]{:S(2)}) copy-start(bf16[32,16,16]{0,2,1:T(8,128)(2,1)} %param.10) | copy-start | bytes 49156
  24.5 8.5 %collective-permute-start.4 = (bf16[2,16,4096]{2,1,0:T(8,128)(2,1)S(1)}, bf16[2,16,4096]{2,1,0:T(8,128)(2,1)S(1)}, u32[]{:S(2)}, u32[]{:S(2)}) collective-permute-start(bf16[2,16,4096]{2,1,0:T(8,128)(2,1)S(1)} %collective-permute-done.2), channel_id=1, source_target_pairs={{0,448},{64,0},{128,64},{192,128},{256,192},{320,256},{384,320},{4... | collective-permute-start | bytes 786440 | tf_op jit(solution)/shard_map/ppermute | solution.py:29
  29.6 8.3 %collective-permute-start.3 = (bf16[2,16,4096]{2,1,0:T(8,128)(2,1)S(1)}, bf16[2,16,4096]{2,1,0:T(8,128)(2,1)S(1)}, u32[]{:S(2)}, u32[]{:S(2)}) collective-permute-start(bf16[2,16,4096]{2,1,0:T(8,128)(2,1)S(1)} %collective-permute-done.1), channel_id=1, source_target_pairs={{0,64},{64,128},{128,192},{192,256},{256,320},{320,384},{384,448},... | collective-permute-start | bytes 786440 | tf_op jit(solution)/shard_map/ppermute | solution.py:29
  33.0 8.3 %collective-permute-start.6 = (bf16[2,16,4096]{2,1,0:T(8,128)(2,1)S(1)}, bf16[2,16,4096]{2,1,0:T(8,128)(2,1)S(1)}, u32[]{:S(2)}, u32[]{:S(2)}) collective-permute-start(bf16[2,16,4096]{2,1,0:T(8,128)(2,1)S(1)} %collective-permute-done.4), channel_id=1, source_target_pairs={{0,448},{64,0},{128,64},{192,128},{256,192},{320,256},{384,320},{4... | collective-permute-start | bytes 786440 | tf_op jit(solution)/shard_map/ppermute | solution.py:29
  37.9 8.3 %collective-permute-start.5 = (bf16[2,16,4096]{2,1,0:T(8,128)(2,1)S(1)}, bf16[2,16,4096]{2,1,0:T(8,128)(2,1)S(1)}, u32[]{:S(2)}, u32[]{:S(2)}) collective-permute-start(bf16[2,16,4096]{2,1,0:T(8,128)(2,1)S(1)} %collective-permute-done.3), channel_id=1, source_target_pairs={{0,64},{64,128},{128,192},{192,256},{256,320},{320,384},{384,448},... | collective-permute-start | bytes 786440 | tf_op jit(solution)/shard_map/ppermute | solution.py:29
  41.3 8.4 %collective-permute-start.8 = (bf16[2,16,2048]{2,1,0:T(8,128)(2,1)S(1)}, bf16[2,16,2048]{2,1,0:T(8,128)(2,1)S(1)}, u32[]{:S(2)}, u32[]{:S(2)}) collective-permute-start(bf16[2,16,2048]{2,1,0:T(8,128)(2,1)S(1)} %split.17), channel_id=1, source_target_pairs={{0,448},{64,0},{128,64},{192,128},{256,192},{320,256},{384,320},{4... | collective-permute-start | bytes 393224 | tf_op jit(solution)/shard_map/ppermute | solution.py:29
  46.3 6.9 %collective-permute-start.7 = (bf16[2,16,2048]{2,1,0:T(8,128)(2,1)S(1)}, bf16[2,16,2048]{2,1,0:T(8,128)(2,1)S(1)}, u32[]{:S(2)}, u32[]{:S(2)}) collective-permute-start(bf16[2,16,2048]{2,1,0:T(8,128)(2,1)S(1)} %split.16), channel_id=1, source_target_pairs={{0,64},{64,128},{128,192},{192,256},{256,320},{320,384},{384,448},... | collective-permute-start | bytes 393224 | tf_op jit(solution)/shard_map/ppermute | solution.py:29
  53.9 12.2 %collective-permute-start.9 = (bf16[8,2,16,4096]{3,2,1,0:T(8,128)(2,1)}, bf16[8,2,16,4096]{3,2,1,0:T(8,128)(2,1)}, u32[]{:S(2)}, u32[]{:S(2)}) collective-permute-start(bf16[8,2,16,4096]{3,2,1,0:T(8,128)(2,1)} %fusion.27), channel_id=1, source_target_pairs={{0,16},{16,0},{1,17},{17,1},{2,18},{18,2},{3,19},{19,3},{4,20},{20... | collective-permute-start | bytes 6291464 | tf_op jit(solution)/shard_map/ppermute | solution.py:34
  72.3 10.7 %copy-start.27 = (bf16[128,16,16]{0,2,1:T(8,128)(2,1)S(1)}, bf16[128,16,16]{0,2,1:T(8,128)(2,1)}, u32[]{:S(2)}) copy-start(bf16[128,16,16]{0,2,1:T(8,128)(2,1)} %param.8) | copy-start | bytes 196612
  73.5 43.6 %all-to-all-start = ((bf16[256,16,160]{0,2,1:T(8,128)(2,1)}), bf16[256,16,160]{0,2,1:T(8,128)(2,1)}, u32[]{:S(2)}, u32[]{:S(2)}) async-start(bf16[256,16,160]{0,2,1:T(8,128)(2,1)} %pad_maximum_fusion), calls=%async_computation | async-start | bytes 2621440 | tf_op jit(solution)/shard_map/all_to_all | solution.py:24
  83.4 36.8 %copy-start.19 = (bf16[128,16,16]{2,1,0:T(8,128)(2,1)}, bf16[128,16,16]{2,1,0:T(8,128)(2,1)S(1)}, u32[]{:S(2)}) copy-start(bf16[128,16,16]{2,1,0:T(8,128)(2,1)S(1)} %copy.96) | copy-start | bytes 196612
  124.3 7.3 %copy-start.18 = (bf16[256,16,32]{0,2,1:T(8,128)(2,1)S(1)}, bf16[256,16,32]{0,2,1:T(8,128)(2,1)}, u32[]{:S(2)}) copy-start(bf16[256,16,32]{0,2,1:T(8,128)(2,1)} %copy-done.17) | copy-start | bytes 786436
  125.8 41.7 %all-to-all-start.1 = ((bf16[256,16,160]{0,2,1:T(8,128)(2,1)}), bf16[256,16,160]{0,2,1:T(8,128)(2,1)S(1)}, u32[]{:S(2)}, u32[]{:S(2)}) async-start(bf16[256,16,160]{0,2,1:T(8,128)(2,1)} %copy.98), calls=%async_computation.1 | async-start | bytes 2621440 | tf_op jit(solution)/shard_map/all_to_all | solution.py:24
  173.9 9.6 %collective-permute-start.10 = (f32[8,2,1,2,16,2048]{5,4,3,1,0,2:T(8,128)S(1)}, f32[8,2,1,2,16,2048]{5,4,3,1,0,2:T(8,128)S(1)}, u32[]{:S(2)}, u32[]{:S(2)}) collective-permute-start(f32[8,2,1,2,16,2048]{5,4,3,1,0,2:T(8,128)S(1)} %bitcast.170), channel_id=1, source_target_pairs={{0,16},{16,0},{1,17},{17,1},{2,18},{18,2},{3,19},{19,3},{4,20},{20... | collective-permute-start | bytes 12582920 | tf_op jit(solution)/shard_map/ppermute | solution.py:34
  184.3 9.7 %copy-start.22 = (bf16[256,512]{1,0:T(8,128)(2,1)S(1)}, bf16[256,512]{1,0:T(8,128)(2,1)}, u32[]{:S(2)}) copy-start(bf16[256,512]{1,0:T(8,128)(2,1)} %param.11) | copy-start | bytes 786436
  184.7 23.0 %copy-start.9 = (bf16[256,16,128]{0,2,1:T(8,128)(2,1)S(1)}, bf16[256,16,128]{0,2,1:T(8,128)(2,1)}, u32[]{:S(2)}) copy-start(bf16[256,16,128]{0,2,1:T(8,128)(2,1)} %copy-done.8) | copy-start | bytes 3145732
  186.7 10.9 %collective-permute-start.11 = (f32[2,1,2,16,1024]{4,3,2,0,1:T(8,128)}, f32[2,1,2,16,1024]{4,3,2,0,1:T(8,128)}, u32[]{:S(2)}, u32[]{:S(2)}) collective-permute-start(f32[2,1,2,16,1024]{4,3,2,0,1:T(8,128)} %dynamic-slice_bitcast_fusion.1), channel_id=1, source_target_pairs={{0,64},{64,128},{128,192},{192,256},{256,320},{320,384},{384,448},... | collective-permute-start | bytes 786440 | tf_op jit(solution)/shard_map/ppermute | solution.py:29
  189.4 12.0 %collective-permute-start.18 = (f32[2,1,2,16,1024]{4,3,2,0,1:T(8,128)}, f32[2,1,2,16,1024]{4,3,2,0,1:T(8,128)}, u32[]{:S(2)}, u32[]{:S(2)}) collective-permute-start(f32[2,1,2,16,1024]{4,3,2,0,1:T(8,128)} %dynamic-slice_bitcast_fusion), channel_id=1, source_target_pairs={{0,448},{64,0},{128,64},{192,128},{256,192},{320,256},{384,320},{4... | collective-permute-start | bytes 786440 | tf_op jit(solution)/shard_map/ppermute | solution.py:29
  199.4 13.8 %collective-permute-start.12 = (f32[2,1,2,16,1024]{4,3,2,0,1:T(8,128)}, f32[2,1,2,16,1024]{4,3,2,0,1:T(8,128)}, u32[]{:S(2)}, u32[]{:S(2)}) collective-permute-start(f32[2,1,2,16,1024]{4,3,2,0,1:T(8,128)} %bitcast_add_fusion.14), channel_id=1, source_target_pairs={{0,64},{64,128},{128,192},{192,256},{256,320},{320,384},{384,448},... | collective-permute-start | bytes 786440 | tf_op jit(solution)/shard_map/ppermute | solution.py:29
  203.1 13.3 %collective-permute-start.19 = (f32[2,1,2,16,1024]{4,3,2,0,1:T(8,128)}, f32[2,1,2,16,1024]{4,3,2,0,1:T(8,128)}, u32[]{:S(2)}, u32[]{:S(2)}) collective-permute-start(f32[2,1,2,16,1024]{4,3,2,0,1:T(8,128)} %bitcast_add_fusion.7), channel_id=1, source_target_pairs={{0,448},{64,0},{128,64},{192,128},{256,192},{320,256},{384,320},{4... | collective-permute-start | bytes 786440 | tf_op jit(solution)/shard_map/ppermute | solution.py:29
  210.6 12.0 %copy-start.25 = (bf16[256,512]{0,1:T(8,128)(2,1)S(1)}, bf16[256,512]{0,1:T(8,128)(2,1)}, u32[]{:S(2)}) copy-start(bf16[256,512]{0,1:T(8,128)(2,1)} %copy.104) | copy-start | bytes 786436
  213.2 9.4 %copy-start.23 = (bf16[256,16,32]{0,2,1:T(8,128)(2,1)}, bf16[256,16,32]{0,2,1:T(8,128)(2,1)S(1)}, u32[]{:S(2)}) copy-start(bf16[256,16,32]{0,2,1:T(8,128)(2,1)S(1)} %slice.49) | copy-start | bytes 786436
  214.4 9.1 %collective-permute-start.13 = (f32[2,1,2,16,1024]{4,3,2,0,1:T(8,128)S(1)}, f32[2,1,2,16,1024]{4,3,2,0,1:T(8,128)S(1)}, u32[]{:S(2)}, u32[]{:S(2)}) collective-permute-start(f32[2,1,2,16,1024]{4,3,2,0,1:T(8,128)S(1)} %bitcast_add_fusion.13), channel_id=1, source_target_pairs={{0,64},{64,128},{128,192},{192,256},{256,320},{320,384},{384,448},... | collective-permute-start | bytes 786440 | tf_op jit(solution)/shard_map/ppermute | solution.py:29
  218.1 8.4 %collective-permute-start.20 = (f32[2,1,2,16,1024]{4,3,2,0,1:T(8,128)}, f32[2,1,2,16,1024]{4,3,2,0,1:T(8,128)}, u32[]{:S(2)}, u32[]{:S(2)}) collective-permute-start(f32[2,1,2,16,1024]{4,3,2,0,1:T(8,128)} %bitcast_add_fusion.6), channel_id=1, source_target_pairs={{0,448},{64,0},{128,64},{192,128},{256,192},{320,256},{384,320},{4... | collective-permute-start | bytes 786440 | tf_op jit(solution)/shard_map/ppermute | solution.py:29
  224.6 13.4 %collective-permute-start.14 = (f32[2,1,2,16,1024]{4,3,2,0,1:T(8,128)S(1)}, f32[2,1,2,16,1024]{4,3,2,0,1:T(8,128)S(1)}, u32[]{:S(2)}, u32[]{:S(2)}) collective-permute-start(f32[2,1,2,16,1024]{4,3,2,0,1:T(8,128)S(1)} %bitcast_add_fusion.12), channel_id=1, source_target_pairs={{0,64},{64,128},{128,192},{192,256},{256,320},{320,384},{384,448},... | collective-permute-start | bytes 786440 | tf_op jit(solution)/shard_map/ppermute | solution.py:29
  227.5 13.4 %collective-permute-start.21 = (f32[2,1,2,16,1024]{4,3,2,0,1:T(8,128)S(1)}, f32[2,1,2,16,1024]{4,3,2,0,1:T(8,128)S(1)}, u32[]{:S(2)}, u32[]{:S(2)}) collective-permute-start(f32[2,1,2,16,1024]{4,3,2,0,1:T(8,128)S(1)} %bitcast_add_fusion.5), channel_id=1, source_target_pairs={{0,448},{64,0},{128,64},{192,128},{256,192},{320,256},{384,320},{4... | collective-permute-start | bytes 786440 | tf_op jit(solution)/shard_map/ppermute | solution.py:29
  232.8 12.7 %collective-permute-start.26 = (f32[160,16,16]{0,2,1:T(8,128)S(1)}, f32[160,16,16]{0,2,1:T(8,128)S(1)}, u32[]{:S(2)}, u32[]{:S(2)}) collective-permute-start(f32[160,16,16]{0,2,1:T(8,128)S(1)} %pad_maximum_fusion.2), channel_id=1, source_target_pairs={{0,16},{16,0},{1,17},{17,1},{2,18},{18,2},{3,19},{19,3},{4,20},{20... | collective-permute-start | bytes 491528 | tf_op jit(solution)/shard_map/ppermute | solution.py:34
  239.0 11.0 %collective-permute-start.15 = (f32[2,1,2,16,1024]{4,3,2,0,1:T(8,128)S(1)}, f32[2,1,2,16,1024]{4,3,2,0,1:T(8,128)S(1)}, u32[]{:S(2)}, u32[]{:S(2)}) collective-permute-start(f32[2,1,2,16,1024]{4,3,2,0,1:T(8,128)S(1)} %bitcast_add_fusion.11), channel_id=1, source_target_pairs={{0,64},{64,128},{128,192},{192,256},{256,320},{320,384},{384,448},... | collective-permute-start | bytes 786440 | tf_op jit(solution)/shard_map/ppermute | solution.py:29
  241.0 12.0 %collective-permute-start.22 = (f32[2,1,2,16,1024]{4,3,2,0,1:T(8,128)S(1)}, f32[2,1,2,16,1024]{4,3,2,0,1:T(8,128)S(1)}, u32[]{:S(2)}, u32[]{:S(2)}) collective-permute-start(f32[2,1,2,16,1024]{4,3,2,0,1:T(8,128)S(1)} %bitcast_add_fusion.4), channel_id=1, source_target_pairs={{0,448},{64,0},{128,64},{192,128},{256,192},{320,256},{384,320},{4... | collective-permute-start | bytes 786440 | tf_op jit(solution)/shard_map/ppermute | solution.py:29
  245.6 12.7 %collective-permute-start.27 = (f32[160,16,16]{0,2,1:T(8,128)S(1)}, f32[160,16,16]{0,2,1:T(8,128)S(1)}, u32[]{:S(2)}, u32[]{:S(2)}) collective-permute-start(f32[160,16,16]{0,2,1:T(8,128)S(1)} %fusion.31), channel_id=1, source_target_pairs={{0,32},{32,0},{1,33},{33,1},{2,34},{34,2},{3,35},{35,3},{4,36},{36... | collective-permute-start | bytes 491528 | tf_op jit(solution)/shard_map/ppermute | solution.py:34
  251.0 10.1 %collective-permute-start.16 = (f32[2,1,2,16,1024]{4,3,2,0,1:T(8,128)S(1)}, f32[2,1,2,16,1024]{4,3,2,0,1:T(8,128)S(1)}, u32[]{:S(2)}, u32[]{:S(2)}) collective-permute-start(f32[2,1,2,16,1024]{4,3,2,0,1:T(8,128)S(1)} %bitcast_add_fusion.10), channel_id=1, source_target_pairs={{0,64},{64,128},{128,192},{192,256},{256,320},{320,384},{384,448},... | collective-permute-start | bytes 786440 | tf_op jit(solution)/shard_map/ppermute | solution.py:29
  253.7 11.8 %collective-permute-start.23 = (f32[2,1,2,16,1024]{4,3,2,0,1:T(8,128)}, f32[2,1,2,16,1024]{4,3,2,0,1:T(8,128)}, u32[]{:S(2)}, u32[]{:S(2)}) collective-permute-start(f32[2,1,2,16,1024]{4,3,2,0,1:T(8,128)} %bitcast_add_fusion.3), channel_id=1, source_target_pairs={{0,448},{64,0},{128,64},{192,128},{256,192},{320,256},{384,320},{4... | collective-permute-start | bytes 786440 | tf_op jit(solution)/shard_map/ppermute | solution.py:29
  258.4 12.8 %collective-permute-start.28 = (f32[160,16,16]{0,2,1:T(8,128)S(1)}, f32[160,16,16]{0,2,1:T(8,128)}, u32[]{:S(2)}, u32[]{:S(2)}) collective-permute-start(f32[160,16,16]{0,2,1:T(8,128)S(1)} %add.282), channel_id=1, source_target_pairs={{0,64},{64,0},{128,192},{192,128},{256,320},{320,256},{384,448},{4... | collective-permute-start | bytes 491528 | tf_op jit(solution)/shard_map/ppermute | solution.py:34
  262.8 17.0 %copy-start.12 = (bf16[256,16,128]{0,2,1:T(8,128)(2,1)S(1)}, bf16[256,16,128]{0,2,1:T(8,128)(2,1)}, u32[]{:S(2)}) copy-start(bf16[256,16,128]{0,2,1:T(8,128)(2,1)} %copy-done.11) | copy-start | bytes 3145732
  262.8 12.0 %collective-permute-start.17 = (f32[2,1,2,16,1024]{4,3,2,0,1:T(8,128)}, f32[2,1,2,16,1024]{4,3,2,0,1:T(8,128)}, u32[]{:S(2)}, u32[]{:S(2)}) collective-permute-start(f32[2,1,2,16,1024]{4,3,2,0,1:T(8,128)} %bitcast_add_fusion.9), channel_id=1, source_target_pairs={{0,64},{64,128},{128,192},{192,256},{256,320},{320,384},{384,448},... | collective-permute-start | bytes 786440 | tf_op jit(solution)/shard_map/ppermute | solution.py:29
  267.3 8.6 %collective-permute-start.24 = (f32[2,1,2,16,1024]{4,3,2,0,1:T(8,128)}, f32[2,1,2,16,1024]{4,3,2,0,1:T(8,128)}, u32[]{:S(2)}, u32[]{:S(2)}) collective-permute-start(f32[2,1,2,16,1024]{4,3,2,0,1:T(8,128)} %bitcast_add_fusion.2), channel_id=1, source_target_pairs={{0,448},{64,0},{128,64},{192,128},{256,192},{320,256},{384,320},{4... | collective-permute-start | bytes 786440 | tf_op jit(solution)/shard_map/ppermute | solution.py:29
  272.9 16.1 %collective-permute-start.29 = (f32[160,16,16]{0,2,1:T(8,128)}, f32[160,16,16]{0,2,1:T(8,128)}, u32[]{:S(2)}, u32[]{:S(2)}) collective-permute-start(f32[160,16,16]{0,2,1:T(8,128)} %add.283), channel_id=1, source_target_pairs={{0,128},{64,192},{128,0},{192,64},{256,384},{320,448},{384,256},{4... | collective-permute-start | bytes 491528 | tf_op jit(solution)/shard_map/ppermute | solution.py:34
  277.7 15.2 %copy-start.7 = (bf16[512,512]{1,0:T(8,128)(2,1)S(1)}, bf16[512,512]{1,0:T(8,128)(2,1)}, u32[]{:S(2)}) copy-start(bf16[512,512]{1,0:T(8,128)(2,1)} %copy-done.6) | copy-start | bytes 1572868
  277.7 15.2 %copy-start.24 = (bf16[256,16,32]{0,2,1:T(8,128)(2,1)S(1)}, bf16[256,16,32]{0,2,1:T(8,128)(2,1)}, u32[]{:S(2)}) copy-start(bf16[256,16,32]{0,2,1:T(8,128)(2,1)} %copy-done.23) | copy-start | bytes 786436
  277.7 31.0 %collective-permute-start.25 = (f32[1,2,16,2048]{3,2,1,0:T(8,128)S(1)}, f32[1,2,16,2048]{3,2,1,0:T(8,128)S(1)}, u32[]{:S(2)}, u32[]{:S(2)}) collective-permute-start(f32[1,2,16,2048]{3,2,1,0:T(8,128)S(1)} %fusion.22), channel_id=1, source_target_pairs={{0,32},{32,0},{1,33},{33,1},{2,34},{34,2},{3,35},{35,3},{4,36},{36... | collective-permute-start | bytes 786440 | tf_op jit(solution)/shard_map/ppermute | solution.py:34
  282.1 26.7 %copy-start.16 = (f32[2,1,2,16,1024]{4,3,2,0,1:T(8,128)S(1)}, f32[2,1,2,16,1024]{4,3,2,0,1:T(8,128)}, u32[]{:S(2)}) copy-start(f32[2,1,2,16,1024]{4,3,2,0,1:T(8,128)} %copy-done.15) | copy-start | bytes 786436
  283.0 25.8 %copy-start.14 = (f32[2,1,2,16,1024]{4,3,2,0,1:T(8,128)S(1)}, f32[2,1,2,16,1024]{4,3,2,0,1:T(8,128)}, u32[]{:S(2)}) copy-start(f32[2,1,2,16,1024]{4,3,2,0,1:T(8,128)} %copy-done.13) | copy-start | bytes 786436
  290.0 17.4 %collective-permute-start.30 = (f32[160,16,16]{0,2,1:T(8,128)S(1)}, f32[160,16,16]{0,2,1:T(8,128)S(1)}, u32[]{:S(2)}, u32[]{:S(2)}) collective-permute-start(f32[160,16,16]{0,2,1:T(8,128)S(1)} %add.284), channel_id=1, source_target_pairs={{0,256},{64,320},{128,384},{192,448},{256,0},{320,64},{384,128},{4... | collective-permute-start | bytes 491528 | tf_op jit(solution)/shard_map/ppermute | solution.py:34
  292.9 17.3 %copy-start.1 = (bf16[256,512]{1,0:T(8,128)(2,1)S(1)}, bf16[256,512]{1,0:T(8,128)(2,1)}, u32[]{:S(2)}) copy-start(bf16[256,512]{1,0:T(8,128)(2,1)} %param.6) | copy-start | bytes 786436
  (13 other events, 29.0 us)

commit v6 on v5

--- a/solution.py
+++ b/solution.py
@@ -86,6 +86,19 @@
     return mine + swap(other, "ylo", 1)
 
 
+def sc_reduce_scatter(part):
+    rows = part.shape[0]
+    rest = part.shape[1:]
+    n_zy = lax.axis_size("z") * lax.axis_size("ylo")
+    x = part.reshape((n_zy, 2, rows // (2 * n_zy)) + rest)
+    core = lax.axis_index("core")
+    mine = lax.dynamic_index_in_dim(x, core, 1, keepdims=False)
+    other = lax.dynamic_index_in_dim(x, 1 - core, 1, keepdims=False)
+    x = mine + swap(other, "core", 1)
+    x = lax.psum_scatter(x, ("z", "ylo"), scatter_dimension=0, tiled=True)
+    return x.reshape((rows // (2 * n_zy),) + rest)
+
+
 def dp_all_gather(local):
     ylo = lax.axis_index("ylo")
     got = swap(local, "ylo", 1)
@@ -134,14 +147,8 @@
     grad_scale = float(tok_rows * n_dp) ** (-0.5)
     tiles_up = group_up // TILE_UP
     tiles_down = group_down // TILE_DOWN
-    hidden_rows = down_left.shape[1]
-    up_rows = up_left.shape[1]
-    weights = jnp.concatenate(
-        [up_left[0], down_left[0].reshape(up_rows, hidden_rows * block_width // up_rows)], axis=1
-    )
-    weights = dp_all_gather(weights)
-    up_full = weights[:, :hidden_width][None]
-    down_full = weights[:, hidden_width:].reshape(1, -1, block_width)
+    down_full = lax.all_gather(down_left, DP_AXES, axis=1, tiled=True)
+    up_full = dp_all_gather(up_left[0])[None]
     token_blocks = tokens.reshape(tok_rows, local_blocks, block_width)
     identity = jnp.eye(group_down, dtype=jnp.bfloat16).reshape(group_down, tiles_down, TILE_DOWN)
     mix_matrix = jnp.einsum(
@@ -197,6 +204,7 @@
     down_part = jnp.einsum(
         "tbh,tbc->hbc", hidden, grad_down_inner, preferred_element_type=jnp.float32
     )
+    grad_down_left = sc_reduce_scatter(down_part * grad_scale).transpose(1, 0, 2)
     down_piece = block_width // feat_count
     second = exchange(
         jnp.concatenate([to_wire(down_inner, feat_count), grad_up_mixed], axis=2)
@@ -226,17 +234,7 @@
     up_part = jnp.einsum(
         "tbi,tbg->ibg", token_blocks, grad_up_inner, preferred_element_type=jnp.float32
     )
-    n_rows = up_part.shape[0] // up_rows
-    parts = jnp.stack(
-        [
-            up_part.reshape(n_rows, up_rows, hidden_width),
-            down_part.reshape(n_rows, up_rows, hidden_width),
-        ],
-        axis=1,
-    )
-    summed = dp_reduce_scatter(parts * grad_scale)[0]
-    grad_up_left = summed[0][None]
-    grad_down_left = summed[1].reshape(1, hidden_rows, block_width)
+    grad_up_left = dp_reduce_scatter(up_part * grad_scale).transpose(1, 0, 2)
     rights = jnp.concatenate([right_up_term, right_down_term], axis=0)
     rights = dp_all_reduce(rights)
     grad_up_right = rights[:group_up]

time: 312 us -> 338 us (1.083); the launches traced: 310 us -> 331 us
  starting transfers between devices: 126 us -> 151 us
  local copies, waits for them, and re-layouts: 47.6 us -> 32.9 us
  other arithmetic: 31.4 us -> 17.3 us
  between operations: 1.87 us -> 15.1 us
  waiting for transfers between devices: 87.9 us -> 96.1 us
  matrix products: 15.3 us -> 19.2 us
    ppermute x9 -> x10, waiting for transfers between devices: 28.6 us -> 13.7 us  [swap(): return lax.ppermute(value, axis, [(i, i ^ mask) for i in range(n)])]
    ppermute x9 -> x10, starting transfers between devices: 30.8 us -> 43.1 us  [swap(): return lax.ppermute(value, axis, [(i, i ^ mask) for i in range(n)])]
    another operation x5 -> x1, local copies, waits for them, and re-layouts: 10.5 us -> 0.11 us  [the longest x1 5.69 us: on_device(): jnp.stack([up_part.reshape(n_rows, up_rows, hidden_width), down_part.resh...]
    all_gather x0 -> x1, waiting for transfers between devices: none -> 10.3 us  [on_device(): down_full = lax.all_gather(down_left, DP_AXES, axis=1, tiled=True)]
    ppermute x22, starting transfers between devices: 80.2 us -> 89.5 us  [shift(): return lax.ppermute(value, axis, [(i, (i + step) % n) for i in range(n)])]
    add x6, other arithmetic: 7.56 us -> 0.11 us  [z_ring_reduce_scatter(): fwd = shift(own_f if fwd is None else fwd + own_f, 'z', 1)]
    add x6, other arithmetic: 6.95 us -> 0.13 us  [z_ring_reduce_scatter(): bwd = shift(own_b if bwd is None else bwd + own_b, 'z', -1)]
    ppermute x22, waiting for transfers between devices: 10 us -> 16.6 us  [shift(): return lax.ppermute(value, axis, [(i, (i + step) % n) for i in range(n)])]
  transfers between devices with their start and end apart: 33 -> 36, of which waited for: 12 -> 16; matrix products, arithmetic and copies ran while one was open for 21% -> 16% of each run, Pallas kernels for 0% -> 0%
where the time goes in v6:
time: 338 us; the launch traced here: 331 us
  starting transfers between devices  151 us (45%)
  waiting for transfers between devices  96.1 us (28%)
  local copies, waits for them, and re-layouts  32.9 us (10%)
  matrix products  19.2 us (6%)
  other arithmetic  17.3 us (5%)
  between operations  15.1 us (4%)
    ppermute x22, starting transfers between devices, shift(): return lax.ppermute(value, axis, [(i, (i + step) % n) for i in range(n)])  89.5 us
    all_to_all x2, waiting for transfers between devices, exchange(): return lax.all_to_all(wired, FEAT_AXES, 1, 1, tiled=True)  55.4 us
    ppermute x10, starting transfers between devices, swap(): return lax.ppermute(value, axis, [(i, i ^ mask) for i in range(n)])  43.1 us
    all_to_all x2, starting transfers between devices, exchange(): return lax.all_to_all(wired, FEAT_AXES, 1, 1, tiled=True)  18.1 us
    ppermute x22, waiting for transfers between devices, shift(): return lax.ppermute(value, axis, [(i, (i + step) % n) for i in range(n)])  16.6 us
    ppermute x10, waiting for transfers between devices, swap(): return lax.ppermute(value, axis, [(i, i ^ mask) for i in range(n)])  13.7 us
    all_gather x1, waiting for transfers between devices, on_device(): down_full = lax.all_gather(down_left, DP_AXES, axis=1, tiled=True)  10.3 us
    unnamed x31, local copies, waits for them, and re-layouts  7.79 us
  transfers between devices with their start and end apart: 36, of which 16 were waited for; matrix products, arithmetic and copies ran while one was open for 16% of the time, Pallas kernels for 0%

profile of v6, /device:TPU:1, one launch (start us, length us, event | category | flops | bytes accessed | tf_op | source)
XLA Modules:
  0.0 331.3 jit_solution(12660459710657170110)
XLA Ops:
  7.2 4.2 %collective-permute-start = (bf16[16,2048]{1,0:T(8,128)(2,1)}, bf16[16,2048]{1,0:T(8,128)(2,1)S(1)}, u32[]{:S(2)}, u32[]{:S(2)}) collective-permute-start(bf16[16,2048]{1,0:T(8,128)(2,1)} %bitcast.195), channel_id=1, source_target_pairs={{0,32},{32,0},{1,33},{33,1},{2,34},{34,2},{3,35},{35,3},{4,36},{36... | collective-permute-start | bytes 196616 | tf_op jit(solution)/shard_map/ppermute | solution.py:34
  14.2 10.8 %collective-permute-start.2 = (bf16[2,16,2048]{2,1,0:T(8,128)(2,1)S(1)}, bf16[2,16,2048]{2,1,0:T(8,128)(2,1)S(1)}, u32[]{:S(2)}, u32[]{:S(2)}) collective-permute-start(bf16[2,16,2048]{2,1,0:T(8,128)(2,1)S(1)} %maximum_select_fusion.2), channel_id=1, source_target_pairs={{0,448},{64,0},{128,64},{192,128},{256,192},{320,256},{384,320},{4... | collective-permute-start | bytes 393224 | tf_op jit(solution)/shard_map/ppermute | solution.py:29
  25.0 1.9 collective-permute-start.1
  29.7 4.6 %collective-permute-start.4 = (bf16[2,16,2048]{2,1,0:T(8,128)(2,1)S(1)}, bf16[2,16,2048]{2,1,0:T(8,128)(2,1)S(1)}, u32[]{:S(2)}, u32[]{:S(2)}) collective-permute-start(bf16[2,16,2048]{2,1,0:T(8,128)(2,1)S(1)} %collective-permute-done.2), channel_id=1, source_target_pairs={{0,448},{64,0},{128,64},{192,128},{256,192},{320,256},{384,320},{4... | collective-permute-start | bytes 393224 | tf_op jit(solution)/shard_map/ppermute | solution.py:29
  34.2 1.9 collective-permute-start.3
  37.5 4.6 %collective-permute-start.6 = (bf16[2,16,2048]{2,1,0:T(8,128)(2,1)S(1)}, bf16[2,16,2048]{2,1,0:T(8,128)(2,1)S(1)}, u32[]{:S(2)}, u32[]{:S(2)}) collective-permute-start(bf16[2,16,2048]{2,1,0:T(8,128)(2,1)S(1)} %collective-permute-done.4), channel_id=1, source_target_pairs={{0,448},{64,0},{128,64},{192,128},{256,192},{320,256},{384,320},{4... | collective-permute-start | bytes 393224 | tf_op jit(solution)/shard_map/ppermute | solution.py:29
  42.1 1.9 collective-permute-start.5
  45.3 4.6 %collective-permute-start.8 = (bf16[2,16,1024]{2,1,0:T(8,128)(2,1)S(1)}, bf16[2,16,1024]{2,1,0:T(8,128)(2,1)S(1)}, u32[]{:S(2)}, u32[]{:S(2)}) collective-permute-start(bf16[2,16,1024]{2,1,0:T(8,128)(2,1)S(1)} %split.17), channel_id=1, source_target_pairs={{0,448},{64,0},{128,64},{192,128},{256,192},{320,256},{384,320},{4... | collective-permute-start | bytes 196616 | tf_op jit(solution)/shard_map/ppermute | solution.py:29
  53.2 3.0 collective-permute-done.7
  56.8 6.8 %collective-permute-start.9 = (bf16[8,2,16,2048]{3,2,1,0:T(8,128)(2,1)}, bf16[8,2,16,2048]{3,2,1,0:T(8,128)(2,1)}, u32[]{:S(2)}, u32[]{:S(2)}) collective-permute-start(bf16[8,2,16,2048]{3,2,1,0:T(8,128)(2,1)} %fusion.32), channel_id=1, source_target_pairs={{0,16},{16,0},{1,17},{17,1},{2,18},{18,2},{3,19},{19,3},{4,20},{20... | collective-permute-start | bytes 3145736 | tf_op jit(solution)/shard_map/ppermute | solution.py:34
  65.3 2.1 reshape.157
  67.7 2.7 maximum_select_fusion
  72.8 9.4 %all-to-all-start = ((bf16[256,16,160]{0,2,1:T(8,128)(2,1)}), bf16[256,16,160]{0,2,1:T(8,128)(2,1)S(1)}, u32[]{:S(2)}, u32[]{:S(2)}) async-start(bf16[256,16,160]{0,2,1:T(8,128)(2,1)} %pad_maximum_fusion), calls=%async_computation | async-start | bytes 2621440 | tf_op jit(solution)/shard_map/all_to_all | solution.py:24
  83.4 40.1 %all-to-all-done = bf16[256,16,160]{0,2,1:T(8,128)(2,1)S(1)} async-done(((bf16[256,16,160]{0,2,1:T(8,128)(2,1)}), bf16[256,16,160]{0,2,1:T(8,128)(2,1)S(1)}, u32[]{:S(2)}, u32[]{:S(2)}) %all-to-all-start) | async-done | bytes 1310752 | tf_op jit(solution)/shard_map/all_to_all | solution.py:24
  123.6 10.3 %all-gather.2.cloned.1.call-done = bf16[1,2048,512]{2,1,0:T(8,128)(2,1)} async-done(((bf16[1,64,512]{2,1,0:T(8,128)(2,1)}), bf16[1,2048,512]{2,1,0:T(8,128)(2,1)}) %all-gather.2.cloned.1.call-update) | async-done | bytes 2097168 | tf_op jit(solution)/shard_map/all_gather | solution.py:150
  133.9 2.3 fusion.1
  136.3 2.1 fusion.8
  146.5 8.7 %all-to-all-start.1 = ((bf16[256,16,160]{0,2,1:T(8,128)(2,1)}), bf16[256,16,160]{0,2,1:T(8,128)(2,1)S(1)}, u32[]{:S(2)}, u32[]{:S(2)}) async-start(bf16[256,16,160]{0,2,1:T(8,128)(2,1)} %copy.52), calls=%async_computation.1 | async-start | bytes 2621440 | tf_op jit(solution)/shard_map/all_to_all | solution.py:24
  155.3 4.0 %multiply_bitcast_fusion = f32[2048,1,512]{0,2,1:T(8,128)} fusion(bf16[256,512]{0,1:T(8,128)(2,1)S(1)} %bitcast.187, bf16[256,2048]{0,1:T(8,128)(2,1)} %bitcast.185), kind=kOutput, calls=%fused_computation | convolution fusion | flops 537919488 | bytes 5505024 | tf_op jit(solution)/shard_map/tbh,tbc->hbc/dot_general | solution.py:204
  159.3 5.4 %copy.59 = f32[2048,1,512]{2,0,1:T(8,128)} copy(f32[2048,1,512]{0,2,1:T(8,128)} %multiply_bitcast_fusion) | data formatting | bytes 8388608 | tf_op jit(solution)/shard_map/mul | solution.py:207
  164.6 3.2 dynamic-slice_bitcast_fusion
  167.8 2.6 collective-permute-start.31
  170.4 15.4 %all-to-all-done.1 = bf16[256,16,160]{0,2,1:T(8,128)(2,1)S(1)} async-done(((bf16[256,16,160]{0,2,1:T(8,128)(2,1)}), bf16[256,16,160]{0,2,1:T(8,128)(2,1)S(1)}, u32[]{:S(2)}, u32[]{:S(2)}) %all-to-all-start.1) | async-done | bytes 1310752 | tf_op jit(solution)/shard_map/all_to_all | solution.py:24
  189.5 4.1 %collective-permute-start.10 = (f32[8,2,16,1,2048]{4,2,1,0,3:T(8,128)}, f32[8,2,16,1,2048]{4,2,1,0,3:T(8,128)}, u32[]{:S(2)}, u32[]{:S(2)}) collective-permute-start(f32[8,2,16,1,2048]{4,2,1,0,3:T(8,128)} %dynamic-slice_bitcast_fusion.1), channel_id=1, source_target_pairs={{0,16},{16,0},{1,17},{17,1},{2,18},{18,2},{3,19},{19,3},{4,20},{20... | collective-permute-start | bytes 6291464 | tf_op jit(solution)/shard_map/ppermute | solution.py:34
  194.4 3.0 convolution_multiply_fusion.1
  204.0 7.2 %collective-permute-start.27 = (f32[160,16,16]{0,2,1:T(8,128)S(1)}, f32[160,16,16]{0,2,1:T(8,128)S(1)}, u32[]{:S(2)}, u32[]{:S(2)}) collective-permute-start(f32[160,16,16]{0,2,1:T(8,128)S(1)} %fusion.34), channel_id=1, source_target_pairs={{0,32},{32,0},{1,33},{33,1},{2,34},{34,2},{3,35},{35,3},{4,36},{36... | collective-permute-start | bytes 491528 | tf_op jit(solution)/shard_map/ppermute | solution.py:34
  211.3 6.4 %collective-permute-done.27 = f32[160,16,16]{0,2,1:T(8,128)S(1)} collective-permute-done((f32[160,16,16]{0,2,1:T(8,128)S(1)}, f32[160,16,16]{0,2,1:T(8,128)S(1)}, u32[]{:S(2)}, u32[]{:S(2)}) %collective-permute-start.27) | collective-permute-done | bytes 163872 | tf_op jit(solution)/shard_map/ppermute | solution.py:34
  217.8 3.2 collective-permute-start.28
  221.0 4.1 %bitcast_add_fusion = f32[16,64,1,512]{3,1,2,0:T(8,128)} fusion(f32[16,64,1,512]{3,1,2,0:T(8,128)} %collective-permute-done.31, f32[16,2,64,1,512]{4,2,1,0,3:T(8,128)} %bitcast.180, s32[]{:T(128)S(6)} %select_n.209), kind=kLoop, calls=%fused_computation.6 | loop fusion | flops 524288 | bytes 6291460 | tf_op jit(solution)/shard_map/add | solution.py:97
  226.8 3.8 %collective-permute-start.29 = (f32[160,16,16]{0,2,1:T(8,128)S(1)}, f32[160,16,16]{0,2,1:T(8,128)}, u32[]{:S(2)}, u32[]{:S(2)}) collective-permute-start(f32[160,16,16]{0,2,1:T(8,128)S(1)} %add.291), channel_id=1, source_target_pairs={{0,128},{64,192},{128,0},{192,64},{256,384},{320,448},{384,256},{4... | collective-permute-start | bytes 491528 | tf_op jit(solution)/shard_map/ppermute | solution.py:34
  230.7 2.5 bitcast_add_fusion.1
  234.0 2.8 collective-permute-start.11
  240.1 2.4 collective-permute-done.29
  243.5 4.5 %collective-permute-start.30 = (f32[160,16,16]{0,2,1:T(8,128)S(1)}, f32[160,16,16]{0,2,1:T(8,128)S(1)}, u32[]{:S(2)}, u32[]{:S(2)}) collective-permute-start(f32[160,16,16]{0,2,1:T(8,128)S(1)} %add.292), channel_id=1, source_target_pairs={{0,256},{64,320},{128,384},{192,448},{256,0},{320,64},{384,128},{4... | collective-permute-start | bytes 491528 | tf_op jit(solution)/shard_map/ppermute | solution.py:34
  248.0 9.8 %collective-permute-start.18 = (f32[2,16,1,1024]{3,1,2,0:T(8,128)S(1)}, f32[2,16,1,1024]{3,1,2,0:T(8,128)S(1)}, u32[]{:S(2)}, u32[]{:S(2)}) collective-permute-start(f32[2,16,1,1024]{3,1,2,0:T(8,128)S(1)} %dynamic-slice_bitcast_fusion.2), channel_id=1, source_target_pairs={{0,448},{64,0},{128,64},{192,128},{256,192},{320,256},{384,320},{4... | collective-permute-start | bytes 393224 | tf_op jit(solution)/shard_map/ppermute | solution.py:29
  257.9 4.3 %collective-permute-start.12 = (f32[2,16,1,1024]{3,1,2,0:T(8,128)S(1)}, f32[2,16,1,1024]{3,1,2,0:T(8,128)S(1)}, u32[]{:S(2)}, u32[]{:S(2)}) collective-permute-start(f32[2,16,1,1024]{3,1,2,0:T(8,128)S(1)} %bitcast_add_fusion.15), channel_id=1, source_target_pairs={{0,64},{64,128},{128,192},{192,256},{256,320},{320,384},{384,448},... | collective-permute-start | bytes 393224 | tf_op jit(solution)/shard_map/ppermute | solution.py:29
  262.3 7.8 %collective-permute-start.19 = (f32[2,16,1,1024]{3,1,2,0:T(8,128)S(1)}, f32[2,16,1,1024]{3,1,2,0:T(8,128)S(1)}, u32[]{:S(2)}, u32[]{:S(2)}) collective-permute-start(f32[2,16,1,1024]{3,1,2,0:T(8,128)S(1)} %bitcast_add_fusion.8), channel_id=1, source_target_pairs={{0,448},{64,0},{128,64},{192,128},{256,192},{320,256},{384,320},{4... | collective-permute-start | bytes 393224 | tf_op jit(solution)/shard_map/ppermute | solution.py:29
  270.1 6.2 %collective-permute-done.12 = f32[2,16,1,1024]{3,1,2,0:T(8,128)S(1)} collective-permute-done((f32[2,16,1,1024]{3,1,2,0:T(8,128)S(1)}, f32[2,16,1,1024]{3,1,2,0:T(8,128)S(1)}, u32[]{:S(2)}, u32[]{:S(2)}) %collective-permute-start.12) | collective-permute-done | bytes 131104 | tf_op jit(solution)/shard_map/ppermute | solution.py:29
  276.4 3.1 collective-permute-start.13
  279.5 3.4 %collective-permute-start.20 = (f32[2,16,1,1024]{3,1,2,0:T(8,128)S(1)}, f32[2,16,1,1024]{3,1,2,0:T(8,128)S(1)}, u32[]{:S(2)}, u32[]{:S(2)}) collective-permute-start(f32[2,16,1,1024]{3,1,2,0:T(8,128)S(1)} %bitcast_add_fusion.7), channel_id=1, source_target_pairs={{0,448},{64,0},{128,64},{192,128},{256,192},{320,256},{384,320},{4... | collective-permute-start | bytes 393224 | tf_op jit(solution)/shard_map/ppermute | solution.py:29
  282.9 2.9 collective-permute-done.13
  285.9 2.3 collective-permute-start.14
  288.2 4.2 %collective-permute-start.21 = (f32[2,16,1,1024]{3,1,2,0:T(8,128)S(1)}, f32[2,16,1,1024]{3,1,2,0:T(8,128)S(1)}, u32[]{:S(2)}, u32[]{:S(2)}) collective-permute-start(f32[2,16,1,1024]{3,1,2,0:T(8,128)S(1)} %bitcast_add_fusion.6), channel_id=1, source_target_pairs={{0,448},{64,0},{128,64},{192,128},{256,192},{320,256},{384,320},{4... | collective-permute-start | bytes 393224 | tf_op jit(solution)/shard_map/ppermute | solution.py:29
  293.6 1.9 collective-permute-start.15
  295.5 4.6 %collective-permute-start.22 = (f32[2,16,1,1024]{3,1,2,0:T(8,128)S(1)}, f32[2,16,1,1024]{3,1,2,0:T(8,128)S(1)}, u32[]{:S(2)}, u32[]{:S(2)}) collective-permute-start(f32[2,16,1,1024]{3,1,2,0:T(8,128)S(1)} %bitcast_add_fusion.5), channel_id=1, source_target_pairs={{0,448},{64,0},{128,64},{192,128},{256,192},{320,256},{384,320},{4... | collective-permute-start | bytes 393224 | tf_op jit(solution)/shard_map/ppermute | solution.py:29
  303.1 4.6 %collective-permute-start.23 = (f32[2,16,1,1024]{3,1,2,0:T(8,128)S(1)}, f32[2,16,1,1024]{3,1,2,0:T(8,128)S(1)}, u32[]{:S(2)}, u32[]{:S(2)}) collective-permute-start(f32[2,16,1,1024]{3,1,2,0:T(8,128)S(1)} %bitcast_add_fusion.4), channel_id=1, source_target_pairs={{0,448},{64,0},{128,64},{192,128},{256,192},{320,256},{384,320},{4... | collective-permute-start | bytes 393224 | tf_op jit(solution)/shard_map/ppermute | solution.py:29
  310.1 4.6 %collective-permute-start.24 = (f32[2,16,1,1024]{3,1,2,0:T(8,128)S(1)}, f32[2,16,1,1024]{3,1,2,0:T(8,128)S(1)}, u32[]{:S(2)}, u32[]{:S(2)}) collective-permute-start(f32[2,16,1,1024]{3,1,2,0:T(8,128)S(1)} %bitcast_add_fusion.3), channel_id=1, source_target_pairs={{0,448},{64,0},{128,64},{192,128},{256,192},{320,256},{384,320},{4... | collective-permute-start | bytes 393224 | tf_op jit(solution)/shard_map/ppermute | solution.py:29
  316.6 4.8 %collective-permute-start.25 = (f32[16,1,2048]{2,0,1:T(8,128)S(1)}, f32[16,1,2048]{2,0,1:T(8,128)S(1)}, u32[]{:S(2)}, u32[]{:S(2)}) collective-permute-start(f32[16,1,2048]{2,0,1:T(8,128)S(1)} %fusion.26), channel_id=1, source_target_pairs={{0,32},{32,0},{1,33},{33,1},{2,34},{34,2},{3,35},{35,3},{4,36},{36... | collective-permute-start | bytes 393224 | tf_op jit(solution)/shard_map/ppermute | solution.py:34
  (130 shorter events, 55.3 us)
Async XLA Ops:
  7.2 63.2 %copy-start = (bf16[256,512]{1,0:T(8,128)(2,1)S(1)}, bf16[256,512]{1,0:T(8,128)(2,1)}, u32[]{:S(2)}) copy-start(bf16[256,512]{1,0:T(8,128)(2,1)} %param.6) | copy-start | bytes 786436
  7.2 56.5 %copy-start.12 = (bf16[32,16,16]{0,2,1:T(8,128)(2,1)S(1)}, bf16[32,16,16]{0,2,1:T(8,128)(2,1)}, u32[]{:S(2)}) copy-start(bf16[32,16,16]{0,2,1:T(8,128)(2,1)} %param.10) | copy-start | bytes 49156
  7.2 126.8 %all-gather.2.cloned.1.call-start = ((), (), s32[]{:S(2)}) async-start(), calls=%async_computation.3 | async-start | bytes 2162688 | tf_op jit(solution)/shard_map/all_gather | solution.py:150
  7.2 6.0 %collective-permute-start = (bf16[16,2048]{1,0:T(8,128)(2,1)}, bf16[16,2048]{1,0:T(8,128)(2,1)S(1)}, u32[]{:S(2)}, u32[]{:S(2)}) collective-permute-start(bf16[16,2048]{1,0:T(8,128)(2,1)} %bitcast.195), channel_id=1, source_target_pairs={{0,32},{32,0},{1,33},{33,1},{2,34},{34,2},{3,35},{35,3},{4,36},{36... | collective-permute-start | bytes 196616 | tf_op jit(solution)/shard_map/ppermute | solution.py:34
  14.2 15.5 %collective-permute-start.2 = (bf16[2,16,2048]{2,1,0:T(8,128)(2,1)S(1)}, bf16[2,16,2048]{2,1,0:T(8,128)(2,1)S(1)}, u32[]{:S(2)}, u32[]{:S(2)}) collective-permute-start(bf16[2,16,2048]{2,1,0:T(8,128)(2,1)S(1)} %maximum_select_fusion.2), channel_id=1, source_target_pairs={{0,448},{64,0},{128,64},{192,128},{256,192},{320,256},{384,320},{4... | collective-permute-start | bytes 393224 | tf_op jit(solution)/shard_map/ppermute | solution.py:29
  25.0 9.2 %collective-permute-start.1 = (bf16[2,16,2048]{2,1,0:T(8,128)(2,1)S(1)}, bf16[2,16,2048]{2,1,0:T(8,128)(2,1)S(1)}, u32[]{:S(2)}, u32[]{:S(2)}) collective-permute-start(bf16[2,16,2048]{2,1,0:T(8,128)(2,1)S(1)} %maximum_select_fusion.2), channel_id=1, source_target_pairs={{0,64},{64,128},{128,192},{192,256},{256,320},{320,384},{384,448},... | collective-permute-start | bytes 393224 | tf_op jit(solution)/shard_map/ppermute | solution.py:29
  29.7 7.8 %collective-permute-start.4 = (bf16[2,16,2048]{2,1,0:T(8,128)(2,1)S(1)}, bf16[2,16,2048]{2,1,0:T(8,128)(2,1)S(1)}, u32[]{:S(2)}, u32[]{:S(2)}) collective-permute-start(bf16[2,16,2048]{2,1,0:T(8,128)(2,1)S(1)} %collective-permute-done.2), channel_id=1, source_target_pairs={{0,448},{64,0},{128,64},{192,128},{256,192},{320,256},{384,320},{4... | collective-permute-start | bytes 393224 | tf_op jit(solution)/shard_map/ppermute | solution.py:29
  34.2 7.8 %collective-permute-start.3 = (bf16[2,16,2048]{2,1,0:T(8,128)(2,1)S(1)}, bf16[2,16,2048]{2,1,0:T(8,128)(2,1)S(1)}, u32[]{:S(2)}, u32[]{:S(2)}) collective-permute-start(bf16[2,16,2048]{2,1,0:T(8,128)(2,1)S(1)} %collective-permute-done.1), channel_id=1, source_target_pairs={{0,64},{64,128},{128,192},{192,256},{256,320},{320,384},{384,448},... | collective-permute-start | bytes 393224 | tf_op jit(solution)/shard_map/ppermute | solution.py:29
  37.5 7.8 %collective-permute-start.6 = (bf16[2,16,2048]{2,1,0:T(8,128)(2,1)S(1)}, bf16[2,16,2048]{2,1,0:T(8,128)(2,1)S(1)}, u32[]{:S(2)}, u32[]{:S(2)}) collective-permute-start(bf16[2,16,2048]{2,1,0:T(8,128)(2,1)S(1)} %collective-permute-done.4), channel_id=1, source_target_pairs={{0,448},{64,0},{128,64},{192,128},{256,192},{320,256},{384,320},{4... | collective-permute-start | bytes 393224 | tf_op jit(solution)/shard_map/ppermute | solution.py:29
  42.1 7.8 %collective-permute-start.5 = (bf16[2,16,2048]{2,1,0:T(8,128)(2,1)S(1)}, bf16[2,16,2048]{2,1,0:T(8,128)(2,1)S(1)}, u32[]{:S(2)}, u32[]{:S(2)}) collective-permute-start(bf16[2,16,2048]{2,1,0:T(8,128)(2,1)S(1)} %collective-permute-done.3), channel_id=1, source_target_pairs={{0,64},{64,128},{128,192},{192,256},{256,320},{320,384},{384,448},... | collective-permute-start | bytes 393224 | tf_op jit(solution)/shard_map/ppermute | solution.py:29
  45.3 7.9 %collective-permute-start.8 = (bf16[2,16,1024]{2,1,0:T(8,128)(2,1)S(1)}, bf16[2,16,1024]{2,1,0:T(8,128)(2,1)S(1)}, u32[]{:S(2)}, u32[]{:S(2)}) collective-permute-start(bf16[2,16,1024]{2,1,0:T(8,128)(2,1)S(1)} %split.17), channel_id=1, source_target_pairs={{0,448},{64,0},{128,64},{192,128},{256,192},{320,256},{384,320},{4... | collective-permute-start | bytes 196616 | tf_op jit(solution)/shard_map/ppermute | solution.py:29
  49.9 6.2 %collective-permute-start.7 = (bf16[2,16,1024]{2,1,0:T(8,128)(2,1)S(1)}, bf16[2,16,1024]{2,1,0:T(8,128)(2,1)S(1)}, u32[]{:S(2)}, u32[]{:S(2)}) collective-permute-start(bf16[2,16,1024]{2,1,0:T(8,128)(2,1)S(1)} %split.16), channel_id=1, source_target_pairs={{0,64},{64,128},{128,192},{192,256},{256,320},{320,384},{384,448},... | collective-permute-start | bytes 196616 | tf_op jit(solution)/shard_map/ppermute | solution.py:29
  56.8 10.8 %collective-permute-start.9 = (bf16[8,2,16,2048]{3,2,1,0:T(8,128)(2,1)}, bf16[8,2,16,2048]{3,2,1,0:T(8,128)(2,1)}, u32[]{:S(2)}, u32[]{:S(2)}) collective-permute-start(bf16[8,2,16,2048]{3,2,1,0:T(8,128)(2,1)} %fusion.32), channel_id=1, source_target_pairs={{0,16},{16,0},{1,17},{17,1},{2,18},{18,2},{3,19},{19,3},{4,20},{20... | collective-permute-start | bytes 3145736 | tf_op jit(solution)/shard_map/ppermute | solution.py:34
  63.8 3.5 %copy-start.10 = (bf16[256,512]{1,0:T(8,128)(2,1)S(1)}, bf16[256,512]{1,0:T(8,128)(2,1)}, u32[]{:S(2)}) copy-start(bf16[256,512]{1,0:T(8,128)(2,1)} %param.11) | copy-start | bytes 786436
  70.4 1.3 copy-start.8
  71.7 10.6 %copy-start.13 = (bf16[128,16,16]{0,2,1:T(8,128)(2,1)S(1)}, bf16[128,16,16]{0,2,1:T(8,128)(2,1)}, u32[]{:S(2)}) copy-start(bf16[128,16,16]{0,2,1:T(8,128)(2,1)} %param.8) | copy-start | bytes 196612
  72.8 50.7 %all-to-all-start = ((bf16[256,16,160]{0,2,1:T(8,128)(2,1)}), bf16[256,16,160]{0,2,1:T(8,128)(2,1)S(1)}, u32[]{:S(2)}, u32[]{:S(2)}) async-start(bf16[256,16,160]{0,2,1:T(8,128)(2,1)} %pad_maximum_fusion), calls=%async_computation | async-start | bytes 2621440 | tf_op jit(solution)/shard_map/all_to_all | solution.py:24
  133.9 2.4 copy-start.7
  138.4 5.0 %copy-start.3 = (bf16[256,16,128]{0,1,2:T(8,128)(2,1)}, bf16[256,16,128]{0,1,2:T(8,128)(2,1)S(1)}, u32[]{:S(2)}) copy-start(bf16[256,16,128]{0,1,2:T(8,128)(2,1)S(1)} %get-tuple-element.27) | copy-start | bytes 3145732
  138.4 2.3 copy-start.2
  146.5 39.2 %all-to-all-start.1 = ((bf16[256,16,160]{0,2,1:T(8,128)(2,1)}), bf16[256,16,160]{0,2,1:T(8,128)(2,1)S(1)}, u32[]{:S(2)}, u32[]{:S(2)}) async-start(bf16[256,16,160]{0,2,1:T(8,128)(2,1)} %copy.52), calls=%async_computation.1 | async-start | bytes 2621440 | tf_op jit(solution)/shard_map/all_to_all | solution.py:24
  155.2 169.2 %reduce-scatter.2.cloned.1.call-start = ((), (), s32[]{:S(2)}) async-start(), calls=%async_computation.4 | async-start | bytes 2228224 | tf_op jit(solution)/shard_map/reduce_scatter | solution.py:98
  167.8 53.2 %collective-permute-start.31 = (f32[16,64,1,512]{3,1,2,0:T(8,128)}, f32[16,64,1,512]{3,1,2,0:T(8,128)}, u32[]{:S(2)}, u32[]{:S(2)}) collective-permute-start(f32[16,64,1,512]{3,1,2,0:T(8,128)} %dynamic-slice_bitcast_fusion), channel_id=1, source_target_pairs={{0,16},{16,0},{1,17},{17,1},{2,18},{18,2},{3,19},{19,3},{4,20},{20... | collective-permute-start | bytes 6291464 | tf_op jit(solution)/shard_map/ppermute | solution.py:34
  186.8 2.6 copy-start.1
  186.8 6.7 %copy-start.11 = (bf16[256,512]{1,0:T(8,128)(2,1)S(1)}, bf16[256,512]{1,0:T(8,128)(2,1)}, u32[]{:S(2)}) copy-start(bf16[256,512]{1,0:T(8,128)(2,1)} %param.11) | copy-start | bytes 786436
  189.5 41.2 %collective-permute-start.10 = (f32[8,2,16,1,2048]{4,2,1,0,3:T(8,128)}, f32[8,2,16,1,2048]{4,2,1,0,3:T(8,128)}, u32[]{:S(2)}, u32[]{:S(2)}) collective-permute-start(f32[8,2,16,1,2048]{4,2,1,0,3:T(8,128)} %dynamic-slice_bitcast_fusion.1), channel_id=1, source_target_pairs={{0,16},{16,0},{1,17},{17,1},{2,18},{18,2},{3,19},{19,3},{4,20},{20... | collective-permute-start | bytes 6291464 | tf_op jit(solution)/shard_map/ppermute | solution.py:34
  200.5 3.4 %collective-permute-start.26 = (f32[160,16,16]{0,2,1:T(8,128)S(1)}, f32[160,16,16]{0,2,1:T(8,128)S(1)}, u32[]{:S(2)}, u32[]{:S(2)}) collective-permute-start(f32[160,16,16]{0,2,1:T(8,128)S(1)} %pad_maximum_fusion.2), channel_id=1, source_target_pairs={{0,16},{16,0},{1,17},{17,1},{2,18},{18,2},{3,19},{19,3},{4,20},{20... | collective-permute-start | bytes 491528 | tf_op jit(solution)/shard_map/ppermute | solution.py:34
  204.0 13.7 %collective-permute-start.27 = (f32[160,16,16]{0,2,1:T(8,128)S(1)}, f32[160,16,16]{0,2,1:T(8,128)S(1)}, u32[]{:S(2)}, u32[]{:S(2)}) collective-permute-start(f32[160,16,16]{0,2,1:T(8,128)S(1)} %fusion.34), channel_id=1, source_target_pairs={{0,32},{32,0},{1,33},{33,1},{2,34},{34,2},{3,35},{35,3},{4,36},{36... | collective-permute-start | bytes 491528 | tf_op jit(solution)/shard_map/ppermute | solution.py:34
  217.8 9.0 %collective-permute-start.28 = (f32[160,16,16]{0,2,1:T(8,128)S(1)}, f32[160,16,16]{0,2,1:T(8,128)S(1)}, u32[]{:S(2)}, u32[]{:S(2)}) collective-permute-start(f32[160,16,16]{0,2,1:T(8,128)S(1)} %add.290), channel_id=1, source_target_pairs={{0,64},{64,0},{128,192},{192,128},{256,320},{320,256},{384,448},{4... | collective-permute-start | bytes 491528 | tf_op jit(solution)/shard_map/ppermute | solution.py:34
  226.8 15.7 %collective-permute-start.29 = (f32[160,16,16]{0,2,1:T(8,128)S(1)}, f32[160,16,16]{0,2,1:T(8,128)}, u32[]{:S(2)}, u32[]{:S(2)}) collective-permute-start(f32[160,16,16]{0,2,1:T(8,128)S(1)} %add.291), channel_id=1, source_target_pairs={{0,128},{64,192},{128,0},{192,64},{256,384},{320,448},{384,256},{4... | collective-permute-start | bytes 491528 | tf_op jit(solution)/shard_map/ppermute | solution.py:34
  233.2 3.7 %copy-start.5 = (bf16[256,16,128]{0,2,1:T(8,128)(2,1)S(1)}, bf16[256,16,128]{0,2,1:T(8,128)(2,1)}, u32[]{:S(2)}) copy-start(bf16[256,16,128]{0,2,1:T(8,128)(2,1)} %copy-done.4) | copy-start | bytes 3145732
  233.2 3.7 %copy-start.9 = (bf16[8,2,2,16,2048]{4,3,2,1,0:T(8,128)(2,1)S(1)}, bf16[8,2,2,16,2048]{4,3,2,1,0:T(8,128)(2,1)}, u32[]{:S(2)}) copy-start(bf16[8,2,2,16,2048]{4,3,2,1,0:T(8,128)(2,1)} %copy-done.8) | copy-start | bytes 6291460
  234.0 23.9 %collective-permute-start.11 = (f32[2,16,1,1024]{3,1,2,0:T(8,128)}, f32[2,16,1,1024]{3,1,2,0:T(8,128)S(1)}, u32[]{:S(2)}, u32[]{:S(2)}) collective-permute-start(f32[2,16,1,1024]{3,1,2,0:T(8,128)} %dynamic-slice_bitcast_fusion.3), channel_id=1, source_target_pairs={{0,64},{64,128},{128,192},{192,256},{256,320},{320,384},{384,448},... | collective-permute-start | bytes 393224 | tf_op jit(solution)/shard_map/ppermute | solution.py:29
  243.5 78.9 %collective-permute-start.30 = (f32[160,16,16]{0,2,1:T(8,128)S(1)}, f32[160,16,16]{0,2,1:T(8,128)S(1)}, u32[]{:S(2)}, u32[]{:S(2)}) collective-permute-start(f32[160,16,16]{0,2,1:T(8,128)S(1)} %add.292), channel_id=1, source_target_pairs={{0,256},{64,320},{128,384},{192,448},{256,0},{320,64},{384,128},{4... | collective-permute-start | bytes 491528 | tf_op jit(solution)/shard_map/ppermute | solution.py:34
  248.0 14.2 %collective-permute-start.18 = (f32[2,16,1,1024]{3,1,2,0:T(8,128)S(1)}, f32[2,16,1,1024]{3,1,2,0:T(8,128)S(1)}, u32[]{:S(2)}, u32[]{:S(2)}) collective-permute-start(f32[2,16,1,1024]{3,1,2,0:T(8,128)S(1)} %dynamic-slice_bitcast_fusion.2), channel_id=1, source_target_pairs={{0,448},{64,0},{128,64},{192,128},{256,192},{320,256},{384,320},{4... | collective-permute-start | bytes 393224 | tf_op jit(solution)/shard_map/ppermute | solution.py:29
  257.9 18.4 %collective-permute-start.12 = (f32[2,16,1,1024]{3,1,2,0:T(8,128)S(1)}, f32[2,16,1,1024]{3,1,2,0:T(8,128)S(1)}, u32[]{:S(2)}, u32[]{:S(2)}) collective-permute-start(f32[2,16,1,1024]{3,1,2,0:T(8,128)S(1)} %bitcast_add_fusion.15), channel_id=1, source_target_pairs={{0,64},{64,128},{128,192},{192,256},{256,320},{320,384},{384,448},... | collective-permute-start | bytes 393224 | tf_op jit(solution)/shard_map/ppermute | solution.py:29
  262.3 17.2 %collective-permute-start.19 = (f32[2,16,1,1024]{3,1,2,0:T(8,128)S(1)}, f32[2,16,1,1024]{3,1,2,0:T(8,128)S(1)}, u32[]{:S(2)}, u32[]{:S(2)}) collective-permute-start(f32[2,16,1,1024]{3,1,2,0:T(8,128)S(1)} %bitcast_add_fusion.8), channel_id=1, source_target_pairs={{0,448},{64,0},{128,64},{192,128},{256,192},{320,256},{384,320},{4... | collective-permute-start | bytes 393224 | tf_op jit(solution)/shard_map/ppermute | solution.py:29
  276.4 9.5 %collective-permute-start.13 = (f32[2,16,1,1024]{3,1,2,0:T(8,128)S(1)}, f32[2,16,1,1024]{3,1,2,0:T(8,128)S(1)}, u32[]{:S(2)}, u32[]{:S(2)}) collective-permute-start(f32[2,16,1,1024]{3,1,2,0:T(8,128)S(1)} %bitcast_add_fusion.14), channel_id=1, source_target_pairs={{0,64},{64,128},{128,192},{192,256},{256,320},{320,384},{384,448},... | collective-permute-start | bytes 393224 | tf_op jit(solution)/shard_map/ppermute | solution.py:29
  279.5 8.7 %collective-permute-start.20 = (f32[2,16,1,1024]{3,1,2,0:T(8,128)S(1)}, f32[2,16,1,1024]{3,1,2,0:T(8,128)S(1)}, u32[]{:S(2)}, u32[]{:S(2)}) collective-permute-start(f32[2,16,1,1024]{3,1,2,0:T(8,128)S(1)} %bitcast_add_fusion.7), channel_id=1, source_target_pairs={{0,448},{64,0},{128,64},{192,128},{256,192},{320,256},{384,320},{4... | collective-permute-start | bytes 393224 | tf_op jit(solution)/shard_map/ppermute | solution.py:29
  285.9 7.7 %collective-permute-start.14 = (f32[2,16,1,1024]{3,1,2,0:T(8,128)S(1)}, f32[2,16,1,1024]{3,1,2,0:T(8,128)S(1)}, u32[]{:S(2)}, u32[]{:S(2)}) collective-permute-start(f32[2,16,1,1024]{3,1,2,0:T(8,128)S(1)} %bitcast_add_fusion.13), channel_id=1, source_target_pairs={{0,64},{64,128},{128,192},{192,256},{256,320},{320,384},{384,448},... | collective-permute-start | bytes 393224 | tf_op jit(solution)/shard_map/ppermute | solution.py:29
  288.2 7.2 %collective-permute-start.21 = (f32[2,16,1,1024]{3,1,2,0:T(8,128)S(1)}, f32[2,16,1,1024]{3,1,2,0:T(8,128)S(1)}, u32[]{:S(2)}, u32[]{:S(2)}) collective-permute-start(f32[2,16,1,1024]{3,1,2,0:T(8,128)S(1)} %bitcast_add_fusion.6), channel_id=1, source_target_pairs={{0,448},{64,0},{128,64},{192,128},{256,192},{320,256},{384,320},{4... | collective-permute-start | bytes 393224 | tf_op jit(solution)/shard_map/ppermute | solution.py:29
  293.6 7.6 %collective-permute-start.15 = (f32[2,16,1,1024]{3,1,2,0:T(8,128)S(1)}, f32[2,16,1,1024]{3,1,2,0:T(8,128)S(1)}, u32[]{:S(2)}, u32[]{:S(2)}) collective-permute-start(f32[2,16,1,1024]{3,1,2,0:T(8,128)S(1)} %bitcast_add_fusion.12), channel_id=1, source_target_pairs={{0,64},{64,128},{128,192},{192,256},{256,320},{320,384},{384,448},... | collective-permute-start | bytes 393224 | tf_op jit(solution)/shard_map/ppermute | solution.py:29
  295.5 7.6 %collective-permute-start.22 = (f32[2,16,1,1024]{3,1,2,0:T(8,128)S(1)}, f32[2,16,1,1024]{3,1,2,0:T(8,128)S(1)}, u32[]{:S(2)}, u32[]{:S(2)}) collective-permute-start(f32[2,16,1,1024]{3,1,2,0:T(8,128)S(1)} %bitcast_add_fusion.5), channel_id=1, source_target_pairs={{0,448},{64,0},{128,64},{192,128},{256,192},{320,256},{384,320},{4... | collective-permute-start | bytes 393224 | tf_op jit(solution)/shard_map/ppermute | solution.py:29
  301.2 6.9 %collective-permute-start.16 = (f32[2,16,1,1024]{3,1,2,0:T(8,128)S(1)}, f32[2,16,1,1024]{3,1,2,0:T(8,128)S(1)}, u32[]{:S(2)}, u32[]{:S(2)}) collective-permute-start(f32[2,16,1,1024]{3,1,2,0:T(8,128)S(1)} %bitcast_add_fusion.11), channel_id=1, source_target_pairs={{0,64},{64,128},{128,192},{192,256},{256,320},{320,384},{384,448},... | collective-permute-start | bytes 393224 | tf_op jit(solution)/shard_map/ppermute | solution.py:29
  303.1 6.9 %collective-permute-start.23 = (f32[2,16,1,1024]{3,1,2,0:T(8,128)S(1)}, f32[2,16,1,1024]{3,1,2,0:T(8,128)S(1)}, u32[]{:S(2)}, u32[]{:S(2)}) collective-permute-start(f32[2,16,1,1024]{3,1,2,0:T(8,128)S(1)} %bitcast_add_fusion.4), channel_id=1, source_target_pairs={{0,448},{64,0},{128,64},{192,128},{256,192},{320,256},{384,320},{4... | collective-permute-start | bytes 393224 | tf_op jit(solution)/shard_map/ppermute | solution.py:29
  308.1 6.9 %collective-permute-start.17 = (f32[2,16,1,1024]{3,1,2,0:T(8,128)S(1)}, f32[2,16,1,1024]{3,1,2,0:T(8,128)S(1)}, u32[]{:S(2)}, u32[]{:S(2)}) collective-permute-start(f32[2,16,1,1024]{3,1,2,0:T(8,128)S(1)} %bitcast_add_fusion.10), channel_id=1, source_target_pairs={{0,64},{64,128},{128,192},{192,256},{256,320},{320,384},{384,448},... | collective-permute-start | bytes 393224 | tf_op jit(solution)/shard_map/ppermute | solution.py:29
  310.1 6.5 %collective-permute-start.24 = (f32[2,16,1,1024]{3,1,2,0:T(8,128)S(1)}, f32[2,16,1,1024]{3,1,2,0:T(8,128)S(1)}, u32[]{:S(2)}, u32[]{:S(2)}) collective-permute-start(f32[2,16,1,1024]{3,1,2,0:T(8,128)S(1)} %bitcast_add_fusion.3), channel_id=1, source_target_pairs={{0,448},{64,0},{128,64},{192,128},{256,192},{320,256},{384,320},{4... | collective-permute-start | bytes 393224 | tf_op jit(solution)/shard_map/ppermute | solution.py:29
  316.6 7.2 %collective-permute-start.25 = (f32[16,1,2048]{2,0,1:T(8,128)S(1)}, f32[16,1,2048]{2,0,1:T(8,128)S(1)}, u32[]{:S(2)}, u32[]{:S(2)}) collective-permute-start(f32[16,1,2048]{2,0,1:T(8,128)S(1)} %fusion.26), channel_id=1, source_target_pairs={{0,32},{32,0},{1,33},{33,1},{2,34},{34,2},{3,35},{35,3},{4,36},{36... | collective-permute-start | bytes 393224 | tf_op jit(solution)/shard_map/ppermute | solution.py:34
  (2 other events, 2.0 us)
Sparse Core Ops, SparseCore 0:
  63.8 70.0 all-gather.1
  225.3 65.2 reduce-scatter.1

commit v7 on v5

--- a/solution.py
+++ b/solution.py
@@ -98,13 +98,12 @@
 
 
 def dp_all_reduce(x):
-    x = x + swap(x, "core", 1)
+    mask = lax.axis_size("z") // 2
+    while mask >= 1:
+        x = x + swap(x, "z", mask)
+        mask //= 2
     x = x + swap(x, "ylo", 1)
-    mask = 1
-    while mask < lax.axis_size("z"):
-        x = x + swap(x, "z", mask)
-        mask *= 2
-    return x
+    return x + swap(x, "core", 1)
 
 
 def to_wire(blocks, feat_count):

time: 312 us -> 304 us (0.974)
  waiting for transfers between devices: 87.9 us -> 77.2 us
    ppermute x9, waiting for transfers between devices: 28.6 us -> 14.4 us  [swap(): return lax.ppermute(value, axis, [(i, i ^ mask) for i in range(n)])]
    ppermute x22, waiting for transfers between devices: 10 us -> 13.5 us  [shift(): return lax.ppermute(value, axis, [(i, (i + step) % n) for i in range(n)])]
  transfers between devices with their start and end apart: 33 -> 33, of which waited for: 12 -> 13; matrix products, arithmetic and copies ran while one was open for 21% -> 21% of each run, Pallas kernels for 0% -> 0%
where the time goes in v7:
time: 304 us; the launch traced here: 302 us
  starting transfers between devices  129 us (42%)
  waiting for transfers between devices  77.2 us (25%)
  local copies, waits for them, and re-layouts  47.6 us (16%)
  other arithmetic  31.5 us (10%)
  matrix products  15.3 us (5%)
    ppermute x22, starting transfers between devices, shift(): return lax.ppermute(value, axis, [(i, (i + step) % n) for i in range(n)])  83.1 us
    all_to_all x2, waiting for transfers between devices, exchange(): return lax.all_to_all(wired, FEAT_AXES, 1, 1, tiled=True)  49.3 us
    ppermute x9, starting transfers between devices, swap(): return lax.ppermute(value, axis, [(i, i ^ mask) for i in range(n)])  30.5 us
    all_to_all x2, starting transfers between devices, exchange(): return lax.all_to_all(wired, FEAT_AXES, 1, 1, tiled=True)  15.2 us
    ppermute x9, waiting for transfers between devices, swap(): return lax.ppermute(value, axis, [(i, i ^ mask) for i in range(n)])  14.4 us
    ppermute x22, waiting for transfers between devices, shift(): return lax.ppermute(value, axis, [(i, (i + step) % n) for i in range(n)])  13.5 us
    unnamed x59, local copies, waits for them, and re-layouts  7.82 us
    add x6, other arithmetic, z_ring_reduce_scatter(): fwd = shift(own_f if fwd is None else fwd + own_f, 'z', 1)  7.57 us
  transfers between devices with their start and end apart: 33, of which 13 were waited for; matrix products, arithmetic and copies ran while one was open for 21% of the time, Pallas kernels for 0%

profile of v7, /device:TPU:1, one launch (start us, length us, event | category | flops | bytes accessed | tf_op | source)
XLA Modules:
  0.0 302.2 jit_solution(10330734388424771910)
XLA Ops:
  2.5 4.0 %collective-permute-start = (bf16[16,4096]{1,0:T(8,128)(2,1)S(1)}, bf16[16,4096]{1,0:T(8,128)(2,1)S(1)}, u32[]{:S(2)}, u32[]{:S(2)}) collective-permute-start(bf16[16,4096]{1,0:T(8,128)(2,1)S(1)} %get-tuple-element.46), channel_id=1, source_target_pairs={{0,32},{32,0},{1,33},{33,1},{2,34},{34,2},{3,35},{35,3},{4,36},{36... | collective-permute-start | bytes 393224 | tf_op jit(solution)/shard_map/ppermute | solution.py:34
  6.6 2.2 collective-permute-done
  8.9 11.4 %collective-permute-start.2 = (bf16[2,16,4096]{2,1,0:T(8,128)(2,1)S(1)}, bf16[2,16,4096]{2,1,0:T(8,128)(2,1)S(1)}, u32[]{:S(2)}, u32[]{:S(2)}) collective-permute-start(bf16[2,16,4096]{2,1,0:T(8,128)(2,1)S(1)} %maximum_select_fusion.2), channel_id=1, source_target_pairs={{0,448},{64,0},{128,64},{192,128},{256,192},{320,256},{384,320},{4... | collective-permute-start | bytes 786440 | tf_op jit(solution)/shard_map/ppermute | solution.py:29
  20.2 1.9 collective-permute-start.1
  24.5 5.1 %collective-permute-start.4 = (bf16[2,16,4096]{2,1,0:T(8,128)(2,1)S(1)}, bf16[2,16,4096]{2,1,0:T(8,128)(2,1)S(1)}, u32[]{:S(2)}, u32[]{:S(2)}) collective-permute-start(bf16[2,16,4096]{2,1,0:T(8,128)(2,1)S(1)} %collective-permute-done.2), channel_id=1, source_target_pairs={{0,448},{64,0},{128,64},{192,128},{256,192},{320,256},{384,320},{4... | collective-permute-start | bytes 786440 | tf_op jit(solution)/shard_map/ppermute | solution.py:29
  29.6 1.9 collective-permute-start.3
  33.0 4.9 %collective-permute-start.6 = (bf16[2,16,4096]{2,1,0:T(8,128)(2,1)S(1)}, bf16[2,16,4096]{2,1,0:T(8,128)(2,1)S(1)}, u32[]{:S(2)}, u32[]{:S(2)}) collective-permute-start(bf16[2,16,4096]{2,1,0:T(8,128)(2,1)S(1)} %collective-permute-done.4), channel_id=1, source_target_pairs={{0,448},{64,0},{128,64},{192,128},{256,192},{320,256},{384,320},{4... | collective-permute-start | bytes 786440 | tf_op jit(solution)/shard_map/ppermute | solution.py:29
  41.3 4.9 %collective-permute-start.8 = (bf16[2,16,2048]{2,1,0:T(8,128)(2,1)S(1)}, bf16[2,16,2048]{2,1,0:T(8,128)(2,1)S(1)}, u32[]{:S(2)}, u32[]{:S(2)}) collective-permute-start(bf16[2,16,2048]{2,1,0:T(8,128)(2,1)S(1)} %split.17), channel_id=1, source_target_pairs={{0,448},{64,0},{128,64},{192,128},{256,192},{320,256},{384,320},{4... | collective-permute-start | bytes 393224 | tf_op jit(solution)/shard_map/ppermute | solution.py:29
  46.3 1.9 collective-permute-start.7
  49.7 3.5 %collective-permute-done.7 = bf16[2,16,2048]{2,1,0:T(8,128)(2,1)S(1)} collective-permute-done((bf16[2,16,2048]{2,1,0:T(8,128)(2,1)S(1)}, bf16[2,16,2048]{2,1,0:T(8,128)(2,1)S(1)}, u32[]{:S(2)}, u32[]{:S(2)}) %collective-permute-start.7) | collective-permute-done | bytes 131104 | tf_op jit(solution)/shard_map/ppermute | solution.py:29
  53.9 8.1 %collective-permute-start.9 = (bf16[8,2,16,4096]{3,2,1,0:T(8,128)(2,1)}, bf16[8,2,16,4096]{3,2,1,0:T(8,128)(2,1)}, u32[]{:S(2)}, u32[]{:S(2)}) collective-permute-start(bf16[8,2,16,4096]{3,2,1,0:T(8,128)(2,1)} %fusion.27), channel_id=1, source_target_pairs={{0,16},{16,0},{1,17},{17,1},{2,18},{18,2},{3,19},{19,3},{4,20},{20... | collective-permute-start | bytes 6291464 | tf_op jit(solution)/shard_map/ppermute | solution.py:34
  63.6 2.1 reshape.176
  66.1 4.2 %maximum_select_fusion = bf16[8,2,2,16,4096]{4,3,2,1,0:T(8,128)(2,1)S(1)} fusion(bf16[8,2,1,16,4096]{4,3,2,1,0:T(8,128)(2,1)} %bitcast.13, bf16[8,2,1,16,4096]{4,3,2,1,0:T(8,128)(2,1)} %bitcast.12, pred[]{:T(512)S(6)} %eq.33), kind=kLoop, calls=%fused_computation.1 | loop fusion | flops 6291456 | bytes 8388609 | tf_op jit(solution)/shard_map/jit(_where)/select_n | solution.py:96
  73.5 9.4 %all-to-all-start = ((bf16[256,16,160]{0,2,1:T(8,128)(2,1)}), bf16[256,16,160]{0,2,1:T(8,128)(2,1)}, u32[]{:S(2)}, u32[]{:S(2)}) async-start(bf16[256,16,160]{0,2,1:T(8,128)(2,1)} %pad_maximum_fusion), calls=%async_computation | async-start | bytes 2621440 | tf_op jit(solution)/shard_map/all_to_all | solution.py:24
  83.4 3.4 %slice.45 = bf16[512,2048]{1,0:T(8,128)(2,1)} slice(bf16[512,4096]{1,0:T(8,128)(2,1)} %bitcast.165), slice={[0:512], [2048:4096]} | slice | bytes 4194304 | tf_op jit(solution)/shard_map/slice | solution.py:143
  86.8 3.1 %reshape.175 = bf16[2048,512]{1,0:T(8,128)(2,1)S(1)} reshape(bf16[512,2048]{1,0:T(8,128)(2,1)} %slice.45) | data formatting | bytes 4194304 | tf_op jit(solution)/shard_map/reshape.5
  89.9 27.2 %all-to-all-done = bf16[256,16,160]{0,2,1:T(8,128)(2,1)} async-done(((bf16[256,16,160]{0,2,1:T(8,128)(2,1)}), bf16[256,16,160]{0,2,1:T(8,128)(2,1)}, u32[]{:S(2)}, u32[]{:S(2)}) %all-to-all-start) | async-done | bytes 1310752 | tf_op jit(solution)/shard_map/all_to_all | solution.py:24
  120.2 2.1 fusion.4
  125.8 5.8 %all-to-all-start.1 = ((bf16[256,16,160]{0,2,1:T(8,128)(2,1)}), bf16[256,16,160]{0,2,1:T(8,128)(2,1)S(1)}, u32[]{:S(2)}, u32[]{:S(2)}) async-start(bf16[256,16,160]{0,2,1:T(8,128)(2,1)} %copy.98), calls=%async_computation.1 | async-start | bytes 2621440 | tf_op jit(solution)/shard_map/all_to_all | solution.py:24
  131.5 2.8 convolution_bitcast_fusion
  134.3 5.4 %copy.101 = f32[2048,1,512]{2,0,1:T(8,128)} copy(f32[2048,1,512]{0,2,1:T(8,128)} %convolution_bitcast_fusion) | data formatting | bytes 8388608 | tf_op jit(solution)/shard_map/tbh,tbc->hbc/transpose | solution.py:196
  139.7 5.7 %stack.56 = f32[8,2,2,1,1,16,2048]{6,5,2,1,0,4,3:T(8,128)} reshape(f32[2048,1,512]{2,0,1:T(8,128)} %copy.101) | data formatting | bytes 8388608 | tf_op jit(solution)/shard_map/stack | solution.py:229
  145.4 22.0 %all-to-all-done.1 = bf16[256,16,160]{0,2,1:T(8,128)(2,1)S(1)} async-done(((bf16[256,16,160]{0,2,1:T(8,128)(2,1)}), bf16[256,16,160]{0,2,1:T(8,128)(2,1)S(1)}, u32[]{:S(2)}, u32[]{:S(2)}) %all-to-all-start.1) | async-done | bytes 1310752 | tf_op jit(solution)/shard_map/all_to_all | solution.py:24
  173.9 2.9 collective-permute-start.10
  176.8 6.8 %collective-permute-done.10 = f32[8,2,1,2,16,2048]{5,4,3,1,0,2:T(8,128)S(1)} collective-permute-done((f32[8,2,1,2,16,2048]{5,4,3,1,0,2:T(8,128)S(1)}, f32[8,2,1,2,16,2048]{5,4,3,1,0,2:T(8,128)S(1)}, u32[]{:S(2)}, u32[]{:S(2)}) %collective-permute-start.10) | collective-permute-done | bytes 4194336 | tf_op jit(solution)/shard_map/ppermute | solution.py:34
  186.7 1.9 collective-permute-start.11
  189.4 4.6 %collective-permute-start.18 = (f32[2,1,2,16,1024]{4,3,2,0,1:T(8,128)}, f32[2,1,2,16,1024]{4,3,2,0,1:T(8,128)}, u32[]{:S(2)}, u32[]{:S(2)}) collective-permute-start(f32[2,1,2,16,1024]{4,3,2,0,1:T(8,128)} %dynamic-slice_bitcast_fusion), channel_id=1, source_target_pairs={{0,448},{64,0},{128,64},{192,128},{256,192},{320,256},{384,320},{4... | collective-permute-start | bytes 786440 | tf_op jit(solution)/shard_map/ppermute | solution.py:29
  194.9 2.8 collective-permute-done.11
  203.1 4.6 %collective-permute-start.19 = (f32[2,1,2,16,1024]{4,3,2,0,1:T(8,128)}, f32[2,1,2,16,1024]{4,3,2,0,1:T(8,128)}, u32[]{:S(2)}, u32[]{:S(2)}) collective-permute-start(f32[2,1,2,16,1024]{4,3,2,0,1:T(8,128)} %bitcast_add_fusion.7), channel_id=1, source_target_pairs={{0,448},{64,0},{128,64},{192,128},{256,192},{320,256},{384,320},{4... | collective-permute-start | bytes 786440 | tf_op jit(solution)/shard_map/ppermute | solution.py:29
  207.6 3.0 convolution_multiply_fusion
  214.4 1.9 collective-permute-start.13
  218.1 4.6 %collective-permute-start.20 = (f32[2,1,2,16,1024]{4,3,2,0,1:T(8,128)}, f32[2,1,2,16,1024]{4,3,2,0,1:T(8,128)}, u32[]{:S(2)}, u32[]{:S(2)}) collective-permute-start(f32[2,1,2,16,1024]{4,3,2,0,1:T(8,128)} %bitcast_add_fusion.6), channel_id=1, source_target_pairs={{0,448},{64,0},{128,64},{192,128},{256,192},{320,256},{384,320},{4... | collective-permute-start | bytes 786440 | tf_op jit(solution)/shard_map/ppermute | solution.py:29
  224.6 1.9 collective-permute-start.14
  227.5 5.3 %collective-permute-start.21 = (f32[2,1,2,16,1024]{4,3,2,0,1:T(8,128)S(1)}, f32[2,1,2,16,1024]{4,3,2,0,1:T(8,128)S(1)}, u32[]{:S(2)}, u32[]{:S(2)}) collective-permute-start(f32[2,1,2,16,1024]{4,3,2,0,1:T(8,128)S(1)} %bitcast_add_fusion.5), channel_id=1, source_target_pairs={{0,448},{64,0},{128,64},{192,128},{256,192},{320,256},{384,320},{4... | collective-permute-start | bytes 786440 | tf_op jit(solution)/shard_map/ppermute | solution.py:29
  232.8 2.0 collective-permute-start.26
  235.9 1.9 collective-permute-start.15
  237.8 6.6 %collective-permute-done.21 = f32[2,1,2,16,1024]{4,3,2,0,1:T(8,128)S(1)} collective-permute-done((f32[2,1,2,16,1024]{4,3,2,0,1:T(8,128)S(1)}, f32[2,1,2,16,1024]{4,3,2,0,1:T(8,128)S(1)}, u32[]{:S(2)}, u32[]{:S(2)}) %collective-permute-start.21) | collective-permute-done | bytes 262176 | tf_op jit(solution)/shard_map/ppermute | solution.py:29
  244.5 5.7 %collective-permute-start.22 = (f32[2,1,2,16,1024]{4,3,2,0,1:T(8,128)S(1)}, f32[2,1,2,16,1024]{4,3,2,0,1:T(8,128)S(1)}, u32[]{:S(2)}, u32[]{:S(2)}) collective-permute-start(f32[2,1,2,16,1024]{4,3,2,0,1:T(8,128)S(1)} %bitcast_add_fusion.4), channel_id=1, source_target_pairs={{0,448},{64,0},{128,64},{192,128},{256,192},{320,256},{384,320},{4... | collective-permute-start | bytes 786440 | tf_op jit(solution)/shard_map/ppermute | solution.py:29
  250.4 1.9 collective-permute-start.27
  253.4 3.2 %collective-permute-start.16 = (f32[2,1,2,16,1024]{4,3,2,0,1:T(8,128)S(1)}, f32[2,1,2,16,1024]{4,3,2,0,1:T(8,128)S(1)}, u32[]{:S(2)}, u32[]{:S(2)}) collective-permute-start(f32[2,1,2,16,1024]{4,3,2,0,1:T(8,128)S(1)} %bitcast_add_fusion.10), channel_id=1, source_target_pairs={{0,64},{64,128},{128,192},{192,256},{256,320},{320,384},{384,448},... | collective-permute-start | bytes 786440 | tf_op jit(solution)/shard_map/ppermute | solution.py:29
  257.4 3.2 %collective-permute-start.23 = (f32[2,1,2,16,1024]{4,3,2,0,1:T(8,128)}, f32[2,1,2,16,1024]{4,3,2,0,1:T(8,128)}, u32[]{:S(2)}, u32[]{:S(2)}) collective-permute-start(f32[2,1,2,16,1024]{4,3,2,0,1:T(8,128)} %bitcast_add_fusion.3), channel_id=1, source_target_pairs={{0,448},{64,0},{128,64},{192,128},{256,192},{320,256},{384,320},{4... | collective-permute-start | bytes 786440 | tf_op jit(solution)/shard_map/ppermute | solution.py:29
  260.7 5.1 %collective-permute-done.27 = f32[160,16,16]{0,2,1:T(8,128)S(1)} collective-permute-done((f32[160,16,16]{0,2,1:T(8,128)S(1)}, f32[160,16,16]{0,2,1:T(8,128)S(1)}, u32[]{:S(2)}, u32[]{:S(2)}) %collective-permute-start.27) | collective-permute-done | bytes 163872 | tf_op jit(solution)/shard_map/ppermute | solution.py:34
  265.9 1.9 collective-permute-start.28
  269.5 3.5 %collective-permute-start.17 = (f32[2,1,2,16,1024]{4,3,2,0,1:T(8,128)}, f32[2,1,2,16,1024]{4,3,2,0,1:T(8,128)}, u32[]{:S(2)}, u32[]{:S(2)}) collective-permute-start(f32[2,1,2,16,1024]{4,3,2,0,1:T(8,128)} %bitcast_add_fusion.9), channel_id=1, source_target_pairs={{0,64},{64,128},{128,192},{192,256},{256,320},{320,384},{384,448},... | collective-permute-start | bytes 786440 | tf_op jit(solution)/shard_map/ppermute | solution.py:29
  274.8 4.9 %collective-permute-start.24 = (f32[2,1,2,16,1024]{4,3,2,0,1:T(8,128)}, f32[2,1,2,16,1024]{4,3,2,0,1:T(8,128)}, u32[]{:S(2)}, u32[]{:S(2)}) collective-permute-start(f32[2,1,2,16,1024]{4,3,2,0,1:T(8,128)} %bitcast_add_fusion.2), channel_id=1, source_target_pairs={{0,448},{64,0},{128,64},{192,128},{256,192},{320,256},{384,320},{4... | collective-permute-start | bytes 786440 | tf_op jit(solution)/shard_map/ppermute | solution.py:29
  286.2 3.5 %collective-permute-start.25 = (f32[1,2,16,2048]{3,2,1,0:T(8,128)S(1)}, f32[1,2,16,2048]{3,2,1,0:T(8,128)S(1)}, u32[]{:S(2)}, u32[]{:S(2)}) collective-permute-start(f32[1,2,16,2048]{3,2,1,0:T(8,128)S(1)} %fusion.22), channel_id=1, source_target_pairs={{0,32},{32,0},{1,33},{33,1},{2,34},{34,2},{3,35},{35,3},{4,36},{36... | collective-permute-start | bytes 786440 | tf_op jit(solution)/shard_map/ppermute | solution.py:34
  289.8 2.3 fusion.15
  294.0 4.2 %collective-permute-start.30 = (f32[160,16,16]{0,2,1:T(8,128)S(1)}, f32[160,16,16]{0,2,1:T(8,128)S(1)}, u32[]{:S(2)}, u32[]{:S(2)}) collective-permute-start(f32[160,16,16]{0,2,1:T(8,128)S(1)} %add.284), channel_id=1, source_target_pairs={{0,16},{16,0},{1,17},{17,1},{2,18},{18,2},{3,19},{19,3},{4,20},{20... | collective-permute-start | bytes 491528 | tf_op jit(solution)/shard_map/ppermute | solution.py:34
  (156 shorter events, 67.0 us)
Async XLA Ops:
  0.6 69.7 %copy-start = (bf16[256,512]{1,0:T(8,128)(2,1)S(1)}, bf16[256,512]{1,0:T(8,128)(2,1)}, u32[]{:S(2)}) copy-start(bf16[256,512]{1,0:T(8,128)(2,1)} %param.6) | copy-start | bytes 786436
  2.5 6.4 %collective-permute-start = (bf16[16,4096]{1,0:T(8,128)(2,1)S(1)}, bf16[16,4096]{1,0:T(8,128)(2,1)S(1)}, u32[]{:S(2)}, u32[]{:S(2)}) collective-permute-start(bf16[16,4096]{1,0:T(8,128)(2,1)S(1)} %get-tuple-element.46), channel_id=1, source_target_pairs={{0,32},{32,0},{1,33},{33,1},{2,34},{34,2},{3,35},{35,3},{4,36},{36... | collective-permute-start | bytes 393224 | tf_op jit(solution)/shard_map/ppermute | solution.py:34
  8.9 15.6 %collective-permute-start.2 = (bf16[2,16,4096]{2,1,0:T(8,128)(2,1)S(1)}, bf16[2,16,4096]{2,1,0:T(8,128)(2,1)S(1)}, u32[]{:S(2)}, u32[]{:S(2)}) collective-permute-start(bf16[2,16,4096]{2,1,0:T(8,128)(2,1)S(1)} %maximum_select_fusion.2), channel_id=1, source_target_pairs={{0,448},{64,0},{128,64},{192,128},{256,192},{320,256},{384,320},{4... | collective-permute-start | bytes 786440 | tf_op jit(solution)/shard_map/ppermute | solution.py:29
  20.2 9.3 %collective-permute-start.1 = (bf16[2,16,4096]{2,1,0:T(8,128)(2,1)S(1)}, bf16[2,16,4096]{2,1,0:T(8,128)(2,1)S(1)}, u32[]{:S(2)}, u32[]{:S(2)}) collective-permute-start(bf16[2,16,4096]{2,1,0:T(8,128)(2,1)S(1)} %maximum_select_fusion.2), channel_id=1, source_target_pairs={{0,64},{64,128},{128,192},{192,256},{256,320},{320,384},{384,448},... | collective-permute-start | bytes 786440 | tf_op jit(solution)/shard_map/ppermute | solution.py:29
  24.5 37.5 %copy-start.26 = (bf16[32,16,16]{0,2,1:T(8,128)(2,1)S(1)}, bf16[32,16,16]{0,2,1:T(8,128)(2,1)}, u32[]{:S(2)}) copy-start(bf16[32,16,16]{0,2,1:T(8,128)(2,1)} %param.10) | copy-start | bytes 49156
  24.5 8.5 %collective-permute-start.4 = (bf16[2,16,4096]{2,1,0:T(8,128)(2,1)S(1)}, bf16[2,16,4096]{2,1,0:T(8,128)(2,1)S(1)}, u32[]{:S(2)}, u32[]{:S(2)}) collective-permute-start(bf16[2,16,4096]{2,1,0:T(8,128)(2,1)S(1)} %collective-permute-done.2), channel_id=1, source_target_pairs={{0,448},{64,0},{128,64},{192,128},{256,192},{320,256},{384,320},{4... | collective-permute-start | bytes 786440 | tf_op jit(solution)/shard_map/ppermute | solution.py:29
  29.6 8.3 %collective-permute-start.3 = (bf16[2,16,4096]{2,1,0:T(8,128)(2,1)S(1)}, bf16[2,16,4096]{2,1,0:T(8,128)(2,1)S(1)}, u32[]{:S(2)}, u32[]{:S(2)}) collective-permute-start(bf16[2,16,4096]{2,1,0:T(8,128)(2,1)S(1)} %collective-permute-done.1), channel_id=1, source_target_pairs={{0,64},{64,128},{128,192},{192,256},{256,320},{320,384},{384,448},... | collective-permute-start | bytes 786440 | tf_op jit(solution)/shard_map/ppermute | solution.py:29
  33.0 8.3 %collective-permute-start.6 = (bf16[2,16,4096]{2,1,0:T(8,128)(2,1)S(1)}, bf16[2,16,4096]{2,1,0:T(8,128)(2,1)S(1)}, u32[]{:S(2)}, u32[]{:S(2)}) collective-permute-start(bf16[2,16,4096]{2,1,0:T(8,128)(2,1)S(1)} %collective-permute-done.4), channel_id=1, source_target_pairs={{0,448},{64,0},{128,64},{192,128},{256,192},{320,256},{384,320},{4... | collective-permute-start | bytes 786440 | tf_op jit(solution)/shard_map/ppermute | solution.py:29
  37.9 8.3 %collective-permute-start.5 = (bf16[2,16,4096]{2,1,0:T(8,128)(2,1)S(1)}, bf16[2,16,4096]{2,1,0:T(8,128)(2,1)S(1)}, u32[]{:S(2)}, u32[]{:S(2)}) collective-permute-start(bf16[2,16,4096]{2,1,0:T(8,128)(2,1)S(1)} %collective-permute-done.3), channel_id=1, source_target_pairs={{0,64},{64,128},{128,192},{192,256},{256,320},{320,384},{384,448},... | collective-permute-start | bytes 786440 | tf_op jit(solution)/shard_map/ppermute | solution.py:29
  41.3 8.4 %collective-permute-start.8 = (bf16[2,16,2048]{2,1,0:T(8,128)(2,1)S(1)}, bf16[2,16,2048]{2,1,0:T(8,128)(2,1)S(1)}, u32[]{:S(2)}, u32[]{:S(2)}) collective-permute-start(bf16[2,16,2048]{2,1,0:T(8,128)(2,1)S(1)} %split.17), channel_id=1, source_target_pairs={{0,448},{64,0},{128,64},{192,128},{256,192},{320,256},{384,320},{4... | collective-permute-start | bytes 393224 | tf_op jit(solution)/shard_map/ppermute | solution.py:29
  46.3 6.9 %collective-permute-start.7 = (bf16[2,16,2048]{2,1,0:T(8,128)(2,1)S(1)}, bf16[2,16,2048]{2,1,0:T(8,128)(2,1)S(1)}, u32[]{:S(2)}, u32[]{:S(2)}) collective-permute-start(bf16[2,16,2048]{2,1,0:T(8,128)(2,1)S(1)} %split.16), channel_id=1, source_target_pairs={{0,64},{64,128},{128,192},{192,256},{256,320},{320,384},{384,448},... | collective-permute-start | bytes 393224 | tf_op jit(solution)/shard_map/ppermute | solution.py:29
  53.9 12.2 %collective-permute-start.9 = (bf16[8,2,16,4096]{3,2,1,0:T(8,128)(2,1)}, bf16[8,2,16,4096]{3,2,1,0:T(8,128)(2,1)}, u32[]{:S(2)}, u32[]{:S(2)}) collective-permute-start(bf16[8,2,16,4096]{3,2,1,0:T(8,128)(2,1)} %fusion.27), channel_id=1, source_target_pairs={{0,16},{16,0},{1,17},{17,1},{2,18},{18,2},{3,19},{19,3},{4,20},{20... | collective-permute-start | bytes 6291464 | tf_op jit(solution)/shard_map/ppermute | solution.py:34
  72.3 10.7 %copy-start.27 = (bf16[128,16,16]{0,2,1:T(8,128)(2,1)S(1)}, bf16[128,16,16]{0,2,1:T(8,128)(2,1)}, u32[]{:S(2)}) copy-start(bf16[128,16,16]{0,2,1:T(8,128)(2,1)} %param.8) | copy-start | bytes 196612
  73.5 43.6 %all-to-all-start = ((bf16[256,16,160]{0,2,1:T(8,128)(2,1)}), bf16[256,16,160]{0,2,1:T(8,128)(2,1)}, u32[]{:S(2)}, u32[]{:S(2)}) async-start(bf16[256,16,160]{0,2,1:T(8,128)(2,1)} %pad_maximum_fusion), calls=%async_computation | async-start | bytes 2621440 | tf_op jit(solution)/shard_map/all_to_all | solution.py:24
  83.4 36.8 %copy-start.19 = (bf16[128,16,16]{2,1,0:T(8,128)(2,1)}, bf16[128,16,16]{2,1,0:T(8,128)(2,1)S(1)}, u32[]{:S(2)}) copy-start(bf16[128,16,16]{2,1,0:T(8,128)(2,1)S(1)} %copy.96) | copy-start | bytes 196612
  124.3 7.3 %copy-start.18 = (bf16[256,16,32]{0,2,1:T(8,128)(2,1)S(1)}, bf16[256,16,32]{0,2,1:T(8,128)(2,1)}, u32[]{:S(2)}) copy-start(bf16[256,16,32]{0,2,1:T(8,128)(2,1)} %copy-done.17) | copy-start | bytes 786436
  125.8 41.7 %all-to-all-start.1 = ((bf16[256,16,160]{0,2,1:T(8,128)(2,1)}), bf16[256,16,160]{0,2,1:T(8,128)(2,1)S(1)}, u32[]{:S(2)}, u32[]{:S(2)}) async-start(bf16[256,16,160]{0,2,1:T(8,128)(2,1)} %copy.98), calls=%async_computation.1 | async-start | bytes 2621440 | tf_op jit(solution)/shard_map/all_to_all | solution.py:24
  173.9 9.6 %collective-permute-start.10 = (f32[8,2,1,2,16,2048]{5,4,3,1,0,2:T(8,128)S(1)}, f32[8,2,1,2,16,2048]{5,4,3,1,0,2:T(8,128)S(1)}, u32[]{:S(2)}, u32[]{:S(2)}) collective-permute-start(f32[8,2,1,2,16,2048]{5,4,3,1,0,2:T(8,128)S(1)} %bitcast.170), channel_id=1, source_target_pairs={{0,16},{16,0},{1,17},{17,1},{2,18},{18,2},{3,19},{19,3},{4,20},{20... | collective-permute-start | bytes 12582920 | tf_op jit(solution)/shard_map/ppermute | solution.py:34
  184.3 9.7 %copy-start.22 = (bf16[256,512]{1,0:T(8,128)(2,1)S(1)}, bf16[256,512]{1,0:T(8,128)(2,1)}, u32[]{:S(2)}) copy-start(bf16[256,512]{1,0:T(8,128)(2,1)} %param.11) | copy-start | bytes 786436
  184.7 23.0 %copy-start.9 = (bf16[256,16,128]{0,2,1:T(8,128)(2,1)S(1)}, bf16[256,16,128]{0,2,1:T(8,128)(2,1)}, u32[]{:S(2)}) copy-start(bf16[256,16,128]{0,2,1:T(8,128)(2,1)} %copy-done.8) | copy-start | bytes 3145732
  186.7 10.9 %collective-permute-start.11 = (f32[2,1,2,16,1024]{4,3,2,0,1:T(8,128)}, f32[2,1,2,16,1024]{4,3,2,0,1:T(8,128)}, u32[]{:S(2)}, u32[]{:S(2)}) collective-permute-start(f32[2,1,2,16,1024]{4,3,2,0,1:T(8,128)} %dynamic-slice_bitcast_fusion.1), channel_id=1, source_target_pairs={{0,64},{64,128},{128,192},{192,256},{256,320},{320,384},{384,448},... | collective-permute-start | bytes 786440 | tf_op jit(solution)/shard_map/ppermute | solution.py:29
  189.4 12.0 %collective-permute-start.18 = (f32[2,1,2,16,1024]{4,3,2,0,1:T(8,128)}, f32[2,1,2,16,1024]{4,3,2,0,1:T(8,128)}, u32[]{:S(2)}, u32[]{:S(2)}) collective-permute-start(f32[2,1,2,16,1024]{4,3,2,0,1:T(8,128)} %dynamic-slice_bitcast_fusion), channel_id=1, source_target_pairs={{0,448},{64,0},{128,64},{192,128},{256,192},{320,256},{384,320},{4... | collective-permute-start | bytes 786440 | tf_op jit(solution)/shard_map/ppermute | solution.py:29
  199.4 13.8 %collective-permute-start.12 = (f32[2,1,2,16,1024]{4,3,2,0,1:T(8,128)}, f32[2,1,2,16,1024]{4,3,2,0,1:T(8,128)}, u32[]{:S(2)}, u32[]{:S(2)}) collective-permute-start(f32[2,1,2,16,1024]{4,3,2,0,1:T(8,128)} %bitcast_add_fusion.14), channel_id=1, source_target_pairs={{0,64},{64,128},{128,192},{192,256},{256,320},{320,384},{384,448},... | collective-permute-start | bytes 786440 | tf_op jit(solution)/shard_map/ppermute | solution.py:29
  203.1 13.3 %collective-permute-start.19 = (f32[2,1,2,16,1024]{4,3,2,0,1:T(8,128)}, f32[2,1,2,16,1024]{4,3,2,0,1:T(8,128)}, u32[]{:S(2)}, u32[]{:S(2)}) collective-permute-start(f32[2,1,2,16,1024]{4,3,2,0,1:T(8,128)} %bitcast_add_fusion.7), channel_id=1, source_target_pairs={{0,448},{64,0},{128,64},{192,128},{256,192},{320,256},{384,320},{4... | collective-permute-start | bytes 786440 | tf_op jit(solution)/shard_map/ppermute | solution.py:29
  210.6 12.0 %copy-start.25 = (bf16[256,512]{0,1:T(8,128)(2,1)S(1)}, bf16[256,512]{0,1:T(8,128)(2,1)}, u32[]{:S(2)}) copy-start(bf16[256,512]{0,1:T(8,128)(2,1)} %copy.104) | copy-start | bytes 786436
  213.2 9.4 %copy-start.23 = (bf16[256,16,32]{0,2,1:T(8,128)(2,1)}, bf16[256,16,32]{0,2,1:T(8,128)(2,1)S(1)}, u32[]{:S(2)}) copy-start(bf16[256,16,32]{0,2,1:T(8,128)(2,1)S(1)} %slice.49) | copy-start | bytes 786436
  214.4 9.1 %collective-permute-start.13 = (f32[2,1,2,16,1024]{4,3,2,0,1:T(8,128)S(1)}, f32[2,1,2,16,1024]{4,3,2,0,1:T(8,128)S(1)}, u32[]{:S(2)}, u32[]{:S(2)}) collective-permute-start(f32[2,1,2,16,1024]{4,3,2,0,1:T(8,128)S(1)} %bitcast_add_fusion.13), channel_id=1, source_target_pairs={{0,64},{64,128},{128,192},{192,256},{256,320},{320,384},{384,448},... | collective-permute-start | bytes 786440 | tf_op jit(solution)/shard_map/ppermute | solution.py:29
  218.1 8.4 %collective-permute-start.20 = (f32[2,1,2,16,1024]{4,3,2,0,1:T(8,128)}, f32[2,1,2,16,1024]{4,3,2,0,1:T(8,128)}, u32[]{:S(2)}, u32[]{:S(2)}) collective-permute-start(f32[2,1,2,16,1024]{4,3,2,0,1:T(8,128)} %bitcast_add_fusion.6), channel_id=1, source_target_pairs={{0,448},{64,0},{128,64},{192,128},{256,192},{320,256},{384,320},{4... | collective-permute-start | bytes 786440 | tf_op jit(solution)/shard_map/ppermute | solution.py:29
  224.6 10.3 %collective-permute-start.14 = (f32[2,1,2,16,1024]{4,3,2,0,1:T(8,128)S(1)}, f32[2,1,2,16,1024]{4,3,2,0,1:T(8,128)S(1)}, u32[]{:S(2)}, u32[]{:S(2)}) collective-permute-start(f32[2,1,2,16,1024]{4,3,2,0,1:T(8,128)S(1)} %bitcast_add_fusion.12), channel_id=1, source_target_pairs={{0,64},{64,128},{128,192},{192,256},{256,320},{320,384},{384,448},... | collective-permute-start | bytes 786440 | tf_op jit(solution)/shard_map/ppermute | solution.py:29
  227.5 17.0 %collective-permute-start.21 = (f32[2,1,2,16,1024]{4,3,2,0,1:T(8,128)S(1)}, f32[2,1,2,16,1024]{4,3,2,0,1:T(8,128)S(1)}, u32[]{:S(2)}, u32[]{:S(2)}) collective-permute-start(f32[2,1,2,16,1024]{4,3,2,0,1:T(8,128)S(1)} %bitcast_add_fusion.5), channel_id=1, source_target_pairs={{0,448},{64,0},{128,64},{192,128},{256,192},{320,256},{384,320},{4... | collective-permute-start | bytes 786440 | tf_op jit(solution)/shard_map/ppermute | solution.py:29
  232.8 17.5 %collective-permute-start.26 = (f32[160,16,16]{0,2,1:T(8,128)S(1)}, f32[160,16,16]{0,2,1:T(8,128)S(1)}, u32[]{:S(2)}, u32[]{:S(2)}) collective-permute-start(f32[160,16,16]{0,2,1:T(8,128)S(1)} %pad_maximum_fusion.2), channel_id=1, source_target_pairs={{0,256},{64,320},{128,384},{192,448},{256,0},{320,64},{384,128},{4... | collective-permute-start | bytes 491528 | tf_op jit(solution)/shard_map/ppermute | solution.py:34
  235.9 16.5 %collective-permute-start.15 = (f32[2,1,2,16,1024]{4,3,2,0,1:T(8,128)S(1)}, f32[2,1,2,16,1024]{4,3,2,0,1:T(8,128)S(1)}, u32[]{:S(2)}, u32[]{:S(2)}) collective-permute-start(f32[2,1,2,16,1024]{4,3,2,0,1:T(8,128)S(1)} %bitcast_add_fusion.11), channel_id=1, source_target_pairs={{0,64},{64,128},{128,192},{192,256},{256,320},{320,384},{384,448},... | collective-permute-start | bytes 786440 | tf_op jit(solution)/shard_map/ppermute | solution.py:29
  244.5 12.2 %collective-permute-start.22 = (f32[2,1,2,16,1024]{4,3,2,0,1:T(8,128)S(1)}, f32[2,1,2,16,1024]{4,3,2,0,1:T(8,128)S(1)}, u32[]{:S(2)}, u32[]{:S(2)}) collective-permute-start(f32[2,1,2,16,1024]{4,3,2,0,1:T(8,128)S(1)} %bitcast_add_fusion.4), channel_id=1, source_target_pairs={{0,448},{64,0},{128,64},{192,128},{256,192},{320,256},{384,320},{4... | collective-permute-start | bytes 786440 | tf_op jit(solution)/shard_map/ppermute | solution.py:29
  250.4 15.5 %collective-permute-start.27 = (f32[160,16,16]{0,2,1:T(8,128)S(1)}, f32[160,16,16]{0,2,1:T(8,128)S(1)}, u32[]{:S(2)}, u32[]{:S(2)}) collective-permute-start(f32[160,16,16]{0,2,1:T(8,128)S(1)} %fusion.31), channel_id=1, source_target_pairs={{0,128},{64,192},{128,0},{192,64},{256,384},{320,448},{384,256},{4... | collective-permute-start | bytes 491528 | tf_op jit(solution)/shard_map/ppermute | solution.py:34
  253.4 14.4 %collective-permute-start.16 = (f32[2,1,2,16,1024]{4,3,2,0,1:T(8,128)S(1)}, f32[2,1,2,16,1024]{4,3,2,0,1:T(8,128)S(1)}, u32[]{:S(2)}, u32[]{:S(2)}) collective-permute-start(f32[2,1,2,16,1024]{4,3,2,0,1:T(8,128)S(1)} %bitcast_add_fusion.10), channel_id=1, source_target_pairs={{0,64},{64,128},{128,192},{192,256},{256,320},{320,384},{384,448},... | collective-permute-start | bytes 786440 | tf_op jit(solution)/shard_map/ppermute | solution.py:29
  257.4 15.6 %collective-permute-start.23 = (f32[2,1,2,16,1024]{4,3,2,0,1:T(8,128)}, f32[2,1,2,16,1024]{4,3,2,0,1:T(8,128)}, u32[]{:S(2)}, u32[]{:S(2)}) collective-permute-start(f32[2,1,2,16,1024]{4,3,2,0,1:T(8,128)} %bitcast_add_fusion.3), channel_id=1, source_target_pairs={{0,448},{64,0},{128,64},{192,128},{256,192},{320,256},{384,320},{4... | collective-permute-start | bytes 786440 | tf_op jit(solution)/shard_map/ppermute | solution.py:29
  265.9 13.8 %collective-permute-start.28 = (f32[160,16,16]{0,2,1:T(8,128)S(1)}, f32[160,16,16]{0,2,1:T(8,128)}, u32[]{:S(2)}, u32[]{:S(2)}) collective-permute-start(f32[160,16,16]{0,2,1:T(8,128)S(1)} %add.282), channel_id=1, source_target_pairs={{0,64},{64,0},{128,192},{192,128},{256,320},{320,256},{384,448},{4... | collective-permute-start | bytes 491528 | tf_op jit(solution)/shard_map/ppermute | solution.py:34
  269.5 20.2 %copy-start.12 = (bf16[256,16,128]{0,2,1:T(8,128)(2,1)S(1)}, bf16[256,16,128]{0,2,1:T(8,128)(2,1)}, u32[]{:S(2)}) copy-start(bf16[256,16,128]{0,2,1:T(8,128)(2,1)} %copy-done.11) | copy-start | bytes 3145732
  269.5 13.8 %collective-permute-start.17 = (f32[2,1,2,16,1024]{4,3,2,0,1:T(8,128)}, f32[2,1,2,16,1024]{4,3,2,0,1:T(8,128)}, u32[]{:S(2)}, u32[]{:S(2)}) collective-permute-start(f32[2,1,2,16,1024]{4,3,2,0,1:T(8,128)} %bitcast_add_fusion.9), channel_id=1, source_target_pairs={{0,64},{64,128},{128,192},{192,256},{256,320},{320,384},{384,448},... | collective-permute-start | bytes 786440 | tf_op jit(solution)/shard_map/ppermute | solution.py:29
  274.8 9.6 %collective-permute-start.24 = (f32[2,1,2,16,1024]{4,3,2,0,1:T(8,128)}, f32[2,1,2,16,1024]{4,3,2,0,1:T(8,128)}, u32[]{:S(2)}, u32[]{:S(2)}) collective-permute-start(f32[2,1,2,16,1024]{4,3,2,0,1:T(8,128)} %bitcast_add_fusion.2), channel_id=1, source_target_pairs={{0,448},{64,0},{128,64},{192,128},{256,192},{320,256},{384,320},{4... | collective-permute-start | bytes 786440 | tf_op jit(solution)/shard_map/ppermute | solution.py:29
  281.4 11.6 %collective-permute-start.29 = (f32[160,16,16]{0,2,1:T(8,128)}, f32[160,16,16]{0,2,1:T(8,128)}, u32[]{:S(2)}, u32[]{:S(2)}) collective-permute-start(f32[160,16,16]{0,2,1:T(8,128)} %add.283), channel_id=1, source_target_pairs={{0,32},{32,0},{1,33},{33,1},{2,34},{34,2},{3,35},{35,3},{4,36},{36... | collective-permute-start | bytes 491528 | tf_op jit(solution)/shard_map/ppermute | solution.py:34
  284.4 7.7 %copy-start.13 = (f32[2,1,2,16,1024]{4,3,2,0,1:T(8,128)}, f32[2,1,2,16,1024]{4,3,2,0,1:T(8,128)S(1)}, u32[]{:S(2)}) copy-start(f32[2,1,2,16,1024]{4,3,2,0,1:T(8,128)S(1)} %bitcast_add_fusion.8) | copy-start | bytes 786436
  286.2 12.1 %copy-start.7 = (bf16[512,512]{1,0:T(8,128)(2,1)S(1)}, bf16[512,512]{1,0:T(8,128)(2,1)}, u32[]{:S(2)}) copy-start(bf16[512,512]{1,0:T(8,128)(2,1)} %copy-done.6) | copy-start | bytes 1572868
  286.2 12.1 %copy-start.24 = (bf16[256,16,32]{0,2,1:T(8,128)(2,1)S(1)}, bf16[256,16,32]{0,2,1:T(8,128)(2,1)}, u32[]{:S(2)}) copy-start(bf16[256,16,32]{0,2,1:T(8,128)(2,1)} %copy-done.23) | copy-start | bytes 786436
  286.2 14.6 %collective-permute-start.25 = (f32[1,2,16,2048]{3,2,1,0:T(8,128)S(1)}, f32[1,2,16,2048]{3,2,1,0:T(8,128)S(1)}, u32[]{:S(2)}, u32[]{:S(2)}) collective-permute-start(f32[1,2,16,2048]{3,2,1,0:T(8,128)S(1)} %fusion.22), channel_id=1, source_target_pairs={{0,32},{32,0},{1,33},{33,1},{2,34},{34,2},{3,35},{35,3},{4,36},{36... | collective-permute-start | bytes 786440 | tf_op jit(solution)/shard_map/ppermute | solution.py:34
  292.1 8.7 %copy-start.16 = (f32[2,1,2,16,1024]{4,3,2,0,1:T(8,128)S(1)}, f32[2,1,2,16,1024]{4,3,2,0,1:T(8,128)}, u32[]{:S(2)}) copy-start(f32[2,1,2,16,1024]{4,3,2,0,1:T(8,128)} %copy-done.15) | copy-start | bytes 786436
  292.9 7.9 %copy-start.14 = (f32[2,1,2,16,1024]{4,3,2,0,1:T(8,128)S(1)}, f32[2,1,2,16,1024]{4,3,2,0,1:T(8,128)}, u32[]{:S(2)}) copy-start(f32[2,1,2,16,1024]{4,3,2,0,1:T(8,128)} %copy-done.13) | copy-start | bytes 786436
  294.0 5.4 %collective-permute-start.30 = (f32[160,16,16]{0,2,1:T(8,128)S(1)}, f32[160,16,16]{0,2,1:T(8,128)S(1)}, u32[]{:S(2)}, u32[]{:S(2)}) collective-permute-start(f32[160,16,16]{0,2,1:T(8,128)S(1)} %add.284), channel_id=1, source_target_pairs={{0,16},{16,0},{1,17},{17,1},{2,18},{18,2},{3,19},{19,3},{4,20},{20... | collective-permute-start | bytes 491528 | tf_op jit(solution)/shard_map/ppermute | solution.py:34
  (13 other events, 26.7 us)

commit v8 on v7

--- a/solution.py
+++ b/solution.py
@@ -37,17 +37,17 @@
 def z_ring_reduce_scatter(x):
     n = x.shape[0]
     me = lax.axis_index("z")
-    lo, hi = jnp.split(x, 2, axis=-1)
+    n_fwd = n // 2
+    n_bwd = n - 1 - n_fwd
     fwd = None
     bwd = None
-    for step in range(1, n):
-        own_f = lax.dynamic_index_in_dim(lo, (me - step) % n, 0, keepdims=False)
-        own_b = lax.dynamic_index_in_dim(hi, (me + step) % n, 0, keepdims=False)
-        fwd = shift(own_f if fwd is None else fwd + own_f, "z", 1)
-        bwd = shift(own_b if bwd is None else bwd + own_b, "z", -1)
-    fwd = fwd + lax.dynamic_index_in_dim(lo, me, 0, keepdims=False)
-    bwd = bwd + lax.dynamic_index_in_dim(hi, me, 0, keepdims=False)
-    return jnp.concatenate([fwd, bwd], axis=-1)
+    for step in range(1, n_fwd + 1):
+        own = lax.dynamic_index_in_dim(x, (me + n_fwd + 1 - step) % n, 0, keepdims=False)
+        fwd = shift(own if fwd is None else fwd + own, "z", 1)
+        if step <= n_bwd:
+            own = lax.dynamic_index_in_dim(x, (me - n_bwd - 1 + step) % n, 0, keepdims=False)
+            bwd = shift(own if bwd is None else bwd + own, "z", -1)
+    return fwd + bwd + lax.dynamic_index_in_dim(x, me, 0, keepdims=False)
 
 
 def z_ring_all_gather(chunk):

time: 304 us -> 301 us (level)
  waiting for transfers between devices: 77.2 us -> 113 us
  starting transfers between devices: 129 us -> 105 us
  other arithmetic: 31.5 us -> 20.2 us
  local copies, waits for them, and re-layouts: 47.6 us -> 43.3 us
    ppermute x22 -> x15, starting transfers between devices: 83.1 us -> 53 us  [shift(): return lax.ppermute(value, axis, [(i, (i + step) % n) for i in range(n)])]
    ppermute x9, waiting for transfers between devices: 14.4 us -> 34.5 us  [swap(): return lax.ppermute(value, axis, [(i, i ^ mask) for i in range(n)])]
    ppermute x22 -> x15, waiting for transfers between devices: 13.5 us -> 29.1 us  [shift(): return lax.ppermute(value, axis, [(i, (i + step) % n) for i in range(n)])]
    add x14 -> x4, other arithmetic: 16.7 us -> 6.11 us  [the longest x2 4.91 us: z_ring_reduce_scatter(): bwd = shift(own if bwd is None else bwd + own, 'z', -1)]
    ppermute x9, starting transfers between devices: 30.5 us -> 36.7 us  [swap(): return lax.ppermute(value, axis, [(i, i ^ mask) for i in range(n)])]
    unnamed x59 -> x43, local copies, waits for them, and re-layouts: 7.82 us -> 5.32 us
  transfers between devices with their start and end apart: 33 -> 26, of which waited for: 13 -> 13; matrix products, arithmetic and copies ran while one was open for 21% -> 17% of each run, Pallas kernels for 0% -> 0%
where the time goes in v8:
time: 301 us; the launch traced here: 299 us
  waiting for transfers between devices  113 us (38%)
  starting transfers between devices  105 us (35%)
  local copies, waits for them, and re-layouts  43.3 us (14%)
  other arithmetic  20.2 us (7%)
  matrix products  16.2 us (5%)
    ppermute x15, starting transfers between devices, shift(): return lax.ppermute(value, axis, [(i, (i + step) % n) for i in range(n)])  53 us
    all_to_all x2, waiting for transfers between devices, exchange(): return lax.all_to_all(wired, FEAT_AXES, 1, 1, tiled=True)  49.3 us
    ppermute x9, starting transfers between devices, swap(): return lax.ppermute(value, axis, [(i, i ^ mask) for i in range(n)])  36.7 us
    ppermute x9, waiting for transfers between devices, swap(): return lax.ppermute(value, axis, [(i, i ^ mask) for i in range(n)])  34.5 us
    ppermute x15, waiting for transfers between devices, shift(): return lax.ppermute(value, axis, [(i, (i + step) % n) for i in range(n)])  29.1 us
    all_to_all x2, starting transfers between devices, exchange(): return lax.all_to_all(wired, FEAT_AXES, 1, 1, tiled=True)  15.2 us
  transfers between devices with their start and end apart: 26, of which 13 were waited for; matrix products, arithmetic and copies ran while one was open for 17% of the time, Pallas kernels for 0%

profile of v8, /device:TPU:1, one launch (start us, length us, event | category | flops | bytes accessed | tf_op | source)
XLA Modules:
  0.0 298.9 jit_solution(5213564849866040293)
XLA Ops:
  2.5 4.0 %collective-permute-start = (bf16[16,4096]{1,0:T(8,128)(2,1)S(1)}, bf16[16,4096]{1,0:T(8,128)(2,1)S(1)}, u32[]{:S(2)}, u32[]{:S(2)}) collective-permute-start(bf16[16,4096]{1,0:T(8,128)(2,1)S(1)} %get-tuple-element.50), channel_id=1, source_target_pairs={{0,32},{32,0},{1,33},{33,1},{2,34},{34,2},{3,35},{35,3},{4,36},{36... | collective-permute-start | bytes 393224 | tf_op jit(solution)/shard_map/ppermute | solution.py:34
  6.6 2.2 collective-permute-done
  8.9 11.4 %collective-permute-start.2 = (bf16[2,16,4096]{2,1,0:T(8,128)(2,1)S(1)}, bf16[2,16,4096]{2,1,0:T(8,128)(2,1)S(1)}, u32[]{:S(2)}, u32[]{:S(2)}) collective-permute-start(bf16[2,16,4096]{2,1,0:T(8,128)(2,1)S(1)} %maximum_select_fusion.2), channel_id=1, source_target_pairs={{0,448},{64,0},{128,64},{192,128},{256,192},{320,256},{384,320},{4... | collective-permute-start | bytes 786440 | tf_op jit(solution)/shard_map/ppermute | solution.py:29
  20.2 1.9 collective-permute-start.1
  24.6 5.0 %collective-permute-start.4 = (bf16[2,16,4096]{2,1,0:T(8,128)(2,1)S(1)}, bf16[2,16,4096]{2,1,0:T(8,128)(2,1)S(1)}, u32[]{:S(2)}, u32[]{:S(2)}) collective-permute-start(bf16[2,16,4096]{2,1,0:T(8,128)(2,1)S(1)} %collective-permute-done.2), channel_id=1, source_target_pairs={{0,448},{64,0},{128,64},{192,128},{256,192},{320,256},{384,320},{4... | collective-permute-start | bytes 786440 | tf_op jit(solution)/shard_map/ppermute | solution.py:29
  29.6 1.9 collective-permute-start.3
  33.0 4.9 %collective-permute-start.6 = (bf16[2,16,4096]{2,1,0:T(8,128)(2,1)S(1)}, bf16[2,16,4096]{2,1,0:T(8,128)(2,1)S(1)}, u32[]{:S(2)}, u32[]{:S(2)}) collective-permute-start(bf16[2,16,4096]{2,1,0:T(8,128)(2,1)S(1)} %collective-permute-done.4), channel_id=1, source_target_pairs={{0,448},{64,0},{128,64},{192,128},{256,192},{320,256},{384,320},{4... | collective-permute-start | bytes 786440 | tf_op jit(solution)/shard_map/ppermute | solution.py:29
  37.9 1.9 collective-permute-start.5
  41.3 4.9 %collective-permute-start.8 = (bf16[2,16,2048]{2,1,0:T(8,128)(2,1)S(1)}, bf16[2,16,2048]{2,1,0:T(8,128)(2,1)S(1)}, u32[]{:S(2)}, u32[]{:S(2)}) collective-permute-start(bf16[2,16,2048]{2,1,0:T(8,128)(2,1)S(1)} %split.9), channel_id=1, source_target_pairs={{0,448},{64,0},{128,64},{192,128},{256,192},{320,256},{384,320},{4... | collective-permute-start | bytes 393224 | tf_op jit(solution)/shard_map/ppermute | solution.py:29
  46.3 1.9 collective-permute-start.7
  49.7 3.5 %collective-permute-done.7 = bf16[2,16,2048]{2,1,0:T(8,128)(2,1)S(1)} collective-permute-done((bf16[2,16,2048]{2,1,0:T(8,128)(2,1)S(1)}, bf16[2,16,2048]{2,1,0:T(8,128)(2,1)S(1)}, u32[]{:S(2)}, u32[]{:S(2)}) %collective-permute-start.7) | collective-permute-done | bytes 131104 | tf_op jit(solution)/shard_map/ppermute | solution.py:29
  53.9 8.1 %collective-permute-start.9 = (bf16[8,2,16,4096]{3,2,1,0:T(8,128)(2,1)}, bf16[8,2,16,4096]{3,2,1,0:T(8,128)(2,1)}, u32[]{:S(2)}, u32[]{:S(2)}) collective-permute-start(bf16[8,2,16,4096]{3,2,1,0:T(8,128)(2,1)} %fusion.22), channel_id=1, source_target_pairs={{0,16},{16,0},{1,17},{17,1},{2,18},{18,2},{3,19},{19,3},{4,20},{20... | collective-permute-start | bytes 6291464 | tf_op jit(solution)/shard_map/ppermute | solution.py:34
  63.6 2.1 reshape.176
  66.1 4.2 %maximum_select_fusion = bf16[8,2,2,16,4096]{4,3,2,1,0:T(8,128)(2,1)S(1)} fusion(bf16[8,2,1,16,4096]{4,3,2,1,0:T(8,128)(2,1)} %bitcast.13, bf16[8,2,1,16,4096]{4,3,2,1,0:T(8,128)(2,1)} %bitcast.12, pred[]{:T(512)S(6)} %eq.26), kind=kLoop, calls=%fused_computation.1 | loop fusion | flops 6291456 | bytes 8388609 | tf_op jit(solution)/shard_map/jit(_where)/select_n | solution.py:96
  73.6 9.4 %all-to-all-start = ((bf16[256,16,160]{0,2,1:T(8,128)(2,1)}), bf16[256,16,160]{0,2,1:T(8,128)(2,1)}, u32[]{:S(2)}, u32[]{:S(2)}) async-start(bf16[256,16,160]{0,2,1:T(8,128)(2,1)} %pad_maximum_fusion), calls=%async_computation | async-start | bytes 2621440 | tf_op jit(solution)/shard_map/all_to_all | solution.py:24
  83.5 3.4 %slice.45 = bf16[512,2048]{1,0:T(8,128)(2,1)} slice(bf16[512,4096]{1,0:T(8,128)(2,1)} %bitcast.147), slice={[0:512], [2048:4096]} | slice | bytes 4194304 | tf_op jit(solution)/shard_map/slice | solution.py:143
  86.9 3.1 %reshape.175 = bf16[2048,512]{1,0:T(8,128)(2,1)S(1)} reshape(bf16[512,2048]{1,0:T(8,128)(2,1)} %slice.45) | data formatting | bytes 4194304 | tf_op jit(solution)/shard_map/reshape.5
  90.0 27.2 %all-to-all-done = bf16[256,16,160]{0,2,1:T(8,128)(2,1)} async-done(((bf16[256,16,160]{0,2,1:T(8,128)(2,1)}), bf16[256,16,160]{0,2,1:T(8,128)(2,1)}, u32[]{:S(2)}, u32[]{:S(2)}) %all-to-all-start) | async-done | bytes 1310752 | tf_op jit(solution)/shard_map/all_to_all | solution.py:24
  120.2 2.1 fusion.4
  125.8 5.8 %all-to-all-start.1 = ((bf16[256,16,160]{0,2,1:T(8,128)(2,1)}), bf16[256,16,160]{0,2,1:T(8,128)(2,1)S(1)}, u32[]{:S(2)}, u32[]{:S(2)}) async-start(bf16[256,16,160]{0,2,1:T(8,128)(2,1)} %copy.90), calls=%async_computation.1 | async-start | bytes 2621440 | tf_op jit(solution)/shard_map/all_to_all | solution.py:24
  131.6 2.8 convolution_bitcast_fusion
  134.4 5.4 %copy.93 = f32[2048,1,512]{2,0,1:T(8,128)} copy(f32[2048,1,512]{0,2,1:T(8,128)} %convolution_bitcast_fusion) | data formatting | bytes 8388608 | tf_op jit(solution)/shard_map/tbh,tbc->hbc/transpose | solution.py:196
  139.8 5.7 %stack.56 = f32[8,2,2,1,1,16,2048]{6,5,2,1,0,4,3:T(8,128)} reshape(f32[2048,1,512]{2,0,1:T(8,128)} %copy.93) | data formatting | bytes 8388608 | tf_op jit(solution)/shard_map/stack | solution.py:229
  145.5 22.0 %all-to-all-done.1 = bf16[256,16,160]{0,2,1:T(8,128)(2,1)S(1)} async-done(((bf16[256,16,160]{0,2,1:T(8,128)(2,1)}), bf16[256,16,160]{0,2,1:T(8,128)(2,1)S(1)}, u32[]{:S(2)}, u32[]{:S(2)}) %all-to-all-start.1) | async-done | bytes 1310752 | tf_op jit(solution)/shard_map/all_to_all | solution.py:24
  173.6 2.9 collective-permute-start.10
  176.4 6.8 %collective-permute-done.10 = f32[8,2,1,2,16,2048]{5,4,3,1,0,2:T(8,128)S(1)} collective-permute-done((f32[8,2,1,2,16,2048]{5,4,3,1,0,2:T(8,128)S(1)}, f32[8,2,1,2,16,2048]{5,4,3,1,0,2:T(8,128)S(1)}, u32[]{:S(2)}, u32[]{:S(2)}) %collective-permute-start.10) | collective-permute-done | bytes 4194336 | tf_op jit(solution)/shard_map/ppermute | solution.py:34
  184.9 1.9 collective-permute-start.11
  186.8 4.6 %collective-permute-start.15 = (f32[2,1,2,16,2048]{4,3,2,0,1:T(8,128)}, f32[2,1,2,16,2048]{4,3,2,0,1:T(8,128)}, u32[]{:S(2)}, u32[]{:S(2)}) collective-permute-start(f32[2,1,2,16,2048]{4,3,2,0,1:T(8,128)} %get-tuple-element.42), channel_id=1, source_target_pairs={{0,448},{64,0},{128,64},{192,128},{256,192},{320,256},{384,320},{4... | collective-permute-start | bytes 1572872 | tf_op jit(solution)/shard_map/ppermute | solution.py:29
  191.4 9.7 %collective-permute-done.11 = f32[2,1,2,16,2048]{4,3,2,0,1:T(8,128)S(1)} collective-permute-done((f32[2,1,2,16,2048]{4,3,2,0,1:T(8,128)S(1)}, f32[2,1,2,16,2048]{4,3,2,0,1:T(8,128)S(1)}, u32[]{:S(2)}, u32[]{:S(2)}) %collective-permute-start.11) | collective-permute-done | bytes 524320 | tf_op jit(solution)/shard_map/ppermute | solution.py:29
  201.2 2.1 collective-permute-start.12
  204.1 12.6 %collective-permute-done.12 = f32[2,1,2,16,2048]{4,3,2,0,1:T(8,128)} collective-permute-done((f32[2,1,2,16,2048]{4,3,2,0,1:T(8,128)S(1)}, f32[2,1,2,16,2048]{4,3,2,0,1:T(8,128)}, u32[]{:S(2)}, u32[]{:S(2)}) %collective-permute-start.12) | collective-permute-done | bytes 524320 | tf_op jit(solution)/shard_map/ppermute | solution.py:29
  216.8 2.6 bitcast_add_fusion.3
  219.4 1.9 collective-permute-start.16
  221.3 3.4 %collective-permute-start.13 = (f32[2,1,2,16,2048]{4,3,2,0,1:T(8,128)}, f32[2,1,2,16,2048]{4,3,2,0,1:T(8,128)}, u32[]{:S(2)}, u32[]{:S(2)}) collective-permute-start(f32[2,1,2,16,2048]{4,3,2,0,1:T(8,128)} %get-tuple-element.41), channel_id=1, source_target_pairs={{0,64},{64,128},{128,192},{192,256},{256,320},{320,384},{384,448},... | collective-permute-start | bytes 1572872 | tf_op jit(solution)/shard_map/ppermute | solution.py:29
  224.7 3.0 convolution_multiply_fusion
  230.8 2.1 collective-permute-start.19
  232.9 3.1 %collective-permute-done.13 = f32[2,1,2,16,2048]{4,3,2,0,1:T(8,128)} collective-permute-done((f32[2,1,2,16,2048]{4,3,2,0,1:T(8,128)}, f32[2,1,2,16,2048]{4,3,2,0,1:T(8,128)}, u32[]{:S(2)}, u32[]{:S(2)}) %collective-permute-start.13) | collective-permute-done | bytes 524320 | tf_op jit(solution)/shard_map/ppermute | solution.py:29
  236.0 2.3 bitcast_add_fusion.2
  240.2 3.4 %collective-permute-start.14 = (f32[2,1,2,16,2048]{4,3,2,0,1:T(8,128)S(1)}, f32[2,1,2,16,2048]{4,3,2,0,1:T(8,128)S(1)}, u32[]{:S(2)}, u32[]{:S(2)}) collective-permute-start(f32[2,1,2,16,2048]{4,3,2,0,1:T(8,128)S(1)} %get-tuple-element.39), channel_id=1, source_target_pairs={{0,64},{64,128},{128,192},{192,256},{256,320},{320,384},{384,448},... | collective-permute-start | bytes 1572872 | tf_op jit(solution)/shard_map/ppermute | solution.py:29
  243.6 4.9 %collective-permute-done.19 = f32[160,16,16]{0,2,1:T(8,128)S(1)} collective-permute-done((f32[160,16,16]{0,2,1:T(8,128)S(1)}, f32[160,16,16]{0,2,1:T(8,128)S(1)}, u32[]{:S(2)}, u32[]{:S(2)}) %collective-permute-start.19) | collective-permute-done | bytes 163872 | tf_op jit(solution)/shard_map/ppermute | solution.py:34
  248.5 2.1 collective-permute-start.20
  250.6 12.3 %collective-permute-done.20 = f32[160,16,16]{0,2,1:T(8,128)S(1)} collective-permute-done((f32[160,16,16]{0,2,1:T(8,128)S(1)}, f32[160,16,16]{0,2,1:T(8,128)S(1)}, u32[]{:S(2)}, u32[]{:S(2)}) %collective-permute-start.20) | collective-permute-done | bytes 163872 | tf_op jit(solution)/shard_map/ppermute | solution.py:34
  262.9 1.9 collective-permute-start.21
  264.9 8.1 %collective-permute-done.21 = f32[160,16,16]{0,2,1:T(8,128)} collective-permute-done((f32[160,16,16]{0,2,1:T(8,128)S(1)}, f32[160,16,16]{0,2,1:T(8,128)}, u32[]{:S(2)}, u32[]{:S(2)}) %collective-permute-start.21) | collective-permute-done | bytes 163872 | tf_op jit(solution)/shard_map/ppermute | solution.py:34
  274.0 1.9 collective-permute-start.22
  277.1 3.5 %collective-permute-start.18 = (f32[1,2,16,2048]{3,2,1,0:T(8,128)S(1)}, f32[1,2,16,2048]{3,2,1,0:T(8,128)S(1)}, u32[]{:S(2)}, u32[]{:S(2)}) collective-permute-start(f32[1,2,16,2048]{3,2,1,0:T(8,128)S(1)} %dynamic-slice_bitcast_fusion.2), channel_id=1, source_target_pairs={{0,32},{32,0},{1,33},{33,1},{2,34},{34,2},{3,35},{35,3},{4,36},{36... | collective-permute-start | bytes 786440 | tf_op jit(solution)/shard_map/ppermute | solution.py:34
  280.6 2.3 fusion.15
  284.8 10.2 %collective-permute-start.23 = (f32[160,16,16]{0,2,1:T(8,128)S(1)}, f32[160,16,16]{0,2,1:T(8,128)S(1)}, u32[]{:S(2)}, u32[]{:S(2)}) collective-permute-start(f32[160,16,16]{0,2,1:T(8,128)S(1)} %add.213), channel_id=1, source_target_pairs={{0,16},{16,0},{1,17},{17,1},{2,18},{18,2},{3,19},{19,3},{4,20},{20... | collective-permute-start | bytes 491528 | tf_op jit(solution)/shard_map/ppermute | solution.py:34
  (114 shorter events, 43.0 us)
Async XLA Ops:
  0.6 69.7 %copy-start = (bf16[256,512]{1,0:T(8,128)(2,1)S(1)}, bf16[256,512]{1,0:T(8,128)(2,1)}, u32[]{:S(2)}) copy-start(bf16[256,512]{1,0:T(8,128)(2,1)} %param.6) | copy-start | bytes 786436
  2.5 6.4 %collective-permute-start = (bf16[16,4096]{1,0:T(8,128)(2,1)S(1)}, bf16[16,4096]{1,0:T(8,128)(2,1)S(1)}, u32[]{:S(2)}, u32[]{:S(2)}) collective-permute-start(bf16[16,4096]{1,0:T(8,128)(2,1)S(1)} %get-tuple-element.50), channel_id=1, source_target_pairs={{0,32},{32,0},{1,33},{33,1},{2,34},{34,2},{3,35},{35,3},{4,36},{36... | collective-permute-start | bytes 393224 | tf_op jit(solution)/shard_map/ppermute | solution.py:34
  8.9 15.7 %collective-permute-start.2 = (bf16[2,16,4096]{2,1,0:T(8,128)(2,1)S(1)}, bf16[2,16,4096]{2,1,0:T(8,128)(2,1)S(1)}, u32[]{:S(2)}, u32[]{:S(2)}) collective-permute-start(bf16[2,16,4096]{2,1,0:T(8,128)(2,1)S(1)} %maximum_select_fusion.2), channel_id=1, source_target_pairs={{0,448},{64,0},{128,64},{192,128},{256,192},{320,256},{384,320},{4... | collective-permute-start | bytes 786440 | tf_op jit(solution)/shard_map/ppermute | solution.py:29
  20.2 9.3 %collective-permute-start.1 = (bf16[2,16,4096]{2,1,0:T(8,128)(2,1)S(1)}, bf16[2,16,4096]{2,1,0:T(8,128)(2,1)S(1)}, u32[]{:S(2)}, u32[]{:S(2)}) collective-permute-start(bf16[2,16,4096]{2,1,0:T(8,128)(2,1)S(1)} %maximum_select_fusion.2), channel_id=1, source_target_pairs={{0,64},{64,128},{128,192},{192,256},{256,320},{320,384},{384,448},... | collective-permute-start | bytes 786440 | tf_op jit(solution)/shard_map/ppermute | solution.py:29
  24.5 37.5 %copy-start.18 = (bf16[32,16,16]{0,2,1:T(8,128)(2,1)S(1)}, bf16[32,16,16]{0,2,1:T(8,128)(2,1)}, u32[]{:S(2)}) copy-start(bf16[32,16,16]{0,2,1:T(8,128)(2,1)} %param.10) | copy-start | bytes 49156
  24.6 8.5 %collective-permute-start.4 = (bf16[2,16,4096]{2,1,0:T(8,128)(2,1)S(1)}, bf16[2,16,4096]{2,1,0:T(8,128)(2,1)S(1)}, u32[]{:S(2)}, u32[]{:S(2)}) collective-permute-start(bf16[2,16,4096]{2,1,0:T(8,128)(2,1)S(1)} %collective-permute-done.2), channel_id=1, source_target_pairs={{0,448},{64,0},{128,64},{192,128},{256,192},{320,256},{384,320},{4... | collective-permute-start | bytes 786440 | tf_op jit(solution)/shard_map/ppermute | solution.py:29
  29.6 8.3 %collective-permute-start.3 = (bf16[2,16,4096]{2,1,0:T(8,128)(2,1)S(1)}, bf16[2,16,4096]{2,1,0:T(8,128)(2,1)S(1)}, u32[]{:S(2)}, u32[]{:S(2)}) collective-permute-start(bf16[2,16,4096]{2,1,0:T(8,128)(2,1)S(1)} %collective-permute-done.1), channel_id=1, source_target_pairs={{0,64},{64,128},{128,192},{192,256},{256,320},{320,384},{384,448},... | collective-permute-start | bytes 786440 | tf_op jit(solution)/shard_map/ppermute | solution.py:29
  33.0 8.3 %collective-permute-start.6 = (bf16[2,16,4096]{2,1,0:T(8,128)(2,1)S(1)}, bf16[2,16,4096]{2,1,0:T(8,128)(2,1)S(1)}, u32[]{:S(2)}, u32[]{:S(2)}) collective-permute-start(bf16[2,16,4096]{2,1,0:T(8,128)(2,1)S(1)} %collective-permute-done.4), channel_id=1, source_target_pairs={{0,448},{64,0},{128,64},{192,128},{256,192},{320,256},{384,320},{4... | collective-permute-start | bytes 786440 | tf_op jit(solution)/shard_map/ppermute | solution.py:29
  37.9 8.3 %collective-permute-start.5 = (bf16[2,16,4096]{2,1,0:T(8,128)(2,1)S(1)}, bf16[2,16,4096]{2,1,0:T(8,128)(2,1)S(1)}, u32[]{:S(2)}, u32[]{:S(2)}) collective-permute-start(bf16[2,16,4096]{2,1,0:T(8,128)(2,1)S(1)} %collective-permute-done.3), channel_id=1, source_target_pairs={{0,64},{64,128},{128,192},{192,256},{256,320},{320,384},{384,448},... | collective-permute-start | bytes 786440 | tf_op jit(solution)/shard_map/ppermute | solution.py:29
  41.3 8.3 %collective-permute-start.8 = (bf16[2,16,2048]{2,1,0:T(8,128)(2,1)S(1)}, bf16[2,16,2048]{2,1,0:T(8,128)(2,1)S(1)}, u32[]{:S(2)}, u32[]{:S(2)}) collective-permute-start(bf16[2,16,2048]{2,1,0:T(8,128)(2,1)S(1)} %split.9), channel_id=1, source_target_pairs={{0,448},{64,0},{128,64},{192,128},{256,192},{320,256},{384,320},{4... | collective-permute-start | bytes 393224 | tf_op jit(solution)/shard_map/ppermute | solution.py:29
  46.3 6.9 %collective-permute-start.7 = (bf16[2,16,2048]{2,1,0:T(8,128)(2,1)S(1)}, bf16[2,16,2048]{2,1,0:T(8,128)(2,1)S(1)}, u32[]{:S(2)}, u32[]{:S(2)}) collective-permute-start(bf16[2,16,2048]{2,1,0:T(8,128)(2,1)S(1)} %split.8), channel_id=1, source_target_pairs={{0,64},{64,128},{128,192},{192,256},{256,320},{320,384},{384,448},... | collective-permute-start | bytes 393224 | tf_op jit(solution)/shard_map/ppermute | solution.py:29
  53.9 12.2 %collective-permute-start.9 = (bf16[8,2,16,4096]{3,2,1,0:T(8,128)(2,1)}, bf16[8,2,16,4096]{3,2,1,0:T(8,128)(2,1)}, u32[]{:S(2)}, u32[]{:S(2)}) collective-permute-start(bf16[8,2,16,4096]{3,2,1,0:T(8,128)(2,1)} %fusion.22), channel_id=1, source_target_pairs={{0,16},{16,0},{1,17},{17,1},{2,18},{18,2},{3,19},{19,3},{4,20},{20... | collective-permute-start | bytes 6291464 | tf_op jit(solution)/shard_map/ppermute | solution.py:34
  62.2 3.5 %copy-start.16 = (bf16[256,512]{1,0:T(8,128)(2,1)S(1)}, bf16[256,512]{1,0:T(8,128)(2,1)}, u32[]{:S(2)}) copy-start(bf16[256,512]{1,0:T(8,128)(2,1)} %param.11) | copy-start | bytes 786436
  65.6 4.7 %copy-start.5 = (bf16[512,512]{1,0:T(8,128)(2,1)}, bf16[512,512]{1,0:T(8,128)(2,1)S(1)}, u32[]{:S(2)}) copy-start(bf16[512,512]{1,0:T(8,128)(2,1)S(1)} %reshape.176) | copy-start | bytes 1572868
  70.4 2.0 copy-start.4
  72.3 10.7 %copy-start.19 = (bf16[128,16,16]{0,2,1:T(8,128)(2,1)S(1)}, bf16[128,16,16]{0,2,1:T(8,128)(2,1)}, u32[]{:S(2)}) copy-start(bf16[128,16,16]{0,2,1:T(8,128)(2,1)} %param.8) | copy-start | bytes 196612
  73.6 43.6 %all-to-all-start = ((bf16[256,16,160]{0,2,1:T(8,128)(2,1)}), bf16[256,16,160]{0,2,1:T(8,128)(2,1)}, u32[]{:S(2)}, u32[]{:S(2)}) async-start(bf16[256,16,160]{0,2,1:T(8,128)(2,1)} %pad_maximum_fusion), calls=%async_computation | async-start | bytes 2621440 | tf_op jit(solution)/shard_map/all_to_all | solution.py:24
  83.5 36.8 %copy-start.14 = (bf16[128,16,16]{2,1,0:T(8,128)(2,1)}, bf16[128,16,16]{2,1,0:T(8,128)(2,1)S(1)}, u32[]{:S(2)}) copy-start(bf16[128,16,16]{2,1,0:T(8,128)(2,1)S(1)} %copy.88) | copy-start | bytes 196612
  118.2 0.7 copy-start.12
  120.2 2.1 copy-start.7
  122.3 1.3 copy-start.9
  122.7 1.1 copy-start.15
  124.3 7.3 %copy-start.13 = (bf16[256,16,32]{0,2,1:T(8,128)(2,1)S(1)}, bf16[256,16,32]{0,2,1:T(8,128)(2,1)}, u32[]{:S(2)}) copy-start(bf16[256,16,32]{0,2,1:T(8,128)(2,1)} %copy-done.12) | copy-start | bytes 786436
  125.8 41.7 %all-to-all-start.1 = ((bf16[256,16,160]{0,2,1:T(8,128)(2,1)}), bf16[256,16,160]{0,2,1:T(8,128)(2,1)S(1)}, u32[]{:S(2)}, u32[]{:S(2)}) async-start(bf16[256,16,160]{0,2,1:T(8,128)(2,1)} %copy.90), calls=%async_computation.1 | async-start | bytes 2621440 | tf_op jit(solution)/shard_map/all_to_all | solution.py:24
  167.6 1.0 copy-start.10
  167.6 2.6 copy-start.3
  173.6 9.6 %collective-permute-start.10 = (f32[8,2,1,2,16,2048]{5,4,3,1,0,2:T(8,128)S(1)}, f32[8,2,1,2,16,2048]{5,4,3,1,0,2:T(8,128)S(1)}, u32[]{:S(2)}, u32[]{:S(2)}) collective-permute-start(f32[8,2,1,2,16,2048]{5,4,3,1,0,2:T(8,128)S(1)} %bitcast.152), channel_id=1, source_target_pairs={{0,16},{16,0},{1,17},{17,1},{2,18},{18,2},{3,19},{19,3},{4,20},{20... | collective-permute-start | bytes 12582920 | tf_op jit(solution)/shard_map/ppermute | solution.py:34
  184.0 17.1 %copy-start.2 = (f32[8,2,1,2,16,2048]{5,4,3,1,0,2:T(8,128)}, f32[8,2,1,2,16,2048]{5,4,3,1,0,2:T(8,128)S(1)}, u32[]{:S(2)}) copy-start(f32[8,2,1,2,16,2048]{5,4,3,1,0,2:T(8,128)S(1)} %bitcast_add_fusion) | copy-start | bytes 12582916
  184.0 19.3 %copy-start.17 = (bf16[256,512]{1,0:T(8,128)(2,1)S(1)}, bf16[256,512]{1,0:T(8,128)(2,1)}, u32[]{:S(2)}) copy-start(bf16[256,512]{1,0:T(8,128)(2,1)} %param.11) | copy-start | bytes 786436
  184.9 16.2 %collective-permute-start.11 = (f32[2,1,2,16,2048]{4,3,2,0,1:T(8,128)S(1)}, f32[2,1,2,16,2048]{4,3,2,0,1:T(8,128)S(1)}, u32[]{:S(2)}, u32[]{:S(2)}) collective-permute-start(f32[2,1,2,16,2048]{4,3,2,0,1:T(8,128)S(1)} %get-tuple-element.43), channel_id=1, source_target_pairs={{0,64},{64,128},{128,192},{192,256},{256,320},{320,384},{384,448},... | collective-permute-start | bytes 1572872 | tf_op jit(solution)/shard_map/ppermute | solution.py:29
  186.8 17.3 %collective-permute-start.15 = (f32[2,1,2,16,2048]{4,3,2,0,1:T(8,128)}, f32[2,1,2,16,2048]{4,3,2,0,1:T(8,128)}, u32[]{:S(2)}, u32[]{:S(2)}) collective-permute-start(f32[2,1,2,16,2048]{4,3,2,0,1:T(8,128)} %get-tuple-element.42), channel_id=1, source_target_pairs={{0,448},{64,0},{128,64},{192,128},{256,192},{320,256},{384,320},{4... | collective-permute-start | bytes 1572872 | tf_op jit(solution)/shard_map/ppermute | solution.py:29
  201.2 23.5 %copy-start.8 = (bf16[256,16,128]{0,2,1:T(8,128)(2,1)S(1)}, bf16[256,16,128]{0,2,1:T(8,128)(2,1)}, u32[]{:S(2)}) copy-start(bf16[256,16,128]{0,2,1:T(8,128)(2,1)} %copy-done.7) | copy-start | bytes 3145732
  201.2 15.6 %collective-permute-start.12 = (f32[2,1,2,16,2048]{4,3,2,0,1:T(8,128)S(1)}, f32[2,1,2,16,2048]{4,3,2,0,1:T(8,128)}, u32[]{:S(2)}, u32[]{:S(2)}) collective-permute-start(f32[2,1,2,16,2048]{4,3,2,0,1:T(8,128)S(1)} %bitcast_add_fusion.6), channel_id=1, source_target_pairs={{0,64},{64,128},{128,192},{192,256},{256,320},{320,384},{384,448},... | collective-permute-start | bytes 1572872 | tf_op jit(solution)/shard_map/ppermute | solution.py:29
  219.4 13.5 %collective-permute-start.16 = (f32[2,1,2,16,2048]{4,3,2,0,1:T(8,128)}, f32[2,1,2,16,2048]{4,3,2,0,1:T(8,128)S(1)}, u32[]{:S(2)}, u32[]{:S(2)}) collective-permute-start(f32[2,1,2,16,2048]{4,3,2,0,1:T(8,128)} %get-tuple-element.40), channel_id=1, source_target_pairs={{0,448},{64,0},{128,64},{192,128},{256,192},{320,256},{384,320},{4... | collective-permute-start | bytes 1572872 | tf_op jit(solution)/shard_map/ppermute | solution.py:29
  221.3 14.7 %collective-permute-start.13 = (f32[2,1,2,16,2048]{4,3,2,0,1:T(8,128)}, f32[2,1,2,16,2048]{4,3,2,0,1:T(8,128)}, u32[]{:S(2)}, u32[]{:S(2)}) collective-permute-start(f32[2,1,2,16,2048]{4,3,2,0,1:T(8,128)} %get-tuple-element.41), channel_id=1, source_target_pairs={{0,64},{64,128},{128,192},{192,256},{256,320},{320,384},{384,448},... | collective-permute-start | bytes 1572872 | tf_op jit(solution)/shard_map/ppermute | solution.py:29
  230.8 17.7 %collective-permute-start.19 = (f32[160,16,16]{0,2,1:T(8,128)S(1)}, f32[160,16,16]{0,2,1:T(8,128)S(1)}, u32[]{:S(2)}, u32[]{:S(2)}) collective-permute-start(f32[160,16,16]{0,2,1:T(8,128)S(1)} %pad_maximum_fusion.2), channel_id=1, source_target_pairs={{0,256},{64,320},{128,384},{192,448},{256,0},{320,64},{384,128},{4... | collective-permute-start | bytes 491528 | tf_op jit(solution)/shard_map/ppermute | solution.py:34
  238.3 37.6 %collective-permute-start.17 = (f32[2,1,2,16,2048]{4,3,2,0,1:T(8,128)}, f32[2,1,2,16,2048]{4,3,2,0,1:T(8,128)S(1)}, u32[]{:S(2)}, u32[]{:S(2)}) collective-permute-start(f32[2,1,2,16,2048]{4,3,2,0,1:T(8,128)} %get-tuple-element.38), channel_id=1, source_target_pairs={{0,448},{64,0},{128,64},{192,128},{256,192},{320,256},{384,320},{4... | collective-permute-start | bytes 1572872 | tf_op jit(solution)/shard_map/ppermute | solution.py:29
  240.2 35.7 %collective-permute-start.14 = (f32[2,1,2,16,2048]{4,3,2,0,1:T(8,128)S(1)}, f32[2,1,2,16,2048]{4,3,2,0,1:T(8,128)S(1)}, u32[]{:S(2)}, u32[]{:S(2)}) collective-permute-start(f32[2,1,2,16,2048]{4,3,2,0,1:T(8,128)S(1)} %get-tuple-element.39), channel_id=1, source_target_pairs={{0,64},{64,128},{128,192},{192,256},{256,320},{320,384},{384,448},... | collective-permute-start | bytes 1572872 | tf_op jit(solution)/shard_map/ppermute | solution.py:29
  248.5 32.1 %copy-start.11 = (bf16[256,16,128]{0,2,1:T(8,128)(2,1)S(1)}, bf16[256,16,128]{0,2,1:T(8,128)(2,1)}, u32[]{:S(2)}) copy-start(bf16[256,16,128]{0,2,1:T(8,128)(2,1)} %copy-done.10) | copy-start | bytes 3145732
  248.5 14.4 %collective-permute-start.20 = (f32[160,16,16]{0,2,1:T(8,128)S(1)}, f32[160,16,16]{0,2,1:T(8,128)S(1)}, u32[]{:S(2)}, u32[]{:S(2)}) collective-permute-start(f32[160,16,16]{0,2,1:T(8,128)S(1)} %fusion.26), channel_id=1, source_target_pairs={{0,128},{64,192},{128,0},{192,64},{256,384},{320,448},{384,256},{4... | collective-permute-start | bytes 491528 | tf_op jit(solution)/shard_map/ppermute | solution.py:34
  262.9 10.0 %collective-permute-start.21 = (f32[160,16,16]{0,2,1:T(8,128)S(1)}, f32[160,16,16]{0,2,1:T(8,128)}, u32[]{:S(2)}, u32[]{:S(2)}) collective-permute-start(f32[160,16,16]{0,2,1:T(8,128)S(1)} %add.211), channel_id=1, source_target_pairs={{0,64},{64,0},{128,192},{192,128},{256,320},{320,256},{384,448},{4... | collective-permute-start | bytes 491528 | tf_op jit(solution)/shard_map/ppermute | solution.py:34
  274.0 9.8 %collective-permute-start.22 = (f32[160,16,16]{0,2,1:T(8,128)S(1)}, f32[160,16,16]{0,2,1:T(8,128)}, u32[]{:S(2)}, u32[]{:S(2)}) collective-permute-start(f32[160,16,16]{0,2,1:T(8,128)S(1)} %add.212), channel_id=1, source_target_pairs={{0,32},{32,0},{1,33},{33,1},{2,34},{34,2},{3,35},{35,3},{4,36},{36... | collective-permute-start | bytes 491528 | tf_op jit(solution)/shard_map/ppermute | solution.py:34
  277.1 18.0 %copy-start.6 = (bf16[512,512]{1,0:T(8,128)(2,1)S(1)}, bf16[512,512]{1,0:T(8,128)(2,1)}, u32[]{:S(2)}) copy-start(bf16[512,512]{1,0:T(8,128)(2,1)} %copy-done.5) | copy-start | bytes 1572868
  277.1 20.5 %collective-permute-start.18 = (f32[1,2,16,2048]{3,2,1,0:T(8,128)S(1)}, f32[1,2,16,2048]{3,2,1,0:T(8,128)S(1)}, u32[]{:S(2)}, u32[]{:S(2)}) collective-permute-start(f32[1,2,16,2048]{3,2,1,0:T(8,128)S(1)} %dynamic-slice_bitcast_fusion.2), channel_id=1, source_target_pairs={{0,32},{32,0},{1,33},{33,1},{2,34},{34,2},{3,35},{35,3},{4,36},{36... | collective-permute-start | bytes 786440 | tf_op jit(solution)/shard_map/ppermute | solution.py:34
  283.8 15.2 %copy-start.1 = (bf16[256,512]{1,0:T(8,128)(2,1)S(1)}, bf16[256,512]{1,0:T(8,128)(2,1)}, u32[]{:S(2)}) copy-start(bf16[256,512]{1,0:T(8,128)(2,1)} %param.6) | copy-start | bytes 786436
  284.8 11.4 %collective-permute-start.23 = (f32[160,16,16]{0,2,1:T(8,128)S(1)}, f32[160,16,16]{0,2,1:T(8,128)S(1)}, u32[]{:S(2)}, u32[]{:S(2)}) collective-permute-start(f32[160,16,16]{0,2,1:T(8,128)S(1)} %add.213), channel_id=1, source_target_pairs={{0,16},{16,0},{1,17},{17,1},{2,18},{18,2},{3,19},{19,3},{4,20},{20... | collective-permute-start | bytes 491528 | tf_op jit(solution)/shard_map/ppermute | solution.py:34

commit v9 on v8

--- a/solution.py
+++ b/solution.py
@@ -43,10 +43,13 @@
     bwd = None
     for step in range(1, n_fwd + 1):
         own = lax.dynamic_index_in_dim(x, (me + n_fwd + 1 - step) % n, 0, keepdims=False)
-        fwd = shift(own if fwd is None else fwd + own, "z", 1)
+        fwd = own if fwd is None else fwd + own
         if step <= n_bwd:
             own = lax.dynamic_index_in_dim(x, (me - n_bwd - 1 + step) % n, 0, keepdims=False)
-            bwd = shift(own if bwd is None else bwd + own, "z", -1)
+            bwd = own if bwd is None else bwd + own
+            fwd, bwd = lax.optimization_barrier((fwd, bwd))
+            bwd = shift(bwd, "z", -1)
+        fwd = shift(fwd, "z", 1)
     return fwd + bwd + lax.dynamic_index_in_dim(x, me, 0, keepdims=False)
 
 

time: 301 us -> 304 us (level)
  starting transfers between devices: 105 us -> 112 us
    ppermute x15, waiting for transfers between devices: 29.1 us -> 23 us  [shift(): return lax.ppermute(value, axis, [(i, (i + step) % n) for i in range(n)])]
    ppermute x9, starting transfers between devices: 36.7 us -> 42 us  [swap(): return lax.ppermute(value, axis, [(i, i ^ mask) for i in range(n)])]
  transfers between devices with their start and end apart: 26 -> 26, of which waited for: 13 -> 14; matrix products, arithmetic and copies ran while one was open for 17% -> 16% of each run, Pallas kernels for 0% -> 0%
where the time goes in v9:
time: 304 us; the launch traced here: 302 us
  starting transfers between devices  112 us (37%)
  waiting for transfers between devices  110 us (36%)
  local copies, waits for them, and re-layouts  42.5 us (14%)
  other arithmetic  19.9 us (7%)
  matrix products  16.2 us (5%)
    ppermute x15, starting transfers between devices, shift(): return lax.ppermute(value, axis, [(i, (i + step) % n) for i in range(n)])  55.1 us
    all_to_all x2, waiting for transfers between devices, exchange(): return lax.all_to_all(wired, FEAT_AXES, 1, 1, tiled=True)  49.3 us
    ppermute x9, starting transfers between devices, swap(): return lax.ppermute(value, axis, [(i, i ^ mask) for i in range(n)])  42 us
    ppermute x9, waiting for transfers between devices, swap(): return lax.ppermute(value, axis, [(i, i ^ mask) for i in range(n)])  37.3 us
    ppermute x15, waiting for transfers between devices, shift(): return lax.ppermute(value, axis, [(i, (i + step) % n) for i in range(n)])  23 us
    all_to_all x2, starting transfers between devices, exchange(): return lax.all_to_all(wired, FEAT_AXES, 1, 1, tiled=True)  15.2 us
  transfers between devices with their start and end apart: 26, of which 14 were waited for; matrix products, arithmetic and copies ran while one was open for 16% of the time, Pallas kernels for 0%

profile of v9, /device:TPU:1, one launch (start us, length us, event | category | flops | bytes accessed | tf_op | source)
XLA Modules:
  0.0 302.0 jit_solution(17864950837039151903)
XLA Ops:
  2.5 4.0 %collective-permute-start = (bf16[16,4096]{1,0:T(8,128)(2,1)S(1)}, bf16[16,4096]{1,0:T(8,128)(2,1)S(1)}, u32[]{:S(2)}, u32[]{:S(2)}) collective-permute-start(bf16[16,4096]{1,0:T(8,128)(2,1)S(1)} %get-tuple-element.62), channel_id=1, source_target_pairs={{0,32},{32,0},{1,33},{33,1},{2,34},{34,2},{3,35},{35,3},{4,36},{36... | collective-permute-start | bytes 393224 | tf_op jit(solution)/shard_map/ppermute | solution.py:34
  6.6 2.2 collective-permute-done
  8.9 11.4 %collective-permute-start.2 = (bf16[2,16,4096]{2,1,0:T(8,128)(2,1)S(1)}, bf16[2,16,4096]{2,1,0:T(8,128)(2,1)S(1)}, u32[]{:S(2)}, u32[]{:S(2)}) collective-permute-start(bf16[2,16,4096]{2,1,0:T(8,128)(2,1)S(1)} %maximum_select_fusion.2), channel_id=1, source_target_pairs={{0,448},{64,0},{128,64},{192,128},{256,192},{320,256},{384,320},{4... | collective-permute-start | bytes 786440 | tf_op jit(solution)/shard_map/ppermute | solution.py:29
  20.2 1.9 collective-permute-start.1
  24.6 5.0 %collective-permute-start.4 = (bf16[2,16,4096]{2,1,0:T(8,128)(2,1)S(1)}, bf16[2,16,4096]{2,1,0:T(8,128)(2,1)S(1)}, u32[]{:S(2)}, u32[]{:S(2)}) collective-permute-start(bf16[2,16,4096]{2,1,0:T(8,128)(2,1)S(1)} %collective-permute-done.2), channel_id=1, source_target_pairs={{0,448},{64,0},{128,64},{192,128},{256,192},{320,256},{384,320},{4... | collective-permute-start | bytes 786440 | tf_op jit(solution)/shard_map/ppermute | solution.py:29
  29.6 1.9 collective-permute-start.3
  33.0 4.9 %collective-permute-start.6 = (bf16[2,16,4096]{2,1,0:T(8,128)(2,1)S(1)}, bf16[2,16,4096]{2,1,0:T(8,128)(2,1)S(1)}, u32[]{:S(2)}, u32[]{:S(2)}) collective-permute-start(bf16[2,16,4096]{2,1,0:T(8,128)(2,1)S(1)} %collective-permute-done.4), channel_id=1, source_target_pairs={{0,448},{64,0},{128,64},{192,128},{256,192},{320,256},{384,320},{4... | collective-permute-start | bytes 786440 | tf_op jit(solution)/shard_map/ppermute | solution.py:29
  37.9 1.9 collective-permute-start.5
  41.3 4.9 %collective-permute-start.8 = (bf16[2,16,2048]{2,1,0:T(8,128)(2,1)S(1)}, bf16[2,16,2048]{2,1,0:T(8,128)(2,1)S(1)}, u32[]{:S(2)}, u32[]{:S(2)}) collective-permute-start(bf16[2,16,2048]{2,1,0:T(8,128)(2,1)S(1)} %split.9), channel_id=1, source_target_pairs={{0,448},{64,0},{128,64},{192,128},{256,192},{320,256},{384,320},{4... | collective-permute-start | bytes 393224 | tf_op jit(solution)/shard_map/ppermute | solution.py:29
  46.3 1.9 collective-permute-start.7
  49.7 3.5 %collective-permute-done.7 = bf16[2,16,2048]{2,1,0:T(8,128)(2,1)S(1)} collective-permute-done((bf16[2,16,2048]{2,1,0:T(8,128)(2,1)S(1)}, bf16[2,16,2048]{2,1,0:T(8,128)(2,1)S(1)}, u32[]{:S(2)}, u32[]{:S(2)}) %collective-permute-start.7) | collective-permute-done | bytes 131104 | tf_op jit(solution)/shard_map/ppermute | solution.py:29
  53.9 8.1 %collective-permute-start.9 = (bf16[8,2,16,4096]{3,2,1,0:T(8,128)(2,1)}, bf16[8,2,16,4096]{3,2,1,0:T(8,128)(2,1)}, u32[]{:S(2)}, u32[]{:S(2)}) collective-permute-start(bf16[8,2,16,4096]{3,2,1,0:T(8,128)(2,1)} %fusion.22), channel_id=1, source_target_pairs={{0,16},{16,0},{1,17},{17,1},{2,18},{18,2},{3,19},{19,3},{4,20},{20... | collective-permute-start | bytes 6291464 | tf_op jit(solution)/shard_map/ppermute | solution.py:34
  63.6 2.1 reshape.176
  66.1 4.2 %maximum_select_fusion = bf16[8,2,2,16,4096]{4,3,2,1,0:T(8,128)(2,1)S(1)} fusion(bf16[8,2,1,16,4096]{4,3,2,1,0:T(8,128)(2,1)} %bitcast.13, bf16[8,2,1,16,4096]{4,3,2,1,0:T(8,128)(2,1)} %bitcast.12, pred[]{:T(512)S(6)} %eq.26), kind=kLoop, calls=%fused_computation.1 | loop fusion | flops 6291456 | bytes 8388609 | tf_op jit(solution)/shard_map/jit(_where)/select_n | solution.py:99
  73.6 9.4 %all-to-all-start = ((bf16[256,16,160]{0,2,1:T(8,128)(2,1)}), bf16[256,16,160]{0,2,1:T(8,128)(2,1)}, u32[]{:S(2)}, u32[]{:S(2)}) async-start(bf16[256,16,160]{0,2,1:T(8,128)(2,1)} %pad_maximum_fusion), calls=%async_computation | async-start | bytes 2621440 | tf_op jit(solution)/shard_map/all_to_all | solution.py:24
  83.5 3.4 %slice.45 = bf16[512,2048]{1,0:T(8,128)(2,1)} slice(bf16[512,4096]{1,0:T(8,128)(2,1)} %bitcast.147), slice={[0:512], [2048:4096]} | slice | bytes 4194304 | tf_op jit(solution)/shard_map/slice | solution.py:146
  86.9 3.1 %reshape.175 = bf16[2048,512]{1,0:T(8,128)(2,1)S(1)} reshape(bf16[512,2048]{1,0:T(8,128)(2,1)} %slice.45) | data formatting | bytes 4194304 | tf_op jit(solution)/shard_map/reshape.5
  90.0 27.2 %all-to-all-done = bf16[256,16,160]{0,2,1:T(8,128)(2,1)} async-done(((bf16[256,16,160]{0,2,1:T(8,128)(2,1)}), bf16[256,16,160]{0,2,1:T(8,128)(2,1)}, u32[]{:S(2)}, u32[]{:S(2)}) %all-to-all-start) | async-done | bytes 1310752 | tf_op jit(solution)/shard_map/all_to_all | solution.py:24
  120.2 2.1 fusion.4
  125.8 5.8 %all-to-all-start.1 = ((bf16[256,16,160]{0,2,1:T(8,128)(2,1)}), bf16[256,16,160]{0,2,1:T(8,128)(2,1)S(1)}, u32[]{:S(2)}, u32[]{:S(2)}) async-start(bf16[256,16,160]{0,2,1:T(8,128)(2,1)} %copy.90), calls=%async_computation.1 | async-start | bytes 2621440 | tf_op jit(solution)/shard_map/all_to_all | solution.py:24
  131.6 2.8 convolution_bitcast_fusion
  134.4 5.4 %copy.93 = f32[2048,1,512]{2,0,1:T(8,128)} copy(f32[2048,1,512]{0,2,1:T(8,128)} %convolution_bitcast_fusion) | data formatting | bytes 8388608 | tf_op jit(solution)/shard_map/tbh,tbc->hbc/transpose | solution.py:199
  139.8 5.7 %stack.56 = f32[8,2,2,1,1,16,2048]{6,5,2,1,0,4,3:T(8,128)} reshape(f32[2048,1,512]{2,0,1:T(8,128)} %copy.93) | data formatting | bytes 8388608 | tf_op jit(solution)/shard_map/stack | solution.py:232
  145.5 22.0 %all-to-all-done.1 = bf16[256,16,160]{0,2,1:T(8,128)(2,1)S(1)} async-done(((bf16[256,16,160]{0,2,1:T(8,128)(2,1)}), bf16[256,16,160]{0,2,1:T(8,128)(2,1)S(1)}, u32[]{:S(2)}, u32[]{:S(2)}) %all-to-all-start.1) | async-done | bytes 1310752 | tf_op jit(solution)/shard_map/all_to_all | solution.py:24
  170.1 1.8 maximum_multiply_fusion
  173.6 2.9 collective-permute-start.10
  176.4 6.8 %collective-permute-done.10 = f32[8,2,1,2,16,2048]{5,4,3,1,0,2:T(8,128)S(1)} collective-permute-done((f32[8,2,1,2,16,2048]{5,4,3,1,0,2:T(8,128)S(1)}, f32[8,2,1,2,16,2048]{5,4,3,1,0,2:T(8,128)S(1)}, u32[]{:S(2)}, u32[]{:S(2)}) %collective-permute-start.10) | collective-permute-done | bytes 4194336 | tf_op jit(solution)/shard_map/ppermute | solution.py:34
  184.1 2.1 collective-permute-start.11
  186.1 4.6 %collective-permute-start.12 = (f32[2,1,2,16,2048]{4,3,2,0,1:T(8,128)S(1)}, f32[2,1,2,16,2048]{4,3,2,0,1:T(8,128)S(1)}, u32[]{:S(2)}, u32[]{:S(2)}) collective-permute-start(f32[2,1,2,16,2048]{4,3,2,0,1:T(8,128)S(1)} %get-tuple-element.13), channel_id=1, source_target_pairs={{0,448},{64,0},{128,64},{192,128},{256,192},{320,256},{384,320},{4... | collective-permute-start | bytes 1572872 | tf_op jit(solution)/shard_map/ppermute | solution.py:29
  190.7 9.7 %collective-permute-done.11 = f32[2,1,2,16,2048]{4,3,2,0,1:T(8,128)S(1)} collective-permute-done((f32[2,1,2,16,2048]{4,3,2,0,1:T(8,128)S(1)}, f32[2,1,2,16,2048]{4,3,2,0,1:T(8,128)S(1)}, u32[]{:S(2)}, u32[]{:S(2)}) %collective-permute-start.11) | collective-permute-done | bytes 524320 | tf_op jit(solution)/shard_map/ppermute | solution.py:29
  202.3 2.0 collective-permute-start.13
  204.3 5.3 %collective-permute-start.14 = (f32[2,1,2,16,2048]{4,3,2,0,1:T(8,128)S(1)}, f32[2,1,2,16,2048]{4,3,2,0,1:T(8,128)}, u32[]{:S(2)}, u32[]{:S(2)}) collective-permute-start(f32[2,1,2,16,2048]{4,3,2,0,1:T(8,128)S(1)} %get-tuple-element.15), channel_id=1, source_target_pairs={{0,448},{64,0},{128,64},{192,128},{256,192},{320,256},{384,320},{4... | collective-permute-start | bytes 1572872 | tf_op jit(solution)/shard_map/ppermute | solution.py:29
  210.5 8.2 %collective-permute-done.13 = f32[2,1,2,16,2048]{4,3,2,0,1:T(8,128)} collective-permute-done((f32[2,1,2,16,2048]{4,3,2,0,1:T(8,128)}, f32[2,1,2,16,2048]{4,3,2,0,1:T(8,128)}, u32[]{:S(2)}, u32[]{:S(2)}) %collective-permute-start.13) | collective-permute-done | bytes 524320 | tf_op jit(solution)/shard_map/ppermute | solution.py:29
  219.3 2.6 bitcast_add_fusion.3
  221.9 1.9 collective-permute-start.15
  223.8 3.0 convolution_multiply_fusion
  230.0 6.3 %collective-permute-start.19 = (f32[160,16,16]{0,2,1:T(8,128)S(1)}, f32[160,16,16]{0,2,1:T(8,128)S(1)}, u32[]{:S(2)}, u32[]{:S(2)}) collective-permute-start(f32[160,16,16]{0,2,1:T(8,128)S(1)} %pad_maximum_fusion.2), channel_id=1, source_target_pairs={{0,256},{64,320},{128,384},{192,448},{256,0},{320,64},{384,128},{4... | collective-permute-start | bytes 491528 | tf_op jit(solution)/shard_map/ppermute | solution.py:34
  236.3 2.6 collective-permute-start.17
  239.9 2.7 collective-permute-start.16
  242.7 2.0 collective-permute-done.19
  244.7 8.7 %collective-permute-start.20 = (f32[160,16,16]{0,2,1:T(8,128)S(1)}, f32[160,16,16]{0,2,1:T(8,128)S(1)}, u32[]{:S(2)}, u32[]{:S(2)}) collective-permute-start(f32[160,16,16]{0,2,1:T(8,128)S(1)} %fusion.26), channel_id=1, source_target_pairs={{0,128},{64,192},{128,0},{192,64},{256,384},{320,448},{384,256},{4... | collective-permute-start | bytes 491528 | tf_op jit(solution)/shard_map/ppermute | solution.py:34
  253.3 18.8 %collective-permute-done.20 = f32[160,16,16]{0,2,1:T(8,128)S(1)} collective-permute-done((f32[160,16,16]{0,2,1:T(8,128)S(1)}, f32[160,16,16]{0,2,1:T(8,128)S(1)}, u32[]{:S(2)}, u32[]{:S(2)}) %collective-permute-start.20) | collective-permute-done | bytes 163872 | tf_op jit(solution)/shard_map/ppermute | solution.py:34
  272.1 1.9 collective-permute-start.21
  274.1 7.4 %collective-permute-done.21 = f32[160,16,16]{0,2,1:T(8,128)} collective-permute-done((f32[160,16,16]{0,2,1:T(8,128)S(1)}, f32[160,16,16]{0,2,1:T(8,128)}, u32[]{:S(2)}, u32[]{:S(2)}) %collective-permute-start.21) | collective-permute-done | bytes 163872 | tf_op jit(solution)/shard_map/ppermute | solution.py:34
  282.5 1.9 collective-permute-start.22
  285.6 3.5 %collective-permute-start.18 = (f32[1,2,16,2048]{3,2,1,0:T(8,128)S(1)}, f32[1,2,16,2048]{3,2,1,0:T(8,128)S(1)}, u32[]{:S(2)}, u32[]{:S(2)}) collective-permute-start(f32[1,2,16,2048]{3,2,1,0:T(8,128)S(1)} %dynamic-slice_bitcast_fusion.2), channel_id=1, source_target_pairs={{0,32},{32,0},{1,33},{33,1},{2,34},{34,2},{3,35},{35,3},{4,36},{36... | collective-permute-start | bytes 786440 | tf_op jit(solution)/shard_map/ppermute | solution.py:34
  289.1 2.3 fusion.15
  293.3 4.8 %collective-permute-start.23 = (f32[160,16,16]{0,2,1:T(8,128)S(1)}, f32[160,16,16]{0,2,1:T(8,128)S(1)}, u32[]{:S(2)}, u32[]{:S(2)}) collective-permute-start(f32[160,16,16]{0,2,1:T(8,128)S(1)} %add.213), channel_id=1, source_target_pairs={{0,16},{16,0},{1,17},{17,1},{2,18},{18,2},{3,19},{19,3},{4,20},{20... | collective-permute-start | bytes 491528 | tf_op jit(solution)/shard_map/ppermute | solution.py:34
  (114 shorter events, 41.9 us)
Async XLA Ops:
  0.6 69.7 %copy-start = (bf16[256,512]{1,0:T(8,128)(2,1)S(1)}, bf16[256,512]{1,0:T(8,128)(2,1)}, u32[]{:S(2)}) copy-start(bf16[256,512]{1,0:T(8,128)(2,1)} %param.6) | copy-start | bytes 786436
  2.5 6.4 %collective-permute-start = (bf16[16,4096]{1,0:T(8,128)(2,1)S(1)}, bf16[16,4096]{1,0:T(8,128)(2,1)S(1)}, u32[]{:S(2)}, u32[]{:S(2)}) collective-permute-start(bf16[16,4096]{1,0:T(8,128)(2,1)S(1)} %get-tuple-element.62), channel_id=1, source_target_pairs={{0,32},{32,0},{1,33},{33,1},{2,34},{34,2},{3,35},{35,3},{4,36},{36... | collective-permute-start | bytes 393224 | tf_op jit(solution)/shard_map/ppermute | solution.py:34
  8.9 15.7 %collective-permute-start.2 = (bf16[2,16,4096]{2,1,0:T(8,128)(2,1)S(1)}, bf16[2,16,4096]{2,1,0:T(8,128)(2,1)S(1)}, u32[]{:S(2)}, u32[]{:S(2)}) collective-permute-start(bf16[2,16,4096]{2,1,0:T(8,128)(2,1)S(1)} %maximum_select_fusion.2), channel_id=1, source_target_pairs={{0,448},{64,0},{128,64},{192,128},{256,192},{320,256},{384,320},{4... | collective-permute-start | bytes 786440 | tf_op jit(solution)/shard_map/ppermute | solution.py:29
  20.2 9.3 %collective-permute-start.1 = (bf16[2,16,4096]{2,1,0:T(8,128)(2,1)S(1)}, bf16[2,16,4096]{2,1,0:T(8,128)(2,1)S(1)}, u32[]{:S(2)}, u32[]{:S(2)}) collective-permute-start(bf16[2,16,4096]{2,1,0:T(8,128)(2,1)S(1)} %maximum_select_fusion.2), channel_id=1, source_target_pairs={{0,64},{64,128},{128,192},{192,256},{256,320},{320,384},{384,448},... | collective-permute-start | bytes 786440 | tf_op jit(solution)/shard_map/ppermute | solution.py:29
  24.5 37.5 %copy-start.18 = (bf16[32,16,16]{0,2,1:T(8,128)(2,1)S(1)}, bf16[32,16,16]{0,2,1:T(8,128)(2,1)}, u32[]{:S(2)}) copy-start(bf16[32,16,16]{0,2,1:T(8,128)(2,1)} %param.10) | copy-start | bytes 49156
  24.6 8.5 %collective-permute-start.4 = (bf16[2,16,4096]{2,1,0:T(8,128)(2,1)S(1)}, bf16[2,16,4096]{2,1,0:T(8,128)(2,1)S(1)}, u32[]{:S(2)}, u32[]{:S(2)}) collective-permute-start(bf16[2,16,4096]{2,1,0:T(8,128)(2,1)S(1)} %collective-permute-done.2), channel_id=1, source_target_pairs={{0,448},{64,0},{128,64},{192,128},{256,192},{320,256},{384,320},{4... | collective-permute-start | bytes 786440 | tf_op jit(solution)/shard_map/ppermute | solution.py:29
  29.6 8.3 %collective-permute-start.3 = (bf16[2,16,4096]{2,1,0:T(8,128)(2,1)S(1)}, bf16[2,16,4096]{2,1,0:T(8,128)(2,1)S(1)}, u32[]{:S(2)}, u32[]{:S(2)}) collective-permute-start(bf16[2,16,4096]{2,1,0:T(8,128)(2,1)S(1)} %collective-permute-done.1), channel_id=1, source_target_pairs={{0,64},{64,128},{128,192},{192,256},{256,320},{320,384},{384,448},... | collective-permute-start | bytes 786440 | tf_op jit(solution)/shard_map/ppermute | solution.py:29
  33.0 8.3 %collective-permute-start.6 = (bf16[2,16,4096]{2,1,0:T(8,128)(2,1)S(1)}, bf16[2,16,4096]{2,1,0:T(8,128)(2,1)S(1)}, u32[]{:S(2)}, u32[]{:S(2)}) collective-permute-start(bf16[2,16,4096]{2,1,0:T(8,128)(2,1)S(1)} %collective-permute-done.4), channel_id=1, source_target_pairs={{0,448},{64,0},{128,64},{192,128},{256,192},{320,256},{384,320},{4... | collective-permute-start | bytes 786440 | tf_op jit(solution)/shard_map/ppermute | solution.py:29
  37.9 8.3 %collective-permute-start.5 = (bf16[2,16,4096]{2,1,0:T(8,128)(2,1)S(1)}, bf16[2,16,4096]{2,1,0:T(8,128)(2,1)S(1)}, u32[]{:S(2)}, u32[]{:S(2)}) collective-permute-start(bf16[2,16,4096]{2,1,0:T(8,128)(2,1)S(1)} %collective-permute-done.3), channel_id=1, source_target_pairs={{0,64},{64,128},{128,192},{192,256},{256,320},{320,384},{384,448},... | collective-permute-start | bytes 786440 | tf_op jit(solution)/shard_map/ppermute | solution.py:29
  41.3 8.3 %collective-permute-start.8 = (bf16[2,16,2048]{2,1,0:T(8,128)(2,1)S(1)}, bf16[2,16,2048]{2,1,0:T(8,128)(2,1)S(1)}, u32[]{:S(2)}, u32[]{:S(2)}) collective-permute-start(bf16[2,16,2048]{2,1,0:T(8,128)(2,1)S(1)} %split.9), channel_id=1, source_target_pairs={{0,448},{64,0},{128,64},{192,128},{256,192},{320,256},{384,320},{4... | collective-permute-start | bytes 393224 | tf_op jit(solution)/shard_map/ppermute | solution.py:29
  46.3 6.9 %collective-permute-start.7 = (bf16[2,16,2048]{2,1,0:T(8,128)(2,1)S(1)}, bf16[2,16,2048]{2,1,0:T(8,128)(2,1)S(1)}, u32[]{:S(2)}, u32[]{:S(2)}) collective-permute-start(bf16[2,16,2048]{2,1,0:T(8,128)(2,1)S(1)} %split.8), channel_id=1, source_target_pairs={{0,64},{64,128},{128,192},{192,256},{256,320},{320,384},{384,448},... | collective-permute-start | bytes 393224 | tf_op jit(solution)/shard_map/ppermute | solution.py:29
  53.9 12.2 %collective-permute-start.9 = (bf16[8,2,16,4096]{3,2,1,0:T(8,128)(2,1)}, bf16[8,2,16,4096]{3,2,1,0:T(8,128)(2,1)}, u32[]{:S(2)}, u32[]{:S(2)}) collective-permute-start(bf16[8,2,16,4096]{3,2,1,0:T(8,128)(2,1)} %fusion.22), channel_id=1, source_target_pairs={{0,16},{16,0},{1,17},{17,1},{2,18},{18,2},{3,19},{19,3},{4,20},{20... | collective-permute-start | bytes 6291464 | tf_op jit(solution)/shard_map/ppermute | solution.py:34
  62.2 3.5 %copy-start.16 = (bf16[256,512]{1,0:T(8,128)(2,1)S(1)}, bf16[256,512]{1,0:T(8,128)(2,1)}, u32[]{:S(2)}) copy-start(bf16[256,512]{1,0:T(8,128)(2,1)} %param.11) | copy-start | bytes 786436
  65.6 4.7 %copy-start.5 = (bf16[512,512]{1,0:T(8,128)(2,1)}, bf16[512,512]{1,0:T(8,128)(2,1)S(1)}, u32[]{:S(2)}) copy-start(bf16[512,512]{1,0:T(8,128)(2,1)S(1)} %reshape.176) | copy-start | bytes 1572868
  70.4 2.0 copy-start.4
  72.3 10.7 %copy-start.19 = (bf16[128,16,16]{0,2,1:T(8,128)(2,1)S(1)}, bf16[128,16,16]{0,2,1:T(8,128)(2,1)}, u32[]{:S(2)}) copy-start(bf16[128,16,16]{0,2,1:T(8,128)(2,1)} %param.8) | copy-start | bytes 196612
  73.6 43.6 %all-to-all-start = ((bf16[256,16,160]{0,2,1:T(8,128)(2,1)}), bf16[256,16,160]{0,2,1:T(8,128)(2,1)}, u32[]{:S(2)}, u32[]{:S(2)}) async-start(bf16[256,16,160]{0,2,1:T(8,128)(2,1)} %pad_maximum_fusion), calls=%async_computation | async-start | bytes 2621440 | tf_op jit(solution)/shard_map/all_to_all | solution.py:24
  83.5 36.8 %copy-start.14 = (bf16[128,16,16]{2,1,0:T(8,128)(2,1)}, bf16[128,16,16]{2,1,0:T(8,128)(2,1)S(1)}, u32[]{:S(2)}) copy-start(bf16[128,16,16]{2,1,0:T(8,128)(2,1)S(1)} %copy.88) | copy-start | bytes 196612
  118.2 0.7 copy-start.12
  120.2 2.1 copy-start.7
  122.3 1.3 copy-start.9
  122.7 1.1 copy-start.15
  124.3 7.3 %copy-start.13 = (bf16[256,16,32]{0,2,1:T(8,128)(2,1)S(1)}, bf16[256,16,32]{0,2,1:T(8,128)(2,1)}, u32[]{:S(2)}) copy-start(bf16[256,16,32]{0,2,1:T(8,128)(2,1)} %copy-done.12) | copy-start | bytes 786436
  125.8 41.7 %all-to-all-start.1 = ((bf16[256,16,160]{0,2,1:T(8,128)(2,1)}), bf16[256,16,160]{0,2,1:T(8,128)(2,1)S(1)}, u32[]{:S(2)}, u32[]{:S(2)}) async-start(bf16[256,16,160]{0,2,1:T(8,128)(2,1)} %copy.90), calls=%async_computation.1 | async-start | bytes 2621440 | tf_op jit(solution)/shard_map/all_to_all | solution.py:24
  167.6 1.0 copy-start.10
  167.6 2.6 copy-start.3
  173.6 9.6 %collective-permute-start.10 = (f32[8,2,1,2,16,2048]{5,4,3,1,0,2:T(8,128)S(1)}, f32[8,2,1,2,16,2048]{5,4,3,1,0,2:T(8,128)S(1)}, u32[]{:S(2)}, u32[]{:S(2)}) collective-permute-start(f32[8,2,1,2,16,2048]{5,4,3,1,0,2:T(8,128)S(1)} %bitcast.152), channel_id=1, source_target_pairs={{0,16},{16,0},{1,17},{17,1},{2,18},{18,2},{3,19},{19,3},{4,20},{20... | collective-permute-start | bytes 12582920 | tf_op jit(solution)/shard_map/ppermute | solution.py:34
  184.0 18.3 %copy-start.2 = (f32[8,2,1,2,16,2048]{5,4,3,1,0,2:T(8,128)}, f32[8,2,1,2,16,2048]{5,4,3,1,0,2:T(8,128)S(1)}, u32[]{:S(2)}) copy-start(f32[8,2,1,2,16,2048]{5,4,3,1,0,2:T(8,128)S(1)} %bitcast_add_fusion) | copy-start | bytes 12582916
  184.1 25.6 %copy-start.17 = (bf16[256,512]{1,0:T(8,128)(2,1)S(1)}, bf16[256,512]{1,0:T(8,128)(2,1)}, u32[]{:S(2)}) copy-start(bf16[256,512]{1,0:T(8,128)(2,1)} %param.11) | copy-start | bytes 786436
  184.1 16.4 %collective-permute-start.11 = (f32[2,1,2,16,2048]{4,3,2,0,1:T(8,128)S(1)}, f32[2,1,2,16,2048]{4,3,2,0,1:T(8,128)S(1)}, u32[]{:S(2)}, u32[]{:S(2)}) collective-permute-start(f32[2,1,2,16,2048]{4,3,2,0,1:T(8,128)S(1)} %get-tuple-element.12), channel_id=1, source_target_pairs={{0,64},{64,128},{128,192},{192,256},{256,320},{320,384},{384,448},... | collective-permute-start | bytes 1572872 | tf_op jit(solution)/shard_map/ppermute | solution.py:29
  186.1 15.2 %collective-permute-start.12 = (f32[2,1,2,16,2048]{4,3,2,0,1:T(8,128)S(1)}, f32[2,1,2,16,2048]{4,3,2,0,1:T(8,128)S(1)}, u32[]{:S(2)}, u32[]{:S(2)}) collective-permute-start(f32[2,1,2,16,2048]{4,3,2,0,1:T(8,128)S(1)} %get-tuple-element.13), channel_id=1, source_target_pairs={{0,448},{64,0},{128,64},{192,128},{256,192},{320,256},{384,320},{4... | collective-permute-start | bytes 1572872 | tf_op jit(solution)/shard_map/ppermute | solution.py:29
  202.3 21.6 %copy-start.8 = (bf16[256,16,128]{0,2,1:T(8,128)(2,1)S(1)}, bf16[256,16,128]{0,2,1:T(8,128)(2,1)}, u32[]{:S(2)}) copy-start(bf16[256,16,128]{0,2,1:T(8,128)(2,1)} %copy-done.7) | copy-start | bytes 3145732
  202.3 16.5 %collective-permute-start.13 = (f32[2,1,2,16,2048]{4,3,2,0,1:T(8,128)}, f32[2,1,2,16,2048]{4,3,2,0,1:T(8,128)}, u32[]{:S(2)}, u32[]{:S(2)}) collective-permute-start(f32[2,1,2,16,2048]{4,3,2,0,1:T(8,128)} %get-tuple-element.14), channel_id=1, source_target_pairs={{0,64},{64,128},{128,192},{192,256},{256,320},{320,384},{384,448},... | collective-permute-start | bytes 1572872 | tf_op jit(solution)/shard_map/ppermute | solution.py:29
  204.3 15.0 %collective-permute-start.14 = (f32[2,1,2,16,2048]{4,3,2,0,1:T(8,128)S(1)}, f32[2,1,2,16,2048]{4,3,2,0,1:T(8,128)}, u32[]{:S(2)}, u32[]{:S(2)}) collective-permute-start(f32[2,1,2,16,2048]{4,3,2,0,1:T(8,128)S(1)} %get-tuple-element.15), channel_id=1, source_target_pairs={{0,448},{64,0},{128,64},{192,128},{256,192},{320,256},{384,320},{4... | collective-permute-start | bytes 1572872 | tf_op jit(solution)/shard_map/ppermute | solution.py:29
  221.9 16.9 %collective-permute-start.15 = (f32[2,1,2,16,2048]{4,3,2,0,1:T(8,128)}, f32[2,1,2,16,2048]{4,3,2,0,1:T(8,128)S(1)}, u32[]{:S(2)}, u32[]{:S(2)}) collective-permute-start(f32[2,1,2,16,2048]{4,3,2,0,1:T(8,128)} %get-tuple-element.16), channel_id=1, source_target_pairs={{0,64},{64,128},{128,192},{192,256},{256,320},{320,384},{384,448},... | collective-permute-start | bytes 1572872 | tf_op jit(solution)/shard_map/ppermute | solution.py:29
  230.0 14.7 %collective-permute-start.19 = (f32[160,16,16]{0,2,1:T(8,128)S(1)}, f32[160,16,16]{0,2,1:T(8,128)S(1)}, u32[]{:S(2)}, u32[]{:S(2)}) collective-permute-start(f32[160,16,16]{0,2,1:T(8,128)S(1)} %pad_maximum_fusion.2), channel_id=1, source_target_pairs={{0,256},{64,320},{128,384},{192,448},{256,0},{320,64},{384,128},{4... | collective-permute-start | bytes 491528 | tf_op jit(solution)/shard_map/ppermute | solution.py:34
  236.3 48.1 %collective-permute-start.17 = (f32[2,1,2,16,2048]{4,3,2,0,1:T(8,128)}, f32[2,1,2,16,2048]{4,3,2,0,1:T(8,128)S(1)}, u32[]{:S(2)}, u32[]{:S(2)}) collective-permute-start(f32[2,1,2,16,2048]{4,3,2,0,1:T(8,128)} %get-tuple-element.17), channel_id=1, source_target_pairs={{0,448},{64,0},{128,64},{192,128},{256,192},{320,256},{384,320},{4... | collective-permute-start | bytes 1572872 | tf_op jit(solution)/shard_map/ppermute | solution.py:29
  239.9 44.5 %collective-permute-start.16 = (f32[2,1,2,16,2048]{4,3,2,0,1:T(8,128)S(1)}, f32[2,1,2,16,2048]{4,3,2,0,1:T(8,128)S(1)}, u32[]{:S(2)}, u32[]{:S(2)}) collective-permute-start(f32[2,1,2,16,2048]{4,3,2,0,1:T(8,128)S(1)} %bitcast_add_fusion.2), channel_id=1, source_target_pairs={{0,64},{64,128},{128,192},{192,256},{256,320},{320,384},{384,448},... | collective-permute-start | bytes 1572872 | tf_op jit(solution)/shard_map/ppermute | solution.py:29
  244.7 44.4 %copy-start.11 = (bf16[256,16,128]{0,2,1:T(8,128)(2,1)S(1)}, bf16[256,16,128]{0,2,1:T(8,128)(2,1)}, u32[]{:S(2)}) copy-start(bf16[256,16,128]{0,2,1:T(8,128)(2,1)} %copy-done.10) | copy-start | bytes 3145732
  244.7 27.4 %collective-permute-start.20 = (f32[160,16,16]{0,2,1:T(8,128)S(1)}, f32[160,16,16]{0,2,1:T(8,128)S(1)}, u32[]{:S(2)}, u32[]{:S(2)}) collective-permute-start(f32[160,16,16]{0,2,1:T(8,128)S(1)} %fusion.26), channel_id=1, source_target_pairs={{0,128},{64,192},{128,0},{192,64},{256,384},{320,448},{384,256},{4... | collective-permute-start | bytes 491528 | tf_op jit(solution)/shard_map/ppermute | solution.py:34
  272.1 9.3 %collective-permute-start.21 = (f32[160,16,16]{0,2,1:T(8,128)S(1)}, f32[160,16,16]{0,2,1:T(8,128)}, u32[]{:S(2)}, u32[]{:S(2)}) collective-permute-start(f32[160,16,16]{0,2,1:T(8,128)S(1)} %add.211), channel_id=1, source_target_pairs={{0,64},{64,0},{128,192},{192,128},{256,320},{320,256},{384,448},{4... | collective-permute-start | bytes 491528 | tf_op jit(solution)/shard_map/ppermute | solution.py:34
  282.5 9.8 %collective-permute-start.22 = (f32[160,16,16]{0,2,1:T(8,128)S(1)}, f32[160,16,16]{0,2,1:T(8,128)}, u32[]{:S(2)}, u32[]{:S(2)}) collective-permute-start(f32[160,16,16]{0,2,1:T(8,128)S(1)} %add.212), channel_id=1, source_target_pairs={{0,32},{32,0},{1,33},{33,1},{2,34},{34,2},{3,35},{35,3},{4,36},{36... | collective-permute-start | bytes 491528 | tf_op jit(solution)/shard_map/ppermute | solution.py:34
  285.6 12.5 %copy-start.6 = (bf16[512,512]{1,0:T(8,128)(2,1)S(1)}, bf16[512,512]{1,0:T(8,128)(2,1)}, u32[]{:S(2)}) copy-start(bf16[512,512]{1,0:T(8,128)(2,1)} %copy-done.5) | copy-start | bytes 1572868
  285.6 15.0 %collective-permute-start.18 = (f32[1,2,16,2048]{3,2,1,0:T(8,128)S(1)}, f32[1,2,16,2048]{3,2,1,0:T(8,128)S(1)}, u32[]{:S(2)}, u32[]{:S(2)}) collective-permute-start(f32[1,2,16,2048]{3,2,1,0:T(8,128)S(1)} %dynamic-slice_bitcast_fusion.2), channel_id=1, source_target_pairs={{0,32},{32,0},{1,33},{33,1},{2,34},{34,2},{3,35},{35,3},{4,36},{36... | collective-permute-start | bytes 786440 | tf_op jit(solution)/shard_map/ppermute | solution.py:34
  292.3 9.7 %copy-start.1 = (bf16[256,512]{1,0:T(8,128)(2,1)S(1)}, bf16[256,512]{1,0:T(8,128)(2,1)}, u32[]{:S(2)}) copy-start(bf16[256,512]{1,0:T(8,128)(2,1)} %param.6) | copy-start | bytes 786436
  293.3 5.9 %collective-permute-start.23 = (f32[160,16,16]{0,2,1:T(8,128)S(1)}, f32[160,16,16]{0,2,1:T(8,128)S(1)}, u32[]{:S(2)}, u32[]{:S(2)}) collective-permute-start(f32[160,16,16]{0,2,1:T(8,128)S(1)} %add.213), channel_id=1, source_target_pairs={{0,16},{16,0},{1,17},{17,1},{2,18},{18,2},{3,19},{19,3},{4,20},{20... | collective-permute-start | bytes 491528 | tf_op jit(solution)/shard_map/ppermute | solution.py:34

commit v10 on v8

--- a/solution.py
+++ b/solution.py
@@ -63,9 +63,7 @@
         bwd = shift(bwd, "z", -1)
         out = lax.dynamic_update_index_in_dim(out, fwd, (me - step) % n, 0)
         out = lax.dynamic_update_index_in_dim(out, bwd, (me + step) % n, 0)
-    lo, _ = jnp.split(fwd, 2, axis=-1)
-    _, hi = jnp.split(bwd, 2, axis=-1)
-    last = jnp.concatenate([shift(lo, "z", 1), shift(hi, "z", -1)], axis=-1)
+    last = shift(fwd, "z", 1)
     out = lax.dynamic_update_index_in_dim(out, last, (me + half) % n, 0)
     return out
 

time: 301 us -> 302 us (level)
  waiting for transfers between devices: 113 us -> 119 us
  starting transfers between devices: 105 us -> 99.9 us
    ppermute x15 -> x14, waiting for transfers between devices: 29.1 us -> 35.5 us  [shift(): return lax.ppermute(value, axis, [(i, (i + step) % n) for i in range(n)])]
    ppermute x15 -> x14, starting transfers between devices: 53 us -> 48.1 us  [shift(): return lax.ppermute(value, axis, [(i, (i + step) % n) for i in range(n)])]
  transfers between devices with their start and end apart: 26 -> 25, of which waited for: 13 -> 14; matrix products, arithmetic and copies ran while one was open for 17% -> 16% of each run, Pallas kernels for 0% -> 0%
where the time goes in v10:
time: 302 us; the launch traced here: 300 us
  waiting for transfers between devices  119 us (39%)
  starting transfers between devices  99.9 us (33%)
  local copies, waits for them, and re-layouts  43.9 us (15%)
  other arithmetic  19.5 us (6%)
  matrix products  16.2 us (5%)
    all_to_all x2, waiting for transfers between devices, exchange(): return lax.all_to_all(wired, FEAT_AXES, 1, 1, tiled=True)  49.3 us
    ppermute x14, starting transfers between devices, shift(): return lax.ppermute(value, axis, [(i, (i + step) % n) for i in range(n)])  48.1 us
    ppermute x9, starting transfers between devices, swap(): return lax.ppermute(value, axis, [(i, i ^ mask) for i in range(n)])  36.7 us
    ppermute x14, waiting for transfers between devices, shift(): return lax.ppermute(value, axis, [(i, (i + step) % n) for i in range(n)])  35.5 us
    ppermute x9, waiting for transfers between devices, swap(): return lax.ppermute(value, axis, [(i, i ^ mask) for i in range(n)])  34.6 us
    all_to_all x2, starting transfers between devices, exchange(): return lax.all_to_all(wired, FEAT_AXES, 1, 1, tiled=True)  15.2 us
  transfers between devices with their start and end apart: 25, of which 14 were waited for; matrix products, arithmetic and copies ran while one was open for 16% of the time, Pallas kernels for 0%

profile of v10, /device:TPU:1, one launch (start us, length us, event | category | flops | bytes accessed | tf_op | source)
XLA Modules:
  0.0 300.3 jit_solution(17890232217049540709)
XLA Ops:
  2.5 4.0 %collective-permute-start = (bf16[16,4096]{1,0:T(8,128)(2,1)S(1)}, bf16[16,4096]{1,0:T(8,128)(2,1)S(1)}, u32[]{:S(2)}, u32[]{:S(2)}) collective-permute-start(bf16[16,4096]{1,0:T(8,128)(2,1)S(1)} %get-tuple-element.50), channel_id=1, source_target_pairs={{0,32},{32,0},{1,33},{33,1},{2,34},{34,2},{3,35},{35,3},{4,36},{36... | collective-permute-start | bytes 393224 | tf_op jit(solution)/shard_map/ppermute | solution.py:34
  6.6 2.2 collective-permute-done
  8.9 11.4 %collective-permute-start.2 = (bf16[2,16,4096]{2,1,0:T(8,128)(2,1)S(1)}, bf16[2,16,4096]{2,1,0:T(8,128)(2,1)S(1)}, u32[]{:S(2)}, u32[]{:S(2)}) collective-permute-start(bf16[2,16,4096]{2,1,0:T(8,128)(2,1)S(1)} %maximum_select_fusion.2), channel_id=1, source_target_pairs={{0,448},{64,0},{128,64},{192,128},{256,192},{320,256},{384,320},{4... | collective-permute-start | bytes 786440 | tf_op jit(solution)/shard_map/ppermute | solution.py:29
  20.2 1.9 collective-permute-start.1
  24.5 5.1 %collective-permute-start.4 = (bf16[2,16,4096]{2,1,0:T(8,128)(2,1)S(1)}, bf16[2,16,4096]{2,1,0:T(8,128)(2,1)S(1)}, u32[]{:S(2)}, u32[]{:S(2)}) collective-permute-start(bf16[2,16,4096]{2,1,0:T(8,128)(2,1)S(1)} %collective-permute-done.2), channel_id=1, source_target_pairs={{0,448},{64,0},{128,64},{192,128},{256,192},{320,256},{384,320},{4... | collective-permute-start | bytes 786440 | tf_op jit(solution)/shard_map/ppermute | solution.py:29
  29.6 1.9 collective-permute-start.3
  33.0 4.9 %collective-permute-start.6 = (bf16[2,16,4096]{2,1,0:T(8,128)(2,1)S(1)}, bf16[2,16,4096]{2,1,0:T(8,128)(2,1)S(1)}, u32[]{:S(2)}, u32[]{:S(2)}) collective-permute-start(bf16[2,16,4096]{2,1,0:T(8,128)(2,1)S(1)} %collective-permute-done.4), channel_id=1, source_target_pairs={{0,448},{64,0},{128,64},{192,128},{256,192},{320,256},{384,320},{4... | collective-permute-start | bytes 786440 | tf_op jit(solution)/shard_map/ppermute | solution.py:29
  37.9 1.9 collective-permute-start.5
  41.3 4.9 %collective-permute-done.5 = bf16[2,16,4096]{2,1,0:T(8,128)(2,1)S(1)} collective-permute-done((bf16[2,16,4096]{2,1,0:T(8,128)(2,1)S(1)}, bf16[2,16,4096]{2,1,0:T(8,128)(2,1)S(1)}, u32[]{:S(2)}, u32[]{:S(2)}) %collective-permute-start.5) | collective-permute-done | bytes 262176 | tf_op jit(solution)/shard_map/ppermute | solution.py:29
  46.2 1.9 collective-permute-start.7
  49.6 5.0 %collective-permute-done.7 = bf16[2,16,4096]{2,1,0:T(8,128)(2,1)S(1)} collective-permute-done((bf16[2,16,4096]{2,1,0:T(8,128)(2,1)S(1)}, bf16[2,16,4096]{2,1,0:T(8,128)(2,1)S(1)}, u32[]{:S(2)}, u32[]{:S(2)}) %collective-permute-start.7) | collective-permute-done | bytes 262176 | tf_op jit(solution)/shard_map/ppermute | solution.py:29
  55.3 8.1 %collective-permute-start.8 = (bf16[8,2,16,4096]{3,2,1,0:T(8,128)(2,1)}, bf16[8,2,16,4096]{3,2,1,0:T(8,128)(2,1)}, u32[]{:S(2)}, u32[]{:S(2)}) collective-permute-start(bf16[8,2,16,4096]{3,2,1,0:T(8,128)(2,1)} %bitcast_dynamic-update-slice_fusion), channel_id=1, source_target_pairs={{0,16},{16,0},{1,17},{17,1},{2,18},{18,2},{3,19},{19,3},{4,20},{20... | collective-permute-start | bytes 6291464 | tf_op jit(solution)/shard_map/ppermute | solution.py:34
  64.9 2.1 reshape.176
  67.5 4.2 %maximum_select_fusion = bf16[8,2,2,16,4096]{4,3,2,1,0:T(8,128)(2,1)S(1)} fusion(bf16[8,2,1,16,4096]{4,3,2,1,0:T(8,128)(2,1)} %bitcast.13, bf16[8,2,1,16,4096]{4,3,2,1,0:T(8,128)(2,1)} %bitcast.12, pred[]{:T(512)S(6)} %eq.26), kind=kLoop, calls=%fused_computation.1 | loop fusion | flops 6291456 | bytes 8388609 | tf_op jit(solution)/shard_map/jit(_where)/select_n | solution.py:94
  74.9 9.4 %all-to-all-start = ((bf16[256,16,160]{0,2,1:T(8,128)(2,1)}), bf16[256,16,160]{0,2,1:T(8,128)(2,1)}, u32[]{:S(2)}, u32[]{:S(2)}) async-start(bf16[256,16,160]{0,2,1:T(8,128)(2,1)} %pad_maximum_fusion), calls=%async_computation | async-start | bytes 2621440 | tf_op jit(solution)/shard_map/all_to_all | solution.py:24
  84.8 3.4 %slice.45 = bf16[512,2048]{1,0:T(8,128)(2,1)} slice(bf16[512,4096]{1,0:T(8,128)(2,1)} %bitcast.145), slice={[0:512], [2048:4096]} | slice | bytes 4194304 | tf_op jit(solution)/shard_map/slice | solution.py:141
  88.2 3.1 %reshape.175 = bf16[2048,512]{1,0:T(8,128)(2,1)S(1)} reshape(bf16[512,2048]{1,0:T(8,128)(2,1)} %slice.45) | data formatting | bytes 4194304 | tf_op jit(solution)/shard_map/reshape.5
  91.3 27.2 %all-to-all-done = bf16[256,16,160]{0,2,1:T(8,128)(2,1)} async-done(((bf16[256,16,160]{0,2,1:T(8,128)(2,1)}), bf16[256,16,160]{0,2,1:T(8,128)(2,1)}, u32[]{:S(2)}, u32[]{:S(2)}) %all-to-all-start) | async-done | bytes 1310752 | tf_op jit(solution)/shard_map/all_to_all | solution.py:24
  121.6 2.1 fusion.4
  127.2 5.8 %all-to-all-start.1 = ((bf16[256,16,160]{0,2,1:T(8,128)(2,1)}), bf16[256,16,160]{0,2,1:T(8,128)(2,1)S(1)}, u32[]{:S(2)}, u32[]{:S(2)}) async-start(bf16[256,16,160]{0,2,1:T(8,128)(2,1)} %copy.90), calls=%async_computation.1 | async-start | bytes 2621440 | tf_op jit(solution)/shard_map/all_to_all | solution.py:24
  133.0 2.8 convolution_bitcast_fusion
  135.7 5.4 %copy.93 = f32[2048,1,512]{2,0,1:T(8,128)} copy(f32[2048,1,512]{0,2,1:T(8,128)} %convolution_bitcast_fusion) | data formatting | bytes 8388608 | tf_op jit(solution)/shard_map/tbh,tbc->hbc/transpose | solution.py:194
  141.1 5.7 %stack.56 = f32[8,2,2,1,1,16,2048]{6,5,2,1,0,4,3:T(8,128)} reshape(f32[2048,1,512]{2,0,1:T(8,128)} %copy.93) | data formatting | bytes 8388608 | tf_op jit(solution)/shard_map/stack | solution.py:227
  146.8 22.0 %all-to-all-done.1 = bf16[256,16,160]{0,2,1:T(8,128)(2,1)S(1)} async-done(((bf16[256,16,160]{0,2,1:T(8,128)(2,1)}), bf16[256,16,160]{0,2,1:T(8,128)(2,1)S(1)}, u32[]{:S(2)}, u32[]{:S(2)}) %all-to-all-start.1) | async-done | bytes 1310752 | tf_op jit(solution)/shard_map/all_to_all | solution.py:24
  174.9 2.9 collective-permute-start.9
  177.8 6.8 %collective-permute-done.9 = f32[8,2,1,2,16,2048]{5,4,3,1,0,2:T(8,128)S(1)} collective-permute-done((f32[8,2,1,2,16,2048]{5,4,3,1,0,2:T(8,128)S(1)}, f32[8,2,1,2,16,2048]{5,4,3,1,0,2:T(8,128)S(1)}, u32[]{:S(2)}, u32[]{:S(2)}) %collective-permute-start.9) | collective-permute-done | bytes 4194336 | tf_op jit(solution)/shard_map/ppermute | solution.py:34
  186.2 1.9 collective-permute-start.10
  188.1 4.6 %collective-permute-start.14 = (f32[2,1,2,16,2048]{4,3,2,0,1:T(8,128)}, f32[2,1,2,16,2048]{4,3,2,0,1:T(8,128)}, u32[]{:S(2)}, u32[]{:S(2)}) collective-permute-start(f32[2,1,2,16,2048]{4,3,2,0,1:T(8,128)} %get-tuple-element.42), channel_id=1, source_target_pairs={{0,448},{64,0},{128,64},{192,128},{256,192},{320,256},{384,320},{4... | collective-permute-start | bytes 1572872 | tf_op jit(solution)/shard_map/ppermute | solution.py:29
  192.7 9.7 %collective-permute-done.10 = f32[2,1,2,16,2048]{4,3,2,0,1:T(8,128)S(1)} collective-permute-done((f32[2,1,2,16,2048]{4,3,2,0,1:T(8,128)S(1)}, f32[2,1,2,16,2048]{4,3,2,0,1:T(8,128)S(1)}, u32[]{:S(2)}, u32[]{:S(2)}) %collective-permute-start.10) | collective-permute-done | bytes 524320 | tf_op jit(solution)/shard_map/ppermute | solution.py:29
  202.5 2.1 collective-permute-start.11
  205.5 12.6 %collective-permute-done.11 = f32[2,1,2,16,2048]{4,3,2,0,1:T(8,128)} collective-permute-done((f32[2,1,2,16,2048]{4,3,2,0,1:T(8,128)S(1)}, f32[2,1,2,16,2048]{4,3,2,0,1:T(8,128)}, u32[]{:S(2)}, u32[]{:S(2)}) %collective-permute-start.11) | collective-permute-done | bytes 524320 | tf_op jit(solution)/shard_map/ppermute | solution.py:29
  218.1 2.6 bitcast_add_fusion.3
  220.7 1.9 collective-permute-start.15
  222.6 3.4 %collective-permute-start.12 = (f32[2,1,2,16,2048]{4,3,2,0,1:T(8,128)}, f32[2,1,2,16,2048]{4,3,2,0,1:T(8,128)}, u32[]{:S(2)}, u32[]{:S(2)}) collective-permute-start(f32[2,1,2,16,2048]{4,3,2,0,1:T(8,128)} %get-tuple-element.41), channel_id=1, source_target_pairs={{0,64},{64,128},{128,192},{192,256},{256,320},{320,384},{384,448},... | collective-permute-start | bytes 1572872 | tf_op jit(solution)/shard_map/ppermute | solution.py:29
  226.0 3.0 convolution_multiply_fusion
  232.1 2.1 collective-permute-start.18
  234.2 3.1 %collective-permute-done.12 = f32[2,1,2,16,2048]{4,3,2,0,1:T(8,128)} collective-permute-done((f32[2,1,2,16,2048]{4,3,2,0,1:T(8,128)}, f32[2,1,2,16,2048]{4,3,2,0,1:T(8,128)}, u32[]{:S(2)}, u32[]{:S(2)}) %collective-permute-start.12) | collective-permute-done | bytes 524320 | tf_op jit(solution)/shard_map/ppermute | solution.py:29
  237.3 2.3 bitcast_add_fusion.2
  241.5 3.4 %collective-permute-start.13 = (f32[2,1,2,16,2048]{4,3,2,0,1:T(8,128)S(1)}, f32[2,1,2,16,2048]{4,3,2,0,1:T(8,128)S(1)}, u32[]{:S(2)}, u32[]{:S(2)}) collective-permute-start(f32[2,1,2,16,2048]{4,3,2,0,1:T(8,128)S(1)} %get-tuple-element.39), channel_id=1, source_target_pairs={{0,64},{64,128},{128,192},{192,256},{256,320},{320,384},{384,448},... | collective-permute-start | bytes 1572872 | tf_op jit(solution)/shard_map/ppermute | solution.py:29
  244.9 4.9 %collective-permute-done.18 = f32[160,16,16]{0,2,1:T(8,128)S(1)} collective-permute-done((f32[160,16,16]{0,2,1:T(8,128)S(1)}, f32[160,16,16]{0,2,1:T(8,128)S(1)}, u32[]{:S(2)}, u32[]{:S(2)}) %collective-permute-start.18) | collective-permute-done | bytes 163872 | tf_op jit(solution)/shard_map/ppermute | solution.py:34
  249.8 2.1 collective-permute-start.19
  251.9 12.3 %collective-permute-done.19 = f32[160,16,16]{0,2,1:T(8,128)S(1)} collective-permute-done((f32[160,16,16]{0,2,1:T(8,128)S(1)}, f32[160,16,16]{0,2,1:T(8,128)S(1)}, u32[]{:S(2)}, u32[]{:S(2)}) %collective-permute-start.19) | collective-permute-done | bytes 163872 | tf_op jit(solution)/shard_map/ppermute | solution.py:34
  264.3 1.9 collective-permute-start.20
  266.2 8.1 %collective-permute-done.20 = f32[160,16,16]{0,2,1:T(8,128)} collective-permute-done((f32[160,16,16]{0,2,1:T(8,128)S(1)}, f32[160,16,16]{0,2,1:T(8,128)}, u32[]{:S(2)}, u32[]{:S(2)}) %collective-permute-start.20) | collective-permute-done | bytes 163872 | tf_op jit(solution)/shard_map/ppermute | solution.py:34
  275.3 1.9 collective-permute-start.21
  278.4 3.5 %collective-permute-start.17 = (f32[1,2,16,2048]{3,2,1,0:T(8,128)S(1)}, f32[1,2,16,2048]{3,2,1,0:T(8,128)S(1)}, u32[]{:S(2)}, u32[]{:S(2)}) collective-permute-start(f32[1,2,16,2048]{3,2,1,0:T(8,128)S(1)} %dynamic-slice_bitcast_fusion.2), channel_id=1, source_target_pairs={{0,32},{32,0},{1,33},{33,1},{2,34},{34,2},{3,35},{35,3},{4,36},{36... | collective-permute-start | bytes 786440 | tf_op jit(solution)/shard_map/ppermute | solution.py:34
  281.9 2.3 fusion.15
  286.1 10.2 %collective-permute-start.22 = (f32[160,16,16]{0,2,1:T(8,128)S(1)}, f32[160,16,16]{0,2,1:T(8,128)S(1)}, u32[]{:S(2)}, u32[]{:S(2)}) collective-permute-start(f32[160,16,16]{0,2,1:T(8,128)S(1)} %add.213), channel_id=1, source_target_pairs={{0,16},{16,0},{1,17},{17,1},{2,18},{18,2},{3,19},{19,3},{4,20},{20... | collective-permute-start | bytes 491528 | tf_op jit(solution)/shard_map/ppermute | solution.py:34
  (110 shorter events, 42.9 us)
Async XLA Ops:
  0.6 71.1 %copy-start = (bf16[256,512]{1,0:T(8,128)(2,1)S(1)}, bf16[256,512]{1,0:T(8,128)(2,1)}, u32[]{:S(2)}) copy-start(bf16[256,512]{1,0:T(8,128)(2,1)} %param.6) | copy-start | bytes 786436
  2.5 6.4 %collective-permute-start = (bf16[16,4096]{1,0:T(8,128)(2,1)S(1)}, bf16[16,4096]{1,0:T(8,128)(2,1)S(1)}, u32[]{:S(2)}, u32[]{:S(2)}) collective-permute-start(bf16[16,4096]{1,0:T(8,128)(2,1)S(1)} %get-tuple-element.50), channel_id=1, source_target_pairs={{0,32},{32,0},{1,33},{33,1},{2,34},{34,2},{3,35},{35,3},{4,36},{36... | collective-permute-start | bytes 393224 | tf_op jit(solution)/shard_map/ppermute | solution.py:34
  8.9 15.7 %collective-permute-start.2 = (bf16[2,16,4096]{2,1,0:T(8,128)(2,1)S(1)}, bf16[2,16,4096]{2,1,0:T(8,128)(2,1)S(1)}, u32[]{:S(2)}, u32[]{:S(2)}) collective-permute-start(bf16[2,16,4096]{2,1,0:T(8,128)(2,1)S(1)} %maximum_select_fusion.2), channel_id=1, source_target_pairs={{0,448},{64,0},{128,64},{192,128},{256,192},{320,256},{384,320},{4... | collective-permute-start | bytes 786440 | tf_op jit(solution)/shard_map/ppermute | solution.py:29
  20.2 9.3 %collective-permute-start.1 = (bf16[2,16,4096]{2,1,0:T(8,128)(2,1)S(1)}, bf16[2,16,4096]{2,1,0:T(8,128)(2,1)S(1)}, u32[]{:S(2)}, u32[]{:S(2)}) collective-permute-start(bf16[2,16,4096]{2,1,0:T(8,128)(2,1)S(1)} %maximum_select_fusion.2), channel_id=1, source_target_pairs={{0,64},{64,128},{128,192},{192,256},{256,320},{320,384},{384,448},... | collective-permute-start | bytes 786440 | tf_op jit(solution)/shard_map/ppermute | solution.py:29
  23.8 39.6 %copy-start.18 = (bf16[32,16,16]{0,2,1:T(8,128)(2,1)S(1)}, bf16[32,16,16]{0,2,1:T(8,128)(2,1)}, u32[]{:S(2)}) copy-start(bf16[32,16,16]{0,2,1:T(8,128)(2,1)} %param.10) | copy-start | bytes 49156
  24.5 8.5 %collective-permute-start.4 = (bf16[2,16,4096]{2,1,0:T(8,128)(2,1)S(1)}, bf16[2,16,4096]{2,1,0:T(8,128)(2,1)S(1)}, u32[]{:S(2)}, u32[]{:S(2)}) collective-permute-start(bf16[2,16,4096]{2,1,0:T(8,128)(2,1)S(1)} %collective-permute-done.2), channel_id=1, source_target_pairs={{0,448},{64,0},{128,64},{192,128},{256,192},{320,256},{384,320},{4... | collective-permute-start | bytes 786440 | tf_op jit(solution)/shard_map/ppermute | solution.py:29
  29.6 8.3 %collective-permute-start.3 = (bf16[2,16,4096]{2,1,0:T(8,128)(2,1)S(1)}, bf16[2,16,4096]{2,1,0:T(8,128)(2,1)S(1)}, u32[]{:S(2)}, u32[]{:S(2)}) collective-permute-start(bf16[2,16,4096]{2,1,0:T(8,128)(2,1)S(1)} %collective-permute-done.1), channel_id=1, source_target_pairs={{0,64},{64,128},{128,192},{192,256},{256,320},{320,384},{384,448},... | collective-permute-start | bytes 786440 | tf_op jit(solution)/shard_map/ppermute | solution.py:29
  33.0 15.9 %collective-permute-start.6 = (bf16[2,16,4096]{2,1,0:T(8,128)(2,1)S(1)}, bf16[2,16,4096]{2,1,0:T(8,128)(2,1)S(1)}, u32[]{:S(2)}, u32[]{:S(2)}) collective-permute-start(bf16[2,16,4096]{2,1,0:T(8,128)(2,1)S(1)} %collective-permute-done.4), channel_id=1, source_target_pairs={{0,448},{64,0},{128,64},{192,128},{256,192},{320,256},{384,320},{4... | collective-permute-start | bytes 786440 | tf_op jit(solution)/shard_map/ppermute | solution.py:29
  37.9 8.3 %collective-permute-start.5 = (bf16[2,16,4096]{2,1,0:T(8,128)(2,1)S(1)}, bf16[2,16,4096]{2,1,0:T(8,128)(2,1)S(1)}, u32[]{:S(2)}, u32[]{:S(2)}) collective-permute-start(bf16[2,16,4096]{2,1,0:T(8,128)(2,1)S(1)} %collective-permute-done.3), channel_id=1, source_target_pairs={{0,64},{64,128},{128,192},{192,256},{256,320},{320,384},{384,448},... | collective-permute-start | bytes 786440 | tf_op jit(solution)/shard_map/ppermute | solution.py:29
  46.2 8.3 %collective-permute-start.7 = (bf16[2,16,4096]{2,1,0:T(8,128)(2,1)S(1)}, bf16[2,16,4096]{2,1,0:T(8,128)(2,1)S(1)}, u32[]{:S(2)}, u32[]{:S(2)}) collective-permute-start(bf16[2,16,4096]{2,1,0:T(8,128)(2,1)S(1)} %collective-permute-done.5), channel_id=1, source_target_pairs={{0,64},{64,128},{128,192},{192,256},{256,320},{320,384},{384,448},... | collective-permute-start | bytes 786440 | tf_op jit(solution)/shard_map/ppermute | solution.py:29
  55.3 12.2 %collective-permute-start.8 = (bf16[8,2,16,4096]{3,2,1,0:T(8,128)(2,1)}, bf16[8,2,16,4096]{3,2,1,0:T(8,128)(2,1)}, u32[]{:S(2)}, u32[]{:S(2)}) collective-permute-start(bf16[8,2,16,4096]{3,2,1,0:T(8,128)(2,1)} %bitcast_dynamic-update-slice_fusion), channel_id=1, source_target_pairs={{0,16},{16,0},{1,17},{17,1},{2,18},{18,2},{3,19},{19,3},{4,20},{20... | collective-permute-start | bytes 6291464 | tf_op jit(solution)/shard_map/ppermute | solution.py:34
  63.5 3.5 %copy-start.16 = (bf16[256,512]{1,0:T(8,128)(2,1)S(1)}, bf16[256,512]{1,0:T(8,128)(2,1)}, u32[]{:S(2)}) copy-start(bf16[256,512]{1,0:T(8,128)(2,1)} %param.11) | copy-start | bytes 786436
  67.0 4.7 %copy-start.5 = (bf16[512,512]{1,0:T(8,128)(2,1)}, bf16[512,512]{1,0:T(8,128)(2,1)S(1)}, u32[]{:S(2)}) copy-start(bf16[512,512]{1,0:T(8,128)(2,1)S(1)} %reshape.176) | copy-start | bytes 1572868
  71.7 2.0 copy-start.4
  73.7 10.7 %copy-start.19 = (bf16[128,16,16]{0,2,1:T(8,128)(2,1)S(1)}, bf16[128,16,16]{0,2,1:T(8,128)(2,1)}, u32[]{:S(2)}) copy-start(bf16[128,16,16]{0,2,1:T(8,128)(2,1)} %param.8) | copy-start | bytes 196612
  74.9 43.6 %all-to-all-start = ((bf16[256,16,160]{0,2,1:T(8,128)(2,1)}), bf16[256,16,160]{0,2,1:T(8,128)(2,1)}, u32[]{:S(2)}, u32[]{:S(2)}) async-start(bf16[256,16,160]{0,2,1:T(8,128)(2,1)} %pad_maximum_fusion), calls=%async_computation | async-start | bytes 2621440 | tf_op jit(solution)/shard_map/all_to_all | solution.py:24
  84.8 36.8 %copy-start.14 = (bf16[128,16,16]{2,1,0:T(8,128)(2,1)}, bf16[128,16,16]{2,1,0:T(8,128)(2,1)S(1)}, u32[]{:S(2)}) copy-start(bf16[128,16,16]{2,1,0:T(8,128)(2,1)S(1)} %copy.88) | copy-start | bytes 196612
  119.5 0.7 copy-start.12
  121.6 2.1 copy-start.7
  123.7 1.3 copy-start.9
  124.0 1.1 copy-start.15
  125.6 7.3 %copy-start.13 = (bf16[256,16,32]{0,2,1:T(8,128)(2,1)S(1)}, bf16[256,16,32]{0,2,1:T(8,128)(2,1)}, u32[]{:S(2)}) copy-start(bf16[256,16,32]{0,2,1:T(8,128)(2,1)} %copy-done.12) | copy-start | bytes 786436
  127.2 41.7 %all-to-all-start.1 = ((bf16[256,16,160]{0,2,1:T(8,128)(2,1)}), bf16[256,16,160]{0,2,1:T(8,128)(2,1)S(1)}, u32[]{:S(2)}, u32[]{:S(2)}) async-start(bf16[256,16,160]{0,2,1:T(8,128)(2,1)} %copy.90), calls=%async_computation.1 | async-start | bytes 2621440 | tf_op jit(solution)/shard_map/all_to_all | solution.py:24
  168.9 1.0 copy-start.10
  168.9 2.6 copy-start.3
  174.9 9.6 %collective-permute-start.9 = (f32[8,2,1,2,16,2048]{5,4,3,1,0,2:T(8,128)S(1)}, f32[8,2,1,2,16,2048]{5,4,3,1,0,2:T(8,128)S(1)}, u32[]{:S(2)}, u32[]{:S(2)}) collective-permute-start(f32[8,2,1,2,16,2048]{5,4,3,1,0,2:T(8,128)S(1)} %bitcast.150), channel_id=1, source_target_pairs={{0,16},{16,0},{1,17},{17,1},{2,18},{18,2},{3,19},{19,3},{4,20},{20... | collective-permute-start | bytes 12582920 | tf_op jit(solution)/shard_map/ppermute | solution.py:34
  185.3 17.1 %copy-start.2 = (f32[8,2,1,2,16,2048]{5,4,3,1,0,2:T(8,128)}, f32[8,2,1,2,16,2048]{5,4,3,1,0,2:T(8,128)S(1)}, u32[]{:S(2)}) copy-start(f32[8,2,1,2,16,2048]{5,4,3,1,0,2:T(8,128)S(1)} %bitcast_add_fusion) | copy-start | bytes 12582916
  185.3 19.3 %copy-start.17 = (bf16[256,512]{1,0:T(8,128)(2,1)S(1)}, bf16[256,512]{1,0:T(8,128)(2,1)}, u32[]{:S(2)}) copy-start(bf16[256,512]{1,0:T(8,128)(2,1)} %param.11) | copy-start | bytes 786436
  186.2 16.2 %collective-permute-start.10 = (f32[2,1,2,16,2048]{4,3,2,0,1:T(8,128)S(1)}, f32[2,1,2,16,2048]{4,3,2,0,1:T(8,128)S(1)}, u32[]{:S(2)}, u32[]{:S(2)}) collective-permute-start(f32[2,1,2,16,2048]{4,3,2,0,1:T(8,128)S(1)} %get-tuple-element.43), channel_id=1, source_target_pairs={{0,64},{64,128},{128,192},{192,256},{256,320},{320,384},{384,448},... | collective-permute-start | bytes 1572872 | tf_op jit(solution)/shard_map/ppermute | solution.py:29
  188.1 17.3 %collective-permute-start.14 = (f32[2,1,2,16,2048]{4,3,2,0,1:T(8,128)}, f32[2,1,2,16,2048]{4,3,2,0,1:T(8,128)}, u32[]{:S(2)}, u32[]{:S(2)}) collective-permute-start(f32[2,1,2,16,2048]{4,3,2,0,1:T(8,128)} %get-tuple-element.42), channel_id=1, source_target_pairs={{0,448},{64,0},{128,64},{192,128},{256,192},{320,256},{384,320},{4... | collective-permute-start | bytes 1572872 | tf_op jit(solution)/shard_map/ppermute | solution.py:29
  202.5 23.5 %copy-start.8 = (bf16[256,16,128]{0,2,1:T(8,128)(2,1)S(1)}, bf16[256,16,128]{0,2,1:T(8,128)(2,1)}, u32[]{:S(2)}) copy-start(bf16[256,16,128]{0,2,1:T(8,128)(2,1)} %copy-done.7) | copy-start | bytes 3145732
  202.5 15.6 %collective-permute-start.11 = (f32[2,1,2,16,2048]{4,3,2,0,1:T(8,128)S(1)}, f32[2,1,2,16,2048]{4,3,2,0,1:T(8,128)}, u32[]{:S(2)}, u32[]{:S(2)}) collective-permute-start(f32[2,1,2,16,2048]{4,3,2,0,1:T(8,128)S(1)} %bitcast_add_fusion.6), channel_id=1, source_target_pairs={{0,64},{64,128},{128,192},{192,256},{256,320},{320,384},{384,448},... | collective-permute-start | bytes 1572872 | tf_op jit(solution)/shard_map/ppermute | solution.py:29
  220.7 13.5 %collective-permute-start.15 = (f32[2,1,2,16,2048]{4,3,2,0,1:T(8,128)}, f32[2,1,2,16,2048]{4,3,2,0,1:T(8,128)S(1)}, u32[]{:S(2)}, u32[]{:S(2)}) collective-permute-start(f32[2,1,2,16,2048]{4,3,2,0,1:T(8,128)} %get-tuple-element.40), channel_id=1, source_target_pairs={{0,448},{64,0},{128,64},{192,128},{256,192},{320,256},{384,320},{4... | collective-permute-start | bytes 1572872 | tf_op jit(solution)/shard_map/ppermute | solution.py:29
  222.6 14.7 %collective-permute-start.12 = (f32[2,1,2,16,2048]{4,3,2,0,1:T(8,128)}, f32[2,1,2,16,2048]{4,3,2,0,1:T(8,128)}, u32[]{:S(2)}, u32[]{:S(2)}) collective-permute-start(f32[2,1,2,16,2048]{4,3,2,0,1:T(8,128)} %get-tuple-element.41), channel_id=1, source_target_pairs={{0,64},{64,128},{128,192},{192,256},{256,320},{320,384},{384,448},... | collective-permute-start | bytes 1572872 | tf_op jit(solution)/shard_map/ppermute | solution.py:29
  232.1 17.7 %collective-permute-start.18 = (f32[160,16,16]{0,2,1:T(8,128)S(1)}, f32[160,16,16]{0,2,1:T(8,128)S(1)}, u32[]{:S(2)}, u32[]{:S(2)}) collective-permute-start(f32[160,16,16]{0,2,1:T(8,128)S(1)} %pad_maximum_fusion.2), channel_id=1, source_target_pairs={{0,256},{64,320},{128,384},{192,448},{256,0},{320,64},{384,128},{4... | collective-permute-start | bytes 491528 | tf_op jit(solution)/shard_map/ppermute | solution.py:34
  239.6 37.6 %collective-permute-start.16 = (f32[2,1,2,16,2048]{4,3,2,0,1:T(8,128)}, f32[2,1,2,16,2048]{4,3,2,0,1:T(8,128)S(1)}, u32[]{:S(2)}, u32[]{:S(2)}) collective-permute-start(f32[2,1,2,16,2048]{4,3,2,0,1:T(8,128)} %get-tuple-element.38), channel_id=1, source_target_pairs={{0,448},{64,0},{128,64},{192,128},{256,192},{320,256},{384,320},{4... | collective-permute-start | bytes 1572872 | tf_op jit(solution)/shard_map/ppermute | solution.py:29
  241.5 35.7 %collective-permute-start.13 = (f32[2,1,2,16,2048]{4,3,2,0,1:T(8,128)S(1)}, f32[2,1,2,16,2048]{4,3,2,0,1:T(8,128)S(1)}, u32[]{:S(2)}, u32[]{:S(2)}) collective-permute-start(f32[2,1,2,16,2048]{4,3,2,0,1:T(8,128)S(1)} %get-tuple-element.39), channel_id=1, source_target_pairs={{0,64},{64,128},{128,192},{192,256},{256,320},{320,384},{384,448},... | collective-permute-start | bytes 1572872 | tf_op jit(solution)/shard_map/ppermute | solution.py:29
  249.8 32.1 %copy-start.11 = (bf16[256,16,128]{0,2,1:T(8,128)(2,1)S(1)}, bf16[256,16,128]{0,2,1:T(8,128)(2,1)}, u32[]{:S(2)}) copy-start(bf16[256,16,128]{0,2,1:T(8,128)(2,1)} %copy-done.10) | copy-start | bytes 3145732
  249.8 14.4 %collective-permute-start.19 = (f32[160,16,16]{0,2,1:T(8,128)S(1)}, f32[160,16,16]{0,2,1:T(8,128)S(1)}, u32[]{:S(2)}, u32[]{:S(2)}) collective-permute-start(f32[160,16,16]{0,2,1:T(8,128)S(1)} %fusion.25), channel_id=1, source_target_pairs={{0,128},{64,192},{128,0},{192,64},{256,384},{320,448},{384,256},{4... | collective-permute-start | bytes 491528 | tf_op jit(solution)/shard_map/ppermute | solution.py:34
  264.3 10.0 %collective-permute-start.20 = (f32[160,16,16]{0,2,1:T(8,128)S(1)}, f32[160,16,16]{0,2,1:T(8,128)}, u32[]{:S(2)}, u32[]{:S(2)}) collective-permute-start(f32[160,16,16]{0,2,1:T(8,128)S(1)} %add.211), channel_id=1, source_target_pairs={{0,64},{64,0},{128,192},{192,128},{256,320},{320,256},{384,448},{4... | collective-permute-start | bytes 491528 | tf_op jit(solution)/shard_map/ppermute | solution.py:34
  275.3 9.8 %collective-permute-start.21 = (f32[160,16,16]{0,2,1:T(8,128)S(1)}, f32[160,16,16]{0,2,1:T(8,128)}, u32[]{:S(2)}, u32[]{:S(2)}) collective-permute-start(f32[160,16,16]{0,2,1:T(8,128)S(1)} %add.212), channel_id=1, source_target_pairs={{0,32},{32,0},{1,33},{33,1},{2,34},{34,2},{3,35},{35,3},{4,36},{36... | collective-permute-start | bytes 491528 | tf_op jit(solution)/shard_map/ppermute | solution.py:34
  278.4 17.9 %copy-start.6 = (bf16[512,512]{1,0:T(8,128)(2,1)S(1)}, bf16[512,512]{1,0:T(8,128)(2,1)}, u32[]{:S(2)}) copy-start(bf16[512,512]{1,0:T(8,128)(2,1)} %copy-done.5) | copy-start | bytes 1572868
  278.4 20.4 %collective-permute-start.17 = (f32[1,2,16,2048]{3,2,1,0:T(8,128)S(1)}, f32[1,2,16,2048]{3,2,1,0:T(8,128)S(1)}, u32[]{:S(2)}, u32[]{:S(2)}) collective-permute-start(f32[1,2,16,2048]{3,2,1,0:T(8,128)S(1)} %dynamic-slice_bitcast_fusion.2), channel_id=1, source_target_pairs={{0,32},{32,0},{1,33},{33,1},{2,34},{34,2},{3,35},{35,3},{4,36},{36... | collective-permute-start | bytes 786440 | tf_op jit(solution)/shard_map/ppermute | solution.py:34
  285.1 15.2 %copy-start.1 = (bf16[256,512]{1,0:T(8,128)(2,1)S(1)}, bf16[256,512]{1,0:T(8,128)(2,1)}, u32[]{:S(2)}) copy-start(bf16[256,512]{1,0:T(8,128)(2,1)} %param.6) | copy-start | bytes 786436
  286.1 11.4 %collective-permute-start.22 = (f32[160,16,16]{0,2,1:T(8,128)S(1)}, f32[160,16,16]{0,2,1:T(8,128)S(1)}, u32[]{:S(2)}, u32[]{:S(2)}) collective-permute-start(f32[160,16,16]{0,2,1:T(8,128)S(1)} %add.213), channel_id=1, source_target_pairs={{0,16},{16,0},{1,17},{17,1},{2,18},{18,2},{3,19},{19,3},{4,20},{20... | collective-permute-start | bytes 491528 | tf_op jit(solution)/shard_map/ppermute | solution.py:34
